TPU v7x, 32 devices: a whole 2x2x4 slice. The times are simulated.
32 devices in a mesh: grp: 2 (over y), chan: 4 (over z), tile: 2 (over x), sub: 2 (over core).
Axes of the slice: x: 2, y: 2, z: 4, core: 2. Of those that a mesh axis runs over, the one named last changes fastest.
Arguments:
- dirty: bfloat16 [128, 32, 8, 128], P(('grp', 'chan'), None, ('tile', 'sub')), parts along dimension 0, may hold values from -6 to 6
- cotangent: bfloat16 [128, 32, 8, 128], P(('grp', 'chan'), None, ('tile', 'sub')), parts along dimension 0, may hold values from -6 to 6
- spatial_kernel: float32 [32, 25], replicated, may hold values from -1.25 to 1.25
- feature_mix: bfloat16 [32, 32], replicated, may hold values from -1 to 1
- spectral_kernel: bfloat16 [7, 32, 32], replicated, may hold values from -0.375 to 0.375
- freq_table: int32 [64], replicated, may hold values from 0 to 63, as said below
Outputs:
- restored: bfloat16 [128, 32, 8, 128], P(('grp', 'chan'), None, ('tile', 'sub')), parts along dimension 0
- dirty_grad: bfloat16 [128, 32, 8, 128], P(('grp', 'chan'), None, ('tile', 'sub')), parts along dimension 0
- spatial_grad: float32 [64, 25], P('grp'), parts along dimension 0
- mix_grad: float32 [64, 32], P('grp'), parts along dimension 0
- spectral_grad: float32 [14, 32, 32], P('grp'), parts along dimension 0
There are 2 independent parts, one for each index of `grp`. A program takes and returns all parts, laid end to end along the dimension named above; an argument that names none is the same for every part. Nothing has to cross between parts.
Inputs may be any that keep to these rules, and one draw needn't show every extreme that they name: freq_table is a permutation of 0..63; the stored channels d * 16 to (d+1) * 16 - 1 hold exactly the frequencies m * 4 + d for m in 0..15, in any order.
All inputs are finite; a program needn't handle non-finite values.
Results may differ from a plain program's by a relative error of at most 0.0062.
Values may be sent and summed in bfloat16 or wider, within the bound.
No kernel may reach another device: no remote copies, remote signals or barrier semaphores. Data moves between devices by JAX's collectives and lax.ppermute only.
A program may use at most 64 MiB of HBM per device.

v0:
```python
import math

import jax
import jax.numpy as jnp
from jax import lax
from jax.sharding import PartitionSpec as P


def padded(block, sides, width):
    for axis, dim in sides:
        count = lax.axis_size(axis)
        forward = [(i, i + 1) for i in range(count - 1)]
        backward = [(target, source) for source, target in forward]
        low = lax.ppermute(
            lax.slice_in_dim(block, block.shape[dim] - width, None, axis=dim), axis, forward
        )
        high = lax.ppermute(lax.slice_in_dim(block, 0, width, axis=dim), axis, backward)
        block = jnp.concatenate([low, block, high], axis=dim)
    return block


def passed_along(block, axis, distance):
    devices = range(lax.axis_size(axis))
    route = [((i - distance) % len(devices), i) for i in devices]
    return lax.ppermute(block, axis, route)


def silu_slope(value):
    sig = jax.nn.sigmoid(value)
    return sig * (1.0 + value * (1.0 - sig))


def move_down(array):
    return jnp.pad(array, ((1, 0), (0, 0), (0, 0)))[:-1]


def move_up(array):
    return jnp.pad(array, ((0, 1), (0, 0), (0, 0)))[1:]


def local(dirty, cotangent, spatial_kernel, feature_mix, spectral_kernel, freq_table):
    chans, feats, rows, cols = dirty.shape
    taps = spectral_kernel.shape[0]
    half = (taps - 1) // 2
    n_chan = lax.axis_size("chan")
    n_rows = lax.axis_size("tile") * lax.axis_size("sub")
    scale = 1.0 / math.sqrt(chans * n_chan * rows * n_rows * cols)
    pixels = rows * cols
    extended = padded(dirty, ((("tile", "sub"), 2),), 2)
    xpad = jnp.pad(extended, ((0, 0), (0, 0), (0, 0), (2, 2)))
    xpad32 = xpad.astype(jnp.float32)
    total = jnp.zeros(dirty.shape, jnp.float32)
    for i in range(5):
        for j in range(5):
            total = (
                total
                + spatial_kernel[:, i * 5 + j][None, :, None, None]
                * xpad32[:, :, i : i + rows, j : j + cols]
            )
    smooth = total.astype(jnp.bfloat16)
    mixed = jnp.einsum("gf,cfhw->cghw", feature_mix, smooth, preferred_element_type=jnp.float32)
    hidden = jax.nn.silu(mixed).astype(jnp.bfloat16)
    hidden_flat = hidden.reshape(chans, feats, pixels)
    grad_flat = cotangent.reshape(chans, feats, pixels)
    device = lax.axis_index("chan")
    start = device * chans
    own = lax.dynamic_slice_in_dim(freq_table, start, chans) // n_chan
    order = jnp.zeros((chans,), jnp.int32).at[own].set(jnp.arange(chans, dtype=jnp.int32))
    h_sorted = hidden_flat[order]
    g_sorted = grad_flat[order]
    fwd_acc = jnp.einsum(
        "gf,mfp->mgp", spectral_kernel[half], h_sorted, preferred_element_type=jnp.float32
    )
    bwd_acc = jnp.einsum(
        "gf,mgp->mfp", spectral_kernel[half], g_sorted, preferred_element_type=jnp.float32
    )
    grad_taps = [None] * taps
    grad_taps[half] = jnp.einsum(
        "mgp,mfp->gf", g_sorted, h_sorted, preferred_element_type=jnp.float32
    )
    for dist in range(1, half + 1):
        for sign in (-1, 1):
            h_far, g_far = passed_along((h_sorted, g_sorted), "chan", -sign * dist)
            if sign < 0:
                wrapped = device < dist
                h_near = jnp.where(wrapped, move_down(h_far), h_far)
                g_near = jnp.where(wrapped, move_down(g_far), g_far)
            else:
                wrapped = device + dist >= n_chan
                h_near = jnp.where(wrapped, move_up(h_far), h_far)
                g_near = jnp.where(wrapped, move_up(g_far), g_far)
            offset = sign * dist
            fwd_acc = fwd_acc + jnp.einsum(
                "gf,mfp->mgp",
                spectral_kernel[half + offset],
                h_near,
                preferred_element_type=jnp.float32,
            )
            bwd_acc = bwd_acc + jnp.einsum(
                "gf,mgp->mfp",
                spectral_kernel[half - offset],
                g_near,
                preferred_element_type=jnp.float32,
            )
            grad_taps[half + offset] = jnp.einsum(
                "mgp,mfp->gf", g_sorted, h_near, preferred_element_type=jnp.float32
            )
    spec_grad = jnp.stack(grad_taps, 0)
    spec_flat = fwd_acc.astype(jnp.bfloat16)[own]
    back_flat = bwd_acc.astype(jnp.bfloat16)[own]
    spec = spec_flat.reshape(chans, feats, rows, cols)
    back = back_flat.reshape(chans, feats, rows, cols)
    restored = (dirty.astype(jnp.float32) + spec.astype(jnp.float32)).astype(jnp.bfloat16)
    dmixed = (back.astype(jnp.float32) * silu_slope(mixed)).astype(jnp.bfloat16)
    mix_term = jnp.einsum("cghw,cfhw->gf", dmixed, smooth, preferred_element_type=jnp.float32)
    dsmooth = jnp.einsum(
        "gf,cghw->cfhw", feature_mix, dmixed, preferred_element_type=jnp.float32
    ).astype(jnp.bfloat16)
    grad_ext = padded(dsmooth, ((("tile", "sub"), 2),), 2)
    dpad32 = jnp.pad(grad_ext, ((0, 0), (0, 0), (0, 0), (2, 2))).astype(jnp.float32)
    conv = jnp.zeros(dirty.shape, jnp.float32)
    terms = []
    for i in range(5):
        for j in range(5):
            conv = (
                conv
                + spatial_kernel[:, i * 5 + j][None, :, None, None]
                * dpad32[:, :, 4 - i : 4 - i + rows, 4 - j : 4 - j + cols]
            )
            terms.append(
                jnp.einsum(
                    "cfhw,cfhw->f",
                    dsmooth,
                    xpad[:, :, i : i + rows, j : j + cols],
                    preferred_element_type=jnp.float32,
                )
            )
    kernel_term = jnp.stack(terms, 1)
    dirty_grad = (cotangent.astype(jnp.float32) + conv).astype(jnp.bfloat16)
    kgrad, mgrad, sgrad = lax.psum((kernel_term, mix_term, spec_grad), ("chan", "tile", "sub"))
    return (restored, dirty_grad, kgrad * scale, mgrad * scale, sgrad * scale)


def solution(mesh):
    in_specs = (
        P(("grp", "chan"), None, ("tile", "sub"), None),
        P(("grp", "chan"), None, ("tile", "sub"), None),
        P(),
        P(),
        P(),
        P(),
    )
    out_specs = (
        P(("grp", "chan"), None, ("tile", "sub"), None),
        P(("grp", "chan"), None, ("tile", "sub"), None),
        P("grp", None),
        P("grp", None),
        P("grp", None, None),
    )
    return jax.shard_map(local, mesh=mesh, in_specs=in_specs, out_specs=out_specs, check_vma=False)
```

profile of v0, /device:TPU:0, one launch (start us, length us, event | category | flops | bytes accessed | tf_op | source)
XLA Modules:
  0.0 144.2 jit_solution(15052567029493651229)
XLA Ops:
  0.7 0.8 compare_select_fusion.1
  1.4 0.6 scatter_custom_fusion
  2.1 1.1 reshape.48
  3.8 4.1 %collective-permute-start.7 = (bf16[16,32,256]{2,1,0:T(8,128)(2,1)S(1)}, bf16[16,32,256]{2,1,0:T(8,128)(2,1)S(1)}, u32[]{:S(2)}, u32[]{:S(2)}) collective-permute-start(bf16[16,32,256]{2,1,0:T(8,128)(2,1)S(1)} %gather_fusion.2), channel_id=1, source_target_pairs={{8,0},{12,4},{0,8},{4,12},{9,1},{13,5},{1,9},{5,13},{10,2},{14,6},... | collective-permute-start | bytes 786440 | tf_op jit(solution)/shard_map/ppermute | solution.py:25
  7.9 1.3 collective-permute-start.6
  9.2 0.7 collective-permute-start.5
  9.9 1.0 copy.27
  10.9 1.3 collective-permute-start.1
  12.2 3.0 %collective-permute-start = (bf16[16,32,2,128]{3,1,2,0:T(8,128)(2,1)S(1)}, bf16[16,32,2,128]{3,1,2,0:T(8,128)(2,1)S(1)}, u32[]{:S(2)}, u32[]{:S(2)}) collective-permute-start(bf16[16,32,2,128]{3,1,2,0:T(8,128)(2,1)S(1)} %copy.27), channel_id=1, source_target_pairs={{0,1},{1,2},{2,3},{4,5},{5,6},{6,7},{8,9},{9,10},{10,11},{12,13},{... | collective-permute-start | bytes 786440 | tf_op jit(solution)/shard_map/ppermute | solution.py:14
  15.3 1.2 slice_reduce_fusion.23
  16.5 2.5 %slice_reduce_fusion.24 = (f32[32]{0:T(128)S(1)}, f32[32]{0:T(128)S(1)}, f32[32]{0:T(128)S(1)}, f32[32]{0:T(128)S(1)}, f32[32]{0:T(128)S(1)}, /*index=5*/f32[32]...) fusion(f32[32,25]{1,0:T(8,128)} %param.8), kind=kLoop, calls=%fused_computation.293 | loop fusion | bytes 4864 | tf_op jit(solution)/shard_map/slice | solution.py:57
  19.0 1.0 fusion.159
  20.0 1.5 %collective-permute-done.7 = bf16[16,32,256]{2,1,0:T(8,128)(2,1)S(1)} collective-permute-done((bf16[16,32,256]{2,1,0:T(8,128)(2,1)S(1)}, bf16[16,32,256]{2,1,0:T(8,128)(2,1)S(1)}, u32[]{:S(2)}, u32[]{:S(2)}) %collective-permute-start.7) | collective-permute-done | bytes 262176 | tf_op jit(solution)/shard_map/ppermute | solution.py:25
  21.5 1.0 fusion.109
  22.8 3.9 %collective-permute-done.5 = bf16[16,32,256]{2,1,0:T(8,128)(2,1)S(1)} collective-permute-done((bf16[16,32,256]{2,1,0:T(8,128)(2,1)S(1)}, bf16[16,32,256]{2,1,0:T(8,128)(2,1)S(1)}, u32[]{:S(2)}, u32[]{:S(2)}) %collective-permute-start.5) | collective-permute-done | bytes 262176 | tf_op jit(solution)/shard_map/ppermute | solution.py:25
  27.9 0.6 gather_fusion.3
  28.5 0.8 select_maximum_fusion.2
  29.4 3.0 %fusion.74 = bf16[16,32,2,128]{3,1,2,0:T(8,128)(2,1)S(1)} fusion(f32[16,32,6,132]{3,1,2,0:T(8,128)S(1)} %get-tuple-element.72, f32[32]{0:T(128)S(1)} %get-tuple-element.66, f32[32]{0:T(128)S(1)} %get-tuple-element.67, f32[32]{0:T(128)S(1)} %get-tuple-element.44, f32[32]{0:T(128)S(1)} %get-tuple-element.45, f32[32]{0:T(128)S(1)} %get-tuple-element.46, ...), kind=kLoop, calls=%fused_computation.150 | loop fusion | flops 6553600 | bytes 13372544 | tf_op jit(solution)/shard_map/convert_element_type | solution.py:60
  32.4 1.1 fusion.46
  34.2 7.2 %collective-permute-start.4 = (bf16[16,32,256]{2,1,0:T(8,128)(2,1)S(1)}, bf16[16,32,256]{2,1,0:T(8,128)(2,1)}, u32[]{:S(2)}, u32[]{:S(2)}) collective-permute-start(bf16[16,32,256]{2,1,0:T(8,128)(2,1)S(1)} %gather_fusion), channel_id=1, source_target_pairs={{8,0},{12,4},{0,8},{4,12},{9,1},{13,5},{1,9},{5,13},{10,2},{14,6},... | collective-permute-start | bytes 786440 | tf_op jit(solution)/shard_map/ppermute | solution.py:25
  41.8 1.6 %collective-permute-start.2 = (bf16[16,32,256]{2,1,0:T(8,128)(2,1)S(1)}, bf16[16,32,256]{2,1,0:T(8,128)(2,1)}, u32[]{:S(2)}, u32[]{:S(2)}) collective-permute-start(bf16[16,32,256]{2,1,0:T(8,128)(2,1)S(1)} %gather_fusion), channel_id=1, source_target_pairs={{12,0},{0,4},{4,8},{8,12},{13,1},{1,5},{5,9},{9,13},{14,2},{2,6},{... | collective-permute-start | bytes 786440 | tf_op jit(solution)/shard_map/ppermute | solution.py:25
  43.6 2.5 %fusion.44 = (f32[32]{0:T(128)}, f32[32]{0:T(128)}, f32[32]{0:T(128)}, f32[32]{0:T(128)}, f32[32]{0:T(128)}, /*index=5*/f32[32]{0:T(128)}, bf16[16,2,128,32]{2,3,1,0:T(8,128)(2,1)S(1)}) fusion(bf16[16,32,6,132]{3,1,2,0:T(8,128)(2,1)S(1)} %get-tuple-element.71, bf16[16,32,2,128]{3,1,2,0:T(8,128)(2,1)} %copy-done.7, ...), kind=kOutput, calls=%fused_computation.93 | convolution fusion | flops 11272000 | bytes 1837824 | tf_op jit(solution)/shard_map/gf,cghw->cfhw/dot_general | solution.py:116
  46.0 2.3 %fusion.45 = (f32[32]{0:T(128)}, f32[32]{0:T(128)}, f32[32]{0:T(128)}, f32[32]{0:T(128)}, f32[32]{0:T(128)}, /*index=5*/f32[32]{0:T(128)}, f32[32]{0:T(128)}, f3...) fusion(bf16[16,32,6,132]{3,1,2,0:T(8,128)(2,1)S(1)} %get-tuple-, ...), kind=kLoop, calls=%fused_computation.94 | loop fusion | flops 7208384 | bytes 4983040 | tf_op jit(solution)/shard_map/cfhw,cfhw->f/dot_general | solution.py:131
  48.4 1.3 collective-permute-start.9
  49.7 3.0 %collective-permute-start.8 = (bf16[16,32,2,128]{3,1,2,0:T(8,128)(2,1)S(1)}, bf16[16,32,2,128]{3,1,2,0:T(8,128)(2,1)S(1)}, u32[]{:S(2)}, u32[]{:S(2)}) collective-permute-start(bf16[16,32,2,128]{3,1,2,0:T(8,128)(2,1)S(1)} %bitcast.338), channel_id=1, source_target_pairs={{0,1},{1,2},{2,3},{4,5},{5,6},{6,7},{8,9},{9,10},{10,11},{12,13},{... | collective-permute-start | bytes 786440 | tf_op jit(solution)/shard_map/ppermute | solution.py:14
  53.0 0.8 multiply_reduce_fusion
  53.8 2.8 %stack.127 = f32[32,25]{0,1:T(8,128)S(1)} concatenate(f32[32,1]{0,1:T(1,128)} %bitcast.361, f32[32,1]{0,1:T(1,128)} %bitcast.359, f32[32,1]{0,1:T(1,128)} %bitcast.362, f32[32,1]{0,1:T(1,128)} %bitcast.358, f32[32,1]{0,1:T(1,128)} %bitcast.357, f32[32,1]{0,1:T(1,128)} %bitcast.356, f32[32,1]{0,1:T(1,128)} %bitcast.355, f32[32,1]{0,1:T(1,128)} %bitcast.363, f32[32,1]{0,1:T(1,128)} %bitcast.354, ...), dimensions={1} | concatenate | bytes 6400 | tf_op jit(solution)/shard_map/stack | solution.py:138
  56.6 3.7 %collective-permute-done.3 = bf16[16,32,256]{2,1,0:T(8,128)(2,1)} collective-permute-done((bf16[16,32,256]{2,1,0:T(8,128)(2,1)S(1)}, bf16[16,32,256]{2,1,0:T(8,128)(2,1)}, u32[]{:S(2)}, u32[]{:S(2)}) %collective-permute-start.3) | collective-permute-done | bytes 262176 | tf_op jit(solution)/shard_map/ppermute | solution.py:25
  60.3 1.3 fusion.21
  61.6 1.3 fusion.20
  63.0 1.3 fusion.19
  64.5 1.3 fusion.17
  65.8 1.3 fusion.16
  67.1 1.3 fusion.15
  68.4 59.4 %all-reduce.14 = (f32[32,25]{0,1:T(8,128)S(1)}, f32[32,32]{1,0:T(8,128)S(1)}, f32[7,32,32]{2,1,0:T(8,128)S(1)}) all-reduce(f32[32,25]{0,1:T(8,128)S(1)} %stack.127, f32[32,32]{1,0:T(8,128)S(1)} %convolution_bitcast_fusion.8, f32[7,32,32]{2,1,0:T(8,128)S(1)} %fusion.15), channel_id=1, replica_groups=mesh['grp'=2,'chan'=4,'tile'=2,'sub'=2] {'chan','tile','sub'}, use_global_device_ids=true, to_apply=%region_1.2 | all-reduce | flops 8992 | bytes 71936 | tf_op jit(solution)/shard_map/psum | solution.py:140
  127.8 0.7 broadcast_multiply_fusion
  128.5 1.3 fusion.130
  129.8 1.3 fusion.136
  131.1 1.3 fusion.139
  132.4 1.3 fusion.133
  133.7 1.3 convolution_add_fusion.1
  135.0 1.3 fusion.14
  136.3 0.6 broadcast_multiply_fusion.1
  137.8 0.7 copy.44
  138.5 1.0 add_convert_fusion
  139.5 0.7 fusion.1
  140.3 3.0 %fusion.49 = bf16[16,32,2,128]{3,1,2,0:T(8,128)(2,1)S(1)} fusion(f32[16,32,6,132]{3,1,2,0:T(8,128)S(1)} %fusion.1, bf16[16,32,2,128]{3,2,1,0:T(2,128)(2,1)S(1)} %copy-done.2, f32[32]{0:T(128)S(1)} %get-tuple-element.66, f32[32]{0:T(128)S(1)} %get-tuple-element.67, f32[32]{0:T(128)S(1)} %get-tuple-element.44, f32[32]{0:T(128)S(1)} %get-tuple-element.45, ...), kind=kLoop, calls=%fused_computation.100 | loop fusion | flops 6815744 | bytes 13634688 | tf_op jit(solution)/shard_map/convert_element_type | solution.py:139
  143.3 0.9 copy.43
  (73 shorter events, 4.7 us)
Async XLA Ops:
  0.6 31.8 %copy-start = (bf16[32,32]{1,0:T(8,128)(2,1)S(1)}, bf16[32,32]{1,0:T(8,128)(2,1)}, u32[]{:S(2)}) copy-start(bf16[32,32]{1,0:T(8,128)(2,1)} %param.9) | copy-start | bytes 6148
  0.6 21.9 %copy-start.8 = (bf16[7,32,32]{2,1,0:T(8,128)(2,1)S(1)}, bf16[7,32,32]{2,1,0:T(8,128)(2,1)}, u32[]{:S(2)}) copy-start(bf16[7,32,32]{2,1,0:T(8,128)(2,1)} %param.10) | copy-start | bytes 43012
  3.8 17.8 %collective-permute-start.7 = (bf16[16,32,256]{2,1,0:T(8,128)(2,1)S(1)}, bf16[16,32,256]{2,1,0:T(8,128)(2,1)S(1)}, u32[]{:S(2)}, u32[]{:S(2)}) collective-permute-start(bf16[16,32,256]{2,1,0:T(8,128)(2,1)S(1)} %gather_fusion.2), channel_id=1, source_target_pairs={{8,0},{12,4},{0,8},{4,12},{9,1},{13,5},{1,9},{5,13},{10,2},{14,6},... | collective-permute-start | bytes 786440 | tf_op jit(solution)/shard_map/ppermute | solution.py:25
  7.9 19.0 %collective-permute-start.6 = (bf16[16,32,256]{2,1,0:T(8,128)(2,1)S(1)}, bf16[16,32,256]{2,1,0:T(8,128)(2,1)S(1)}, u32[]{:S(2)}, u32[]{:S(2)}) collective-permute-start(bf16[16,32,256]{2,1,0:T(8,128)(2,1)S(1)} %gather_fusion.2), channel_id=1, source_target_pairs={{4,0},{8,4},{12,8},{0,12},{5,1},{9,5},{13,9},{1,13},{6,2},{10,6},{... | collective-permute-start | bytes 786440 | tf_op jit(solution)/shard_map/ppermute | solution.py:25
  9.2 17.4 %collective-permute-start.5 = (bf16[16,32,256]{2,1,0:T(8,128)(2,1)S(1)}, bf16[16,32,256]{2,1,0:T(8,128)(2,1)S(1)}, u32[]{:S(2)}, u32[]{:S(2)}) collective-permute-start(bf16[16,32,256]{2,1,0:T(8,128)(2,1)S(1)} %gather_fusion.2), channel_id=1, source_target_pairs={{12,0},{0,4},{4,8},{8,12},{13,1},{1,5},{5,9},{9,13},{14,2},{2,6},{... | collective-permute-start | bytes 786440 | tf_op jit(solution)/shard_map/ppermute | solution.py:25
  10.9 17.6 %copy-start.3 = (bf16[16,32,2,128]{3,1,2,0:T(8,128)(2,1)}, bf16[16,32,2,128]{3,1,2,0:T(8,128)(2,1)S(1)}, u32[]{:S(2)}) copy-start(bf16[16,32,2,128]{3,1,2,0:T(8,128)(2,1)S(1)} %copy.27) | copy-start | bytes 786436
  10.9 17.6 %collective-permute-start.1 = (bf16[16,32,2,128]{3,1,2,0:T(8,128)(2,1)S(1)}, bf16[16,32,2,128]{3,1,2,0:T(8,128)(2,1)S(1)}, u32[]{:S(2)}, u32[]{:S(2)}) collective-permute-start(bf16[16,32,2,128]{3,1,2,0:T(8,128)(2,1)S(1)} %copy.27), channel_id=1, source_target_pairs={{1,0},{2,1},{3,2},{5,4},{6,5},{7,6},{9,8},{10,9},{11,10},{13,12},{... | collective-permute-start | bytes 786440 | tf_op jit(solution)/shard_map/ppermute | solution.py:17
  12.2 16.3 %collective-permute-start = (bf16[16,32,2,128]{3,1,2,0:T(8,128)(2,1)S(1)}, bf16[16,32,2,128]{3,1,2,0:T(8,128)(2,1)S(1)}, u32[]{:S(2)}, u32[]{:S(2)}) collective-permute-start(bf16[16,32,2,128]{3,1,2,0:T(8,128)(2,1)S(1)} %copy.27), channel_id=1, source_target_pairs={{0,1},{1,2},{2,3},{4,5},{5,6},{6,7},{8,9},{9,10},{10,11},{12,13},{... | collective-permute-start | bytes 786440 | tf_op jit(solution)/shard_map/ppermute | solution.py:14
  27.8 1.5 %copy-start.9 = (f32[32]{0:T(128)S(1)}, f32[32]{0:T(128)}, u32[]{:S(2)}) copy-start(f32[32]{0:T(128)} %get-tuple-element.55) | copy-start | bytes 388
  27.8 1.5 %copy-start.11 = (f32[32]{0:T(128)S(1)}, f32[32]{0:T(128)}, u32[]{:S(2)}) copy-start(f32[32]{0:T(128)} %get-tuple-element.56) | copy-start | bytes 388
  27.8 1.5 %copy-start.13 = (f32[32]{0:T(128)S(1)}, f32[32]{0:T(128)}, u32[]{:S(2)}) copy-start(f32[32]{0:T(128)} %get-tuple-element.57) | copy-start | bytes 388
  27.8 1.5 %copy-start.15 = (f32[32]{0:T(128)S(1)}, f32[32]{0:T(128)}, u32[]{:S(2)}) copy-start(f32[32]{0:T(128)} %get-tuple-element.58) | copy-start | bytes 388
  27.9 1.5 %copy-start.17 = (f32[32]{0:T(128)S(1)}, f32[32]{0:T(128)}, u32[]{:S(2)}) copy-start(f32[32]{0:T(128)} %get-tuple-element.59) | copy-start | bytes 388
  27.9 1.5 %copy-start.19 = (f32[32]{0:T(128)S(1)}, f32[32]{0:T(128)}, u32[]{:S(2)}) copy-start(f32[32]{0:T(128)} %get-tuple-element.60) | copy-start | bytes 388
  27.9 1.5 %copy-start.21 = (f32[32]{0:T(128)S(1)}, f32[32]{0:T(128)}, u32[]{:S(2)}) copy-start(f32[32]{0:T(128)} %get-tuple-element.61) | copy-start | bytes 388
  28.5 3.9 %copy-start.6 = (bf16[16,32,2,128]{3,1,2,0:T(8,128)(2,1)}, bf16[16,32,2,128]{3,1,2,0:T(8,128)(2,1)S(1)}, u32[]{:S(2)}) copy-start(bf16[16,32,2,128]{3,1,2,0:T(8,128)(2,1)S(1)} %collective-permute-done.1) | copy-start | bytes 786436
  28.5 0.8 copy-start.7
  32.4 11.1 %copy-start.4 = (bf16[16,32,2,128]{3,1,2,0:T(8,128)(2,1)S(1)}, bf16[16,32,2,128]{3,1,2,0:T(8,128)(2,1)}, u32[]{:S(2)}) copy-start(bf16[16,32,2,128]{3,1,2,0:T(8,128)(2,1)} %copy-done.3) | copy-start | bytes 786436
  34.2 27.5 %collective-permute-start.4 = (bf16[16,32,256]{2,1,0:T(8,128)(2,1)S(1)}, bf16[16,32,256]{2,1,0:T(8,128)(2,1)}, u32[]{:S(2)}, u32[]{:S(2)}) collective-permute-start(bf16[16,32,256]{2,1,0:T(8,128)(2,1)S(1)} %gather_fusion), channel_id=1, source_target_pairs={{8,0},{12,4},{0,8},{4,12},{9,1},{13,5},{1,9},{5,13},{10,2},{14,6},... | collective-permute-start | bytes 786440 | tf_op jit(solution)/shard_map/ppermute | solution.py:25
  41.3 19.0 %collective-permute-start.3 = (bf16[16,32,256]{2,1,0:T(8,128)(2,1)S(1)}, bf16[16,32,256]{2,1,0:T(8,128)(2,1)}, u32[]{:S(2)}, u32[]{:S(2)}) collective-permute-start(bf16[16,32,256]{2,1,0:T(8,128)(2,1)S(1)} %gather_fusion), channel_id=1, source_target_pairs={{4,0},{8,4},{12,8},{0,12},{5,1},{9,5},{13,9},{1,13},{6,2},{10,6},{... | collective-permute-start | bytes 786440 | tf_op jit(solution)/shard_map/ppermute | solution.py:25
  41.8 21.2 %collective-permute-start.2 = (bf16[16,32,256]{2,1,0:T(8,128)(2,1)S(1)}, bf16[16,32,256]{2,1,0:T(8,128)(2,1)}, u32[]{:S(2)}, u32[]{:S(2)}) collective-permute-start(bf16[16,32,256]{2,1,0:T(8,128)(2,1)S(1)} %gather_fusion), channel_id=1, source_target_pairs={{12,0},{0,4},{4,8},{8,12},{13,1},{1,5},{5,9},{9,13},{14,2},{2,6},{... | collective-permute-start | bytes 786440 | tf_op jit(solution)/shard_map/ppermute | solution.py:25
  46.0 6.8 %copy-start.5 = (bf16[16,32,2,128]{3,1,2,0:T(8,128)(2,1)S(1)}, bf16[16,32,2,128]{3,1,2,0:T(8,128)(2,1)}, u32[]{:S(2)}) copy-start(bf16[16,32,2,128]{3,1,2,0:T(8,128)(2,1)} %get-tuple-element.73) | copy-start | bytes 786436
  46.0 7.0 %copy-start.1 = (bf16[16,32,2,128]{3,2,1,0:T(2,128)(2,1)S(1)}, bf16[16,32,2,128]{3,2,1,0:T(2,128)(2,1)}, u32[]{:S(2)}) copy-start(bf16[16,32,2,128]{3,2,1,0:T(2,128)(2,1)} %param.6) | copy-start | bytes 786436
  48.4 91.1 %collective-permute-start.9 = (bf16[16,32,2,128]{3,1,2,0:T(8,128)(2,1)S(1)}, bf16[16,32,2,128]{3,1,2,0:T(8,128)(2,1)S(1)}, u32[]{:S(2)}, u32[]{:S(2)}) collective-permute-start(bf16[16,32,2,128]{3,1,2,0:T(8,128)(2,1)S(1)} %bitcast.337), channel_id=1, source_target_pairs={{1,0},{2,1},{3,2},{5,4},{6,5},{7,6},{9,8},{10,9},{11,10},{13,12},{... | collective-permute-start | bytes 786440 | tf_op jit(solution)/shard_map/ppermute | solution.py:17
  49.7 89.8 %collective-permute-start.8 = (bf16[16,32,2,128]{3,1,2,0:T(8,128)(2,1)S(1)}, bf16[16,32,2,128]{3,1,2,0:T(8,128)(2,1)S(1)}, u32[]{:S(2)}, u32[]{:S(2)}) collective-permute-start(bf16[16,32,2,128]{3,1,2,0:T(8,128)(2,1)S(1)} %bitcast.338), channel_id=1, source_target_pairs={{0,1},{1,2},{2,3},{4,5},{5,6},{6,7},{8,9},{9,10},{10,11},{12,13},{... | collective-permute-start | bytes 786440 | tf_op jit(solution)/shard_map/ppermute | solution.py:14
  136.9 3.3 %copy-start.2 = (bf16[16,32,2,128]{3,2,1,0:T(2,128)(2,1)S(1)}, bf16[16,32,2,128]{3,2,1,0:T(2,128)(2,1)}, u32[]{:S(2)}) copy-start(bf16[16,32,2,128]{3,2,1,0:T(2,128)(2,1)} %param.7) | copy-start | bytes 786436
  136.9 3.3 %copy-start.10 = (f32[32]{0:T(128)S(1)}, f32[32]{0:T(128)}, u32[]{:S(2)}) copy-start(f32[32]{0:T(128)} %get-tuple-element.55) | copy-start | bytes 388
  136.9 3.3 %copy-start.12 = (f32[32]{0:T(128)S(1)}, f32[32]{0:T(128)}, u32[]{:S(2)}) copy-start(f32[32]{0:T(128)} %get-tuple-element.56) | copy-start | bytes 388
  136.9 3.3 %copy-start.14 = (f32[32]{0:T(128)S(1)}, f32[32]{0:T(128)}, u32[]{:S(2)}) copy-start(f32[32]{0:T(128)} %get-tuple-element.57) | copy-start | bytes 388
  136.9 3.3 %copy-start.16 = (f32[32]{0:T(128)S(1)}, f32[32]{0:T(128)}, u32[]{:S(2)}) copy-start(f32[32]{0:T(128)} %get-tuple-element.58) | copy-start | bytes 388
  136.9 3.3 %copy-start.18 = (f32[32]{0:T(128)S(1)}, f32[32]{0:T(128)}, u32[]{:S(2)}) copy-start(f32[32]{0:T(128)} %get-tuple-element.59) | copy-start | bytes 388
  136.9 3.3 %copy-start.20 = (f32[32]{0:T(128)S(1)}, f32[32]{0:T(128)}, u32[]{:S(2)}) copy-start(f32[32]{0:T(128)} %get-tuple-element.60) | copy-start | bytes 388
  137.0 3.3 %copy-start.22 = (f32[32]{0:T(128)S(1)}, f32[32]{0:T(128)}, u32[]{:S(2)}) copy-start(f32[32]{0:T(128)} %get-tuple-element.61) | copy-start | bytes 388
where the time goes:
time: 145 us; the launch traced here: 144 us
  blocking collectives  59.4 us (41%)
  starting transfers between devices  24 us (17%)
  matrix products  23.1 us (16%)
  other arithmetic  13.7 us (9%)
  local copies, waits for them, and re-layouts  13.6 us (9%)
  waiting for transfers between devices  9.18 us (6%)
    psum x1, blocking collectives, local(): lax.psum((kernel_term, mix_term, spec_grad), ('chan', 'tile', 'sub'))  59.4 us
    ppermute x6, starting transfers between devices, passed_along(): return lax.ppermute(block, axis, route)  15.3 us
    ppermute x6, waiting for transfers between devices, passed_along(): return lax.ppermute(block, axis, route)  9.17 us
    dot_general x6, matrix products, local(): jnp.einsum('gf,mfp->mgp', spectral_kernel[half + offset], h_near, preferr...  7.81 us
    dot_general x6, matrix products, local(): jnp.einsum('mgp,mfp->gf', g_sorted, h_near, preferred_element_type=jnp.fl...  7.77 us
    ppermute x2, starting transfers between devices, padded(): lax.ppermute(lax.slice_in_dim(block, block.shape[dim] - width, None, axis...  6.09 us
    slice x2, local copies, waits for them, and re-layouts, local(): spatial_kernel[:, i * 5 + j][None, :, None, None]  3.76 us
    dot_general x2, other arithmetic, local(): jnp.einsum('cfhw,cfhw->f', dsmooth, xpad[:, :, i:i + rows, j:j + cols], p...  3.12 us
  transfers between devices with their start and end apart: 10, of which 3 were waited for; matrix products, arithmetic and copies ran while one was open for 26% of the time, Pallas kernels for 0%

commit v1 on v0

--- a/solution.py
+++ b/solution.py
@@ -23,6 +23,19 @@
     devices = range(lax.axis_size(axis))
     route = [((i - distance) % len(devices), i) for i in devices]
     return lax.ppermute(block, axis, route)
+
+
+def all_summed(value, axes):
+    for axis in axes:
+        count = lax.axis_size(axis)
+        if count & (count - 1):
+            value = lax.psum(value, axis)
+            continue
+        step = 1
+        while step < count:
+            value = value + lax.ppermute(value, axis, [(i, i ^ step) for i in range(count)])
+            step *= 2
+    return value
 
 
 def silu_slope(value):
@@ -137,7 +150,13 @@
             )
     kernel_term = jnp.stack(terms, 1)
     dirty_grad = (cotangent.astype(jnp.float32) + conv).astype(jnp.bfloat16)
-    kgrad, mgrad, sgrad = lax.psum((kernel_term, mix_term, spec_grad), ("chan", "tile", "sub"))
+    parts = (kernel_term, mix_term, spec_grad)
+    flat = all_summed(jnp.concatenate([part.reshape(-1) for part in parts]), ("sub", "tile", "chan"))
+    sizes = [part.size for part in parts]
+    kgrad, mgrad, sgrad = (
+        piece.reshape(part.shape)
+        for piece, part in zip(jnp.split(flat, [sizes[0], sizes[0] + sizes[1]]), parts)
+    )
     return (restored, dirty_grad, kgrad * scale, mgrad * scale, sgrad * scale)
 
 

time: 145 us -> 97.2 us (0.67)
  blocking collectives: 59.4 us -> 0 us
  starting transfers between devices: 24 us -> 31.5 us
  waiting for transfers between devices: 9.18 us -> 12.2 us
  local copies, waits for them, and re-layouts: 13.6 us -> 15.5 us
    psum x1 -> x0, blocking collectives: 59.4 us -> none  [local(): lax.psum((kernel_term, mix_term, spec_grad), ('chan', 'tile', 'sub'))]
    ppermute x0 -> x4, starting transfers between devices: none -> 7.32 us  [all_summed(): lax.ppermute(value, axis, [(i, i ^ step) for i in range(count)])]
    ppermute x0 -> x4, waiting for transfers between devices: none -> 3.52 us  [all_summed(): lax.ppermute(value, axis, [(i, i ^ step) for i in range(count)])]
    mul x0 -> x3, local copies, waits for them, and re-layouts: none -> 2.12 us  [local(): return (restored, dirty_grad, kgrad * scale, mgrad * scale, sgrad * scale)]
  transfers between devices with their start and end apart: 10 -> 14, of which waited for: 3 -> 5; matrix products, arithmetic and copies ran while one was open for 26% -> 42% of each run, Pallas kernels for 0% -> 0%
where the time goes in v1:
time: 97.2 us; the launch traced here: 96.3 us
  starting transfers between devices  31.5 us (32%)
  matrix products  23.2 us (24%)
  local copies, waits for them, and re-layouts  15.5 us (16%)
  other arithmetic  12.6 us (13%)
  waiting for transfers between devices  12.2 us (13%)
  between operations  1.33 us (1%)
    ppermute x6, starting transfers between devices, passed_along(): return lax.ppermute(block, axis, route)  15.3 us
    ppermute x6, waiting for transfers between devices, passed_along(): return lax.ppermute(block, axis, route)  8.66 us
    dot_general x6, matrix products, local(): jnp.einsum('gf,mfp->mgp', spectral_kernel[half + offset], h_near, preferr...  7.8 us
    dot_general x6, matrix products, local(): jnp.einsum('mgp,mfp->gf', g_sorted, h_near, preferred_element_type=jnp.fl...  7.8 us
    ppermute x4, starting transfers between devices, all_summed(): lax.ppermute(value, axis, [(i, i ^ step) for i in range(count)])  7.32 us
    ppermute x2, starting transfers between devices, padded(): lax.ppermute(lax.slice_in_dim(block, block.shape[dim] - width, None, axis...  6.27 us
    slice x2, local copies, waits for them, and re-layouts, local(): spatial_kernel[:, i * 5 + j][None, :, None, None]  3.76 us
    ppermute x4, waiting for transfers between devices, all_summed(): lax.ppermute(value, axis, [(i, i ^ step) for i in range(count)])  3.52 us
  transfers between devices with their start and end apart: 14, of which 5 were waited for; matrix products, arithmetic and copies ran while one was open for 42% of the time, Pallas kernels for 0%

profile of v1, /device:TPU:0, one launch (start us, length us, event | category | flops | bytes accessed | tf_op | source)
XLA Modules:
  0.0 96.3 jit_solution(8970294698932594277)
XLA Ops:
  0.7 0.8 compare_select_fusion.1
  2.1 1.1 %reshape.74 = bf16[16,32,256]{2,1,0:T(8,128)(2,1)S(1)} reshape(bf16[16,32,2,128]{3,2,1,0:T(2,128)(2,1)} %param.7) | data formatting | bytes 524288 | tf_op jit(solution)/shard_map/reshape | solution.py:77
  3.8 4.1 %collective-permute-start.7 = (bf16[16,32,256]{2,1,0:T(8,128)(2,1)S(1)}, bf16[16,32,256]{2,1,0:T(8,128)(2,1)S(1)}, u32[]{:S(2)}, u32[]{:S(2)}) collective-permute-start(bf16[16,32,256]{2,1,0:T(8,128)(2,1)S(1)} %gather_fusion.2), channel_id=1, source_target_pairs={{8,0},{12,4},{0,8},{4,12},{9,1},{13,5},{1,9},{5,13},{10,2},{14,6},... | collective-permute-start | bytes 786440 | tf_op jit(solution)/shard_map/ppermute | solution.py:25
  7.9 1.3 %collective-permute-start.6 = (bf16[16,32,256]{2,1,0:T(8,128)(2,1)S(1)}, bf16[16,32,256]{2,1,0:T(8,128)(2,1)S(1)}, u32[]{:S(2)}, u32[]{:S(2)}) collective-permute-start(bf16[16,32,256]{2,1,0:T(8,128)(2,1)S(1)} %gather_fusion.2), channel_id=1, source_target_pairs={{4,0},{8,4},{12,8},{0,12},{5,1},{9,5},{13,9},{1,13},{6,2},{10,6},{... | collective-permute-start | bytes 786440 | tf_op jit(solution)/shard_map/ppermute | solution.py:25
  9.2 0.7 collective-permute-start.5
  9.9 1.0 %copy.26 = bf16[16,32,2,128]{3,1,2,0:T(8,128)(2,1)S(1)} copy(bf16[16,32,2,128]{3,2,1,0:T(2,128)(2,1)} %param.6) | data formatting | bytes 524288 | tf_op args[0]
  10.9 1.3 %collective-permute-start.1 = (bf16[16,32,2,128]{3,1,2,0:T(8,128)(2,1)S(1)}, bf16[16,32,2,128]{3,1,2,0:T(8,128)(2,1)S(1)}, u32[]{:S(2)}, u32[]{:S(2)}) collective-permute-start(bf16[16,32,2,128]{3,1,2,0:T(8,128)(2,1)S(1)} %copy.26), channel_id=1, source_target_pairs={{1,0},{2,1},{3,2},{5,4},{6,5},{7,6},{9,8},{10,9},{11,10},{13,12},{... | collective-permute-start | bytes 786440 | tf_op jit(solution)/shard_map/ppermute | solution.py:17
  12.2 3.0 %collective-permute-start = (bf16[16,32,2,128]{3,1,2,0:T(8,128)(2,1)S(1)}, bf16[16,32,2,128]{3,1,2,0:T(8,128)(2,1)S(1)}, u32[]{:S(2)}, u32[]{:S(2)}) collective-permute-start(bf16[16,32,2,128]{3,1,2,0:T(8,128)(2,1)S(1)} %copy.26), channel_id=1, source_target_pairs={{0,1},{1,2},{2,3},{4,5},{5,6},{6,7},{8,9},{9,10},{10,11},{12,13},{... | collective-permute-start | bytes 786440 | tf_op jit(solution)/shard_map/ppermute | solution.py:14
  15.3 1.2 %slice_reduce_fusion.23 = (f32[32]{0:T(128)S(1)}, f32[32]{0:T(128)S(1)}, f32[32]{0:T(128)S(1)}, f32[32]{0:T(128)S(1)}, f32[32]{0:T(128)S(1)}, /*index=5*/f32[32]{0:T(128)S(1)}) fusion(f32[32,25]{1,0:T(8,128)} %param.8), kind=kLoop, calls=%fused_computation.292 | loop fusion | bytes 1536 | tf_op jit(solution)/shard_map/slice | solution.py:70
  16.5 2.5 %slice_reduce_fusion.24 = (f32[32]{0:T(128)S(1)}, f32[32]{0:T(128)S(1)}, f32[32]{0:T(128)S(1)}, f32[32]{0:T(128)S(1)}, f32[32]{0:T(128)S(1)}, /*index=5*/f32[32]...) fusion(f32[32,25]{1,0:T(8,128)} %param.8), kind=kLoop, calls=%fused_computation.293 | loop fusion | bytes 4864 | tf_op jit(solution)/shard_map/slice | solution.py:70
  19.0 1.0 %fusion.159 = f32[16,256,32]{1,2,0:T(8,128)S(1)} fusion(bf16[16,32,256]{2,1,0:T(8,128)(2,1)S(1)} %gather_fusion.2, bf16[7,32,32]{2,1,0:T(8,128)(2,1)} %param.10), kind=kOutput, calls=%fused_computation.308 | convolution fusion | flops 8388608 | bytes 794624 | tf_op jit(solution)/shard_map/gf,mgp->mfp/dot_general | solution.py:87
  20.0 1.5 %collective-permute-done.7 = bf16[16,32,256]{2,1,0:T(8,128)(2,1)S(1)} collective-permute-done((bf16[16,32,256]{2,1,0:T(8,128)(2,1)S(1)}, bf16[16,32,256]{2,1,0:T(8,128)(2,1)S(1)}, u32[]{:S(2)}, u32[]{:S(2)}) %collective-permute-start.7) | collective-permute-done | bytes 262176 | tf_op jit(solution)/shard_map/ppermute | solution.py:25
  21.5 1.0 fusion.109
  22.8 3.9 %collective-permute-done.5 = bf16[16,32,256]{2,1,0:T(8,128)(2,1)S(1)} collective-permute-done((bf16[16,32,256]{2,1,0:T(8,128)(2,1)S(1)}, bf16[16,32,256]{2,1,0:T(8,128)(2,1)S(1)}, u32[]{:S(2)}, u32[]{:S(2)}) %collective-permute-start.5) | collective-permute-done | bytes 262176 | tf_op jit(solution)/shard_map/ppermute | solution.py:25
  28.5 0.8 select_maximum_fusion.2
  29.4 3.0 %fusion.74 = bf16[16,32,2,128]{3,1,2,0:T(8,128)(2,1)S(1)} fusion(f32[16,32,6,132]{3,1,2,0:T(8,128)S(1)} %get-tuple-element.69, f32[32]{0:T(128)S(1)} %get-tuple-element.66, f32[32]{0:T(128)S(1)} %get-tuple-element.67, f32[32]{0:T(128)S(1)} %get-tuple-element.44, f32[32]{0:T(128)S(1)} %get-tuple-element.45, f32[32]{0:T(128)S(1)} %get-tuple-element.46, ...), kind=kLoop, calls=%fused_computation.150 | loop fusion | flops 6553600 | bytes 13372544 | tf_op jit(solution)/shard_map/convert_element_type | solution.py:73
  32.4 1.1 %fusion.46 = (bf16[16,32,2,128]{3,1,2,0:T(8,128)(2,1)}, bf16[16,2,4,8,128]{4,3,2,1,0:T(8,128)(2,1)S(1)}) fusion(bf16[16,32,2,128]{3,1,2,0:T(8,128)(2,1)S(1)} %fusion.74, bf16[32,32]{1,0:T(8,128)(2,1)S(1)} %copy-done, bf16[16,32,256]{2,1,0:T(8,128)(2,1)S(1)} %gather_fusion.3), kind=kOutput, calls=%fused_computation.96 | convolution fusion | flops 9961472 | bytes 1050624 | tf_op jit(solution)/shard_map/gf,cfhw->cghw/dot_general | solution.py:74
  34.2 7.2 %collective-permute-start.4 = (bf16[16,32,256]{2,1,0:T(8,128)(2,1)S(1)}, bf16[16,32,256]{2,1,0:T(8,128)(2,1)}, u32[]{:S(2)}, u32[]{:S(2)}) collective-permute-start(bf16[16,32,256]{2,1,0:T(8,128)(2,1)S(1)} %gather_fusion), channel_id=1, source_target_pairs={{8,0},{12,4},{0,8},{4,12},{9,1},{13,5},{1,9},{5,13},{10,2},{14,6},... | collective-permute-start | bytes 786440 | tf_op jit(solution)/shard_map/ppermute | solution.py:25
  41.8 1.6 %collective-permute-start.2 = (bf16[16,32,256]{2,1,0:T(8,128)(2,1)S(1)}, bf16[16,32,256]{2,1,0:T(8,128)(2,1)}, u32[]{:S(2)}, u32[]{:S(2)}) collective-permute-start(bf16[16,32,256]{2,1,0:T(8,128)(2,1)S(1)} %gather_fusion), channel_id=1, source_target_pairs={{12,0},{0,4},{4,8},{8,12},{13,1},{1,5},{5,9},{9,13},{14,2},{2,6},{... | collective-permute-start | bytes 786440 | tf_op jit(solution)/shard_map/ppermute | solution.py:25
  43.5 2.6 %fusion.44 = (f32[32]{0:T(128)}, f32[32]{0:T(128)}, f32[32]{0:T(128)}, f32[32]{0:T(128)}, f32[32]{0:T(128)}, /*index=5*/f32[32]{0:T(128)}, bf16[16,2,128,32]{2,3,1,0:T(8,128)(2,1)S(1)}) fusion(bf16[16,32,6,132]{3,1,2,0:T(8,128)(2,1)S(1)} %get-tuple-element.68, bf16[16,32,2,128]{3,1,2,0:T(8,128)(2,1)} %copy-done.6, bf16[16,32,2,128]{3,1,2,0:T(8,128)(2,1)} %copy-done.3, ...), kind=kOutput, calls=%fused_computation.93 | convolution fusion | flops 11272000 | bytes 1837824 | tf_op jit(solution)/shard_map/gf,cghw->cfhw/dot_general | solution.py:129
  46.1 2.4 %fusion.45 = (f32[32]{0:T(128)}, f32[32]{0:T(128)}, f32[32]{0:T(128)}, f32[32]{0:T(128)}, f32[32]{0:T(128)}, /*index=5*/f32[32]{0:T(128)}, f32[32]{0:T(128)}, f3...) fusion(bf16[16,32,6,132]{3,1,2,0:T(8,128)(2,1)S(1)} %get-tuple-, ...), kind=kLoop, calls=%fused_computation.94 | loop fusion | flops 7208384 | bytes 4983040 | tf_op jit(solution)/shard_map/cfhw,cfhw->f/dot_general | solution.py:144
  48.5 1.3 %collective-permute-start.9 = (bf16[16,32,2,128]{3,1,2,0:T(8,128)(2,1)S(1)}, bf16[16,32,2,128]{3,1,2,0:T(8,128)(2,1)S(1)}, u32[]{:S(2)}, u32[]{:S(2)}) collective-permute-start(bf16[16,32,2,128]{3,1,2,0:T(8,128)(2,1)S(1)} %bitcast.337), channel_id=1, source_target_pairs={{1,0},{2,1},{3,2},{5,4},{6,5},{7,6},{9,8},{10,9},{11,10},{13,12},{... | collective-permute-start | bytes 786440 | tf_op jit(solution)/shard_map/ppermute | solution.py:17
  49.8 3.2 %collective-permute-start.8 = (bf16[16,32,2,128]{3,1,2,0:T(8,128)(2,1)S(1)}, bf16[16,32,2,128]{3,1,2,0:T(8,128)(2,1)S(1)}, u32[]{:S(2)}, u32[]{:S(2)}) collective-permute-start(bf16[16,32,2,128]{3,1,2,0:T(8,128)(2,1)S(1)} %bitcast.338), channel_id=1, source_target_pairs={{0,1},{1,2},{2,3},{4,5},{5,6},{6,7},{8,9},{9,10},{10,11},{12,13},{... | collective-permute-start | bytes 786440 | tf_op jit(solution)/shard_map/ppermute | solution.py:14
  53.1 0.8 multiply_reduce_fusion
  54.1 2.8 %stack.127 = f32[32,25]{0,1:T(8,128)S(1)} concatenate(f32[32,1]{0,1:T(1,128)} %bitcast.361, f32[32,1]{0,1:T(1,128)} %bitcast.359, f32[32,1]{0,1:T(1,128)} %bitcast.362, f32[32,1]{0,1:T(1,128)} %bitcast.358, f32[32,1]{0,1:T(1,128)} %bitcast.357, f32[32,1]{0,1:T(1,128)} %bitcast.356, f32[32,1]{0,1:T(1,128)} %bitcast.355, f32[32,1]{0,1:T(1,128)} %bitcast.363, f32[32,1]{0,1:T(1,128)} %bitcast.354, ...), dimensions={1} | concatenate | bytes 6400 | tf_op jit(solution)/shard_map/stack | solution.py:151
  57.1 3.2 %collective-permute-done.3 = bf16[16,32,256]{2,1,0:T(8,128)(2,1)} collective-permute-done((bf16[16,32,256]{2,1,0:T(8,128)(2,1)S(1)}, bf16[16,32,256]{2,1,0:T(8,128)(2,1)}, u32[]{:S(2)}, u32[]{:S(2)}) %collective-permute-start.3) | collective-permute-done | bytes 262176 | tf_op jit(solution)/shard_map/ppermute | solution.py:25
  60.3 1.3 %fusion.21 = f32[7,32,32]{2,1,0:T(8,128)S(1)} fusion(bf16[16,32,256]{2,1,0:T(8,128)(2,1)S(1)} %gather_fusion.2, bf16[16,32,256]{2,1,0:T(8,128)(2,1)} %collective-permute-done.3, pred[]{:T(512)S(6)} %lt.26), kind=kOutput, calls=%fused_computation.69 | convolution fusion | flops 8519679 | bytes 540673 | tf_op jit(solution)/shard_map/mgp,mfp->gf/dot_general | solution.py:118
  61.6 1.3 %fusion.20 = f32[7,32,32]{2,1,0:T(8,128)S(1)} fusion(f32[7,32,32]{2,1,0:T(8,128)S(1)} %fusion.21, bf16[16,32,256]{2,1,0:T(8,128)(2,1)S(1)} %gather_fusion.2, bf16[16,32,256]{2,1,0:T(8,128)(2,1)} %collective-permute-done.4, pred[]{:T(512)S(6)} %lt.25), kind=kOutput, calls=%fused_computation.67 | convolution fusion | flops 8519680 | bytes 540673 | tf_op jit(solution)/shard_map/mgp,mfp->gf/dot_general | solution.py:118
  63.0 1.3 %fusion.19 = f32[7,32,32]{2,1,0:T(8,128)S(1)} fusion(f32[7,32,32]{2,1,0:T(8,128)S(1)} %fusion.20, bf16[16,32,256]{2,1,0:T(8,128)(2,1)S(1)} %gather_fusion.2, bf16[16,32,256]{2,1,0:T(8,128)(2,1)} %collective-permute-done.2, pred[]{:T(512)S(6)} %lt.24), kind=kOutput, calls=%fused_computation.65 | convolution fusion | flops 8519680 | bytes 540673 | tf_op jit(solution)/shard_map/mgp,mfp->gf/dot_general | solution.py:118
  64.4 1.3 %fusion.17 = f32[7,32,32]{2,1,0:T(8,128)S(1)} fusion(f32[7,32,32]{2,1,0:T(8,128)S(1)} %fusion.18, bf16[16,32,256]{2,1,0:T(8,128)(2,1)S(1)} %gather_fusion.2, bf16[16,32,256]{2,1,0:T(8,128)(2,1)} %collective-permute-done.3, pred[]{:T(512)S(6)} %ge.9), kind=kOutput, calls=%fused_computation.61 | convolution fusion | flops 8519680 | bytes 540673 | tf_op jit(solution)/shard_map/mgp,mfp->gf/dot_general | solution.py:118
  65.8 1.3 %fusion.16 = f32[7,32,32]{2,1,0:T(8,128)S(1)} fusion(f32[7,32,32]{2,1,0:T(8,128)S(1)} %fusion.17, bf16[16,32,256]{2,1,0:T(8,128)(2,1)S(1)} %gather_fusion.2, bf16[16,32,256]{2,1,0:T(8,128)(2,1)} %collective-permute-done.4, pred[]{:T(512)S(6)} %ge.10), kind=kOutput, calls=%fused_computation.59 | convolution fusion | flops 8519680 | bytes 540673 | tf_op jit(solution)/shard_map/mgp,mfp->gf/dot_general | solution.py:118
  67.2 1.3 %fusion.15 = f32[7,32,32]{2,1,0:T(8,128)S(1)} fusion(f32[7,32,32]{2,1,0:T(8,128)S(1)} %fusion.16, bf16[16,32,256]{2,1,0:T(8,128)(2,1)S(1)} %gather_fusion.2, bf16[16,32,256]{2,1,0:T(8,128)(2,1)} %collective-permute-done.2, pred[]{:T(512)S(6)} %ge.11), kind=kOutput, calls=%fused_computation.57 | convolution fusion | flops 8519680 | bytes 540673 | tf_op jit(solution)/shard_map/mgp,mfp->gf/dot_general | solution.py:118
  68.8 0.7 fusion.1
  69.6 3.0 %fusion.49 = bf16[16,32,2,128]{3,1,2,0:T(8,128)(2,1)S(1)} fusion(f32[16,32,6,132]{3,1,2,0:T(8,128)S(1)} %fusion.1, bf16[16,32,2,128]{3,2,1,0:T(2,128)(2,1)S(1)} %copy-done.2, f32[32]{0:T(128)S(1)} %get-tuple-element.66, f32[32]{0:T(128)S(1)} %get-tuple-element.67, f32[32]{0:T(128)S(1)} %get-tuple-element.44, f32[32]{0:T(128)S(1)} %get-tuple-element.45, ...), kind=kLoop, calls=%fused_computation.100 | loop fusion | flops 6815744 | bytes 13634688 | tf_op jit(solution)/shard_map/convert_element_type | solution.py:152
  72.6 1.3 %fusion.130 = f32[16,256,32]{1,2,0:T(8,128)S(1)} fusion(bf16[16,32,256]{2,1,0:T(8,128)(2,1)} %collective-permute-done.2, pred[]{:T(512)S(6)} %ge.11, bf16[7,32,32]{2,1,0:T(8,128)(2,1)S(1)} %copy-done.7), kind=kOutput, calls=%fused_computation.264 | convolution fusion | flops 8519680 | bytes 794625 | tf_op jit(solution)/shard_map/gf,mfp->mgp/dot_general | solution.py:106
  73.9 1.3 %fusion.136 = f32[16,256,32]{1,2,0:T(8,128)S(1)} fusion(bf16[16,32,256]{2,1,0:T(8,128)(2,1)} %collective-permute-done.4, pred[]{:T(512)S(6)} %ge.10, bf16[7,32,32]{2,1,0:T(8,128)(2,1)S(1)} %copy-done.7), kind=kOutput, calls=%fused_computation.266 | convolution fusion | flops 8519680 | bytes 794625 | tf_op jit(solution)/shard_map/gf,mfp->mgp/dot_general | solution.py:106
  75.2 1.3 %convolution_add_fusion.1 = f32[16,256,32]{1,2,0:T(8,128)S(1)} fusion(f32[16,256,32]{1,2,0:T(8,128)S(1)} %fusion.161, bf16[16,32,256]{2,1,0:T(8,128)(2,1)} %collective-permute-done.2, pred[]{:T(512)S(6)} %lt.24, bf16[7,32,32]{2,1,0:T(8,128)(2,1)S(1)} %copy-done.7), kind=kOutput, calls=%fused_computation.39 | convolution fusion | flops 8650752 | bytes 1318913 | tf_op jit(solution)/shard_map/gf,mfp->mgp/dot_general | solution.py:106
  76.5 1.3 %fusion.139 = f32[16,256,32]{1,2,0:T(8,128)S(1)} fusion(bf16[16,32,256]{2,1,0:T(8,128)(2,1)} %collective-permute-done.4, pred[]{:T(512)S(6)} %lt.25, bf16[7,32,32]{2,1,0:T(8,128)(2,1)S(1)} %copy-done.7), kind=kOutput, calls=%fused_computation.267 | convolution fusion | flops 8519680 | bytes 794625 | tf_op jit(solution)/shard_map/gf,mfp->mgp/dot_general | solution.py:106
  77.8 1.6 %collective-permute-start.11 = (f32[8992]{0:T(1024)S(1)}, f32[8992]{0:T(1024)S(1)}, u32[]{:S(2)}, u32[]{:S(2)}) collective-permute-start(f32[8992]{0:T(1024)S(1)} %add.340), channel_id=1, source_target_pairs={{0,2},{2,0},{1,3},{3,1},{4,6},{6,4},{5,7},{7,5},{8,10},{10,8},{9,1... | collective-permute-start | bytes 107912 | tf_op jit(solution)/shard_map/ppermute | solution.py:36
  79.4 1.3 %fusion.133 = f32[16,256,32]{1,2,0:T(8,128)S(1)} fusion(bf16[16,32,256]{2,1,0:T(8,128)(2,1)} %collective-permute-done.3, pred[]{:T(512)S(6)} %lt.26, bf16[7,32,32]{2,1,0:T(8,128)(2,1)S(1)} %copy-done.7), kind=kOutput, calls=%fused_computation.265 | convolution fusion | flops 8519680 | bytes 794625 | tf_op jit(solution)/shard_map/gf,mfp->mgp/dot_general | solution.py:106
  80.7 1.1 %collective-permute-done.11 = f32[8992]{0:T(1024)S(1)} collective-permute-done((f32[8992]{0:T(1024)S(1)}, f32[8992]{0:T(1024)S(1)}, u32[]{:S(2)}, u32[]{:S(2)}) %collective-permute-start.11) | collective-permute-done | bytes 36000 | tf_op jit(solution)/shard_map/ppermute | solution.py:36
  81.9 5.0 %collective-permute-start.12 = (f32[8992]{0:T(1024)S(1)}, f32[8992]{0:T(1024)S(1)}, u32[]{:S(2)}, u32[]{:S(2)}) collective-permute-start(f32[8992]{0:T(1024)S(1)} %add.341), channel_id=1, source_target_pairs={{0,4},{4,0},{8,12},{12,8},{1,5},{5,1},{9,13},{13,9},{2,6},{6,2},{1... | collective-permute-start | bytes 107912 | tf_op jit(solution)/shard_map/ppermute | solution.py:36
  86.9 1.3 %fusion.14 = bf16[16,32,256]{2,1,0:T(8,128)(2,1)S(1)} fusion(f32[16,256,32]{1,2,0:T(8,128)S(1)} %fusion.130, f32[16,256,32]{1,2,0:T(8,128)S(1)} %fusion.133, f32[16,256,32]{1,2,0:T(8,128)S(1)} %fusion.136, f32[16,256,32]{1,2,0:T(8,128)S(1)} %fusion.139, f32[16,256,32]{1,2,0:T(8,128)S(1)} %convolution_add_fusion.1, ...), kind=kOutput, calls=%fused_computation.55 | convolution fusion | flops 9306112 | bytes 3153921 | tf_op jit(solution)/shard_map/gf,mfp->mgp/dot_general | solution.py:106
  89.7 1.0 %add_convert_fusion = bf16[16,32,2,128]{3,2,1,0:T(2,128)(2,1)} fusion(f32[16,32,2,128]{3,2,1,0:T(2,128)S(1)} %reshape.78, bf16[16,32,2,128]{3,2,1,0:T(2,128)(2,1)S(1)} %copy-done.1), kind=kLoop, calls=%fused_computation.200 | loop fusion | flops 393216 | bytes 1048576 | tf_op jit(solution)/shard_map/convert_element_type | solution.py:126
  90.7 0.9 copy.43
  91.7 2.4 %collective-permute-done.13 = f32[8992]{0:T(1024)S(1)} collective-permute-done((f32[8992]{0:T(1024)S(1)}, f32[8992]{0:T(1024)S(1)}, u32[]{:S(2)}, u32[]{:S(2)}) %collective-permute-start.13) | collective-permute-done | bytes 36000 | tf_op jit(solution)/shard_map/ppermute | solution.py:36
  94.2 0.7 mul.550
  95.6 0.7 mul.556
  (89 shorter events, 7.9 us)
Async XLA Ops:
  0.6 31.8 %copy-start = (bf16[32,32]{1,0:T(8,128)(2,1)S(1)}, bf16[32,32]{1,0:T(8,128)(2,1)}, u32[]{:S(2)}) copy-start(bf16[32,32]{1,0:T(8,128)(2,1)} %param.9) | copy-start | bytes 6148
  0.6 21.9 %copy-start.7 = (bf16[7,32,32]{2,1,0:T(8,128)(2,1)S(1)}, bf16[7,32,32]{2,1,0:T(8,128)(2,1)}, u32[]{:S(2)}) copy-start(bf16[7,32,32]{2,1,0:T(8,128)(2,1)} %param.10) | copy-start | bytes 43012
  3.8 17.8 %collective-permute-start.7 = (bf16[16,32,256]{2,1,0:T(8,128)(2,1)S(1)}, bf16[16,32,256]{2,1,0:T(8,128)(2,1)S(1)}, u32[]{:S(2)}, u32[]{:S(2)}) collective-permute-start(bf16[16,32,256]{2,1,0:T(8,128)(2,1)S(1)} %gather_fusion.2), channel_id=1, source_target_pairs={{8,0},{12,4},{0,8},{4,12},{9,1},{13,5},{1,9},{5,13},{10,2},{14,6},... | collective-permute-start | bytes 786440 | tf_op jit(solution)/shard_map/ppermute | solution.py:25
  7.9 19.0 %collective-permute-start.6 = (bf16[16,32,256]{2,1,0:T(8,128)(2,1)S(1)}, bf16[16,32,256]{2,1,0:T(8,128)(2,1)S(1)}, u32[]{:S(2)}, u32[]{:S(2)}) collective-permute-start(bf16[16,32,256]{2,1,0:T(8,128)(2,1)S(1)} %gather_fusion.2), channel_id=1, source_target_pairs={{4,0},{8,4},{12,8},{0,12},{5,1},{9,5},{13,9},{1,13},{6,2},{10,6},{... | collective-permute-start | bytes 786440 | tf_op jit(solution)/shard_map/ppermute | solution.py:25
  9.2 17.4 %collective-permute-start.5 = (bf16[16,32,256]{2,1,0:T(8,128)(2,1)S(1)}, bf16[16,32,256]{2,1,0:T(8,128)(2,1)S(1)}, u32[]{:S(2)}, u32[]{:S(2)}) collective-permute-start(bf16[16,32,256]{2,1,0:T(8,128)(2,1)S(1)} %gather_fusion.2), channel_id=1, source_target_pairs={{12,0},{0,4},{4,8},{8,12},{13,1},{1,5},{5,9},{9,13},{14,2},{2,6},{... | collective-permute-start | bytes 786440 | tf_op jit(solution)/shard_map/ppermute | solution.py:25
  10.9 17.6 %copy-start.3 = (bf16[16,32,2,128]{3,1,2,0:T(8,128)(2,1)}, bf16[16,32,2,128]{3,1,2,0:T(8,128)(2,1)S(1)}, u32[]{:S(2)}) copy-start(bf16[16,32,2,128]{3,1,2,0:T(8,128)(2,1)S(1)} %copy.26) | copy-start | bytes 786436
  10.9 17.6 %collective-permute-start.1 = (bf16[16,32,2,128]{3,1,2,0:T(8,128)(2,1)S(1)}, bf16[16,32,2,128]{3,1,2,0:T(8,128)(2,1)S(1)}, u32[]{:S(2)}, u32[]{:S(2)}) collective-permute-start(bf16[16,32,2,128]{3,1,2,0:T(8,128)(2,1)S(1)} %copy.26), channel_id=1, source_target_pairs={{1,0},{2,1},{3,2},{5,4},{6,5},{7,6},{9,8},{10,9},{11,10},{13,12},{... | collective-permute-start | bytes 786440 | tf_op jit(solution)/shard_map/ppermute | solution.py:17
  12.2 16.3 %collective-permute-start = (bf16[16,32,2,128]{3,1,2,0:T(8,128)(2,1)S(1)}, bf16[16,32,2,128]{3,1,2,0:T(8,128)(2,1)S(1)}, u32[]{:S(2)}, u32[]{:S(2)}) collective-permute-start(bf16[16,32,2,128]{3,1,2,0:T(8,128)(2,1)S(1)} %copy.26), channel_id=1, source_target_pairs={{0,1},{1,2},{2,3},{4,5},{5,6},{6,7},{8,9},{9,10},{10,11},{12,13},{... | collective-permute-start | bytes 786440 | tf_op jit(solution)/shard_map/ppermute | solution.py:14
  27.8 1.5 %copy-start.8 = (f32[32]{0:T(128)S(1)}, f32[32]{0:T(128)}, u32[]{:S(2)}) copy-start(f32[32]{0:T(128)} %get-tuple-element.55) | copy-start | bytes 388
  27.8 1.5 %copy-start.10 = (f32[32]{0:T(128)S(1)}, f32[32]{0:T(128)}, u32[]{:S(2)}) copy-start(f32[32]{0:T(128)} %get-tuple-element.56) | copy-start | bytes 388
  27.8 1.5 %copy-start.12 = (f32[32]{0:T(128)S(1)}, f32[32]{0:T(128)}, u32[]{:S(2)}) copy-start(f32[32]{0:T(128)} %get-tuple-element.57) | copy-start | bytes 388
  27.9 1.5 %copy-start.14 = (f32[32]{0:T(128)S(1)}, f32[32]{0:T(128)}, u32[]{:S(2)}) copy-start(f32[32]{0:T(128)} %get-tuple-element.58) | copy-start | bytes 388
  27.9 1.5 %copy-start.16 = (f32[32]{0:T(128)S(1)}, f32[32]{0:T(128)}, u32[]{:S(2)}) copy-start(f32[32]{0:T(128)} %get-tuple-element.59) | copy-start | bytes 388
  27.9 1.5 %copy-start.18 = (f32[32]{0:T(128)S(1)}, f32[32]{0:T(128)}, u32[]{:S(2)}) copy-start(f32[32]{0:T(128)} %get-tuple-element.60) | copy-start | bytes 388
  27.9 1.5 %copy-start.20 = (f32[32]{0:T(128)S(1)}, f32[32]{0:T(128)}, u32[]{:S(2)}) copy-start(f32[32]{0:T(128)} %get-tuple-element.61) | copy-start | bytes 388
  28.5 3.9 %copy-start.5 = (bf16[16,32,2,128]{3,1,2,0:T(8,128)(2,1)}, bf16[16,32,2,128]{3,1,2,0:T(8,128)(2,1)S(1)}, u32[]{:S(2)}) copy-start(bf16[16,32,2,128]{3,1,2,0:T(8,128)(2,1)S(1)} %collective-permute-done.1) | copy-start | bytes 786436
  28.5 0.8 copy-start.6
  34.2 27.5 %collective-permute-start.4 = (bf16[16,32,256]{2,1,0:T(8,128)(2,1)S(1)}, bf16[16,32,256]{2,1,0:T(8,128)(2,1)}, u32[]{:S(2)}, u32[]{:S(2)}) collective-permute-start(bf16[16,32,256]{2,1,0:T(8,128)(2,1)S(1)} %gather_fusion), channel_id=1, source_target_pairs={{8,0},{12,4},{0,8},{4,12},{9,1},{13,5},{1,9},{5,13},{10,2},{14,6},... | collective-permute-start | bytes 786440 | tf_op jit(solution)/shard_map/ppermute | solution.py:25
  41.3 19.0 %collective-permute-start.3 = (bf16[16,32,256]{2,1,0:T(8,128)(2,1)S(1)}, bf16[16,32,256]{2,1,0:T(8,128)(2,1)}, u32[]{:S(2)}, u32[]{:S(2)}) collective-permute-start(bf16[16,32,256]{2,1,0:T(8,128)(2,1)S(1)} %gather_fusion), channel_id=1, source_target_pairs={{4,0},{8,4},{12,8},{0,12},{5,1},{9,5},{13,9},{1,13},{6,2},{10,6},{... | collective-permute-start | bytes 786440 | tf_op jit(solution)/shard_map/ppermute | solution.py:25
  41.8 21.2 %collective-permute-start.2 = (bf16[16,32,256]{2,1,0:T(8,128)(2,1)S(1)}, bf16[16,32,256]{2,1,0:T(8,128)(2,1)}, u32[]{:S(2)}, u32[]{:S(2)}) collective-permute-start(bf16[16,32,256]{2,1,0:T(8,128)(2,1)S(1)} %gather_fusion), channel_id=1, source_target_pairs={{12,0},{0,4},{4,8},{8,12},{13,1},{1,5},{5,9},{9,13},{14,2},{2,6},{... | collective-permute-start | bytes 786440 | tf_op jit(solution)/shard_map/ppermute | solution.py:25
  46.1 6.9 %copy-start.1 = (bf16[16,32,2,128]{3,2,1,0:T(2,128)(2,1)S(1)}, bf16[16,32,2,128]{3,2,1,0:T(2,128)(2,1)}, u32[]{:S(2)}) copy-start(bf16[16,32,2,128]{3,2,1,0:T(2,128)(2,1)} %param.6) | copy-start | bytes 786436
  46.1 7.7 %copy-start.4 = (bf16[16,32,2,128]{3,1,2,0:T(8,128)(2,1)S(1)}, bf16[16,32,2,128]{3,1,2,0:T(8,128)(2,1)}, u32[]{:S(2)}) copy-start(bf16[16,32,2,128]{3,1,2,0:T(8,128)(2,1)} %get-tuple-element.70) | copy-start | bytes 786436
  48.5 20.3 %collective-permute-start.9 = (bf16[16,32,2,128]{3,1,2,0:T(8,128)(2,1)S(1)}, bf16[16,32,2,128]{3,1,2,0:T(8,128)(2,1)S(1)}, u32[]{:S(2)}, u32[]{:S(2)}) collective-permute-start(bf16[16,32,2,128]{3,1,2,0:T(8,128)(2,1)S(1)} %bitcast.337), channel_id=1, source_target_pairs={{1,0},{2,1},{3,2},{5,4},{6,5},{7,6},{9,8},{10,9},{11,10},{13,12},{... | collective-permute-start | bytes 786440 | tf_op jit(solution)/shard_map/ppermute | solution.py:17
  49.8 19.0 %collective-permute-start.8 = (bf16[16,32,2,128]{3,1,2,0:T(8,128)(2,1)S(1)}, bf16[16,32,2,128]{3,1,2,0:T(8,128)(2,1)S(1)}, u32[]{:S(2)}, u32[]{:S(2)}) collective-permute-start(bf16[16,32,2,128]{3,1,2,0:T(8,128)(2,1)S(1)} %bitcast.338), channel_id=1, source_target_pairs={{0,1},{1,2},{2,3},{4,5},{5,6},{6,7},{8,9},{9,10},{10,11},{12,13},{... | collective-permute-start | bytes 786440 | tf_op jit(solution)/shard_map/ppermute | solution.py:14
  65.7 3.7 %copy-start.2 = (bf16[16,32,2,128]{3,2,1,0:T(2,128)(2,1)S(1)}, bf16[16,32,2,128]{3,2,1,0:T(2,128)(2,1)}, u32[]{:S(2)}) copy-start(bf16[16,32,2,128]{3,2,1,0:T(2,128)(2,1)} %param.7) | copy-start | bytes 786436
  65.8 3.7 %copy-start.9 = (f32[32]{0:T(128)S(1)}, f32[32]{0:T(128)}, u32[]{:S(2)}) copy-start(f32[32]{0:T(128)} %get-tuple-element.55) | copy-start | bytes 388
  65.8 3.7 %copy-start.11 = (f32[32]{0:T(128)S(1)}, f32[32]{0:T(128)}, u32[]{:S(2)}) copy-start(f32[32]{0:T(128)} %get-tuple-element.56) | copy-start | bytes 388
  65.8 3.7 %copy-start.13 = (f32[32]{0:T(128)S(1)}, f32[32]{0:T(128)}, u32[]{:S(2)}) copy-start(f32[32]{0:T(128)} %get-tuple-element.57) | copy-start | bytes 388
  65.8 3.7 %copy-start.15 = (f32[32]{0:T(128)S(1)}, f32[32]{0:T(128)}, u32[]{:S(2)}) copy-start(f32[32]{0:T(128)} %get-tuple-element.58) | copy-start | bytes 388
  65.8 3.7 %copy-start.17 = (f32[32]{0:T(128)S(1)}, f32[32]{0:T(128)}, u32[]{:S(2)}) copy-start(f32[32]{0:T(128)} %get-tuple-element.59) | copy-start | bytes 388
  65.8 3.7 %copy-start.19 = (f32[32]{0:T(128)S(1)}, f32[32]{0:T(128)}, u32[]{:S(2)}) copy-start(f32[32]{0:T(128)} %get-tuple-element.60) | copy-start | bytes 388
  65.8 3.7 %copy-start.21 = (f32[32]{0:T(128)S(1)}, f32[32]{0:T(128)}, u32[]{:S(2)}) copy-start(f32[32]{0:T(128)} %get-tuple-element.61) | copy-start | bytes 388
  68.7 9.1 %collective-permute-start.10 = (f32[8992]{0:T(1024)S(1)}, f32[8992]{0:T(1024)S(1)}, u32[]{:S(2)}, u32[]{:S(2)}) collective-permute-start(f32[8992]{0:T(1024)S(1)} %concatenate.19), channel_id=1, source_target_pairs={{0,1},{1,0},{2,3},{3,2},{4,5},{5,4},{6,7},{7,6},{8,9},{9,8},{10,11... | collective-permute-start | bytes 107912 | tf_op jit(solution)/shard_map/ppermute | solution.py:36
  77.8 4.0 %collective-permute-start.11 = (f32[8992]{0:T(1024)S(1)}, f32[8992]{0:T(1024)S(1)}, u32[]{:S(2)}, u32[]{:S(2)}) collective-permute-start(f32[8992]{0:T(1024)S(1)} %add.340), channel_id=1, source_target_pairs={{0,2},{2,0},{1,3},{3,1},{4,6},{6,4},{5,7},{7,5},{8,10},{10,8},{9,1... | collective-permute-start | bytes 107912 | tf_op jit(solution)/shard_map/ppermute | solution.py:36
  81.9 7.2 %collective-permute-start.12 = (f32[8992]{0:T(1024)S(1)}, f32[8992]{0:T(1024)S(1)}, u32[]{:S(2)}, u32[]{:S(2)}) collective-permute-start(f32[8992]{0:T(1024)S(1)} %add.341), channel_id=1, source_target_pairs={{0,4},{4,0},{8,12},{12,8},{1,5},{5,1},{9,13},{13,9},{2,6},{6,2},{1... | collective-permute-start | bytes 107912 | tf_op jit(solution)/shard_map/ppermute | solution.py:36
  89.1 4.9 %collective-permute-start.13 = (f32[8992]{0:T(1024)S(1)}, f32[8992]{0:T(1024)S(1)}, u32[]{:S(2)}, u32[]{:S(2)}) collective-permute-start(f32[8992]{0:T(1024)S(1)} %add.342), channel_id=1, source_target_pairs={{0,8},{4,12},{8,0},{12,4},{1,9},{5,13},{9,1},{13,5},{2,10},{6,14},... | collective-permute-start | bytes 107912 | tf_op jit(solution)/shard_map/ppermute | solution.py:36

commit v2 on v1

--- a/solution.py
+++ b/solution.py
@@ -81,19 +81,12 @@
     order = jnp.zeros((chans,), jnp.int32).at[own].set(jnp.arange(chans, dtype=jnp.int32))
     h_sorted = hidden_flat[order]
     g_sorted = grad_flat[order]
-    fwd_acc = jnp.einsum(
-        "gf,mfp->mgp", spectral_kernel[half], h_sorted, preferred_element_type=jnp.float32
-    )
-    bwd_acc = jnp.einsum(
-        "gf,mgp->mfp", spectral_kernel[half], g_sorted, preferred_element_type=jnp.float32
-    )
-    grad_taps = [None] * taps
-    grad_taps[half] = jnp.einsum(
-        "mgp,mfp->gf", g_sorted, h_sorted, preferred_element_type=jnp.float32
-    )
+    h_taps = [h_sorted] * taps
+    g_taps = [g_sorted] * taps
     for dist in range(1, half + 1):
         for sign in (-1, 1):
-            h_far, g_far = passed_along((h_sorted, g_sorted), "chan", -sign * dist)
+            h_far = passed_along(h_sorted, "chan", -sign * dist)
+            g_far = passed_along(g_sorted, "chan", -sign * dist)
             if sign < 0:
                 wrapped = device < dist
                 h_near = jnp.where(wrapped, move_down(h_far), h_far)
@@ -102,23 +95,17 @@
                 wrapped = device + dist >= n_chan
                 h_near = jnp.where(wrapped, move_up(h_far), h_far)
                 g_near = jnp.where(wrapped, move_up(g_far), g_far)
-            offset = sign * dist
-            fwd_acc = fwd_acc + jnp.einsum(
-                "gf,mfp->mgp",
-                spectral_kernel[half + offset],
-                h_near,
-                preferred_element_type=jnp.float32,
-            )
-            bwd_acc = bwd_acc + jnp.einsum(
-                "gf,mgp->mfp",
-                spectral_kernel[half - offset],
-                g_near,
-                preferred_element_type=jnp.float32,
-            )
-            grad_taps[half + offset] = jnp.einsum(
-                "mgp,mfp->gf", g_sorted, h_near, preferred_element_type=jnp.float32
-            )
-    spec_grad = jnp.stack(grad_taps, 0)
+            h_taps[half + sign * dist] = h_near
+            g_taps[half + sign * dist] = g_near
+    h_stack = jnp.stack(h_taps, 1).reshape(chans, taps * feats, pixels)
+    g_stack = jnp.stack(g_taps, 1).reshape(chans, taps * feats, pixels)
+    fwd_weight = spectral_kernel.transpose(1, 0, 2).reshape(feats, taps * feats)
+    bwd_weight = spectral_kernel[::-1].transpose(2, 0, 1).reshape(feats, taps * feats)
+    fwd_acc = jnp.einsum("gK,mKp->mgp", fwd_weight, h_stack, preferred_element_type=jnp.float32)
+    bwd_acc = jnp.einsum("fK,mKp->mfp", bwd_weight, g_stack, preferred_element_type=jnp.float32)
+    spec_grad = jnp.einsum(
+        "mKp,mfp->Kf", g_stack, h_sorted, preferred_element_type=jnp.float32
+    ).reshape(taps, feats, feats)[::-1]
     spec_flat = fwd_acc.astype(jnp.bfloat16)[own]
     back_flat = bwd_acc.astype(jnp.bfloat16)[own]
     spec = spec_flat.reshape(chans, feats, rows, cols)
@@ -151,13 +138,14 @@
     kernel_term = jnp.stack(terms, 1)
     dirty_grad = (cotangent.astype(jnp.float32) + conv).astype(jnp.bfloat16)
     parts = (kernel_term, mix_term, spec_grad)
-    flat = all_summed(jnp.concatenate([part.reshape(-1) for part in parts]), ("sub", "tile", "chan"))
+    flat = jnp.concatenate([part.reshape(-1) for part in parts]) * scale
+    flat = all_summed(flat, ("sub", "tile", "chan"))
     sizes = [part.size for part in parts]
     kgrad, mgrad, sgrad = (
         piece.reshape(part.shape)
         for piece, part in zip(jnp.split(flat, [sizes[0], sizes[0] + sizes[1]]), parts)
     )
-    return (restored, dirty_grad, kgrad * scale, mgrad * scale, sgrad * scale)
+    return (restored, dirty_grad, kgrad, mgrad, sgrad)
 
 
 def solution(mesh):

time: 97.2 us -> 87.9 us (0.904)
  matrix products: 23.2 us -> 5.29 us
  waiting for transfers between devices: 12.2 us -> 24 us
  local copies, waits for them, and re-layouts: 15.5 us -> 12.4 us
  starting transfers between devices: 31.5 us -> 29.8 us
  other arithmetic: 12.6 us -> 14 us
    dot_general x21 -> x3, matrix products: 19.3 us -> 1.67 us  [the longest x1 0.62 us: local(): jnp.einsum('gK,mKp->mgp', fwd_weight, h_stack, preferred_element_type=jnp...]
    ppermute x6, waiting for transfers between devices: 8.66 us -> 17.7 us  [passed_along(): return lax.ppermute(block, axis, route)]
    ppermute x4, starting transfers between devices: 7.32 us -> 3.11 us  [all_summed(): lax.ppermute(value, axis, [(i, i ^ step) for i in range(count)])]
    ppermute x4, waiting for transfers between devices: 3.52 us -> 6.3 us  [all_summed(): lax.ppermute(value, axis, [(i, i ^ step) for i in range(count)])]
    another operation x2, local copies, waits for them, and re-layouts: 2.89 us -> 0.18 us  [local(): kernel_term = jnp.stack(terms, 1)]
    mul x3 -> x0, local copies, waits for them, and re-layouts: 2.12 us -> none  [local(): return (restored, dirty_grad, kgrad * scale, mgrad * scale, sgrad * scale)]
    ppermute x6, starting transfers between devices: 15.3 us -> 17.2 us  [passed_along(): return lax.ppermute(block, axis, route)]
    reshape x3 -> x5, local copies, waits for them, and re-layouts: 0.28 us -> 1.7 us  [the longest x2 1.44 us: local(): piece.reshape(part.shape)]
  transfers between devices with their start and end apart: 14 -> 14, of which waited for: 5 -> 5; matrix products, arithmetic and copies ran while one was open for 42% -> 12% of each run, Pallas kernels for 0% -> 0%
where the time goes in v2:
time: 87.9 us; the launch traced here: 87.4 us
  starting transfers between devices  29.8 us (34%)
  waiting for transfers between devices  24 us (27%)
  other arithmetic  14 us (16%)
  local copies, waits for them, and re-layouts  12.4 us (14%)
  matrix products  5.29 us (6%)
  between operations  1.9 us (2%)
    ppermute x6, waiting for transfers between devices, passed_along(): return lax.ppermute(block, axis, route)  17.7 us
    ppermute x6, starting transfers between devices, passed_along(): return lax.ppermute(block, axis, route)  17.2 us
    ppermute x2, starting transfers between devices, padded(): lax.ppermute(lax.slice_in_dim(block, block.shape[dim] - width, None, axis...  6.96 us
    ppermute x4, waiting for transfers between devices, all_summed(): lax.ppermute(value, axis, [(i, i ^ step) for i in range(count)])  6.3 us
    ppermute x4, starting transfers between devices, all_summed(): lax.ppermute(value, axis, [(i, i ^ step) for i in range(count)])  3.11 us
    dot_general x2, other arithmetic, local(): jnp.einsum('cfhw,cfhw->f', dsmooth, xpad[:, :, i:i + rows, j:j + cols], p...  3.05 us
    convert_element_type x1, other arithmetic, local(): dirty_grad = (cotangent.astype(jnp.float32) + conv).astype(jnp.bfloat16)  3.04 us
    convert_element_type x1, other arithmetic, local(): smooth = total.astype(jnp.bfloat16)  3.03 us
  transfers between devices with their start and end apart: 14, of which 5 were waited for; matrix products, arithmetic and copies ran while one was open for 12% of the time, Pallas kernels for 0%

profile of v2, /device:TPU:0, one launch (start us, length us, event | category | flops | bytes accessed | tf_op | source)
XLA Modules:
  0.0 87.4 jit_solution(4812934920714832387)
XLA Ops:
  0.7 0.8 compare_select_fusion.1
  1.4 0.6 scatter_custom_fusion
  2.1 1.1 %reshape.80 = bf16[16,32,256]{2,1,0:T(8,128)(2,1)S(1)} reshape(bf16[16,32,2,128]{3,2,1,0:T(2,128)(2,1)} %param.7) | data formatting | bytes 524288 | tf_op jit(solution)/shard_map/reshape | solution.py:77
  3.2 0.6 gather_fusion.2
  3.8 3.1 %collective-permute-start.7 = (bf16[16,32,256]{2,1,0:T(8,128)(2,1)S(1)}, bf16[16,32,256]{2,1,0:T(8,128)(2,1)S(1)}, u32[]{:S(2)}, u32[]{:S(2)}) collective-permute-start(bf16[16,32,256]{2,1,0:T(8,128)(2,1)S(1)} %gather_fusion.2), channel_id=1, source_target_pairs={{12,0},{0,4},{4,8},{8,12},{13,1},{1,5},{5,9},{9,13},{14,2},{2,6},{... | collective-permute-start | bytes 786440 | tf_op jit(solution)/shard_map/ppermute | solution.py:25
  6.9 2.6 %collective-permute-start.6 = (bf16[16,32,256]{2,1,0:T(8,128)(2,1)S(1)}, bf16[16,32,256]{2,1,0:T(8,128)(2,1)S(1)}, u32[]{:S(2)}, u32[]{:S(2)}) collective-permute-start(bf16[16,32,256]{2,1,0:T(8,128)(2,1)S(1)} %gather_fusion.2), channel_id=1, source_target_pairs={{8,0},{12,4},{0,8},{4,12},{9,1},{13,5},{1,9},{5,13},{10,2},{14,6},... | collective-permute-start | bytes 786440 | tf_op jit(solution)/shard_map/ppermute | solution.py:25
  9.5 1.3 %collective-permute-start.5 = (bf16[16,32,256]{2,1,0:T(8,128)(2,1)S(1)}, bf16[16,32,256]{2,1,0:T(8,128)(2,1)S(1)}, u32[]{:S(2)}, u32[]{:S(2)}) collective-permute-start(bf16[16,32,256]{2,1,0:T(8,128)(2,1)S(1)} %gather_fusion.2), channel_id=1, source_target_pairs={{4,0},{8,4},{12,8},{0,12},{5,1},{9,5},{13,9},{1,13},{6,2},{10,6},{... | collective-permute-start | bytes 786440 | tf_op jit(solution)/shard_map/ppermute | solution.py:25
  10.8 1.0 %copy.27 = bf16[16,32,2,128]{3,1,2,0:T(8,128)(2,1)S(1)} copy(bf16[16,32,2,128]{3,2,1,0:T(2,128)(2,1)} %param.6) | data formatting | bytes 524288 | tf_op args[0]
  11.8 1.3 %collective-permute-start.1 = (bf16[16,32,2,128]{3,1,2,0:T(8,128)(2,1)S(1)}, bf16[16,32,2,128]{3,1,2,0:T(8,128)(2,1)S(1)}, u32[]{:S(2)}, u32[]{:S(2)}) collective-permute-start(bf16[16,32,2,128]{3,1,2,0:T(8,128)(2,1)S(1)} %copy.27), channel_id=1, source_target_pairs={{1,0},{2,1},{3,2},{5,4},{6,5},{7,6},{9,8},{10,9},{11,10},{13,12},{... | collective-permute-start | bytes 786440 | tf_op jit(solution)/shard_map/ppermute | solution.py:17
  13.1 3.7 %collective-permute-start = (bf16[16,32,2,128]{3,1,2,0:T(8,128)(2,1)S(1)}, bf16[16,32,2,128]{3,1,2,0:T(8,128)(2,1)}, u32[]{:S(2)}, u32[]{:S(2)}) collective-permute-start(bf16[16,32,2,128]{3,1,2,0:T(8,128)(2,1)S(1)} %copy.27), channel_id=1, source_target_pairs={{0,1},{1,2},{2,3},{4,5},{5,6},{6,7},{8,9},{9,10},{10,11},{12,13},{... | collective-permute-start | bytes 786440 | tf_op jit(solution)/shard_map/ppermute | solution.py:14
  16.8 1.7 %slice_reduce_fusion.23 = (f32[32]{0:T(128)S(1)}, f32[32]{0:T(128)S(1)}, f32[32]{0:T(128)S(1)}, f32[32]{0:T(128)S(1)}, f32[32]{0:T(128)}, /*index=5*/f32[32]{0:T(128)}) fusion(f32[32,25]{1,0:T(8,128)} %param.8), kind=kLoop, calls=%fused_computation.286 | loop fusion | bytes 1536 | tf_op jit(solution)/shard_map/slice | solution.py:70
  18.6 1.1 %slice_reduce_fusion.24 = (f32[32]{0:T(128)}, f32[32]{0:T(128)}, f32[32]{0:T(128)}, f32[32]{0:T(128)}, f32[32]{0:T(128)}, /*index=5*/f32[32]{0:T(128)}, f32[32]{...) fusion(f32[32,25]{1,0:T(8,128)S(1)} %copy-done.1), kind=kLoop, calls=%fused_computation.287 | loop fusion | bytes 4864 | tf_op jit(solution)/shard_map/slice | solution.py:70
  19.7 4.0 %collective-permute-done.5 = bf16[16,32,256]{2,1,0:T(8,128)(2,1)S(1)} collective-permute-done((bf16[16,32,256]{2,1,0:T(8,128)(2,1)S(1)}, bf16[16,32,256]{2,1,0:T(8,128)(2,1)S(1)}, u32[]{:S(2)}, u32[]{:S(2)}) %collective-permute-start.5) | collective-permute-done | bytes 262176 | tf_op jit(solution)/shard_map/ppermute | solution.py:25
  23.8 2.8 %collective-permute-done.6 = bf16[16,32,256]{2,1,0:T(8,128)(2,1)S(1)} collective-permute-done((bf16[16,32,256]{2,1,0:T(8,128)(2,1)S(1)}, bf16[16,32,256]{2,1,0:T(8,128)(2,1)S(1)}, u32[]{:S(2)}, u32[]{:S(2)}) %collective-permute-start.6) | collective-permute-done | bytes 262176 | tf_op jit(solution)/shard_map/ppermute | solution.py:25
  26.9 0.5 fusion.8
  27.4 0.6 gather_fusion.3
  28.2 1.7 %select_maximum_fusion.2 = (bf16[16,32,6,132]{3,1,2,0:T(8,128)(2,1)S(1)}, f32[16,32,6,132]{3,1,2,0:T(8,128)S(1)}) fusion(bf16[16,32,2,128]{3,1,2,0:T(8,128)(2,1)S(1)} %collective-permute-done.1, bf16[16,32,2,128]{3,1,2,0:T(8,128)(2,1)S(1)} %copy.27, bf16[16,32,2,128]{3,1,2,0:T(8,128)(2,1)} %collective-permute-done), kind=kLoop, calls=%fused_computation.37 | loop fusion | flops 5271552 | bytes 3219456 | tf_op jit(solution)/shard_map/concatenate | solution.py:18
  30.1 3.0 %fusion.64 = bf16[16,32,2,128]{3,1,2,0:T(8,128)(2,1)S(1)} fusion(f32[16,32,6,132]{3,1,2,0:T(8,128)S(1)} %get-tuple-element.69, f32[32]{0:T(128)S(1)} %copy-done.6, f32[32]{0:T(128)S(1)} %copy-done.7, f32[32]{0:T(128)S(1)} %copy-done.9, f32[32]{0:T(128)S(1)} %copy-done.10, f32[32]{0:T(128)S(1)} %copy-done.11, f32[32]{0:T(128)S(1)} %copy-done.12, ...), kind=kLoop, calls=%fused_computation.129 | loop fusion | flops 6553600 | bytes 13372544 | tf_op jit(solution)/shard_map/convert_element_type | solution.py:73
  33.2 1.1 %fusion.36 = (bf16[16,32,2,128]{3,1,2,0:T(8,128)(2,1)S(1)}, bf16[16,2,4,8,128]{4,3,2,1,0:T(8,128)(2,1)}) fusion(bf16[16,32,2,128]{3,1,2,0:T(8,128)(2,1)S(1)} %fusion.64, bf16[32,32]{1,0:T(8,128)(2,1)S(1)} %copy-done, bf16[16,32,256]{2,1,0:T(8,128)(2,1)S(1)} %gather_fusion.3), kind=kOutput, calls=%fused_computation.75 | convolution fusion | flops 9961472 | bytes 1050624 | tf_op jit(solution)/shard_map/gf,cfhw->cghw/dot_general | solution.py:74
  34.3 0.2 convolution_bitcast_fusion.3
  34.5 2.3 %fusion.34 = (f32[32]{0:T(128)}, f32[32]{0:T(128)}, f32[32]{0:T(128)}, f32[32]{0:T(128)}, f32[32]{0:T(128)}, /*index=5*/f32[32]{0:T(128)}, bf16[16,2,128,32]{2,3,1,0:T(8,128)(2,1)S(1)}) fusion(bf16[16,32,6,132]{3,1,2,0:T(8,128)(2,1)S(1)} %get-tuple-element.68, bf16[16,32,2,128]{3,1,2,0:T(8,128)(2,1)} %collective-permute-done, ...), kind=kOutput, calls=%fused_computation.72 | convolution fusion | flops 11272000 | bytes 1837824 | tf_op jit(solution)/shard_map/gf,cghw->cfhw/dot_general | solution.py:116
  36.8 2.3 %fusion.35 = (f32[32]{0:T(128)}, f32[32]{0:T(128)}, f32[32]{0:T(128)}, f32[32]{0:T(128)}, f32[32]{0:T(128)}, /*index=5*/f32[32]{0:T(128)}, f32[32]{0:T(128)}, f3...) fusion(bf16[16,32,6,132]{3,1,2,0:T(8,128)(2,1)S(1)} %get-tuple-, ...), kind=kLoop, calls=%fused_computation.73 | loop fusion | flops 7208384 | bytes 4983040 | tf_op jit(solution)/shard_map/cfhw,cfhw->f/dot_general | solution.py:131
  39.3 0.6 gather_fusion
  40.1 0.6 fusion.9
  40.8 0.8 multiply_reduce_fusion
  42.0 0.1 reshape.81
  42.3 7.2 %collective-permute-start.2 = (bf16[16,32,256]{2,1,0:T(8,128)(2,1)S(1)}, bf16[16,32,256]{2,1,0:T(8,128)(2,1)S(1)}, u32[]{:S(2)}, u32[]{:S(2)}) collective-permute-start(bf16[16,32,256]{2,1,0:T(8,128)(2,1)S(1)} %gather_fusion), channel_id=1, source_target_pairs={{4,0},{8,4},{12,8},{0,12},{5,1},{9,5},{13,9},{1,13},{6,2},{10,6},{... | collective-permute-start | bytes 786440 | tf_op jit(solution)/shard_map/ppermute | solution.py:25
  49.4 1.6 %collective-permute-start.11 = (f32[8992]{0:T(1024)S(1)}, f32[8992]{0:T(1024)S(1)}, u32[]{:S(2)}, u32[]{:S(2)}) collective-permute-start(f32[8992]{0:T(1024)S(1)} %fusion.134), channel_id=1, source_target_pairs={{0,2},{2,0},{1,3},{3,1},{4,6},{6,4},{5,7},{7,5},{8,10},{10,8},{9,1... | collective-permute-start | bytes 107912 | tf_op jit(solution)/shard_map/ppermute | solution.py:36
  51.0 2.5 %collective-permute-done.11 = f32[8992]{0:T(1024)S(1)} collective-permute-done((f32[8992]{0:T(1024)S(1)}, f32[8992]{0:T(1024)S(1)}, u32[]{:S(2)}, u32[]{:S(2)}) %collective-permute-start.11) | collective-permute-done | bytes 36000 | tf_op jit(solution)/shard_map/ppermute | solution.py:36
  53.5 0.1 collective-permute-start.12
  53.6 3.8 %collective-permute-done.12 = f32[8992]{0:T(1024)S(1)} collective-permute-done((f32[8992]{0:T(1024)S(1)}, f32[8992]{0:T(1024)S(1)}, u32[]{:S(2)}, u32[]{:S(2)}) %collective-permute-start.12) | collective-permute-done | bytes 36000 | tf_op jit(solution)/shard_map/ppermute | solution.py:36
  57.4 1.4 %collective-permute-start.13 = (f32[8992]{0:T(1024)S(1)}, f32[8992]{0:T(1024)S(1)}, u32[]{:S(2)}, u32[]{:S(2)}) collective-permute-start(f32[8992]{0:T(1024)S(1)} %add.280), channel_id=1, source_target_pairs={{0,8},{4,12},{8,0},{12,4},{1,9},{5,13},{9,1},{13,5},{2,10},{6,14},... | collective-permute-start | bytes 107912 | tf_op jit(solution)/shard_map/ppermute | solution.py:36
  58.8 1.6 %collective-permute-start.3 = (bf16[16,32,256]{2,1,0:T(8,128)(2,1)S(1)}, bf16[16,32,256]{2,1,0:T(8,128)(2,1)S(1)}, u32[]{:S(2)}, u32[]{:S(2)}) collective-permute-start(bf16[16,32,256]{2,1,0:T(8,128)(2,1)S(1)} %gather_fusion), channel_id=1, source_target_pairs={{8,0},{12,4},{0,8},{4,12},{9,1},{13,5},{1,9},{5,13},{10,2},{14,6},... | collective-permute-start | bytes 786440 | tf_op jit(solution)/shard_map/ppermute | solution.py:25
  60.4 1.4 %collective-permute-start.4 = (bf16[16,32,256]{2,1,0:T(8,128)(2,1)S(1)}, bf16[16,32,256]{2,1,0:T(8,128)(2,1)S(1)}, u32[]{:S(2)}, u32[]{:S(2)}) collective-permute-start(bf16[16,32,256]{2,1,0:T(8,128)(2,1)S(1)} %gather_fusion), channel_id=1, source_target_pairs={{12,0},{0,4},{4,8},{8,12},{13,1},{1,5},{5,9},{9,13},{14,2},{2,6},{... | collective-permute-start | bytes 786440 | tf_op jit(solution)/shard_map/ppermute | solution.py:25
  61.8 1.3 %collective-permute-start.9 = (bf16[16,32,2,128]{3,1,2,0:T(8,128)(2,1)S(1)}, bf16[16,32,2,128]{3,1,2,0:T(8,128)(2,1)S(1)}, u32[]{:S(2)}, u32[]{:S(2)}) collective-permute-start(bf16[16,32,2,128]{3,1,2,0:T(8,128)(2,1)S(1)} %bitcast.343), channel_id=1, source_target_pairs={{1,0},{2,1},{3,2},{5,4},{6,5},{7,6},{9,8},{10,9},{11,10},{13,12},{... | collective-permute-start | bytes 786440 | tf_op jit(solution)/shard_map/ppermute | solution.py:17
  63.1 3.2 %collective-permute-start.8 = (bf16[16,32,2,128]{3,1,2,0:T(8,128)(2,1)S(1)}, bf16[16,32,2,128]{3,1,2,0:T(8,128)(2,1)S(1)}, u32[]{:S(2)}, u32[]{:S(2)}) collective-permute-start(bf16[16,32,2,128]{3,1,2,0:T(8,128)(2,1)S(1)} %bitcast.344), channel_id=1, source_target_pairs={{0,1},{1,2},{2,3},{4,5},{5,6},{6,7},{8,9},{9,10},{10,11},{12,13},{... | collective-permute-start | bytes 786440 | tf_op jit(solution)/shard_map/ppermute | solution.py:14
  66.5 0.7 reshape.85
  67.2 0.7 split.13
  67.9 0.7 reshape.86
  68.7 10.9 %collective-permute-done.3 = bf16[16,32,256]{2,1,0:T(8,128)(2,1)S(1)} collective-permute-done((bf16[16,32,256]{2,1,0:T(8,128)(2,1)S(1)}, bf16[16,32,256]{2,1,0:T(8,128)(2,1)S(1)}, u32[]{:S(2)}, u32[]{:S(2)}) %collective-permute-start.3) | collective-permute-done | bytes 262176 | tf_op jit(solution)/shard_map/ppermute | solution.py:25
  79.9 0.6 fusion.7
  80.6 0.6 gather_fusion.1
  81.2 0.3 reshape.87
  81.4 1.0 %add_convert_fusion = bf16[16,32,2,128]{3,2,1,0:T(2,128)(2,1)} fusion(f32[16,32,2,128]{3,2,1,0:T(2,128)S(1)} %reshape.87, bf16[16,32,2,128]{3,2,1,0:T(2,128)(2,1)S(1)} %copy-done.2), kind=kLoop, calls=%fused_computation.179 | loop fusion | flops 393216 | bytes 1048576 | tf_op jit(solution)/shard_map/convert_element_type | solution.py:113
  82.5 0.7 fusion.3
  83.2 0.1 copy-done.3
  83.5 3.0 %fusion.39 = bf16[16,32,2,128]{3,1,2,0:T(8,128)(2,1)S(1)} fusion(f32[16,32,6,132]{3,1,2,0:T(8,128)S(1)} %fusion.3, bf16[16,32,2,128]{3,2,1,0:T(2,128)(2,1)S(1)} %copy-done.3, f32[32]{0:T(128)S(1)} %copy-done.6, f32[32]{0:T(128)S(1)} %copy-done.7, f32[32]{0:T(128)S(1)} %copy-done.9, f32[32]{0:T(128)S(1)} %copy-done.10, f32[32]{0:T(128)S(1)} %copy-done.11, ...), kind=kLoop, calls=%fused_computation.79 | loop fusion | flops 6815744 | bytes 13634688 | tf_op jit(solution)/shard_map/convert_element_type | solution.py:139
  86.5 0.9 %copy.48 = bf16[16,32,2,128]{3,2,1,0:T(2,128)(2,1)} copy(bf16[16,32,2,128]{3,1,2,0:T(8,128)(2,1)S(1)} %fusion.39) | data formatting | bytes 524288
  (170 shorter events, 1.8 us)
Async XLA Ops:
  0.6 32.5 %copy-start = (bf16[32,32]{1,0:T(8,128)(2,1)S(1)}, bf16[32,32]{1,0:T(8,128)(2,1)}, u32[]{:S(2)}) copy-start(bf16[32,32]{1,0:T(8,128)(2,1)} %param.9) | copy-start | bytes 6148
  0.6 17.9 %copy-start.1 = (f32[32,25]{1,0:T(8,128)S(1)}, f32[32,25]{1,0:T(8,128)}, u32[]{:S(2)}) copy-start(f32[32,25]{1,0:T(8,128)} %param.8) | copy-start | bytes 9604
  0.7 19.0 %copy-start.5 = (bf16[7,32,32]{2,1,0:T(8,128)(2,1)S(1)}, bf16[7,32,32]{2,1,0:T(8,128)(2,1)}, u32[]{:S(2)}) copy-start(bf16[7,32,32]{2,1,0:T(8,128)(2,1)} %param.10) | copy-start | bytes 43012
  3.8 22.8 %collective-permute-start.7 = (bf16[16,32,256]{2,1,0:T(8,128)(2,1)S(1)}, bf16[16,32,256]{2,1,0:T(8,128)(2,1)S(1)}, u32[]{:S(2)}, u32[]{:S(2)}) collective-permute-start(bf16[16,32,256]{2,1,0:T(8,128)(2,1)S(1)} %gather_fusion.2), channel_id=1, source_target_pairs={{12,0},{0,4},{4,8},{8,12},{13,1},{1,5},{5,9},{9,13},{14,2},{2,6},{... | collective-permute-start | bytes 786440 | tf_op jit(solution)/shard_map/ppermute | solution.py:25
  6.9 19.7 %collective-permute-start.6 = (bf16[16,32,256]{2,1,0:T(8,128)(2,1)S(1)}, bf16[16,32,256]{2,1,0:T(8,128)(2,1)S(1)}, u32[]{:S(2)}, u32[]{:S(2)}) collective-permute-start(bf16[16,32,256]{2,1,0:T(8,128)(2,1)S(1)} %gather_fusion.2), channel_id=1, source_target_pairs={{8,0},{12,4},{0,8},{4,12},{9,1},{13,5},{1,9},{5,13},{10,2},{14,6},... | collective-permute-start | bytes 786440 | tf_op jit(solution)/shard_map/ppermute | solution.py:25
  9.5 14.3 %collective-permute-start.5 = (bf16[16,32,256]{2,1,0:T(8,128)(2,1)S(1)}, bf16[16,32,256]{2,1,0:T(8,128)(2,1)S(1)}, u32[]{:S(2)}, u32[]{:S(2)}) collective-permute-start(bf16[16,32,256]{2,1,0:T(8,128)(2,1)S(1)} %gather_fusion.2), channel_id=1, source_target_pairs={{4,0},{8,4},{12,8},{0,12},{5,1},{9,5},{13,9},{1,13},{6,2},{10,6},{... | collective-permute-start | bytes 786440 | tf_op jit(solution)/shard_map/ppermute | solution.py:25
  11.8 16.4 %collective-permute-start.1 = (bf16[16,32,2,128]{3,1,2,0:T(8,128)(2,1)S(1)}, bf16[16,32,2,128]{3,1,2,0:T(8,128)(2,1)S(1)}, u32[]{:S(2)}, u32[]{:S(2)}) collective-permute-start(bf16[16,32,2,128]{3,1,2,0:T(8,128)(2,1)S(1)} %copy.27), channel_id=1, source_target_pairs={{1,0},{2,1},{3,2},{5,4},{6,5},{7,6},{9,8},{10,9},{11,10},{13,12},{... | collective-permute-start | bytes 786440 | tf_op jit(solution)/shard_map/ppermute | solution.py:17
  13.1 15.1 %collective-permute-start = (bf16[16,32,2,128]{3,1,2,0:T(8,128)(2,1)S(1)}, bf16[16,32,2,128]{3,1,2,0:T(8,128)(2,1)}, u32[]{:S(2)}, u32[]{:S(2)}) collective-permute-start(bf16[16,32,2,128]{3,1,2,0:T(8,128)(2,1)S(1)} %copy.27), channel_id=1, source_target_pairs={{0,1},{1,2},{2,3},{4,5},{5,6},{6,7},{8,9},{9,10},{10,11},{12,13},{... | collective-permute-start | bytes 786440 | tf_op jit(solution)/shard_map/ppermute | solution.py:14
  28.0 2.0 %copy-start.6 = (f32[32]{0:T(128)S(1)}, f32[32]{0:T(128)}, u32[]{:S(2)}) copy-start(f32[32]{0:T(128)} %get-tuple-element.66) | copy-start | bytes 388
  28.0 2.0 %copy-start.7 = (f32[32]{0:T(128)S(1)}, f32[32]{0:T(128)}, u32[]{:S(2)}) copy-start(f32[32]{0:T(128)} %get-tuple-element.67) | copy-start | bytes 388
  28.0 2.0 %copy-start.8 = (f32[32]{0:T(128)S(1)}, f32[32]{0:T(128)}, u32[]{:S(2)}) copy-start(f32[32]{0:T(128)} %get-tuple-element.43) | copy-start | bytes 388
  28.0 2.0 %copy-start.9 = (f32[32]{0:T(128)S(1)}, f32[32]{0:T(128)}, u32[]{:S(2)}) copy-start(f32[32]{0:T(128)} %get-tuple-element.44) | copy-start | bytes 388
  28.0 2.0 %copy-start.10 = (f32[32]{0:T(128)S(1)}, f32[32]{0:T(128)}, u32[]{:S(2)}) copy-start(f32[32]{0:T(128)} %get-tuple-element.45) | copy-start | bytes 388
  28.0 2.0 %copy-start.11 = (f32[32]{0:T(128)S(1)}, f32[32]{0:T(128)}, u32[]{:S(2)}) copy-start(f32[32]{0:T(128)} %get-tuple-element.46) | copy-start | bytes 388
  28.0 2.0 %copy-start.12 = (f32[32]{0:T(128)S(1)}, f32[32]{0:T(128)}, u32[]{:S(2)}) copy-start(f32[32]{0:T(128)} %get-tuple-element.47) | copy-start | bytes 388
  28.0 2.0 %copy-start.13 = (f32[32]{0:T(128)S(1)}, f32[32]{0:T(128)}, u32[]{:S(2)}) copy-start(f32[32]{0:T(128)} %get-tuple-element.48) | copy-start | bytes 388
  28.0 2.0 %copy-start.14 = (f32[32]{0:T(128)S(1)}, f32[32]{0:T(128)}, u32[]{:S(2)}) copy-start(f32[32]{0:T(128)} %get-tuple-element.49) | copy-start | bytes 388
  28.1 2.0 %copy-start.15 = (f32[32]{0:T(128)S(1)}, f32[32]{0:T(128)}, u32[]{:S(2)}) copy-start(f32[32]{0:T(128)} %get-tuple-element.50) | copy-start | bytes 388
  28.1 2.0 %copy-start.17 = (f32[32]{0:T(128)S(1)}, f32[32]{0:T(128)}, u32[]{:S(2)}) copy-start(f32[32]{0:T(128)} %get-tuple-element.51) | copy-start | bytes 388
  28.1 2.0 %copy-start.19 = (f32[32]{0:T(128)S(1)}, f32[32]{0:T(128)}, u32[]{:S(2)}) copy-start(f32[32]{0:T(128)} %get-tuple-element.52) | copy-start | bytes 388
  28.1 2.0 %copy-start.21 = (f32[32]{0:T(128)S(1)}, f32[32]{0:T(128)}, u32[]{:S(2)}) copy-start(f32[32]{0:T(128)} %get-tuple-element.53) | copy-start | bytes 388
  28.1 2.0 %copy-start.23 = (f32[32]{0:T(128)S(1)}, f32[32]{0:T(128)}, u32[]{:S(2)}) copy-start(f32[32]{0:T(128)} %get-tuple-element.54) | copy-start | bytes 388
  28.1 2.0 %copy-start.25 = (f32[32]{0:T(128)S(1)}, f32[32]{0:T(128)}, u32[]{:S(2)}) copy-start(f32[32]{0:T(128)} %get-tuple-element.55) | copy-start | bytes 388
  28.1 2.0 %copy-start.27 = (f32[32]{0:T(128)S(1)}, f32[32]{0:T(128)}, u32[]{:S(2)}) copy-start(f32[32]{0:T(128)} %get-tuple-element.56) | copy-start | bytes 388
  28.1 2.0 %copy-start.29 = (f32[32]{0:T(128)S(1)}, f32[32]{0:T(128)}, u32[]{:S(2)}) copy-start(f32[32]{0:T(128)} %get-tuple-element.57) | copy-start | bytes 388
  28.1 2.0 %copy-start.31 = (f32[32]{0:T(128)S(1)}, f32[32]{0:T(128)}, u32[]{:S(2)}) copy-start(f32[32]{0:T(128)} %get-tuple-element.58) | copy-start | bytes 388
  28.1 2.0 %copy-start.33 = (f32[32]{0:T(128)S(1)}, f32[32]{0:T(128)}, u32[]{:S(2)}) copy-start(f32[32]{0:T(128)} %get-tuple-element.59) | copy-start | bytes 388
  28.2 2.0 %copy-start.35 = (f32[32]{0:T(128)S(1)}, f32[32]{0:T(128)}, u32[]{:S(2)}) copy-start(f32[32]{0:T(128)} %get-tuple-element.60) | copy-start | bytes 388
  28.2 2.0 %copy-start.37 = (f32[32]{0:T(128)S(1)}, f32[32]{0:T(128)}, u32[]{:S(2)}) copy-start(f32[32]{0:T(128)} %get-tuple-element.61) | copy-start | bytes 388
  36.8 2.4 %copy-start.4 = (bf16[16,2,4,8,128]{4,3,2,1,0:T(8,128)(2,1)S(1)}, bf16[16,2,4,8,128]{4,3,2,1,0:T(8,128)(2,1)}, u32[]{:S(2)}) copy-start(bf16[16,2,4,8,128]{4,3,2,1,0:T(8,128)(2,1)} %get-tuple-element.71) | copy-start | bytes 786436
  39.9 1.7 %copy-start.39 = (f32[32]{0:T(128)S(1)}, f32[32]{0:T(128)}, u32[]{:S(2)}) copy-start(f32[32]{0:T(128)} %get-tuple-element.15) | copy-start | bytes 388
  39.9 1.7 %copy-start.40 = (f32[32]{0:T(128)S(1)}, f32[32]{0:T(128)}, u32[]{:S(2)}) copy-start(f32[32]{0:T(128)} %get-tuple-element.16) | copy-start | bytes 388
  39.9 1.7 %copy-start.41 = (f32[32]{0:T(128)S(1)}, f32[32]{0:T(128)}, u32[]{:S(2)}) copy-start(f32[32]{0:T(128)} %get-tuple-element.17) | copy-start | bytes 388
  39.9 1.7 %copy-start.42 = (f32[32]{0:T(128)S(1)}, f32[32]{0:T(128)}, u32[]{:S(2)}) copy-start(f32[32]{0:T(128)} %get-tuple-element.18) | copy-start | bytes 388
  39.9 1.7 %copy-start.43 = (f32[32]{0:T(128)S(1)}, f32[32]{0:T(128)}, u32[]{:S(2)}) copy-start(f32[32]{0:T(128)} %get-tuple-element.19) | copy-start | bytes 388
  39.9 1.7 %copy-start.44 = (f32[32]{0:T(128)S(1)}, f32[32]{0:T(128)}, u32[]{:S(2)}) copy-start(f32[32]{0:T(128)} %get-tuple-element.20) | copy-start | bytes 388
  39.9 1.7 %copy-start.45 = (f32[32]{0:T(128)S(1)}, f32[32]{0:T(128)}, u32[]{:S(2)}) copy-start(f32[32]{0:T(128)} %get-tuple-element.21) | copy-start | bytes 388
  39.9 1.7 %copy-start.46 = (f32[32]{0:T(128)S(1)}, f32[32]{0:T(128)}, u32[]{:S(2)}) copy-start(f32[32]{0:T(128)} %get-tuple-element.22) | copy-start | bytes 388
  39.9 1.7 %copy-start.47 = (f32[32]{0:T(128)S(1)}, f32[32]{0:T(128)}, u32[]{:S(2)}) copy-start(f32[32]{0:T(128)} %get-tuple-element.23) | copy-start | bytes 388
  42.2 7.2 %collective-permute-start.10 = (f32[8992]{0:T(1024)S(1)}, f32[8992]{0:T(1024)S(1)}, u32[]{:S(2)}, u32[]{:S(2)}) collective-permute-start(f32[8992]{0:T(1024)S(1)} %broadcast_multiply_fusion), channel_id=1, source_target_pairs={{0,1},{1,0},{2,3},{3,2},{4,5},{5,4},{6,7},{7,6},{8,9},{9,8},{10,11... | collective-permute-start | bytes 107912 | tf_op jit(solution)/shard_map/ppermute | solution.py:36
  42.3 26.4 %collective-permute-start.2 = (bf16[16,32,256]{2,1,0:T(8,128)(2,1)S(1)}, bf16[16,32,256]{2,1,0:T(8,128)(2,1)S(1)}, u32[]{:S(2)}, u32[]{:S(2)}) collective-permute-start(bf16[16,32,256]{2,1,0:T(8,128)(2,1)S(1)} %gather_fusion), channel_id=1, source_target_pairs={{4,0},{8,4},{12,8},{0,12},{5,1},{9,5},{13,9},{1,13},{6,2},{10,6},{... | collective-permute-start | bytes 786440 | tf_op jit(solution)/shard_map/ppermute | solution.py:25
  49.4 4.0 %collective-permute-start.11 = (f32[8992]{0:T(1024)S(1)}, f32[8992]{0:T(1024)S(1)}, u32[]{:S(2)}, u32[]{:S(2)}) collective-permute-start(f32[8992]{0:T(1024)S(1)} %fusion.134), channel_id=1, source_target_pairs={{0,2},{2,0},{1,3},{3,1},{4,6},{6,4},{5,7},{7,5},{8,10},{10,8},{9,1... | collective-permute-start | bytes 107912 | tf_op jit(solution)/shard_map/ppermute | solution.py:36
  53.5 4.0 %collective-permute-start.12 = (f32[8992]{0:T(1024)S(1)}, f32[8992]{0:T(1024)S(1)}, u32[]{:S(2)}, u32[]{:S(2)}) collective-permute-start(f32[8992]{0:T(1024)S(1)} %add.279), channel_id=1, source_target_pairs={{0,4},{4,0},{8,12},{12,8},{1,5},{5,1},{9,13},{13,9},{2,6},{6,2},{1... | collective-permute-start | bytes 107912 | tf_op jit(solution)/shard_map/ppermute | solution.py:36
  57.4 5.7 %collective-permute-start.13 = (f32[8992]{0:T(1024)S(1)}, f32[8992]{0:T(1024)S(1)}, u32[]{:S(2)}, u32[]{:S(2)}) collective-permute-start(f32[8992]{0:T(1024)S(1)} %add.280), channel_id=1, source_target_pairs={{0,8},{4,12},{8,0},{12,4},{1,9},{5,13},{9,1},{13,5},{2,10},{6,14},... | collective-permute-start | bytes 107912 | tf_op jit(solution)/shard_map/ppermute | solution.py:36
  58.8 20.8 %collective-permute-start.3 = (bf16[16,32,256]{2,1,0:T(8,128)(2,1)S(1)}, bf16[16,32,256]{2,1,0:T(8,128)(2,1)S(1)}, u32[]{:S(2)}, u32[]{:S(2)}) collective-permute-start(bf16[16,32,256]{2,1,0:T(8,128)(2,1)S(1)} %gather_fusion), channel_id=1, source_target_pairs={{8,0},{12,4},{0,8},{4,12},{9,1},{13,5},{1,9},{5,13},{10,2},{14,6},... | collective-permute-start | bytes 786440 | tf_op jit(solution)/shard_map/ppermute | solution.py:25
  60.4 19.3 %collective-permute-start.4 = (bf16[16,32,256]{2,1,0:T(8,128)(2,1)S(1)}, bf16[16,32,256]{2,1,0:T(8,128)(2,1)S(1)}, u32[]{:S(2)}, u32[]{:S(2)}) collective-permute-start(bf16[16,32,256]{2,1,0:T(8,128)(2,1)S(1)} %gather_fusion), channel_id=1, source_target_pairs={{12,0},{0,4},{4,8},{8,12},{13,1},{1,5},{5,9},{9,13},{14,2},{2,6},{... | collective-permute-start | bytes 786440 | tf_op jit(solution)/shard_map/ppermute | solution.py:25
  61.8 20.7 %collective-permute-start.9 = (bf16[16,32,2,128]{3,1,2,0:T(8,128)(2,1)S(1)}, bf16[16,32,2,128]{3,1,2,0:T(8,128)(2,1)S(1)}, u32[]{:S(2)}, u32[]{:S(2)}) collective-permute-start(bf16[16,32,2,128]{3,1,2,0:T(8,128)(2,1)S(1)} %bitcast.343), channel_id=1, source_target_pairs={{1,0},{2,1},{3,2},{5,4},{6,5},{7,6},{9,8},{10,9},{11,10},{13,12},{... | collective-permute-start | bytes 786440 | tf_op jit(solution)/shard_map/ppermute | solution.py:17
  63.1 19.4 %collective-permute-start.8 = (bf16[16,32,2,128]{3,1,2,0:T(8,128)(2,1)S(1)}, bf16[16,32,2,128]{3,1,2,0:T(8,128)(2,1)S(1)}, u32[]{:S(2)}, u32[]{:S(2)}) collective-permute-start(bf16[16,32,2,128]{3,1,2,0:T(8,128)(2,1)S(1)} %bitcast.344), channel_id=1, source_target_pairs={{0,1},{1,2},{2,3},{4,5},{5,6},{6,7},{8,9},{9,10},{10,11},{12,13},{... | collective-permute-start | bytes 786440 | tf_op jit(solution)/shard_map/ppermute | solution.py:14
  (29 other events, 39.6 us)

commit v3 on v2

--- a/solution.py
+++ b/solution.py
@@ -25,16 +25,22 @@
     return lax.ppermute(block, axis, route)
 
 
-def all_summed(value, axes):
+def all_summed(value, axes, tied=None):
+    rounds = []
     for axis in axes:
         count = lax.axis_size(axis)
         if count & (count - 1):
+            rounds.append((axis, 0))
+        else:
+            rounds.extend((axis, 1 << bit) for bit in range(count.bit_length() - 1))
+    for index, (axis, step) in enumerate(rounds):
+        if tied is not None and index == len(rounds) - 1:
+            value, _ = lax.optimization_barrier((value, tied))
+        if step == 0:
             value = lax.psum(value, axis)
-            continue
-        step = 1
-        while step < count:
+        else:
+            count = lax.axis_size(axis)
             value = value + lax.ppermute(value, axis, [(i, i ^ step) for i in range(count)])
-            step *= 2
     return value
 
 
@@ -82,21 +88,26 @@
     h_sorted = hidden_flat[order]
     g_sorted = grad_flat[order]
     h_taps = [h_sorted] * taps
+    h_received = []
+    g_received = []
     g_taps = [g_sorted] * taps
     for dist in range(1, half + 1):
         for sign in (-1, 1):
             h_far = passed_along(h_sorted, "chan", -sign * dist)
+            h_received.append(h_far)
             g_far = passed_along(g_sorted, "chan", -sign * dist)
-            if sign < 0:
-                wrapped = device < dist
-                h_near = jnp.where(wrapped, move_down(h_far), h_far)
-                g_near = jnp.where(wrapped, move_down(g_far), g_far)
-            else:
-                wrapped = device + dist >= n_chan
-                h_near = jnp.where(wrapped, move_up(h_far), h_far)
-                g_near = jnp.where(wrapped, move_up(g_far), g_far)
-            h_taps[half + sign * dist] = h_near
-            g_taps[half + sign * dist] = g_near
+            g_received.append(g_far)
+    g_received, mixed_late = lax.optimization_barrier((g_received, mixed))
+    for index, (dist, sign) in enumerate((d, s) for d in range(1, half + 1) for s in (-1, 1)):
+        if sign < 0:
+            wrapped = device < dist
+            shift = move_down
+        else:
+            wrapped = device + dist >= n_chan
+            shift = move_up
+        h_far, g_far = h_received[index], g_received[index]
+        h_taps[half + sign * dist] = jnp.where(wrapped, shift(h_far), h_far)
+        g_taps[half + sign * dist] = jnp.where(wrapped, shift(g_far), g_far)
     h_stack = jnp.stack(h_taps, 1).reshape(chans, taps * feats, pixels)
     g_stack = jnp.stack(g_taps, 1).reshape(chans, taps * feats, pixels)
     fwd_weight = spectral_kernel.transpose(1, 0, 2).reshape(feats, taps * feats)
@@ -111,7 +122,7 @@
     spec = spec_flat.reshape(chans, feats, rows, cols)
     back = back_flat.reshape(chans, feats, rows, cols)
     restored = (dirty.astype(jnp.float32) + spec.astype(jnp.float32)).astype(jnp.bfloat16)
-    dmixed = (back.astype(jnp.float32) * silu_slope(mixed)).astype(jnp.bfloat16)
+    dmixed = (back.astype(jnp.float32) * silu_slope(mixed_late)).astype(jnp.bfloat16)
     mix_term = jnp.einsum("cghw,cfhw->gf", dmixed, smooth, preferred_element_type=jnp.float32)
     dsmooth = jnp.einsum(
         "gf,cghw->cfhw", feature_mix, dmixed, preferred_element_type=jnp.float32
@@ -139,7 +150,7 @@
     dirty_grad = (cotangent.astype(jnp.float32) + conv).astype(jnp.bfloat16)
     parts = (kernel_term, mix_term, spec_grad)
     flat = jnp.concatenate([part.reshape(-1) for part in parts]) * scale
-    flat = all_summed(flat, ("sub", "tile", "chan"))
+    flat = all_summed(flat, ("sub", "tile", "chan"), tied=h_received)
     sizes = [part.size for part in parts]
     kgrad, mgrad, sgrad = (
         piece.reshape(part.shape)

time: 87.9 us -> 93.2 us (1.060)
  waiting for transfers between devices: 24 us -> 36.7 us
  starting transfers between devices: 29.8 us -> 20.2 us
  local copies, waits for them, and re-layouts: 12.4 us -> 15.8 us
    ppermute x6, waiting for transfers between devices: 17.7 us -> 33.7 us  [passed_along(): return lax.ppermute(block, axis, route)]
    ppermute x6, starting transfers between devices: 17.2 us -> 9.7 us  [passed_along(): return lax.ppermute(block, axis, route)]
    ppermute x2, starting transfers between devices: 6.96 us -> 3.67 us  [padded(): lax.ppermute(lax.slice_in_dim(block, block.shape[dim] - width, None, axis...]
    ppermute x4, waiting for transfers between devices: 6.3 us -> 3.04 us  [all_summed(): lax.ppermute(value, axis, [(i, i ^ step) for i in range(count)])]
    unnamed x130 -> x76, local copies, waits for them, and re-layouts: 2.38 us -> 3.8 us
    another operation x2, local copies, waits for them, and re-layouts: 0.18 us -> 1.52 us  [local(): kernel_term = jnp.stack(terms, 1)]
    slice x2, local copies, waits for them, and re-layouts: 2.85 us -> 1.75 us  [local(): spatial_kernel[:, i * 5 + j][None, :, None, None]]
    gather x1, local copies, waits for them, and re-layouts: 0.56 us -> 1.55 us  [local(): h_sorted = hidden_flat[order]]
  transfers between devices with their start and end apart: 14 -> 14, of which waited for: 5 -> 6; matrix products, arithmetic and copies ran while one was open for 12% -> 19% of each run, Pallas kernels for 0% -> 0%
where the time goes in v3:
time: 93.2 us; the launch traced here: 92.7 us
  waiting for transfers between devices  36.7 us (39%)
  starting transfers between devices  20.2 us (22%)
  local copies, waits for them, and re-layouts  15.8 us (17%)
  other arithmetic  14.2 us (15%)
  matrix products  4.38 us (5%)
  between operations  1.47 us (2%)
    ppermute x6, waiting for transfers between devices, passed_along(): return lax.ppermute(block, axis, route)  33.7 us
    ppermute x6, starting transfers between devices, passed_along(): return lax.ppermute(block, axis, route)  9.7 us
    ppermute x4, starting transfers between devices, all_summed(): lax.ppermute(value, axis, [(i, i ^ step) for i in range(count)])  4.05 us
    unnamed x76, local copies, waits for them, and re-layouts  3.8 us
    ppermute x2, starting transfers between devices, padded(): lax.ppermute(lax.slice_in_dim(block, block.shape[dim] - width, None, axis...  3.67 us
    dot_general x2, other arithmetic, local(): jnp.einsum('cfhw,cfhw->f', dsmooth, xpad[:, :, i:i + rows, j:j + cols], p...  3.11 us
    ppermute x4, waiting for transfers between devices, all_summed(): lax.ppermute(value, axis, [(i, i ^ step) for i in range(count)])  3.04 us
    convert_element_type x1, other arithmetic, local(): dirty_grad = (cotangent.astype(jnp.float32) + conv).astype(jnp.bfloat16)  3.04 us
  transfers between devices with their start and end apart: 14, of which 6 were waited for; matrix products, arithmetic and copies ran while one was open for 19% of the time, Pallas kernels for 0%

profile of v3, /device:TPU:0, one launch (start us, length us, event | category | flops | bytes accessed | tf_op | source)
XLA Modules:
  0.0 92.7 jit_solution(4518128309115958977)
XLA Ops:
  0.7 1.0 %copy.27 = bf16[16,32,2,128]{3,1,2,0:T(8,128)(2,1)S(1)} copy(bf16[16,32,2,128]{3,2,1,0:T(2,128)(2,1)} %param.6) | data formatting | bytes 524288 | tf_op args[0]
  1.7 2.4 %collective-permute-start = (bf16[16,32,2,128]{3,1,2,0:T(8,128)(2,1)S(1)}, bf16[16,32,2,128]{3,1,2,0:T(8,128)(2,1)S(1)}, u32[]{:S(2)}, u32[]{:S(2)}) collective-permute-start(bf16[16,32,2,128]{3,1,2,0:T(8,128)(2,1)S(1)} %copy.27), channel_id=1, source_target_pairs={{0,1},{1,2},{2,3},{4,5},{5,6},{6,7},{8,9},{9,10},{10,11},{12,13},{... | collective-permute-start | bytes 786440 | tf_op jit(solution)/shard_map/ppermute | solution.py:14
  4.1 1.3 %collective-permute-start.1 = (bf16[16,32,2,128]{3,1,2,0:T(8,128)(2,1)S(1)}, bf16[16,32,2,128]{3,1,2,0:T(8,128)(2,1)S(1)}, u32[]{:S(2)}, u32[]{:S(2)}) collective-permute-start(bf16[16,32,2,128]{3,1,2,0:T(8,128)(2,1)S(1)} %copy.27), channel_id=1, source_target_pairs={{1,0},{2,1},{3,2},{5,4},{6,5},{7,6},{9,8},{10,9},{11,10},{13,12},{... | collective-permute-start | bytes 786440 | tf_op jit(solution)/shard_map/ppermute | solution.py:17
  5.4 0.7 compare_select_fusion.1
  6.1 0.6 scatter_custom_fusion
  6.8 1.1 %reshape.80 = bf16[16,32,256]{2,1,0:T(8,128)(2,1)S(1)} reshape(bf16[16,32,2,128]{3,2,1,0:T(2,128)(2,1)} %param.7) | data formatting | bytes 524288 | tf_op jit(solution)/shard_map/reshape | solution.py:83
  7.9 0.6 gather_fusion.2
  8.5 2.5 %collective-permute-start.5 = (bf16[16,32,256]{2,1,0:T(8,128)(2,1)S(1)}, bf16[16,32,256]{2,1,0:T(8,128)(2,1)S(1)}, u32[]{:S(2)}, u32[]{:S(2)}) collective-permute-start(bf16[16,32,256]{2,1,0:T(8,128)(2,1)S(1)} %gather_fusion.2), channel_id=1, source_target_pairs={{12,0},{0,4},{4,8},{8,12},{13,1},{1,5},{5,9},{9,13},{14,2},{2,6},{... | collective-permute-start | bytes 786440 | tf_op jit(solution)/shard_map/ppermute | solution.py:25
  10.9 2.1 %collective-permute-start.6 = (bf16[16,32,256]{2,1,0:T(8,128)(2,1)S(1)}, bf16[16,32,256]{2,1,0:T(8,128)(2,1)S(1)}, u32[]{:S(2)}, u32[]{:S(2)}) collective-permute-start(bf16[16,32,256]{2,1,0:T(8,128)(2,1)S(1)} %gather_fusion.2), channel_id=1, source_target_pairs={{4,0},{8,4},{12,8},{0,12},{5,1},{9,5},{13,9},{1,13},{6,2},{10,6},{... | collective-permute-start | bytes 786440 | tf_op jit(solution)/shard_map/ppermute | solution.py:25
  13.0 0.9 %collective-permute-start.7 = (bf16[16,32,256]{2,1,0:T(8,128)(2,1)S(1)}, bf16[16,32,256]{2,1,0:T(8,128)(2,1)S(1)}, u32[]{:S(2)}, u32[]{:S(2)}) collective-permute-start(bf16[16,32,256]{2,1,0:T(8,128)(2,1)S(1)} %gather_fusion.2), channel_id=1, source_target_pairs={{8,0},{12,4},{0,8},{4,12},{9,1},{13,5},{1,9},{5,13},{10,2},{14,6},... | collective-permute-start | bytes 786440 | tf_op jit(solution)/shard_map/ppermute | solution.py:25
  14.0 0.8 rev.6
  14.8 1.2 %slice_reduce_fusion.23 = (f32[32]{0:T(128)S(1)}, f32[32]{0:T(128)S(1)}, f32[32]{0:T(128)S(1)}, f32[32]{0:T(128)S(1)}, f32[32]{0:T(128)S(1)}, /*index=5*/f32[32]{0:T(128)S(1)}) fusion(f32[32,25]{1,0:T(8,128)} %param.8), kind=kLoop, calls=%fused_computation.285 | loop fusion | bytes 1536 | tf_op jit(solution)/shard_map/slice | solution.py:76
  16.0 0.5 slice_reduce_fusion.24
  16.7 0.8 select_maximum_fusion.2
  17.5 3.0 %fusion.64 = bf16[16,32,2,128]{3,1,2,0:T(8,128)(2,1)S(1)} fusion(f32[16,32,6,132]{3,1,2,0:T(8,128)S(1)} %get-tuple-element.85, f32[32]{0:T(128)S(1)} %get-tuple-element.82, f32[32]{0:T(128)S(1)} %get-tuple-element.83, f32[32]{0:T(128)S(1)} %get-tuple-element.60, f32[32]{0:T(128)S(1)} %get-tuple-element.61, f32[32]{0:T(128)S(1)} %get-tuple-element.62, ...), kind=kLoop, calls=%fused_computation.129 | loop fusion | flops 6553600 | bytes 13372544 | tf_op jit(solution)/shard_map/convert_element_type | solution.py:79
  20.8 0.9 copy_bitcast_fusion
  21.6 3.9 %collective-permute-done.6 = bf16[16,32,256]{2,1,0:T(8,128)(2,1)S(1)} collective-permute-done((bf16[16,32,256]{2,1,0:T(8,128)(2,1)S(1)}, bf16[16,32,256]{2,1,0:T(8,128)(2,1)S(1)}, u32[]{:S(2)}, u32[]{:S(2)}) %collective-permute-start.6) | collective-permute-done | bytes 262176 | tf_op jit(solution)/shard_map/ppermute | solution.py:25
  25.6 11.3 %collective-permute-done.7 = bf16[16,32,256]{2,1,0:T(8,128)(2,1)S(1)} collective-permute-done((bf16[16,32,256]{2,1,0:T(8,128)(2,1)S(1)}, bf16[16,32,256]{2,1,0:T(8,128)(2,1)S(1)}, u32[]{:S(2)}, u32[]{:S(2)}) %collective-permute-start.7) | collective-permute-done | bytes 262176 | tf_op jit(solution)/shard_map/ppermute | solution.py:25
  37.3 1.2 %copy-done.2 = bf16[16,7,32,256]{3,2,0,1:T(8,128)(2,1)} copy-done((bf16[16,7,32,256]{3,2,0,1:T(8,128)(2,1)}, bf16[16,7,32,256]{3,2,0,1:T(8,128)(2,1)S(1)}, u32[]{:S(2)}) %copy-start.2) | copy-done | bytes 1835032
  38.6 0.4 fusion.8
  39.0 0.6 gather_fusion.3
  40.0 2.3 %fusion.34 = (f32[32]{0:T(128)}, f32[32]{0:T(128)}, f32[32]{0:T(128)}, f32[32]{0:T(128)}, f32[32]{0:T(128)}, /*index=5*/f32[32]{0:T(128)}, bf16[16,2,128,32]{2,3,1,0:T(8,128)(2,1)S(1)}) fusion(bf16[16,32,6,132]{3,1,2,0:T(8,128)(2,1)S(1)} %get-tuple-element.84, bf16[16,32,2,128]{3,1,2,0:T(8,128)(2,1)S(1)} %copy-done.11, ...), kind=kOutput, calls=%fused_computation.72 | convolution fusion | flops 11272000 | bytes 1837824 | tf_op jit(solution)/shard_map/gf,cghw->cfhw/dot_general | solution.py:127
  42.4 2.3 %fusion.35 = (f32[32]{0:T(128)S(1)}, f32[32]{0:T(128)S(1)}, f32[32]{0:T(128)S(1)}, f32[32]{0:T(128)S(1)}, f32[32]{0:T(128)S(1)}, /*index=5*/f32[32]{0:T(128)S(1)...) fusion(bf16[16,32,6,132]{3,1,2,0:T(8,128)(2,1)S(1)} %get-tuple-, ...), kind=kLoop, calls=%fused_computation.73 | loop fusion | flops 7208384 | bytes 4983040 | tf_op jit(solution)/shard_map/cfhw,cfhw->f/dot_general | solution.py:142
  44.8 1.5 %gather_fusion = bf16[16,32,256]{2,1,0:T(8,128)(2,1)S(1)} fusion(bf16[16,32,256]{2,1,0:T(8,128)(2,1)} %copy_bitcast_fusion, s32[1024]{0:T(1024)S(1)} %pad_clamp_fusion.1), kind=kCustom, calls=%fused_computation | custom fusion | bytes 524352 | tf_op jit(solution)/shard_map/gather | solution.py:88
  46.4 0.6 fusion.9
  47.2 0.8 multiply_reduce_fusion
  48.0 1.4 %stack.167 = f32[32,25]{0,1:T(8,128)S(1)} concatenate(f32[32,1]{0,1:T(1,128)} %bitcast.361, f32[32,1]{0,1:T(1,128)S(1)} %bitcast.359, f32[32,1]{0,1:T(1,128)} %bitcast.362, f32[32,1]{0,1:T(1,128)S(1)} %bitcast.358, f32[32,1]{0,1:T(1,128)S(1)} %bitcast.357, f32[32,1]{0,1:T(1,128)S(1)} %bitcast.356, f32[32,1]{0,1:T(1,128)S(1)} %bitcast.355, f32[32,1]{0,1:T(1,128)} %bitcast.363, ...), dimensions={1} | concatenate | bytes 6400 | tf_op jit(solution)/shard_map/stack | solution.py:149
  49.9 1.1 %collective-permute-done.10 = f32[8992]{0:T(1024)S(1)} collective-permute-done((f32[8992]{0:T(1024)S(1)}, f32[8992]{0:T(1024)S(1)}, u32[]{:S(2)}, u32[]{:S(2)}) %collective-permute-start.10) | collective-permute-done | bytes 36000 | tf_op jit(solution)/shard_map/ppermute | solution.py:43
  51.0 2.2 %collective-permute-start.11 = (f32[8992]{0:T(1024)S(1)}, f32[8992]{0:T(1024)S(1)}, u32[]{:S(2)}, u32[]{:S(2)}) collective-permute-start(f32[8992]{0:T(1024)S(1)} %fusion.134), channel_id=1, source_target_pairs={{0,2},{2,0},{1,3},{3,1},{4,6},{6,4},{5,7},{7,5},{8,10},{10,8},{9,1... | collective-permute-start | bytes 107912 | tf_op jit(solution)/shard_map/ppermute | solution.py:43
  53.2 1.9 %collective-permute-done.11 = f32[8992]{0:T(1024)S(1)} collective-permute-done((f32[8992]{0:T(1024)S(1)}, f32[8992]{0:T(1024)S(1)}, u32[]{:S(2)}, u32[]{:S(2)}) %collective-permute-start.11) | collective-permute-done | bytes 36000 | tf_op jit(solution)/shard_map/ppermute | solution.py:43
  55.2 1.7 %collective-permute-start.2 = (bf16[16,32,256]{2,1,0:T(8,128)(2,1)S(1)}, bf16[16,32,256]{2,1,0:T(8,128)(2,1)S(1)}, u32[]{:S(2)}, u32[]{:S(2)}) collective-permute-start(bf16[16,32,256]{2,1,0:T(8,128)(2,1)S(1)} %gather_fusion), channel_id=1, source_target_pairs={{4,0},{8,4},{12,8},{0,12},{5,1},{9,5},{13,9},{1,13},{6,2},{10,6},{... | collective-permute-start | bytes 786440 | tf_op jit(solution)/shard_map/ppermute | solution.py:25
  56.8 1.8 %collective-permute-start.3 = (bf16[16,32,256]{2,1,0:T(8,128)(2,1)S(1)}, bf16[16,32,256]{2,1,0:T(8,128)(2,1)S(1)}, u32[]{:S(2)}, u32[]{:S(2)}) collective-permute-start(bf16[16,32,256]{2,1,0:T(8,128)(2,1)S(1)} %gather_fusion), channel_id=1, source_target_pairs={{8,0},{12,4},{0,8},{4,12},{9,1},{13,5},{1,9},{5,13},{10,2},{14,6},... | collective-permute-start | bytes 786440 | tf_op jit(solution)/shard_map/ppermute | solution.py:25
  58.6 0.7 collective-permute-start.4
  59.4 1.3 %collective-permute-start.8 = (bf16[16,32,2,128]{3,1,2,0:T(8,128)(2,1)S(1)}, bf16[16,32,2,128]{3,1,2,0:T(8,128)(2,1)S(1)}, u32[]{:S(2)}, u32[]{:S(2)}) collective-permute-start(bf16[16,32,2,128]{3,1,2,0:T(8,128)(2,1)S(1)} %bitcast.338), channel_id=1, source_target_pairs={{0,1},{1,2},{2,3},{4,5},{5,6},{6,7},{8,9},{9,10},{10,11},{12,13},{... | collective-permute-start | bytes 786440 | tf_op jit(solution)/shard_map/ppermute | solution.py:14
  60.7 1.5 %collective-permute-start.9 = (bf16[16,32,2,128]{3,1,2,0:T(8,128)(2,1)S(1)}, bf16[16,32,2,128]{3,1,2,0:T(8,128)(2,1)S(1)}, u32[]{:S(2)}, u32[]{:S(2)}) collective-permute-start(bf16[16,32,2,128]{3,1,2,0:T(8,128)(2,1)S(1)} %bitcast.339), channel_id=1, source_target_pairs={{1,0},{2,1},{3,2},{5,4},{6,5},{7,6},{9,8},{10,9},{11,10},{13,12},{... | collective-permute-start | bytes 786440 | tf_op jit(solution)/shard_map/ppermute | solution.py:17
  62.3 2.0 %collective-permute-done.2 = bf16[16,32,256]{2,1,0:T(8,128)(2,1)S(1)} collective-permute-done((bf16[16,32,256]{2,1,0:T(8,128)(2,1)S(1)}, bf16[16,32,256]{2,1,0:T(8,128)(2,1)S(1)}, u32[]{:S(2)}, u32[]{:S(2)}) %collective-permute-start.2) | collective-permute-done | bytes 262176 | tf_op jit(solution)/shard_map/ppermute | solution.py:25
  64.3 16.4 %collective-permute-done.3 = bf16[16,32,256]{2,1,0:T(8,128)(2,1)S(1)} collective-permute-done((bf16[16,32,256]{2,1,0:T(8,128)(2,1)S(1)}, bf16[16,32,256]{2,1,0:T(8,128)(2,1)S(1)}, u32[]{:S(2)}, u32[]{:S(2)}) %collective-permute-start.3) | collective-permute-done | bytes 262176 | tf_op jit(solution)/shard_map/ppermute | solution.py:25
  80.7 1.7 %collective-permute-start.13 = (f32[8992]{0:T(1024)S(1)}, f32[8992]{0:T(1024)S(1)}, u32[]{:S(2)}, u32[]{:S(2)}) collective-permute-start(f32[8992]{0:T(1024)S(1)} %add.283), channel_id=1, source_target_pairs={{0,8},{4,12},{8,0},{12,4},{1,9},{5,13},{9,1},{13,5},{2,10},{6,14},... | collective-permute-start | bytes 107912 | tf_op jit(solution)/shard_map/ppermute | solution.py:43
  82.4 0.7 fusion.3
  83.2 3.0 %fusion.39 = bf16[16,32,2,128]{3,1,2,0:T(8,128)(2,1)S(1)} fusion(f32[16,32,6,132]{3,1,2,0:T(8,128)S(1)} %fusion.3, bf16[16,32,2,128]{3,2,1,0:T(2,128)(2,1)S(1)} %copy-done.7, f32[32]{0:T(128)S(1)} %get-tuple-element.82, f32[32]{0:T(128)S(1)} %get-tuple-element.83, f32[32]{0:T(128)S(1)} %get-tuple-element.60, f32[32]{0:T(128)S(1)} %get-tuple-element.61, ...), kind=kLoop, calls=%fused_computation.79 | loop fusion | flops 6815744 | bytes 13634688 | tf_op jit(solution)/shard_map/convert_element_type | solution.py:150
  86.6 0.4 copy-done.13
  87.1 0.6 fusion.7
  87.7 0.6 gather_fusion.1
  88.5 1.0 %add_convert_fusion = bf16[16,32,2,128]{3,2,1,0:T(2,128)(2,1)} fusion(f32[16,32,2,128]{3,2,1,0:T(2,128)S(1)} %reshape.87, bf16[16,32,2,128]{3,2,1,0:T(2,128)(2,1)S(1)} %copy-done.4), kind=kLoop, calls=%fused_computation.179 | loop fusion | flops 393216 | bytes 1048576 | tf_op jit(solution)/shard_map/convert_element_type | solution.py:124
  89.5 0.9 %copy.48 = bf16[16,32,2,128]{3,2,1,0:T(2,128)(2,1)} copy(bf16[16,32,2,128]{3,1,2,0:T(8,128)(2,1)S(1)} %fusion.39) | data formatting | bytes 524288
  90.6 0.7 reshape.86
  91.4 0.7 reshape.85
  92.1 0.7 split.13
  (117 shorter events, 2.6 us)
Async XLA Ops:
  0.6 19.9 %copy-start = (bf16[32,32]{1,0:T(8,128)(2,1)S(1)}, bf16[32,32]{1,0:T(8,128)(2,1)}, u32[]{:S(2)}) copy-start(bf16[32,32]{1,0:T(8,128)(2,1)} %param.9) | copy-start | bytes 6148
  0.6 15.3 %copy-start.1 = (f32[32,25]{1,0:T(8,128)S(1)}, f32[32,25]{1,0:T(8,128)}, u32[]{:S(2)}) copy-start(f32[32,25]{1,0:T(8,128)} %param.8) | copy-start | bytes 9604
  1.7 15.8 %copy-start.8 = (bf16[16,32,2,128]{3,1,2,0:T(8,128)(2,1)}, bf16[16,32,2,128]{3,1,2,0:T(8,128)(2,1)S(1)}, u32[]{:S(2)}) copy-start(bf16[16,32,2,128]{3,1,2,0:T(8,128)(2,1)S(1)} %copy.27) | copy-start | bytes 786436
  1.7 14.9 %collective-permute-start = (bf16[16,32,2,128]{3,1,2,0:T(8,128)(2,1)S(1)}, bf16[16,32,2,128]{3,1,2,0:T(8,128)(2,1)S(1)}, u32[]{:S(2)}, u32[]{:S(2)}) collective-permute-start(bf16[16,32,2,128]{3,1,2,0:T(8,128)(2,1)S(1)} %copy.27), channel_id=1, source_target_pairs={{0,1},{1,2},{2,3},{4,5},{5,6},{6,7},{8,9},{9,10},{10,11},{12,13},{... | collective-permute-start | bytes 786440 | tf_op jit(solution)/shard_map/ppermute | solution.py:14
  4.1 12.6 %collective-permute-start.1 = (bf16[16,32,2,128]{3,1,2,0:T(8,128)(2,1)S(1)}, bf16[16,32,2,128]{3,1,2,0:T(8,128)(2,1)S(1)}, u32[]{:S(2)}, u32[]{:S(2)}) collective-permute-start(bf16[16,32,2,128]{3,1,2,0:T(8,128)(2,1)S(1)} %copy.27), channel_id=1, source_target_pairs={{1,0},{2,1},{3,2},{5,4},{6,5},{7,6},{9,8},{10,9},{11,10},{13,12},{... | collective-permute-start | bytes 786440 | tf_op jit(solution)/shard_map/ppermute | solution.py:17
  8.5 13.2 %collective-permute-start.5 = (bf16[16,32,256]{2,1,0:T(8,128)(2,1)S(1)}, bf16[16,32,256]{2,1,0:T(8,128)(2,1)S(1)}, u32[]{:S(2)}, u32[]{:S(2)}) collective-permute-start(bf16[16,32,256]{2,1,0:T(8,128)(2,1)S(1)} %gather_fusion.2), channel_id=1, source_target_pairs={{12,0},{0,4},{4,8},{8,12},{13,1},{1,5},{5,9},{9,13},{14,2},{2,6},{... | collective-permute-start | bytes 786440 | tf_op jit(solution)/shard_map/ppermute | solution.py:25
  10.9 14.6 %collective-permute-start.6 = (bf16[16,32,256]{2,1,0:T(8,128)(2,1)S(1)}, bf16[16,32,256]{2,1,0:T(8,128)(2,1)S(1)}, u32[]{:S(2)}, u32[]{:S(2)}) collective-permute-start(bf16[16,32,256]{2,1,0:T(8,128)(2,1)S(1)} %gather_fusion.2), channel_id=1, source_target_pairs={{4,0},{8,4},{12,8},{0,12},{5,1},{9,5},{13,9},{1,13},{6,2},{10,6},{... | collective-permute-start | bytes 786440 | tf_op jit(solution)/shard_map/ppermute | solution.py:25
  13.0 23.9 %collective-permute-start.7 = (bf16[16,32,256]{2,1,0:T(8,128)(2,1)S(1)}, bf16[16,32,256]{2,1,0:T(8,128)(2,1)S(1)}, u32[]{:S(2)}, u32[]{:S(2)}) collective-permute-start(bf16[16,32,256]{2,1,0:T(8,128)(2,1)S(1)} %gather_fusion.2), channel_id=1, source_target_pairs={{8,0},{12,4},{0,8},{4,12},{9,1},{13,5},{1,9},{5,13},{10,2},{14,6},... | collective-permute-start | bytes 786440 | tf_op jit(solution)/shard_map/ppermute | solution.py:25
  16.5 0.9 copy-start.14
  16.6 0.9 copy-start.16
  16.6 0.9 copy-start.18
  16.6 0.9 copy-start.20
  16.6 0.9 copy-start.22
  16.6 0.9 copy-start.24
  16.6 0.9 copy-start.26
  16.6 0.9 copy-start.12
  37.3 1.3 %copy-start.2 = (bf16[16,7,32,256]{3,2,0,1:T(8,128)(2,1)}, bf16[16,7,32,256]{3,2,0,1:T(8,128)(2,1)S(1)}, u32[]{:S(2)}) copy-start(bf16[16,7,32,256]{3,2,0,1:T(8,128)(2,1)S(1)} %fusion.123) | copy-start | bytes 5505028
  38.6 1.4 %copy-start.9 = (bf16[16,32,2,128]{3,1,2,0:T(8,128)(2,1)S(1)}, bf16[16,32,2,128]{3,1,2,0:T(8,128)(2,1)}, u32[]{:S(2)}) copy-start(bf16[16,32,2,128]{3,1,2,0:T(8,128)(2,1)} %copy-done.8) | copy-start | bytes 786436
  38.6 1.5 %copy-start.11 = (bf16[16,32,2,128]{3,1,2,0:T(8,128)(2,1)S(1)}, bf16[16,32,2,128]{3,1,2,0:T(8,128)(2,1)}, u32[]{:S(2)}) copy-start(bf16[16,32,2,128]{3,1,2,0:T(8,128)(2,1)} %copy-done.10) | copy-start | bytes 786436
  42.3 2.4 %copy-start.5 = (bf16[16,2,128,32]{2,3,1,0:T(8,128)(2,1)}, bf16[16,2,128,32]{2,3,1,0:T(8,128)(2,1)S(1)}, u32[]{:S(2)}) copy-start(bf16[16,2,128,32]{2,3,1,0:T(8,128)(2,1)S(1)} %get-tuple-element.86) | copy-start | bytes 786436
  42.3 4.0 %copy-start.3 = (bf16[16,7,32,256]{3,2,0,1:T(8,128)(2,1)S(1)}, bf16[16,7,32,256]{3,2,0,1:T(8,128)(2,1)}, u32[]{:S(2)}) copy-start(bf16[16,7,32,256]{3,2,0,1:T(8,128)(2,1)} %copy-done.2) | copy-start | bytes 5505028
  44.7 2.5 %copy-start.4 = (bf16[16,32,2,128]{3,2,1,0:T(2,128)(2,1)S(1)}, bf16[16,32,2,128]{3,2,1,0:T(2,128)(2,1)}, u32[]{:S(2)}) copy-start(bf16[16,32,2,128]{3,2,1,0:T(2,128)(2,1)} %param.6) | copy-start | bytes 786436
  46.3 1.6 %copy-start.28 = (f32[32]{0:T(128)S(1)}, f32[32]{0:T(128)}, u32[]{:S(2)}) copy-start(f32[32]{0:T(128)} %get-tuple-element.41) | copy-start | bytes 388
  46.3 1.6 %copy-start.29 = (f32[32]{0:T(128)S(1)}, f32[32]{0:T(128)}, u32[]{:S(2)}) copy-start(f32[32]{0:T(128)} %get-tuple-element.42) | copy-start | bytes 388
  46.3 1.6 %copy-start.30 = (f32[32]{0:T(128)S(1)}, f32[32]{0:T(128)}, u32[]{:S(2)}) copy-start(f32[32]{0:T(128)} %get-tuple-element.43) | copy-start | bytes 388
  46.4 1.6 %copy-start.31 = (f32[32]{0:T(128)S(1)}, f32[32]{0:T(128)}, u32[]{:S(2)}) copy-start(f32[32]{0:T(128)} %get-tuple-element.44) | copy-start | bytes 388
  46.4 1.6 %copy-start.32 = (f32[32]{0:T(128)S(1)}, f32[32]{0:T(128)}, u32[]{:S(2)}) copy-start(f32[32]{0:T(128)} %get-tuple-element.45) | copy-start | bytes 388
  46.4 1.6 %copy-start.33 = (f32[32]{0:T(128)S(1)}, f32[32]{0:T(128)}, u32[]{:S(2)}) copy-start(f32[32]{0:T(128)} %get-tuple-element.46) | copy-start | bytes 388
  46.4 1.6 %copy-start.34 = (f32[32]{0:T(128)S(1)}, f32[32]{0:T(128)}, u32[]{:S(2)}) copy-start(f32[32]{0:T(128)} %get-tuple-element.47) | copy-start | bytes 388
  46.4 1.6 %copy-start.35 = (f32[32]{0:T(128)S(1)}, f32[32]{0:T(128)}, u32[]{:S(2)}) copy-start(f32[32]{0:T(128)} %get-tuple-element.48) | copy-start | bytes 388
  46.4 13.0 %copy-start.6 = (bf16[16,2,128,32]{2,3,1,0:T(8,128)(2,1)S(1)}, bf16[16,2,128,32]{2,3,1,0:T(8,128)(2,1)}, u32[]{:S(2)}) copy-start(bf16[16,2,128,32]{2,3,1,0:T(8,128)(2,1)} %copy-done.5) | copy-start | bytes 786436
  49.8 1.3 %collective-permute-start.10 = (f32[8992]{0:T(1024)S(1)}, f32[8992]{0:T(1024)S(1)}, u32[]{:S(2)}, u32[]{:S(2)}) collective-permute-start(f32[8992]{0:T(1024)S(1)} %broadcast_multiply_fusion), channel_id=1, source_target_pairs={{0,1},{1,0},{2,3},{3,2},{4,5},{5,4},{6,7},{7,6},{8,9},{9,8},{10,11... | collective-permute-start | bytes 107912 | tf_op jit(solution)/shard_map/ppermute | solution.py:43
  51.0 4.1 %collective-permute-start.11 = (f32[8992]{0:T(1024)S(1)}, f32[8992]{0:T(1024)S(1)}, u32[]{:S(2)}, u32[]{:S(2)}) collective-permute-start(f32[8992]{0:T(1024)S(1)} %fusion.134), channel_id=1, source_target_pairs={{0,2},{2,0},{1,3},{3,1},{4,6},{6,4},{5,7},{7,5},{8,10},{10,8},{9,1... | collective-permute-start | bytes 107912 | tf_op jit(solution)/shard_map/ppermute | solution.py:43
  55.2 5.5 %collective-permute-start.12 = (f32[8992]{0:T(1024)S(1)}, f32[8992]{0:T(1024)S(1)}, u32[]{:S(2)}, u32[]{:S(2)}) collective-permute-start(f32[8992]{0:T(1024)S(1)} %add.282), channel_id=1, source_target_pairs={{0,4},{4,0},{8,12},{12,8},{1,5},{5,1},{9,13},{13,9},{2,6},{6,2},{1... | collective-permute-start | bytes 107912 | tf_op jit(solution)/shard_map/ppermute | solution.py:43
  55.2 9.1 %collective-permute-start.2 = (bf16[16,32,256]{2,1,0:T(8,128)(2,1)S(1)}, bf16[16,32,256]{2,1,0:T(8,128)(2,1)S(1)}, u32[]{:S(2)}, u32[]{:S(2)}) collective-permute-start(bf16[16,32,256]{2,1,0:T(8,128)(2,1)S(1)} %gather_fusion), channel_id=1, source_target_pairs={{4,0},{8,4},{12,8},{0,12},{5,1},{9,5},{13,9},{1,13},{6,2},{10,6},{... | collective-permute-start | bytes 786440 | tf_op jit(solution)/shard_map/ppermute | solution.py:25
  56.8 23.9 %collective-permute-start.3 = (bf16[16,32,256]{2,1,0:T(8,128)(2,1)S(1)}, bf16[16,32,256]{2,1,0:T(8,128)(2,1)S(1)}, u32[]{:S(2)}, u32[]{:S(2)}) collective-permute-start(bf16[16,32,256]{2,1,0:T(8,128)(2,1)S(1)} %gather_fusion), channel_id=1, source_target_pairs={{8,0},{12,4},{0,8},{4,12},{9,1},{13,5},{1,9},{5,13},{10,2},{14,6},... | collective-permute-start | bytes 786440 | tf_op jit(solution)/shard_map/ppermute | solution.py:25
  58.6 22.1 %collective-permute-start.4 = (bf16[16,32,256]{2,1,0:T(8,128)(2,1)S(1)}, bf16[16,32,256]{2,1,0:T(8,128)(2,1)S(1)}, u32[]{:S(2)}, u32[]{:S(2)}) collective-permute-start(bf16[16,32,256]{2,1,0:T(8,128)(2,1)S(1)} %gather_fusion), channel_id=1, source_target_pairs={{12,0},{0,4},{4,8},{8,12},{13,1},{1,5},{5,9},{9,13},{14,2},{2,6},{... | collective-permute-start | bytes 786440 | tf_op jit(solution)/shard_map/ppermute | solution.py:25
  59.4 23.0 %collective-permute-start.8 = (bf16[16,32,2,128]{3,1,2,0:T(8,128)(2,1)S(1)}, bf16[16,32,2,128]{3,1,2,0:T(8,128)(2,1)S(1)}, u32[]{:S(2)}, u32[]{:S(2)}) collective-permute-start(bf16[16,32,2,128]{3,1,2,0:T(8,128)(2,1)S(1)} %bitcast.338), channel_id=1, source_target_pairs={{0,1},{1,2},{2,3},{4,5},{5,6},{6,7},{8,9},{9,10},{10,11},{12,13},{... | collective-permute-start | bytes 786440 | tf_op jit(solution)/shard_map/ppermute | solution.py:14
  60.7 21.7 %collective-permute-start.9 = (bf16[16,32,2,128]{3,1,2,0:T(8,128)(2,1)S(1)}, bf16[16,32,2,128]{3,1,2,0:T(8,128)(2,1)S(1)}, u32[]{:S(2)}, u32[]{:S(2)}) collective-permute-start(bf16[16,32,2,128]{3,1,2,0:T(8,128)(2,1)S(1)} %bitcast.339), channel_id=1, source_target_pairs={{1,0},{2,1},{3,2},{5,4},{6,5},{7,6},{9,8},{10,9},{11,10},{13,12},{... | collective-permute-start | bytes 786440 | tf_op jit(solution)/shard_map/ppermute | solution.py:17
  62.2 20.9 %copy-start.7 = (bf16[16,32,2,128]{3,2,1,0:T(2,128)(2,1)S(1)}, bf16[16,32,2,128]{3,2,1,0:T(2,128)(2,1)}, u32[]{:S(2)}) copy-start(bf16[16,32,2,128]{3,2,1,0:T(2,128)(2,1)} %param.7) | copy-start | bytes 786436
  62.2 20.9 %copy-start.15 = (f32[32]{0:T(128)S(1)}, f32[32]{0:T(128)}, u32[]{:S(2)}) copy-start(f32[32]{0:T(128)} %copy-done.14) | copy-start | bytes 388
  62.2 20.9 %copy-start.17 = (f32[32]{0:T(128)S(1)}, f32[32]{0:T(128)}, u32[]{:S(2)}) copy-start(f32[32]{0:T(128)} %copy-done.16) | copy-start | bytes 388
  62.2 20.9 %copy-start.19 = (f32[32]{0:T(128)S(1)}, f32[32]{0:T(128)}, u32[]{:S(2)}) copy-start(f32[32]{0:T(128)} %copy-done.18) | copy-start | bytes 388
  62.2 20.9 %copy-start.21 = (f32[32]{0:T(128)S(1)}, f32[32]{0:T(128)}, u32[]{:S(2)}) copy-start(f32[32]{0:T(128)} %copy-done.20) | copy-start | bytes 388
  62.2 20.9 %copy-start.23 = (f32[32]{0:T(128)S(1)}, f32[32]{0:T(128)}, u32[]{:S(2)}) copy-start(f32[32]{0:T(128)} %copy-done.22) | copy-start | bytes 388
  62.2 20.9 %copy-start.25 = (f32[32]{0:T(128)S(1)}, f32[32]{0:T(128)}, u32[]{:S(2)}) copy-start(f32[32]{0:T(128)} %copy-done.24) | copy-start | bytes 388
  62.3 20.9 %copy-start.27 = (f32[32]{0:T(128)S(1)}, f32[32]{0:T(128)}, u32[]{:S(2)}) copy-start(f32[32]{0:T(128)} %copy-done.26) | copy-start | bytes 388
  80.7 9.8 %collective-permute-start.13 = (f32[8992]{0:T(1024)S(1)}, f32[8992]{0:T(1024)S(1)}, u32[]{:S(2)}, u32[]{:S(2)}) collective-permute-start(f32[8992]{0:T(1024)S(1)} %add.283), channel_id=1, source_target_pairs={{0,8},{4,12},{8,0},{12,4},{1,9},{5,13},{9,1},{13,5},{2,10},{6,14},... | collective-permute-start | bytes 107912 | tf_op jit(solution)/shard_map/ppermute | solution.py:43
  (2 other events, 1.6 us)

commit v4 on v3

--- a/solution.py
+++ b/solution.py
@@ -34,7 +34,7 @@
         else:
             rounds.extend((axis, 1 << bit) for bit in range(count.bit_length() - 1))
     for index, (axis, step) in enumerate(rounds):
-        if tied is not None and index == len(rounds) - 1:
+        if tied is not None and index == [name for name, _ in rounds].index(axes[-1]):
             value, _ = lax.optimization_barrier((value, tied))
         if step == 0:
             value = lax.psum(value, axis)
@@ -47,6 +47,10 @@
 def silu_slope(value):
     sig = jax.nn.sigmoid(value)
     return sig * (1.0 + value * (1.0 - sig))
+
+
+def order_of(inverse, source, chans, n_chan):
+    return lax.dynamic_index_in_dim(inverse.reshape(chans, n_chan), source, 1, keepdims=False) - source * chans
 
 
 def move_down(array):
@@ -84,20 +88,22 @@
     device = lax.axis_index("chan")
     start = device * chans
     own = lax.dynamic_slice_in_dim(freq_table, start, chans) // n_chan
-    order = jnp.zeros((chans,), jnp.int32).at[own].set(jnp.arange(chans, dtype=jnp.int32))
+    total_chans = freq_table.shape[0]
+    inverse = jnp.zeros((total_chans,), jnp.int32).at[freq_table].set(jnp.arange(total_chans, dtype=jnp.int32))
+    order = order_of(inverse, device, chans, n_chan)
     h_sorted = hidden_flat[order]
     g_sorted = grad_flat[order]
-    h_taps = [h_sorted] * taps
     h_received = []
     g_received = []
-    g_taps = [g_sorted] * taps
     for dist in range(1, half + 1):
         for sign in (-1, 1):
-            h_far = passed_along(h_sorted, "chan", -sign * dist)
-            h_received.append(h_far)
-            g_far = passed_along(g_sorted, "chan", -sign * dist)
-            g_received.append(g_far)
-    g_received, mixed_late = lax.optimization_barrier((g_received, mixed))
+            g_received.append(passed_along(grad_flat, "chan", -sign * dist))
+    g_received, h_sorted, mixed_late = lax.optimization_barrier((g_received, h_sorted, mixed))
+    for dist in range(1, half + 1):
+        for sign in (-1, 1):
+            h_received.append(passed_along(h_sorted, "chan", -sign * dist))
+    h_taps = [h_sorted] * taps
+    g_taps = [g_sorted] * taps
     for index, (dist, sign) in enumerate((d, s) for d in range(1, half + 1) for s in (-1, 1)):
         if sign < 0:
             wrapped = device < dist
@@ -105,7 +111,9 @@
         else:
             wrapped = device + dist >= n_chan
             shift = move_up
-        h_far, g_far = h_received[index], g_received[index]
+        source = (device + sign * dist) % n_chan
+        h_far = h_received[index]
+        g_far = g_received[index][order_of(inverse, source, chans, n_chan)]
         h_taps[half + sign * dist] = jnp.where(wrapped, shift(h_far), h_far)
         g_taps[half + sign * dist] = jnp.where(wrapped, shift(g_far), g_far)
     h_stack = jnp.stack(h_taps, 1).reshape(chans, taps * feats, pixels)

time: 93.2 us -> 97.9 us (1.050)
  waiting for transfers between devices: 36.7 us -> 30.4 us
  other arithmetic: 14.2 us -> 20.5 us
  local copies, waits for them, and re-layouts: 15.8 us -> 19.5 us
    ppermute x6, waiting for transfers between devices: 33.7 us -> 28.3 us  [passed_along(): return lax.ppermute(block, axis, route)]
    unnamed x11, other arithmetic: 0.6 us -> 5.25 us
    gather x0 -> x6, local copies, waits for them, and re-layouts: none -> 4.32 us  [local(): g_far = g_received[index][order_of(inverse, source, chans, n_chan)]]
    ppermute x6, starting transfers between devices: 9.7 us -> 7.64 us  [passed_along(): return lax.ppermute(block, axis, route)]
    ppermute x4, starting transfers between devices: 4.05 us -> 5.73 us  [all_summed(): lax.ppermute(value, axis, [(i, i ^ step) for i in range(count)])]
    gather x1, local copies, waits for them, and re-layouts: 0.56 us -> 2.24 us  [local(): g_sorted = grad_flat[order]]
    dot_general x1, matrix products: 0.45 us -> 2.01 us  [local(): jnp.einsum('fK,mKp->mfp', bwd_weight, g_stack, preferred_element_type=jnp...]
    another operation x2, local copies, waits for them, and re-layouts: 1.52 us -> 0.17 us  [local(): kernel_term = jnp.stack(terms, 1)]
  transfers between devices with their start and end apart: 14 -> 14, of which waited for: 6 -> 5; matrix products, arithmetic and copies ran while one was open for 19% -> 22% of each run, Pallas kernels for 0% -> 0%
where the time goes in v4:
time: 97.9 us; the launch traced here: 97.4 us
  waiting for transfers between devices  30.4 us (31%)
  other arithmetic  20.5 us (21%)
  starting transfers between devices  19.8 us (20%)
  local copies, waits for them, and re-layouts  19.5 us (20%)
  matrix products  5.35 us (5%)
  between operations  1.94 us (2%)
    ppermute x6, waiting for transfers between devices, passed_along(): return lax.ppermute(block, axis, route)  28.3 us
    ppermute x6, starting transfers between devices, passed_along(): return lax.ppermute(block, axis, route)  7.64 us
    ppermute x4, starting transfers between devices, all_summed(): lax.ppermute(value, axis, [(i, i ^ step) for i in range(count)])  5.73 us
    unnamed x11, other arithmetic  5.25 us
    gather x6, local copies, waits for them, and re-layouts, local(): g_far = g_received[index][order_of(inverse, source, chans, n_chan)]  4.32 us
    unnamed x128, local copies, waits for them, and re-layouts  4.01 us
    ppermute x2, starting transfers between devices, padded(): lax.ppermute(lax.slice_in_dim(block, block.shape[dim] - width, None, axis...  3.67 us
    convert_element_type x1, other arithmetic, local(): dirty_grad = (cotangent.astype(jnp.float32) + conv).astype(jnp.bfloat16)  3.04 us
  transfers between devices with their start and end apart: 14, of which 5 were waited for; matrix products, arithmetic and copies ran while one was open for 22% of the time, Pallas kernels for 0%

profile of v4, /device:TPU:0, one launch (start us, length us, event | category | flops | bytes accessed | tf_op | source)
XLA Modules:
  0.0 97.4 jit_solution(10121763108676397788)
XLA Ops:
  0.7 1.0 %copy.27 = bf16[16,32,2,128]{3,1,2,0:T(8,128)(2,1)S(1)} copy(bf16[16,32,2,128]{3,2,1,0:T(2,128)(2,1)} %param.6) | data formatting | bytes 524288 | tf_op args[0]
  1.7 2.4 %collective-permute-start.3 = (bf16[16,32,2,128]{3,1,2,0:T(8,128)(2,1)S(1)}, bf16[16,32,2,128]{3,1,2,0:T(8,128)(2,1)S(1)}, u32[]{:S(2)}, u32[]{:S(2)}) collective-permute-start(bf16[16,32,2,128]{3,1,2,0:T(8,128)(2,1)S(1)} %copy.27), channel_id=1, source_target_pairs={{0,1},{1,2},{2,3},{4,5},{5,6},{6,7},{8,9},{9,10},{10,11},{12,13},{... | collective-permute-start | bytes 786440 | tf_op jit(solution)/shard_map/ppermute | solution.py:14
  4.1 1.3 %collective-permute-start.4 = (bf16[16,32,2,128]{3,1,2,0:T(8,128)(2,1)S(1)}, bf16[16,32,2,128]{3,1,2,0:T(8,128)(2,1)S(1)}, u32[]{:S(2)}, u32[]{:S(2)}) collective-permute-start(bf16[16,32,2,128]{3,1,2,0:T(8,128)(2,1)S(1)} %copy.27), channel_id=1, source_target_pairs={{1,0},{2,1},{3,2},{5,4},{6,5},{7,6},{9,8},{10,9},{11,10},{13,12},{... | collective-permute-start | bytes 786440 | tf_op jit(solution)/shard_map/ppermute | solution.py:17
  5.4 1.8 %reshape.88 = bf16[16,32,256]{2,1,0:T(8,128)(2,1)} reshape(bf16[16,32,2,128]{3,2,1,0:T(2,128)(2,1)} %param.7) | data formatting | bytes 524288 | tf_op jit(solution)/shard_map/reshape | solution.py:87
  7.2 2.4 %collective-permute-start = (bf16[16,32,256]{2,1,0:T(8,128)(2,1)}, bf16[16,32,256]{2,1,0:T(8,128)(2,1)S(1)}, u32[]{:S(2)}, u32[]{:S(2)}) collective-permute-start(bf16[16,32,256]{2,1,0:T(8,128)(2,1)} %reshape.88), channel_id=1, source_target_pairs={{12,0},{0,4},{4,8},{8,12},{13,1},{1,5},{5,9},{9,13},{14,2},{2,6},{... | collective-permute-start | bytes 786440 | tf_op jit(solution)/shard_map/ppermute | solution.py:25
  9.6 2.0 %collective-permute-start.1 = (bf16[16,32,256]{2,1,0:T(8,128)(2,1)}, bf16[16,32,256]{2,1,0:T(8,128)(2,1)S(1)}, u32[]{:S(2)}, u32[]{:S(2)}) collective-permute-start(bf16[16,32,256]{2,1,0:T(8,128)(2,1)} %reshape.88), channel_id=1, source_target_pairs={{4,0},{8,4},{12,8},{0,12},{5,1},{9,5},{13,9},{1,13},{6,2},{10,6},{... | collective-permute-start | bytes 786440 | tf_op jit(solution)/shard_map/ppermute | solution.py:25
  11.6 1.0 %collective-permute-start.2 = (bf16[16,32,256]{2,1,0:T(8,128)(2,1)}, bf16[16,32,256]{2,1,0:T(8,128)(2,1)S(1)}, u32[]{:S(2)}, u32[]{:S(2)}) collective-permute-start(bf16[16,32,256]{2,1,0:T(8,128)(2,1)} %reshape.88), channel_id=1, source_target_pairs={{8,0},{12,4},{0,8},{4,12},{9,1},{13,5},{1,9},{5,13},{10,2},{14,6},... | collective-permute-start | bytes 786440 | tf_op jit(solution)/shard_map/ppermute | solution.py:25
  12.6 0.7 compare_select_fusion.8
  13.3 0.8 scatter_custom_fusion
  14.5 0.7 compare_select_fusion.7
  15.2 0.6 pad_clamp_fusion.4
  16.5 2.2 %gather_fusion.5 = bf16[16,32,256]{2,1,0:T(8,128)(2,1)} fusion(bf16[16,32,256]{2,1,0:T(8,128)(2,1)} %reshape.88, s32[1024]{0:T(1024)S(1)} %pad_clamp_fusion.7), kind=kCustom, calls=%fused_computation.5 | custom fusion | bytes 524352 | tf_op jit(solution)/shard_map/gather | solution.py:95
  19.8 0.8 select_maximum_fusion.2
  20.9 3.0 %fusion.64 = bf16[16,32,2,128]{3,1,2,0:T(8,128)(2,1)S(1)} fusion(f32[16,32,6,132]{3,1,2,0:T(8,128)S(1)} %get-tuple-element.94, f32[32]{0:T(128)S(1)} %get-tuple-element.84, f32[32]{0:T(128)S(1)} %get-tuple-element.85, f32[32]{0:T(128)S(1)} %get-tuple-element.62, f32[32]{0:T(128)S(1)} %get-tuple-element.63, f32[32]{0:T(128)S(1)} %get-tuple-element.64, ...), kind=kLoop, calls=%fused_computation.135 | loop fusion | flops 6553600 | bytes 13372544 | tf_op jit(solution)/shard_map/convert_element_type | solution.py:83
  24.3 1.3 %gather_fusion = bf16[16,32,256]{2,1,0:T(8,128)(2,1)} fusion(bf16[16,32,256]{2,1,0:T(8,128)(2,1)S(1)} %copy_bitcast_fusion, s32[1024]{0:T(1024)S(1)} %pad_clamp_fusion.7), kind=kCustom, calls=%fused_computation | custom fusion | bytes 524352 | tf_op jit(solution)/shard_map/gather | solution.py:94
  25.6 10.2 %collective-permute-done.2 = bf16[16,32,256]{2,1,0:T(8,128)(2,1)S(1)} collective-permute-done((bf16[16,32,256]{2,1,0:T(8,128)(2,1)}, bf16[16,32,256]{2,1,0:T(8,128)(2,1)S(1)}, u32[]{:S(2)}, u32[]{:S(2)}) %collective-permute-start.2) | collective-permute-done | bytes 262176 | tf_op jit(solution)/shard_map/ppermute | solution.py:25
  35.8 0.7 gather_fusion.2
  36.5 0.8 fusion.108
  37.8 1.4 %gather_fusion.4 = bf16[16,32,256]{2,1,0:T(8,128)(2,1)} fusion(bf16[16,32,256]{2,1,0:T(8,128)(2,1)S(1)} %collective-permute-done, s32[1024]{0:T(1024)} %get-tuple-element.99), kind=kCustom, calls=%fused_computation.4 | custom fusion | bytes 524352 | tf_op jit(solution)/shard_map/gather | solution.py:116
  39.2 0.8 fusion.111
  40.0 1.9 %fusion.114 = bf16[16,7,32,256]{3,2,0,1:T(8,128)(2,1)} fusion(bf16[16,7,32,256]{3,2,0,1:T(8,128)(2,1)} %fusion.111, bf16[16,32,256]{2,1,0:T(8,128)(2,1)} %gather_fusion.4, pred[]{:T(512)S(6)} %lt.101), kind=kLoop, calls=%fused_computation.225 | loop fusion | flops 131072 | bytes 524289
  41.8 1.7 %bitcast_dynamic-update-slice_fusion.1 = bf16[16,7,32,256]{3,2,0,1:T(8,128)(2,1)} fusion(bf16[16,7,32,256]{3,2,0,1:T(8,128)(2,1)} %fusion.114, bf16[16,32,256]{2,1,0:T(8,128)(2,1)} %gather_fusion.5), kind=kLoop, calls=%fused_computation.263 | loop fusion | bytes 524288
  45.2 0.8 fusion.117
  46.0 0.8 fusion.120
  46.8 0.8 fusion.123
  47.5 2.0 %fusion.8 = bf16[16,32,256]{2,1,0:T(8,128)(2,1)S(1)} fusion(bf16[16,7,32,256]{3,2,0,1:T(8,128)(2,1)} %fusion.123, bf16[7,32,32]{2,1,0:T(8,128)(2,1)S(1)} %rev.6), kind=kOutput, calls=%fused_computation.53 | convolution fusion | flops 58851328 | bytes 2111488 | tf_op jit(solution)/shard_map/fK,mKp->mfp/dot_general | solution.py:124
  50.5 1.7 %fusion.34 = (f32[32]{0:T(128)S(1)}, f32[32]{0:T(128)S(1)}, f32[32]{0:T(128)S(1)}, f32[32]{0:T(128)S(1)}, f32[32]{0:T(128)S(1)}, /*index=5*/f32[32]{0:T(128)S(1)}, bf16[16,2,128,32]{2,3,1,0:T(8,128)(2,1)S(1)}) fusion(bf16[16,32,6,132]{3,1,2,0:T(8,128)(2,1)S(1)} %get-tuple-element.93, bf16[16,32,2,128]{3,1,2,0:T(8,128)(2,1)S(1)} %copy-done.9, ...), kind=kOutput, calls=%fused_computation.78 | convolution fusion | flops 11272000 | bytes 1837824 | tf_op jit(solution)/shard_map/gf,cghw->cfhw/dot_general | solution.py:135
  52.3 1.8 %fusion.35 = (f32[32]{0:T(128)S(1)}, f32[32]{0:T(128)S(1)}, f32[32]{0:T(128)S(1)}, f32[32]{0:T(128)S(1)}, f32[32]{0:T(128)S(1)}, /*index=5*/f32[32]{0:T(128)S(1)...) fusion(bf16[16,32,6,132]{3,1,2,0:T(8,128)(2,1)S(1)} %get-tuple-, ...), kind=kLoop, calls=%fused_computation.79 | loop fusion | flops 7208384 | bytes 4983040 | tf_op jit(solution)/shard_map/cfhw,cfhw->f/dot_general | solution.py:150
  54.2 0.6 fusion.9
  55.0 0.8 multiply_reduce_fusion
  56.4 1.1 %collective-permute-done.10 = f32[8992]{0:T(1024)S(1)} collective-permute-done((f32[8992]{0:T(1024)S(1)}, f32[8992]{0:T(1024)S(1)}, u32[]{:S(2)}, u32[]{:S(2)}) %collective-permute-start.10) | collective-permute-done | bytes 36000 | tf_op jit(solution)/shard_map/ppermute | solution.py:43
  57.5 2.2 %collective-permute-start.11 = (f32[8992]{0:T(1024)S(1)}, f32[8992]{0:T(1024)S(1)}, u32[]{:S(2)}, u32[]{:S(2)}) collective-permute-start(f32[8992]{0:T(1024)S(1)} %fusion.141), channel_id=1, source_target_pairs={{0,2},{2,0},{1,3},{3,1},{4,6},{6,4},{5,7},{7,5},{8,10},{10,8},{9,1... | collective-permute-start | bytes 107912 | tf_op jit(solution)/shard_map/ppermute | solution.py:43
  59.6 1.6 %collective-permute-start.5 = (bf16[16,32,256]{2,1,0:T(8,128)(2,1)S(1)}, bf16[16,32,256]{2,1,0:T(8,128)(2,1)S(1)}, u32[]{:S(2)}, u32[]{:S(2)}) collective-permute-start(bf16[16,32,256]{2,1,0:T(8,128)(2,1)S(1)} %copy-done.5), channel_id=1, source_target_pairs={{4,0},{8,4},{12,8},{0,12},{5,1},{9,5},{13,9},{1,13},{6,2},{10,6},{... | collective-permute-start | bytes 786440 | tf_op jit(solution)/shard_map/ppermute | solution.py:25
  61.8 1.3 %collective-permute-start.8 = (bf16[16,32,2,128]{3,1,2,0:T(8,128)(2,1)S(1)}, bf16[16,32,2,128]{3,1,2,0:T(8,128)(2,1)S(1)}, u32[]{:S(2)}, u32[]{:S(2)}) collective-permute-start(bf16[16,32,2,128]{3,1,2,0:T(8,128)(2,1)S(1)} %bitcast.338), channel_id=1, source_target_pairs={{0,1},{1,2},{2,3},{4,5},{5,6},{6,7},{8,9},{9,10},{10,11},{12,13},{... | collective-permute-start | bytes 786440 | tf_op jit(solution)/shard_map/ppermute | solution.py:14
  63.1 1.5 %collective-permute-start.9 = (bf16[16,32,2,128]{3,1,2,0:T(8,128)(2,1)S(1)}, bf16[16,32,2,128]{3,1,2,0:T(8,128)(2,1)S(1)}, u32[]{:S(2)}, u32[]{:S(2)}) collective-permute-start(bf16[16,32,2,128]{3,1,2,0:T(8,128)(2,1)S(1)} %bitcast.339), channel_id=1, source_target_pairs={{1,0},{2,1},{3,2},{5,4},{6,5},{7,6},{9,8},{10,9},{11,10},{13,12},{... | collective-permute-start | bytes 786440 | tf_op jit(solution)/shard_map/ppermute | solution.py:17
  64.9 4.5 %collective-permute-done.5 = bf16[16,32,256]{2,1,0:T(8,128)(2,1)S(1)} collective-permute-done((bf16[16,32,256]{2,1,0:T(8,128)(2,1)S(1)}, bf16[16,32,256]{2,1,0:T(8,128)(2,1)S(1)}, u32[]{:S(2)}, u32[]{:S(2)}) %collective-permute-start.5) | collective-permute-done | bytes 262176 | tf_op jit(solution)/shard_map/ppermute | solution.py:25
  69.3 13.6 %collective-permute-done.6 = bf16[16,32,256]{2,1,0:T(8,128)(2,1)S(1)} collective-permute-done((bf16[16,32,256]{2,1,0:T(8,128)(2,1)S(1)}, bf16[16,32,256]{2,1,0:T(8,128)(2,1)S(1)}, u32[]{:S(2)}, u32[]{:S(2)}) %collective-permute-start.6) | collective-permute-done | bytes 262176 | tf_op jit(solution)/shard_map/ppermute | solution.py:25
  82.9 1.4 %collective-permute-start.12 = (f32[8992]{0:T(1024)S(1)}, f32[8992]{0:T(1024)S(1)}, u32[]{:S(2)}, u32[]{:S(2)}) collective-permute-start(f32[8992]{0:T(1024)S(1)} %add.389), channel_id=1, source_target_pairs={{0,4},{4,0},{8,12},{12,8},{1,5},{5,1},{9,13},{13,9},{2,6},{6,2},{1... | collective-permute-start | bytes 107912 | tf_op jit(solution)/shard_map/ppermute | solution.py:43
  84.3 0.7 fusion.3
  85.3 3.0 %fusion.39 = bf16[16,32,2,128]{3,1,2,0:T(8,128)(2,1)S(1)} fusion(f32[16,32,6,132]{3,1,2,0:T(8,128)S(1)} %fusion.3, bf16[16,32,2,128]{3,2,1,0:T(2,128)(2,1)S(1)} %copy-done.4, f32[32]{0:T(128)S(1)} %copy-done.21, f32[32]{0:T(128)S(1)} %copy-done.23, f32[32]{0:T(128)S(1)} %copy-done.27, f32[32]{0:T(128)S(1)} %copy-done.29, f32[32]{0:T(128)S(1)} %copy-done.31, ...), kind=kLoop, calls=%fused_computation.85 | loop fusion | flops 6815744 | bytes 13634688 | tf_op jit(solution)/shard_map/convert_element_type | solution.py:158
  88.7 0.6 fusion.7
  90.2 2.0 %collective-permute-start.13 = (f32[8992]{0:T(1024)S(1)}, f32[8992]{0:T(1024)S(1)}, u32[]{:S(2)}, u32[]{:S(2)}) collective-permute-start(f32[8992]{0:T(1024)S(1)} %add.390), channel_id=1, source_target_pairs={{0,8},{4,12},{8,0},{12,4},{1,9},{5,13},{9,1},{13,5},{2,10},{6,14},... | collective-permute-start | bytes 107912 | tf_op jit(solution)/shard_map/ppermute | solution.py:43
  92.2 1.0 %add_convert_fusion = bf16[16,32,2,128]{3,2,1,0:T(2,128)(2,1)} fusion(f32[16,32,2,128]{3,2,1,0:T(2,128)S(1)} %reshape.97, bf16[16,32,2,128]{3,2,1,0:T(2,128)(2,1)S(1)} %copy-done.3), kind=kLoop, calls=%fused_computation.185 | loop fusion | flops 393216 | bytes 1048576 | tf_op jit(solution)/shard_map/convert_element_type | solution.py:132
  93.2 0.9 copy.48
  94.2 1.0 %collective-permute-done.13 = f32[8992]{0:T(1024)S(1)} collective-permute-done((f32[8992]{0:T(1024)S(1)}, f32[8992]{0:T(1024)S(1)}, u32[]{:S(2)}, u32[]{:S(2)}) %collective-permute-start.13) | collective-permute-done | bytes 36000 | tf_op jit(solution)/shard_map/ppermute | solution.py:43
  95.3 0.7 reshape.96
  96.1 0.7 reshape.95
  96.8 0.7 split.13
  (180 shorter events, 8.5 us)
Async XLA Ops:
  0.6 23.3 %copy-start = (bf16[32,32]{1,0:T(8,128)(2,1)S(1)}, bf16[32,32]{1,0:T(8,128)(2,1)}, u32[]{:S(2)}) copy-start(bf16[32,32]{1,0:T(8,128)(2,1)} %param.9) | copy-start | bytes 6148
  0.6 18.1 %copy-start.11 = (bf16[7,32,32]{2,1,0:T(8,128)(2,1)S(1)}, bf16[7,32,32]{2,1,0:T(8,128)(2,1)}, u32[]{:S(2)}) copy-start(bf16[7,32,32]{2,1,0:T(8,128)(2,1)} %param.10) | copy-start | bytes 43012
  0.7 18.1 %copy-start.1 = (f32[32,25]{1,0:T(8,128)S(1)}, f32[32,25]{1,0:T(8,128)}, u32[]{:S(2)}) copy-start(f32[32,25]{1,0:T(8,128)} %param.8) | copy-start | bytes 9604
  1.7 18.9 %copy-start.6 = (bf16[16,32,2,128]{3,1,2,0:T(8,128)(2,1)}, bf16[16,32,2,128]{3,1,2,0:T(8,128)(2,1)S(1)}, u32[]{:S(2)}) copy-start(bf16[16,32,2,128]{3,1,2,0:T(8,128)(2,1)S(1)} %copy.27) | copy-start | bytes 786436
  1.7 18.1 %collective-permute-start.3 = (bf16[16,32,2,128]{3,1,2,0:T(8,128)(2,1)S(1)}, bf16[16,32,2,128]{3,1,2,0:T(8,128)(2,1)S(1)}, u32[]{:S(2)}, u32[]{:S(2)}) collective-permute-start(bf16[16,32,2,128]{3,1,2,0:T(8,128)(2,1)S(1)} %copy.27), channel_id=1, source_target_pairs={{0,1},{1,2},{2,3},{4,5},{5,6},{6,7},{8,9},{9,10},{10,11},{12,13},{... | collective-permute-start | bytes 786440 | tf_op jit(solution)/shard_map/ppermute | solution.py:14
  4.1 15.7 %collective-permute-start.4 = (bf16[16,32,2,128]{3,1,2,0:T(8,128)(2,1)S(1)}, bf16[16,32,2,128]{3,1,2,0:T(8,128)(2,1)S(1)}, u32[]{:S(2)}, u32[]{:S(2)}) collective-permute-start(bf16[16,32,2,128]{3,1,2,0:T(8,128)(2,1)S(1)} %copy.27), channel_id=1, source_target_pairs={{1,0},{2,1},{3,2},{5,4},{6,5},{7,6},{9,8},{10,9},{11,10},{13,12},{... | collective-permute-start | bytes 786440 | tf_op jit(solution)/shard_map/ppermute | solution.py:17
  7.2 18.4 %collective-permute-start = (bf16[16,32,256]{2,1,0:T(8,128)(2,1)}, bf16[16,32,256]{2,1,0:T(8,128)(2,1)S(1)}, u32[]{:S(2)}, u32[]{:S(2)}) collective-permute-start(bf16[16,32,256]{2,1,0:T(8,128)(2,1)} %reshape.88), channel_id=1, source_target_pairs={{12,0},{0,4},{4,8},{8,12},{13,1},{1,5},{5,9},{9,13},{14,2},{2,6},{... | collective-permute-start | bytes 786440 | tf_op jit(solution)/shard_map/ppermute | solution.py:25
  9.6 16.0 %collective-permute-start.1 = (bf16[16,32,256]{2,1,0:T(8,128)(2,1)}, bf16[16,32,256]{2,1,0:T(8,128)(2,1)S(1)}, u32[]{:S(2)}, u32[]{:S(2)}) collective-permute-start(bf16[16,32,256]{2,1,0:T(8,128)(2,1)} %reshape.88), channel_id=1, source_target_pairs={{4,0},{8,4},{12,8},{0,12},{5,1},{9,5},{13,9},{1,13},{6,2},{10,6},{... | collective-permute-start | bytes 786440 | tf_op jit(solution)/shard_map/ppermute | solution.py:25
  11.6 24.2 %collective-permute-start.2 = (bf16[16,32,256]{2,1,0:T(8,128)(2,1)}, bf16[16,32,256]{2,1,0:T(8,128)(2,1)S(1)}, u32[]{:S(2)}, u32[]{:S(2)}) collective-permute-start(bf16[16,32,256]{2,1,0:T(8,128)(2,1)} %reshape.88), channel_id=1, source_target_pairs={{8,0},{12,4},{0,8},{4,12},{9,1},{13,5},{1,9},{5,13},{10,2},{14,6},... | collective-permute-start | bytes 786440 | tf_op jit(solution)/shard_map/ppermute | solution.py:25
  47.5 3.0 %copy-start.7 = (bf16[16,32,2,128]{3,1,2,0:T(8,128)(2,1)S(1)}, bf16[16,32,2,128]{3,1,2,0:T(8,128)(2,1)}, u32[]{:S(2)}) copy-start(bf16[16,32,2,128]{3,1,2,0:T(8,128)(2,1)} %copy-done.6) | copy-start | bytes 786436
  47.5 3.0 %copy-start.9 = (bf16[16,32,2,128]{3,1,2,0:T(8,128)(2,1)S(1)}, bf16[16,32,2,128]{3,1,2,0:T(8,128)(2,1)}, u32[]{:S(2)}) copy-start(bf16[16,32,2,128]{3,1,2,0:T(8,128)(2,1)} %copy-done.8) | copy-start | bytes 786436
  52.3 1.9 %copy-start.2 = (bf16[16,7,32,256]{3,2,0,1:T(8,128)(2,1)S(1)}, bf16[16,7,32,256]{3,2,0,1:T(8,128)(2,1)}, u32[]{:S(2)}) copy-start(bf16[16,7,32,256]{3,2,0,1:T(8,128)(2,1)} %fusion.123) | copy-start | bytes 5505028
  52.3 1.9 %copy-start.5 = (bf16[16,32,256]{2,1,0:T(8,128)(2,1)S(1)}, bf16[16,32,256]{2,1,0:T(8,128)(2,1)}, u32[]{:S(2)}) copy-start(bf16[16,32,256]{2,1,0:T(8,128)(2,1)} %gather_fusion) | copy-start | bytes 786436
  56.2 1.3 %collective-permute-start.10 = (f32[8992]{0:T(1024)S(1)}, f32[8992]{0:T(1024)S(1)}, u32[]{:S(2)}, u32[]{:S(2)}) collective-permute-start(f32[8992]{0:T(1024)S(1)} %broadcast_multiply_fusion), channel_id=1, source_target_pairs={{0,1},{1,0},{2,3},{3,2},{4,5},{5,4},{6,7},{7,6},{8,9},{9,8},{10,11... | collective-permute-start | bytes 107912 | tf_op jit(solution)/shard_map/ppermute | solution.py:43
  57.5 5.7 %collective-permute-start.11 = (f32[8992]{0:T(1024)S(1)}, f32[8992]{0:T(1024)S(1)}, u32[]{:S(2)}, u32[]{:S(2)}) collective-permute-start(f32[8992]{0:T(1024)S(1)} %fusion.141), channel_id=1, source_target_pairs={{0,2},{2,0},{1,3},{3,1},{4,6},{6,4},{5,7},{7,5},{8,10},{10,8},{9,1... | collective-permute-start | bytes 107912 | tf_op jit(solution)/shard_map/ppermute | solution.py:43
  59.6 9.7 %collective-permute-start.5 = (bf16[16,32,256]{2,1,0:T(8,128)(2,1)S(1)}, bf16[16,32,256]{2,1,0:T(8,128)(2,1)S(1)}, u32[]{:S(2)}, u32[]{:S(2)}) collective-permute-start(bf16[16,32,256]{2,1,0:T(8,128)(2,1)S(1)} %copy-done.5), channel_id=1, source_target_pairs={{4,0},{8,4},{12,8},{0,12},{5,1},{9,5},{13,9},{1,13},{6,2},{10,6},{... | collective-permute-start | bytes 786440 | tf_op jit(solution)/shard_map/ppermute | solution.py:25
  61.2 21.7 %collective-permute-start.6 = (bf16[16,32,256]{2,1,0:T(8,128)(2,1)S(1)}, bf16[16,32,256]{2,1,0:T(8,128)(2,1)S(1)}, u32[]{:S(2)}, u32[]{:S(2)}) collective-permute-start(bf16[16,32,256]{2,1,0:T(8,128)(2,1)S(1)} %copy-done.5), channel_id=1, source_target_pairs={{8,0},{12,4},{0,8},{4,12},{9,1},{13,5},{1,9},{5,13},{10,2},{14,6},... | collective-permute-start | bytes 786440 | tf_op jit(solution)/shard_map/ppermute | solution.py:25
  61.2 21.7 %collective-permute-start.7 = (bf16[16,32,256]{2,1,0:T(8,128)(2,1)S(1)}, bf16[16,32,256]{2,1,0:T(8,128)(2,1)S(1)}, u32[]{:S(2)}, u32[]{:S(2)}) collective-permute-start(bf16[16,32,256]{2,1,0:T(8,128)(2,1)S(1)} %copy-done.5), channel_id=1, source_target_pairs={{12,0},{0,4},{4,8},{8,12},{13,1},{1,5},{5,9},{9,13},{14,2},{2,6},{... | collective-permute-start | bytes 786440 | tf_op jit(solution)/shard_map/ppermute | solution.py:25
  61.8 22.5 %collective-permute-start.8 = (bf16[16,32,2,128]{3,1,2,0:T(8,128)(2,1)S(1)}, bf16[16,32,2,128]{3,1,2,0:T(8,128)(2,1)S(1)}, u32[]{:S(2)}, u32[]{:S(2)}) collective-permute-start(bf16[16,32,2,128]{3,1,2,0:T(8,128)(2,1)S(1)} %bitcast.338), channel_id=1, source_target_pairs={{0,1},{1,2},{2,3},{4,5},{5,6},{6,7},{8,9},{9,10},{10,11},{12,13},{... | collective-permute-start | bytes 786440 | tf_op jit(solution)/shard_map/ppermute | solution.py:14
  63.1 21.2 %collective-permute-start.9 = (bf16[16,32,2,128]{3,1,2,0:T(8,128)(2,1)S(1)}, bf16[16,32,2,128]{3,1,2,0:T(8,128)(2,1)S(1)}, u32[]{:S(2)}, u32[]{:S(2)}) collective-permute-start(bf16[16,32,2,128]{3,1,2,0:T(8,128)(2,1)S(1)} %bitcast.339), channel_id=1, source_target_pairs={{1,0},{2,1},{3,2},{5,4},{6,5},{7,6},{9,8},{10,9},{11,10},{13,12},{... | collective-permute-start | bytes 786440 | tf_op jit(solution)/shard_map/ppermute | solution.py:17
  64.6 20.4 %copy-start.4 = (bf16[16,32,2,128]{3,2,1,0:T(2,128)(2,1)S(1)}, bf16[16,32,2,128]{3,2,1,0:T(2,128)(2,1)}, u32[]{:S(2)}) copy-start(bf16[16,32,2,128]{3,2,1,0:T(2,128)(2,1)} %param.7) | copy-start | bytes 786436
  64.6 20.4 %copy-start.13 = (f32[32]{0:T(128)S(1)}, f32[32]{0:T(128)}, u32[]{:S(2)}) copy-start(f32[32]{0:T(128)} %copy-done.12) | copy-start | bytes 388
  64.6 20.4 %copy-start.15 = (f32[32]{0:T(128)S(1)}, f32[32]{0:T(128)}, u32[]{:S(2)}) copy-start(f32[32]{0:T(128)} %copy-done.14) | copy-start | bytes 388
  64.7 20.4 %copy-start.17 = (f32[32]{0:T(128)S(1)}, f32[32]{0:T(128)}, u32[]{:S(2)}) copy-start(f32[32]{0:T(128)} %copy-done.16) | copy-start | bytes 388
  64.7 20.4 %copy-start.19 = (f32[32]{0:T(128)S(1)}, f32[32]{0:T(128)}, u32[]{:S(2)}) copy-start(f32[32]{0:T(128)} %copy-done.18) | copy-start | bytes 388
  64.7 20.4 %copy-start.21 = (f32[32]{0:T(128)S(1)}, f32[32]{0:T(128)}, u32[]{:S(2)}) copy-start(f32[32]{0:T(128)} %copy-done.20) | copy-start | bytes 388
  64.7 20.4 %copy-start.23 = (f32[32]{0:T(128)S(1)}, f32[32]{0:T(128)}, u32[]{:S(2)}) copy-start(f32[32]{0:T(128)} %copy-done.22) | copy-start | bytes 388
  64.7 20.4 %copy-start.25 = (f32[32]{0:T(128)S(1)}, f32[32]{0:T(128)}, u32[]{:S(2)}) copy-start(f32[32]{0:T(128)} %copy-done.24) | copy-start | bytes 388
  64.7 20.4 %copy-start.27 = (f32[32]{0:T(128)S(1)}, f32[32]{0:T(128)}, u32[]{:S(2)}) copy-start(f32[32]{0:T(128)} %copy-done.26) | copy-start | bytes 388
  64.7 20.4 %copy-start.29 = (f32[32]{0:T(128)S(1)}, f32[32]{0:T(128)}, u32[]{:S(2)}) copy-start(f32[32]{0:T(128)} %copy-done.28) | copy-start | bytes 388
  64.7 20.4 %copy-start.31 = (f32[32]{0:T(128)S(1)}, f32[32]{0:T(128)}, u32[]{:S(2)}) copy-start(f32[32]{0:T(128)} %copy-done.30) | copy-start | bytes 388
  64.7 20.4 %copy-start.33 = (f32[32]{0:T(128)S(1)}, f32[32]{0:T(128)}, u32[]{:S(2)}) copy-start(f32[32]{0:T(128)} %copy-done.32) | copy-start | bytes 388
  64.7 20.4 %copy-start.35 = (f32[32]{0:T(128)S(1)}, f32[32]{0:T(128)}, u32[]{:S(2)}) copy-start(f32[32]{0:T(128)} %copy-done.34) | copy-start | bytes 388
  64.8 20.4 %copy-start.37 = (f32[32]{0:T(128)S(1)}, f32[32]{0:T(128)}, u32[]{:S(2)}) copy-start(f32[32]{0:T(128)} %copy-done.36) | copy-start | bytes 388
  64.8 20.4 %copy-start.39 = (f32[32]{0:T(128)S(1)}, f32[32]{0:T(128)}, u32[]{:S(2)}) copy-start(f32[32]{0:T(128)} %copy-done.38) | copy-start | bytes 388
  64.8 20.4 %copy-start.41 = (f32[32]{0:T(128)S(1)}, f32[32]{0:T(128)}, u32[]{:S(2)}) copy-start(f32[32]{0:T(128)} %copy-done.40) | copy-start | bytes 388
  64.8 20.4 %copy-start.43 = (f32[32]{0:T(128)S(1)}, f32[32]{0:T(128)}, u32[]{:S(2)}) copy-start(f32[32]{0:T(128)} %copy-done.42) | copy-start | bytes 388
  64.8 20.4 %copy-start.45 = (f32[32]{0:T(128)S(1)}, f32[32]{0:T(128)}, u32[]{:S(2)}) copy-start(f32[32]{0:T(128)} %copy-done.44) | copy-start | bytes 388
  64.8 20.4 %copy-start.47 = (f32[32]{0:T(128)S(1)}, f32[32]{0:T(128)}, u32[]{:S(2)}) copy-start(f32[32]{0:T(128)} %copy-done.46) | copy-start | bytes 388
  64.8 20.4 %copy-start.49 = (f32[32]{0:T(128)S(1)}, f32[32]{0:T(128)}, u32[]{:S(2)}) copy-start(f32[32]{0:T(128)} %copy-done.48) | copy-start | bytes 388
  64.8 20.4 %copy-start.51 = (f32[32]{0:T(128)S(1)}, f32[32]{0:T(128)}, u32[]{:S(2)}) copy-start(f32[32]{0:T(128)} %copy-done.50) | copy-start | bytes 388
  64.8 20.4 %copy-start.53 = (f32[32]{0:T(128)S(1)}, f32[32]{0:T(128)}, u32[]{:S(2)}) copy-start(f32[32]{0:T(128)} %copy-done.52) | copy-start | bytes 388
  64.8 20.4 %copy-start.55 = (f32[32]{0:T(128)S(1)}, f32[32]{0:T(128)}, u32[]{:S(2)}) copy-start(f32[32]{0:T(128)} %copy-done.54) | copy-start | bytes 388
  64.9 20.4 %copy-start.57 = (f32[32]{0:T(128)S(1)}, f32[32]{0:T(128)}, u32[]{:S(2)}) copy-start(f32[32]{0:T(128)} %copy-done.56) | copy-start | bytes 388
  64.9 20.4 %copy-start.59 = (f32[32]{0:T(128)S(1)}, f32[32]{0:T(128)}, u32[]{:S(2)}) copy-start(f32[32]{0:T(128)} %copy-done.58) | copy-start | bytes 388
  64.9 20.4 %copy-start.61 = (f32[32]{0:T(128)S(1)}, f32[32]{0:T(128)}, u32[]{:S(2)}) copy-start(f32[32]{0:T(128)} %copy-done.60) | copy-start | bytes 388
  82.9 7.3 %collective-permute-start.12 = (f32[8992]{0:T(1024)S(1)}, f32[8992]{0:T(1024)S(1)}, u32[]{:S(2)}, u32[]{:S(2)}) collective-permute-start(f32[8992]{0:T(1024)S(1)} %add.389), channel_id=1, source_target_pairs={{0,4},{4,0},{8,12},{12,8},{1,5},{5,1},{9,13},{13,9},{2,6},{6,2},{1... | collective-permute-start | bytes 107912 | tf_op jit(solution)/shard_map/ppermute | solution.py:43
  90.2 4.9 %collective-permute-start.13 = (f32[8992]{0:T(1024)S(1)}, f32[8992]{0:T(1024)S(1)}, u32[]{:S(2)}, u32[]{:S(2)}) collective-permute-start(f32[8992]{0:T(1024)S(1)} %add.390), channel_id=1, source_target_pairs={{0,8},{4,12},{8,0},{12,4},{1,9},{5,13},{9,1},{13,5},{2,10},{6,14},... | collective-permute-start | bytes 107912 | tf_op jit(solution)/shard_map/ppermute | solution.py:43
  (28 other events, 33.4 us)

commit v5 on v2

--- a/solution.py
+++ b/solution.py
@@ -38,6 +38,18 @@
     return value
 
 
+def exchanged(pieces, axis):
+    count = lax.axis_size(axis)
+    if count > 8:
+        return lax.all_to_all(pieces, axis, 0, 0), jnp.arange(count)
+    device = lax.axis_index(axis)
+    held = [lax.dynamic_index_in_dim(pieces, device, 0, keepdims=False)]
+    for step in range(1, count):
+        piece = lax.dynamic_index_in_dim(pieces, (device + step) % count, 0, keepdims=False)
+        held.append(lax.ppermute(piece, axis, [(i, (i + step) % count) for i in range(count)]))
+    return jnp.stack(held, 0), (device - jnp.arange(count)) % count
+
+
 def silu_slope(value):
     sig = jax.nn.sigmoid(value)
     return sig * (1.0 + value * (1.0 - sig))
@@ -73,43 +85,42 @@
     smooth = total.astype(jnp.bfloat16)
     mixed = jnp.einsum("gf,cfhw->cghw", feature_mix, smooth, preferred_element_type=jnp.float32)
     hidden = jax.nn.silu(mixed).astype(jnp.bfloat16)
-    hidden_flat = hidden.reshape(chans, feats, pixels)
-    grad_flat = cotangent.reshape(chans, feats, pixels)
-    device = lax.axis_index("chan")
-    start = device * chans
-    own = lax.dynamic_slice_in_dim(freq_table, start, chans) // n_chan
-    order = jnp.zeros((chans,), jnp.int32).at[own].set(jnp.arange(chans, dtype=jnp.int32))
-    h_sorted = hidden_flat[order]
-    g_sorted = grad_flat[order]
-    h_taps = [h_sorted] * taps
-    g_taps = [g_sorted] * taps
-    for dist in range(1, half + 1):
-        for sign in (-1, 1):
-            h_far = passed_along(h_sorted, "chan", -sign * dist)
-            g_far = passed_along(g_sorted, "chan", -sign * dist)
-            if sign < 0:
-                wrapped = device < dist
-                h_near = jnp.where(wrapped, move_down(h_far), h_far)
-                g_near = jnp.where(wrapped, move_down(g_far), g_far)
-            else:
-                wrapped = device + dist >= n_chan
-                h_near = jnp.where(wrapped, move_up(h_far), h_far)
-                g_near = jnp.where(wrapped, move_up(g_far), g_far)
-            h_taps[half + sign * dist] = h_near
-            g_taps[half + sign * dist] = g_near
-    h_stack = jnp.stack(h_taps, 1).reshape(chans, taps * feats, pixels)
-    g_stack = jnp.stack(g_taps, 1).reshape(chans, taps * feats, pixels)
+    total_chans = freq_table.shape[0]
+    chunk = pixels // n_chan
+    inverse = jnp.zeros((total_chans,), jnp.int32).at[freq_table].set(
+        jnp.arange(total_chans, dtype=jnp.int32)
+    )
+
+    def to_freq_major(block):
+        pieces = block.reshape(chans, feats, n_chan, chunk).transpose(2, 0, 1, 3)
+        held, slot = exchanged(pieces, "chan")
+        rows_of = slot[inverse // chans] * chans + inverse % chans
+        return held.reshape(n_chan * chans, feats, chunk)[rows_of]
+
+    def to_pixel_major(values):
+        pieces = values.astype(jnp.bfloat16)[freq_table.reshape(n_chan, chans)]
+        held, slot = exchanged(pieces, "chan")
+        return held[slot].transpose(1, 2, 0, 3).reshape(chans, feats, rows, cols)
+
+    def stacked(values):
+        ends = jnp.pad(values, ((half, half), (0, 0), (0, 0)))
+        return jnp.stack([ends[k : k + total_chans] for k in range(taps)], 1).reshape(
+            total_chans, taps * feats, chunk
+        )
+
+    g_freq = to_freq_major(cotangent)
+    g_stack = stacked(g_freq)
+    bwd_weight = spectral_kernel[::-1].transpose(2, 0, 1).reshape(feats, taps * feats)
+    bwd_acc = jnp.einsum("fK,qKp->qfp", bwd_weight, g_stack, preferred_element_type=jnp.float32)
+    back = to_pixel_major(bwd_acc)
+    h_freq = to_freq_major(hidden)
+    h_stack = stacked(h_freq)
     fwd_weight = spectral_kernel.transpose(1, 0, 2).reshape(feats, taps * feats)
-    bwd_weight = spectral_kernel[::-1].transpose(2, 0, 1).reshape(feats, taps * feats)
-    fwd_acc = jnp.einsum("gK,mKp->mgp", fwd_weight, h_stack, preferred_element_type=jnp.float32)
-    bwd_acc = jnp.einsum("fK,mKp->mfp", bwd_weight, g_stack, preferred_element_type=jnp.float32)
+    fwd_acc = jnp.einsum("gK,qKp->qgp", fwd_weight, h_stack, preferred_element_type=jnp.float32)
+    spec = to_pixel_major(fwd_acc)
     spec_grad = jnp.einsum(
-        "mKp,mfp->Kf", g_stack, h_sorted, preferred_element_type=jnp.float32
+        "qKp,qfp->Kf", g_stack, h_freq, preferred_element_type=jnp.float32
     ).reshape(taps, feats, feats)[::-1]
-    spec_flat = fwd_acc.astype(jnp.bfloat16)[own]
-    back_flat = bwd_acc.astype(jnp.bfloat16)[own]
-    spec = spec_flat.reshape(chans, feats, rows, cols)
-    back = back_flat.reshape(chans, feats, rows, cols)
     restored = (dirty.astype(jnp.float32) + spec.astype(jnp.float32)).astype(jnp.bfloat16)
     dmixed = (back.astype(jnp.float32) * silu_slope(mixed)).astype(jnp.bfloat16)
     mix_term = jnp.einsum("cghw,cfhw->gf", dmixed, smooth, preferred_element_type=jnp.float32)

time: 87.9 us -> 118 us (1.34)
  starting transfers between devices: 29.8 us -> 46.9 us
  local copies, waits for them, and re-layouts: 12.4 us -> 27.4 us
  waiting for transfers between devices: 24 us -> 19 us
  matrix products: 5.29 us -> 8.1 us
    ppermute x6 -> x12, starting transfers between devices: 17.2 us -> 27.8 us  [exchanged(): lax.ppermute(piece, axis, [(i, (i + step) % count) for i in range(count)])]
    unnamed x130 -> x36, local copies, waits for them, and re-layouts: 2.38 us -> 10.3 us
    ppermute x4, starting transfers between devices: 3.11 us -> 10.4 us  [all_summed(): lax.ppermute(value, axis, [(i, i ^ step) for i in range(count)])]
    dot_general x3, matrix products: 1.67 us -> 6.84 us  [the longest x1 3.12 us: local(): jnp.einsum('qKp,qfp->Kf', g_stack, h_freq, preferred_element_type=jnp.flo...]
    ppermute x4, waiting for transfers between devices: 6.3 us -> 1.73 us  [all_summed(): lax.ppermute(value, axis, [(i, i ^ step) for i in range(count)])]
    another operation x0 -> x4, local copies, waits for them, and re-layouts: none -> 3.27 us
    gather x4 -> x7, local copies, waits for them, and re-layouts: 2.29 us -> 4.54 us  [the longest x2 1.33 us: to_pixel_major(): pieces = values.astype(jnp.bfloat16)[freq_table.reshape(n_chan, chans)]]
    slice x2, local copies, waits for them, and re-layouts: 2.85 us -> 0.81 us  [local(): spatial_kernel[:, i * 5 + j][None, :, None, None]]
  transfers between devices with their start and end apart: 14 -> 20, of which waited for: 5 -> 8; matrix products, arithmetic and copies ran while one was open for 12% -> 31% of each run, Pallas kernels for 0% -> 0%
where the time goes in v5:
time: 118 us; the launch traced here: 117 us
  starting transfers between devices  46.9 us (40%)
  local copies, waits for them, and re-layouts  27.4 us (23%)
  waiting for transfers between devices  19 us (16%)
  other arithmetic  14.6 us (12%)
  matrix products  8.1 us (7%)
  between operations  1.29 us (1%)
    ppermute x12, starting transfers between devices, exchanged(): lax.ppermute(piece, axis, [(i, (i + step) % count) for i in range(count)])  27.8 us
    ppermute x12, waiting for transfers between devices, exchanged(): lax.ppermute(piece, axis, [(i, (i + step) % count) for i in range(count)])  17.3 us
    ppermute x4, starting transfers between devices, all_summed(): lax.ppermute(value, axis, [(i, i ^ step) for i in range(count)])  10.4 us
    unnamed x36, local copies, waits for them, and re-layouts  10.3 us
    ppermute x2, starting transfers between devices, padded(): lax.ppermute(lax.slice_in_dim(block, block.shape[dim] - width, None, axis...  6.09 us
    dot_general x1, matrix products, local(): jnp.einsum('qKp,qfp->Kf', g_stack, h_freq, preferred_element_type=jnp.flo...  3.12 us
    convert_element_type x1, other arithmetic, local(): dirty_grad = (cotangent.astype(jnp.float32) + conv).astype(jnp.bfloat16)  3.04 us
    convert_element_type x1, other arithmetic, local(): smooth = total.astype(jnp.bfloat16)  3.03 us
  transfers between devices with their start and end apart: 20, of which 8 were waited for; matrix products, arithmetic and copies ran while one was open for 31% of the time, Pallas kernels for 0%

profile of v5, /device:TPU:0, one launch (start us, length us, event | category | flops | bytes accessed | tf_op | source)
XLA Modules:
  0.0 117.2 jit_solution(13375766952555056360)
XLA Ops:
  0.7 1.0 copy.62
  1.7 1.3 %collective-permute-start.1 = (bf16[16,32,2,128]{3,1,2,0:T(8,128)(2,1)S(1)}, bf16[16,32,2,128]{3,1,2,0:T(8,128)(2,1)S(1)}, u32[]{:S(2)}, u32[]{:S(2)}) collective-permute-start(bf16[16,32,2,128]{3,1,2,0:T(8,128)(2,1)S(1)} %copy.62), channel_id=1, source_target_pairs={{1,0},{2,1},{3,2},{5,4},{6,5},{7,6},{9,8},{10,9},{11,10},{13,12},{... | collective-permute-start | bytes 786440 | tf_op jit(solution)/shard_map/ppermute | solution.py:17
  3.0 3.0 %collective-permute-start = (bf16[16,32,2,128]{3,1,2,0:T(8,128)(2,1)S(1)}, bf16[16,32,2,128]{3,1,2,0:T(8,128)(2,1)S(1)}, u32[]{:S(2)}, u32[]{:S(2)}) collective-permute-start(bf16[16,32,2,128]{3,1,2,0:T(8,128)(2,1)S(1)} %copy.62), channel_id=1, source_target_pairs={{0,1},{1,2},{2,3},{4,5},{5,6},{6,7},{8,9},{9,10},{10,11},{12,13},{... | collective-permute-start | bytes 786440 | tf_op jit(solution)/shard_map/ppermute | solution.py:14
  6.1 1.2 %reshape.183 = bf16[16,32,4,64]{3,2,1,0:T(4,128)(2,1)S(1)} reshape(bf16[16,32,2,128]{3,2,1,0:T(2,128)(2,1)} %param.7) | data formatting | bytes 524288 | tf_op jit(solution)/shard_map/reshape | solution.py:95
  7.3 1.1 constant_dynamic-slice_fusion.4
  8.5 3.1 %collective-permute-start.8 = (bf16[16,32,64]{2,1,0:T(8,128)(2,1)S(1)}, bf16[16,32,64]{2,1,0:T(8,128)(2,1)S(1)}, u32[]{:S(2)}, u32[]{:S(2)}) collective-permute-start(bf16[16,32,64]{2,1,0:T(8,128)(2,1)S(1)} %bitcast.392), channel_id=1, source_target_pairs={{0,4},{4,8},{8,12},{12,0},{1,5},{5,9},{9,13},{13,1},{2,6},{6,10},{... | collective-permute-start | bytes 196616 | tf_op jit(solution)/shard_map/ppermute | solution.py:49
  11.6 2.7 %collective-permute-start.9 = (bf16[16,32,64]{2,1,0:T(8,128)(2,1)S(1)}, bf16[16,32,64]{2,1,0:T(8,128)(2,1)S(1)}, u32[]{:S(2)}, u32[]{:S(2)}) collective-permute-start(bf16[16,32,64]{2,1,0:T(8,128)(2,1)S(1)} %bitcast.393), channel_id=1, source_target_pairs={{0,8},{4,12},{8,0},{12,4},{1,9},{5,13},{9,1},{13,5},{2,10},{6,14},... | collective-permute-start | bytes 196616 | tf_op jit(solution)/shard_map/ppermute | solution.py:49
  14.3 1.4 %collective-permute-start.10 = (bf16[16,32,64]{2,1,0:T(8,128)(2,1)S(1)}, bf16[16,32,64]{2,1,0:T(8,128)(2,1)S(1)}, u32[]{:S(2)}, u32[]{:S(2)}) collective-permute-start(bf16[16,32,64]{2,1,0:T(8,128)(2,1)S(1)} %bitcast.394), channel_id=1, source_target_pairs={{0,12},{4,0},{8,4},{12,8},{1,13},{5,1},{9,5},{13,9},{2,14},{6,2},{... | collective-permute-start | bytes 196616 | tf_op jit(solution)/shard_map/ppermute | solution.py:49
  17.3 0.8 scatter_custom_fusion
  18.1 2.6 %compare_select_fusion.2 = s32[64]{0:T(128)S(1)} fusion(s32[64]{0:T(128)S(1)} %scatter_custom_fusion, s32[]{:T(128)} %bitcast.57, s32[]{:T(128)} %bitcast.58, s32[]{:T(128)} %bitcast.59, s32[]{:T(128)} %bitcast.60), kind=kLoop, calls=%fused_computation.288 | loop fusion | flops 2112 | bytes 528 | tf_op jit(solution)/shard_map/select_n | solution.py:98
  20.7 2.8 %collective-permute-done.9 = bf16[16,32,64]{2,1,0:T(8,128)(2,1)S(1)} collective-permute-done((bf16[16,32,64]{2,1,0:T(8,128)(2,1)S(1)}, bf16[16,32,64]{2,1,0:T(8,128)(2,1)S(1)}, u32[]{:S(2)}, u32[]{:S(2)}) %collective-permute-start.9) | collective-permute-done | bytes 65568 | tf_op jit(solution)/shard_map/ppermute | solution.py:49
  25.3 1.8 %copy-done.1 = bf16[64,7,32,64]{3,2,1,0:T(8,128)(2,1)} copy-done((bf16[64,7,32,64]{3,2,1,0:T(8,128)(2,1)}, bf16[64,7,32,64]{3,2,1,0:T(8,128)(2,1)S(1)}, u32[]{:S(2)}) %copy-start.1) | copy-done | bytes 1835032
  28.6 2.4 %collective-permute-start.12 = (bf16[16,32,64]{2,1,0:T(8,128)(2,1)S(1)}, bf16[16,32,64]{2,1,0:T(8,128)(2,1)S(1)}, u32[]{:S(2)}, u32[]{:S(2)}) collective-permute-start(bf16[16,32,64]{2,1,0:T(8,128)(2,1)S(1)} %get-tuple-element.78), channel_id=1, source_target_pairs={{0,8},{4,12},{8,0},{12,4},{1,9},{5,13},{9,1},{13,5},{2,10},{6,14},... | collective-permute-start | bytes 196616 | tf_op jit(solution)/shard_map/ppermute | solution.py:49
  31.0 2.8 %collective-permute-start.11 = (bf16[16,32,64]{2,1,0:T(8,128)(2,1)S(1)}, bf16[16,32,64]{2,1,0:T(8,128)(2,1)S(1)}, u32[]{:S(2)}, u32[]{:S(2)}) collective-permute-start(bf16[16,32,64]{2,1,0:T(8,128)(2,1)S(1)} %get-tuple-element.79), channel_id=1, source_target_pairs={{0,4},{4,8},{8,12},{12,0},{1,5},{5,9},{9,13},{13,1},{2,6},{6,10},{... | collective-permute-start | bytes 196616 | tf_op jit(solution)/shard_map/ppermute | solution.py:49
  33.8 1.0 collective-permute-start.13
  35.0 6.5 %collective-permute-done.11 = bf16[16,32,64]{2,1,0:T(8,128)(2,1)S(1)} collective-permute-done((bf16[16,32,64]{2,1,0:T(8,128)(2,1)S(1)}, bf16[16,32,64]{2,1,0:T(8,128)(2,1)S(1)}, u32[]{:S(2)}, u32[]{:S(2)}) %collective-permute-start.11) | collective-permute-done | bytes 65568 | tf_op jit(solution)/shard_map/ppermute | solution.py:49
  43.2 0.8 reshape.192
  44.0 0.8 select_maximum_fusion.2
  44.8 3.0 %fusion.63 = bf16[16,32,2,128]{3,1,2,0:T(8,128)(2,1)S(1)} fusion(f32[16,32,6,132]{3,1,2,0:T(8,128)S(1)} %get-tuple-element.74, f32[32]{0:T(128)S(1)} %get-tuple-element.71, f32[32]{0:T(128)S(1)} %get-tuple-element.72, f32[32]{0:T(128)S(1)} %get-tuple-element.49, f32[32]{0:T(128)S(1)} %get-tuple-element.50, f32[32]{0:T(128)S(1)} %get-tuple-element.51, ...), kind=kLoop, calls=%fused_computation.131 | loop fusion | flops 6553600 | bytes 13372544 | tf_op jit(solution)/shard_map/convert_element_type | solution.py:85
  48.9 1.8 %fusion.35 = (f32[32]{0:T(128)S(1)}, f32[32]{0:T(128)S(1)}, f32[32]{0:T(128)S(1)}, f32[32]{0:T(128)S(1)}, f32[32]{0:T(128)S(1)}, /*index=5*/f32[32]{0:T(128)S(1)...) fusion(bf16[16,32,6,132]{3,1,2,0:T(8,128)(2,1)S(1)} %get-tuple-, ...), kind=kLoop, calls=%fused_computation.77 | loop fusion | flops 7208384 | bytes 4983040 | tf_op jit(solution)/shard_map/cfhw,cfhw->f/dot_general | solution.py:142
  50.7 1.3 %collective-permute-start.15 = (bf16[16,32,2,128]{3,1,2,0:T(8,128)(2,1)S(1)}, bf16[16,32,2,128]{3,1,2,0:T(8,128)(2,1)S(1)}, u32[]{:S(2)}, u32[]{:S(2)}) collective-permute-start(bf16[16,32,2,128]{3,1,2,0:T(8,128)(2,1)S(1)} %bitcast.383), channel_id=1, source_target_pairs={{1,0},{2,1},{3,2},{5,4},{6,5},{7,6},{9,8},{10,9},{11,10},{13,12},{... | collective-permute-start | bytes 786440 | tf_op jit(solution)/shard_map/ppermute | solution.py:17
  52.0 3.0 %collective-permute-start.14 = (bf16[16,32,2,128]{3,1,2,0:T(8,128)(2,1)S(1)}, bf16[16,32,2,128]{3,1,2,0:T(8,128)(2,1)S(1)}, u32[]{:S(2)}, u32[]{:S(2)}) collective-permute-start(bf16[16,32,2,128]{3,1,2,0:T(8,128)(2,1)S(1)} %bitcast.384), channel_id=1, source_target_pairs={{0,1},{1,2},{2,3},{4,5},{5,6},{6,7},{8,9},{9,10},{10,11},{12,13},{... | collective-permute-start | bytes 786440 | tf_op jit(solution)/shard_map/ppermute | solution.py:14
  56.3 1.1 constant_dynamic-slice_fusion.9
  57.5 2.5 %collective-permute-start.2 = (bf16[16,32,64]{2,1,0:T(8,128)(2,1)S(1)}, bf16[16,32,64]{2,1,0:T(8,128)(2,1)S(1)}, u32[]{:S(2)}, u32[]{:S(2)}) collective-permute-start(bf16[16,32,64]{2,1,0:T(8,128)(2,1)S(1)} %bitcast.397), channel_id=1, source_target_pairs={{0,4},{4,8},{8,12},{12,0},{1,5},{5,9},{9,13},{13,1},{2,6},{6,10},{... | collective-permute-start | bytes 196616 | tf_op jit(solution)/shard_map/ppermute | solution.py:49
  60.1 1.9 %collective-permute-start.3 = (bf16[16,32,64]{2,1,0:T(8,128)(2,1)S(1)}, bf16[16,32,64]{2,1,0:T(8,128)(2,1)S(1)}, u32[]{:S(2)}, u32[]{:S(2)}) collective-permute-start(bf16[16,32,64]{2,1,0:T(8,128)(2,1)S(1)} %bitcast.396), channel_id=1, source_target_pairs={{0,8},{4,12},{8,0},{12,4},{1,9},{5,13},{9,1},{13,5},{2,10},{6,14},... | collective-permute-start | bytes 196616 | tf_op jit(solution)/shard_map/ppermute | solution.py:49
  62.0 2.8 %collective-permute-start.4 = (bf16[16,32,64]{2,1,0:T(8,128)(2,1)S(1)}, bf16[16,32,64]{2,1,0:T(8,128)(2,1)S(1)}, u32[]{:S(2)}, u32[]{:S(2)}) collective-permute-start(bf16[16,32,64]{2,1,0:T(8,128)(2,1)S(1)} %bitcast.395), channel_id=1, source_target_pairs={{0,12},{4,0},{8,4},{12,8},{1,13},{5,1},{9,5},{13,9},{2,14},{6,2},{... | collective-permute-start | bytes 196616 | tf_op jit(solution)/shard_map/ppermute | solution.py:49
  65.4 5.4 %collective-permute-done.3 = bf16[16,32,64]{2,1,0:T(8,128)(2,1)S(1)} collective-permute-done((bf16[16,32,64]{2,1,0:T(8,128)(2,1)S(1)}, bf16[16,32,64]{2,1,0:T(8,128)(2,1)S(1)}, u32[]{:S(2)}, u32[]{:S(2)}) %collective-permute-start.3) | collective-permute-done | bytes 65568 | tf_op jit(solution)/shard_map/ppermute | solution.py:49
  71.6 3.1 %fusion.9 = f32[7,32,32]{2,1,0:T(8,128)S(1)} fusion(bf16[64,7,32,64]{3,2,1,0:T(8,128)(2,1)} %copy-done.1, bf16[64,32,64]{2,1,0:T(8,128)(2,1)S(1)} %gather_fusion), kind=kOutput, calls=%fused_computation.50 | convolution fusion | flops 58720256 | bytes 2125824 | tf_op jit(solution)/shard_map/qKp,qfp->Kf/dot_general | solution.py:121
  74.8 0.9 bitcast_dynamic-update-slice_fusion.11
  76.1 0.9 bitcast_dynamic-update-slice_fusion.10
  77.0 0.9 bitcast_dynamic-update-slice_fusion.9
  78.0 0.9 bitcast_dynamic-update-slice_fusion.8
  78.9 0.9 bitcast_dynamic-update-slice_fusion.7
  79.8 0.9 bitcast_dynamic-update-slice_fusion.6
  80.7 0.9 bitcast_dynamic-update-slice_fusion.13
  81.7 3.0 %fusion.7 = bf16[64,32,64]{2,1,0:T(8,128)(2,1)S(1)} fusion(bf16[64,7,32,64]{3,2,1,0:T(8,128)(2,1)} %bitcast_dynamic-update-slice_fusion.13, bf16[7,32,32]{2,1,0:T(8,128)(2,1)S(1)} %copy-done.5), kind=kOutput, calls=%fused_computation.46 | convolution fusion | flops 58851328 | bytes 2111488 | tf_op jit(solution)/shard_map/gK,qKp->qgp/dot_general | solution.py:119
  85.4 3.2 %collective-permute-start.6 = (bf16[16,32,64]{2,1,0:T(8,128)(2,1)S(1)}, bf16[16,32,64]{2,1,0:T(8,128)(2,1)S(1)}, u32[]{:S(2)}, u32[]{:S(2)}) collective-permute-start(bf16[16,32,64]{2,1,0:T(8,128)(2,1)S(1)} %get-tuple-element.86), channel_id=1, source_target_pairs={{0,8},{4,12},{8,0},{12,4},{1,9},{5,13},{9,1},{13,5},{2,10},{6,14},... | collective-permute-start | bytes 196616 | tf_op jit(solution)/shard_map/ppermute | solution.py:49
  88.5 4.0 %collective-permute-start.5 = (bf16[16,32,64]{2,1,0:T(8,128)(2,1)S(1)}, bf16[16,32,64]{2,1,0:T(8,128)(2,1)S(1)}, u32[]{:S(2)}, u32[]{:S(2)}) collective-permute-start(bf16[16,32,64]{2,1,0:T(8,128)(2,1)S(1)} %get-tuple-element.87), channel_id=1, source_target_pairs={{0,4},{4,8},{8,12},{12,0},{1,5},{5,9},{9,13},{13,1},{2,6},{6,10},{... | collective-permute-start | bytes 196616 | tf_op jit(solution)/shard_map/ppermute | solution.py:49
  92.5 5.6 %collective-permute-start.17 = (f32[8992]{0:T(1024)S(1)}, f32[8992]{0:T(1024)S(1)}, u32[]{:S(2)}, u32[]{:S(2)}) collective-permute-start(f32[8992]{0:T(1024)S(1)} %fusion.102), channel_id=1, source_target_pairs={{0,2},{2,0},{1,3},{3,1},{4,6},{6,4},{5,7},{7,5},{8,10},{10,8},{9,1... | collective-permute-start | bytes 107912 | tf_op jit(solution)/shard_map/ppermute | solution.py:36
  98.2 1.0 collective-permute-done.5
  99.2 1.3 %collective-permute-done.7 = bf16[16,32,64]{2,1,0:T(8,128)(2,1)S(1)} collective-permute-done((bf16[16,32,64]{2,1,0:T(8,128)(2,1)S(1)}, bf16[16,32,64]{2,1,0:T(8,128)(2,1)S(1)}, u32[]{:S(2)}, u32[]{:S(2)}) %collective-permute-start.7) | collective-permute-done | bytes 65568 | tf_op jit(solution)/shard_map/ppermute | solution.py:49
  101.4 1.7 %collective-permute-start.18 = (f32[8992]{0:T(1024)S(1)}, f32[8992]{0:T(1024)S(1)}, u32[]{:S(2)}, u32[]{:S(2)}) collective-permute-start(f32[8992]{0:T(1024)S(1)} %add.379), channel_id=1, source_target_pairs={{0,4},{4,0},{8,12},{12,8},{1,5},{5,1},{9,13},{13,9},{2,6},{6,2},{1... | collective-permute-start | bytes 107912 | tf_op jit(solution)/shard_map/ppermute | solution.py:36
  103.9 0.8 reshape.191
  105.4 2.9 %collective-permute-start.19 = (f32[8992]{0:T(1024)S(1)}, f32[8992]{0:T(1024)S(1)}, u32[]{:S(2)}, u32[]{:S(2)}) collective-permute-start(f32[8992]{0:T(1024)S(1)} %add.380), channel_id=1, source_target_pairs={{0,8},{4,12},{8,0},{12,4},{1,9},{5,13},{9,1},{13,5},{2,10},{6,14},... | collective-permute-start | bytes 107912 | tf_op jit(solution)/shard_map/ppermute | solution.py:36
  108.3 1.0 add_convert_fusion
  109.2 1.0 collective-permute-done.19
  113.2 3.0 %fusion.38 = bf16[16,32,2,128]{3,1,2,0:T(8,128)(2,1)S(1)} fusion(f32[16,32,6,132]{3,1,2,0:T(8,128)S(1)} %fusion.3, bf16[16,32,2,128]{3,2,1,0:T(2,128)(2,1)S(1)} %copy-done.4, f32[32]{0:T(128)S(1)} %get-tuple-element.71, f32[32]{0:T(128)S(1)} %get-tuple-element.72, f32[32]{0:T(128)S(1)} %get-tuple-element.49, f32[32]{0:T(128)S(1)} %get-tuple-element.50, ...), kind=kLoop, calls=%fused_computation.81 | loop fusion | flops 6815744 | bytes 13634688 | tf_op jit(solution)/shard_map/convert_element_type | solution.py:150
  116.3 0.9 copy.89
  (100 shorter events, 17.0 us)
Async XLA Ops:
  0.6 47.2 %copy-start = (bf16[32,32]{1,0:T(8,128)(2,1)S(1)}, bf16[32,32]{1,0:T(8,128)(2,1)}, u32[]{:S(2)}) copy-start(bf16[32,32]{1,0:T(8,128)(2,1)} %param.9) | copy-start | bytes 6148
  0.6 15.0 %copy-start.6 = (s32[64]{0:T(128)S(1)}, s32[64]{0:T(128)}, u32[]{:S(2)}) copy-start(s32[64]{0:T(128)} %param.11) | copy-start | bytes 772
  0.7 15.1 %copy-start.2 = (f32[32,25]{1,0:T(8,128)S(1)}, f32[32,25]{1,0:T(8,128)}, u32[]{:S(2)}) copy-start(f32[32,25]{1,0:T(8,128)} %param.8) | copy-start | bytes 9604
  0.7 16.6 %copy-start.5 = (bf16[7,32,32]{2,1,0:T(8,128)(2,1)S(1)}, bf16[7,32,32]{2,1,0:T(8,128)(2,1)}, u32[]{:S(2)}) copy-start(bf16[7,32,32]{2,1,0:T(8,128)(2,1)} %param.10) | copy-start | bytes 43012
  1.7 42.3 %collective-permute-start.1 = (bf16[16,32,2,128]{3,1,2,0:T(8,128)(2,1)S(1)}, bf16[16,32,2,128]{3,1,2,0:T(8,128)(2,1)S(1)}, u32[]{:S(2)}, u32[]{:S(2)}) collective-permute-start(bf16[16,32,2,128]{3,1,2,0:T(8,128)(2,1)S(1)} %copy.62), channel_id=1, source_target_pairs={{1,0},{2,1},{3,2},{5,4},{6,5},{7,6},{9,8},{10,9},{11,10},{13,12},{... | collective-permute-start | bytes 786440 | tf_op jit(solution)/shard_map/ppermute | solution.py:17
  3.0 41.0 %collective-permute-start = (bf16[16,32,2,128]{3,1,2,0:T(8,128)(2,1)S(1)}, bf16[16,32,2,128]{3,1,2,0:T(8,128)(2,1)S(1)}, u32[]{:S(2)}, u32[]{:S(2)}) collective-permute-start(bf16[16,32,2,128]{3,1,2,0:T(8,128)(2,1)S(1)} %copy.62), channel_id=1, source_target_pairs={{0,1},{1,2},{2,3},{4,5},{5,6},{6,7},{8,9},{9,10},{10,11},{12,13},{... | collective-permute-start | bytes 786440 | tf_op jit(solution)/shard_map/ppermute | solution.py:14
  8.5 12.3 %collective-permute-start.8 = (bf16[16,32,64]{2,1,0:T(8,128)(2,1)S(1)}, bf16[16,32,64]{2,1,0:T(8,128)(2,1)S(1)}, u32[]{:S(2)}, u32[]{:S(2)}) collective-permute-start(bf16[16,32,64]{2,1,0:T(8,128)(2,1)S(1)} %bitcast.392), channel_id=1, source_target_pairs={{0,4},{4,8},{8,12},{12,0},{1,5},{5,9},{9,13},{13,1},{2,6},{6,10},{... | collective-permute-start | bytes 196616 | tf_op jit(solution)/shard_map/ppermute | solution.py:49
  11.6 12.0 %collective-permute-start.9 = (bf16[16,32,64]{2,1,0:T(8,128)(2,1)S(1)}, bf16[16,32,64]{2,1,0:T(8,128)(2,1)S(1)}, u32[]{:S(2)}, u32[]{:S(2)}) collective-permute-start(bf16[16,32,64]{2,1,0:T(8,128)(2,1)S(1)} %bitcast.393), channel_id=1, source_target_pairs={{0,8},{4,12},{8,0},{12,4},{1,9},{5,13},{9,1},{13,5},{2,10},{6,14},... | collective-permute-start | bytes 196616 | tf_op jit(solution)/shard_map/ppermute | solution.py:49
  14.3 9.3 %collective-permute-start.10 = (bf16[16,32,64]{2,1,0:T(8,128)(2,1)S(1)}, bf16[16,32,64]{2,1,0:T(8,128)(2,1)S(1)}, u32[]{:S(2)}, u32[]{:S(2)}) collective-permute-start(bf16[16,32,64]{2,1,0:T(8,128)(2,1)S(1)} %bitcast.394), channel_id=1, source_target_pairs={{0,12},{4,0},{8,4},{12,8},{1,13},{5,1},{9,5},{13,9},{2,14},{6,2},{... | collective-permute-start | bytes 196616 | tf_op jit(solution)/shard_map/ppermute | solution.py:49
  25.3 1.8 %copy-start.1 = (bf16[64,7,32,64]{3,2,1,0:T(8,128)(2,1)}, bf16[64,7,32,64]{3,2,1,0:T(8,128)(2,1)S(1)}, u32[]{:S(2)}) copy-start(bf16[64,7,32,64]{3,2,1,0:T(8,128)(2,1)S(1)} %bitcast_dynamic-update-slice_fusion.12) | copy-start | bytes 5505028
  28.6 6.5 %collective-permute-start.12 = (bf16[16,32,64]{2,1,0:T(8,128)(2,1)S(1)}, bf16[16,32,64]{2,1,0:T(8,128)(2,1)S(1)}, u32[]{:S(2)}, u32[]{:S(2)}) collective-permute-start(bf16[16,32,64]{2,1,0:T(8,128)(2,1)S(1)} %get-tuple-element.78), channel_id=1, source_target_pairs={{0,8},{4,12},{8,0},{12,4},{1,9},{5,13},{9,1},{13,5},{2,10},{6,14},... | collective-permute-start | bytes 196616 | tf_op jit(solution)/shard_map/ppermute | solution.py:49
  31.0 10.6 %collective-permute-start.11 = (bf16[16,32,64]{2,1,0:T(8,128)(2,1)S(1)}, bf16[16,32,64]{2,1,0:T(8,128)(2,1)S(1)}, u32[]{:S(2)}, u32[]{:S(2)}) collective-permute-start(bf16[16,32,64]{2,1,0:T(8,128)(2,1)S(1)} %get-tuple-element.79), channel_id=1, source_target_pairs={{0,4},{4,8},{8,12},{12,0},{1,5},{5,9},{9,13},{13,1},{2,6},{6,10},{... | collective-permute-start | bytes 196616 | tf_op jit(solution)/shard_map/ppermute | solution.py:49
  33.8 7.8 %collective-permute-start.13 = (bf16[16,32,64]{2,1,0:T(8,128)(2,1)S(1)}, bf16[16,32,64]{2,1,0:T(8,128)(2,1)S(1)}, u32[]{:S(2)}, u32[]{:S(2)}) collective-permute-start(bf16[16,32,64]{2,1,0:T(8,128)(2,1)S(1)} %get-tuple-element.80), channel_id=1, source_target_pairs={{0,12},{4,0},{8,4},{12,8},{1,13},{5,1},{9,5},{13,9},{2,14},{6,2},{... | collective-permute-start | bytes 196616 | tf_op jit(solution)/shard_map/ppermute | solution.py:49
  48.9 6.7 %copy-start.3 = (bf16[16,32,2,128]{3,2,1,0:T(2,128)(2,1)S(1)}, bf16[16,32,2,128]{3,2,1,0:T(2,128)(2,1)}, u32[]{:S(2)}) copy-start(bf16[16,32,2,128]{3,2,1,0:T(2,128)(2,1)} %param.6) | copy-start | bytes 786436
  50.7 61.9 %collective-permute-start.15 = (bf16[16,32,2,128]{3,1,2,0:T(8,128)(2,1)S(1)}, bf16[16,32,2,128]{3,1,2,0:T(8,128)(2,1)S(1)}, u32[]{:S(2)}, u32[]{:S(2)}) collective-permute-start(bf16[16,32,2,128]{3,1,2,0:T(8,128)(2,1)S(1)} %bitcast.383), channel_id=1, source_target_pairs={{1,0},{2,1},{3,2},{5,4},{6,5},{7,6},{9,8},{10,9},{11,10},{13,12},{... | collective-permute-start | bytes 786440 | tf_op jit(solution)/shard_map/ppermute | solution.py:17
  52.0 60.6 %collective-permute-start.14 = (bf16[16,32,2,128]{3,1,2,0:T(8,128)(2,1)S(1)}, bf16[16,32,2,128]{3,1,2,0:T(8,128)(2,1)S(1)}, u32[]{:S(2)}, u32[]{:S(2)}) collective-permute-start(bf16[16,32,2,128]{3,1,2,0:T(8,128)(2,1)S(1)} %bitcast.384), channel_id=1, source_target_pairs={{0,1},{1,2},{2,3},{4,5},{5,6},{6,7},{8,9},{9,10},{10,11},{12,13},{... | collective-permute-start | bytes 786440 | tf_op jit(solution)/shard_map/ppermute | solution.py:14
  57.5 7.9 %collective-permute-start.2 = (bf16[16,32,64]{2,1,0:T(8,128)(2,1)S(1)}, bf16[16,32,64]{2,1,0:T(8,128)(2,1)S(1)}, u32[]{:S(2)}, u32[]{:S(2)}) collective-permute-start(bf16[16,32,64]{2,1,0:T(8,128)(2,1)S(1)} %bitcast.397), channel_id=1, source_target_pairs={{0,4},{4,8},{8,12},{12,0},{1,5},{5,9},{9,13},{13,1},{2,6},{6,10},{... | collective-permute-start | bytes 196616 | tf_op jit(solution)/shard_map/ppermute | solution.py:49
  60.1 10.7 %collective-permute-start.3 = (bf16[16,32,64]{2,1,0:T(8,128)(2,1)S(1)}, bf16[16,32,64]{2,1,0:T(8,128)(2,1)S(1)}, u32[]{:S(2)}, u32[]{:S(2)}) collective-permute-start(bf16[16,32,64]{2,1,0:T(8,128)(2,1)S(1)} %bitcast.396), channel_id=1, source_target_pairs={{0,8},{4,12},{8,0},{12,4},{1,9},{5,13},{9,1},{13,5},{2,10},{6,14},... | collective-permute-start | bytes 196616 | tf_op jit(solution)/shard_map/ppermute | solution.py:49
  62.0 8.8 %collective-permute-start.4 = (bf16[16,32,64]{2,1,0:T(8,128)(2,1)S(1)}, bf16[16,32,64]{2,1,0:T(8,128)(2,1)S(1)}, u32[]{:S(2)}, u32[]{:S(2)}) collective-permute-start(bf16[16,32,64]{2,1,0:T(8,128)(2,1)S(1)} %bitcast.395), channel_id=1, source_target_pairs={{0,12},{4,0},{8,4},{12,8},{1,13},{5,1},{9,5},{13,9},{2,14},{6,2},{... | collective-permute-start | bytes 196616 | tf_op jit(solution)/shard_map/ppermute | solution.py:49
  75.9 16.6 %collective-permute-start.16 = (f32[8992]{0:T(1024)S(1)}, f32[8992]{0:T(1024)S(1)}, u32[]{:S(2)}, u32[]{:S(2)}) collective-permute-start(f32[8992]{0:T(1024)S(1)} %broadcast_multiply_fusion), channel_id=1, source_target_pairs={{0,1},{1,0},{2,3},{3,2},{4,5},{5,4},{6,7},{7,6},{8,9},{9,8},{10,11... | collective-permute-start | bytes 107912 | tf_op jit(solution)/shard_map/ppermute | solution.py:36
  85.4 7.2 %collective-permute-start.6 = (bf16[16,32,64]{2,1,0:T(8,128)(2,1)S(1)}, bf16[16,32,64]{2,1,0:T(8,128)(2,1)S(1)}, u32[]{:S(2)}, u32[]{:S(2)}) collective-permute-start(bf16[16,32,64]{2,1,0:T(8,128)(2,1)S(1)} %get-tuple-element.86), channel_id=1, source_target_pairs={{0,8},{4,12},{8,0},{12,4},{1,9},{5,13},{9,1},{13,5},{2,10},{6,14},... | collective-permute-start | bytes 196616 | tf_op jit(solution)/shard_map/ppermute | solution.py:49
  88.5 10.7 %collective-permute-start.5 = (bf16[16,32,64]{2,1,0:T(8,128)(2,1)S(1)}, bf16[16,32,64]{2,1,0:T(8,128)(2,1)S(1)}, u32[]{:S(2)}, u32[]{:S(2)}) collective-permute-start(bf16[16,32,64]{2,1,0:T(8,128)(2,1)S(1)} %get-tuple-element.87), channel_id=1, source_target_pairs={{0,4},{4,8},{8,12},{12,0},{1,5},{5,9},{9,13},{13,1},{2,6},{6,10},{... | collective-permute-start | bytes 196616 | tf_op jit(solution)/shard_map/ppermute | solution.py:49
  92.5 8.0 %collective-permute-start.7 = (bf16[16,32,64]{2,1,0:T(8,128)(2,1)S(1)}, bf16[16,32,64]{2,1,0:T(8,128)(2,1)S(1)}, u32[]{:S(2)}, u32[]{:S(2)}) collective-permute-start(bf16[16,32,64]{2,1,0:T(8,128)(2,1)S(1)} %get-tuple-element.88), channel_id=1, source_target_pairs={{0,12},{4,0},{8,4},{12,8},{1,13},{5,1},{9,5},{13,9},{2,14},{6,2},{... | collective-permute-start | bytes 196616 | tf_op jit(solution)/shard_map/ppermute | solution.py:49
  92.5 8.8 %collective-permute-start.17 = (f32[8992]{0:T(1024)S(1)}, f32[8992]{0:T(1024)S(1)}, u32[]{:S(2)}, u32[]{:S(2)}) collective-permute-start(f32[8992]{0:T(1024)S(1)} %fusion.102), channel_id=1, source_target_pairs={{0,2},{2,0},{1,3},{3,1},{4,6},{6,4},{5,7},{7,5},{8,10},{10,8},{9,1... | collective-permute-start | bytes 107912 | tf_op jit(solution)/shard_map/ppermute | solution.py:36
  101.4 4.0 %collective-permute-start.18 = (f32[8992]{0:T(1024)S(1)}, f32[8992]{0:T(1024)S(1)}, u32[]{:S(2)}, u32[]{:S(2)}) collective-permute-start(f32[8992]{0:T(1024)S(1)} %add.379), channel_id=1, source_target_pairs={{0,4},{4,0},{8,12},{12,8},{1,5},{5,1},{9,13},{13,9},{2,6},{6,2},{1... | collective-permute-start | bytes 107912 | tf_op jit(solution)/shard_map/ppermute | solution.py:36
  103.9 9.3 %copy-start.4 = (bf16[16,32,2,128]{3,2,1,0:T(2,128)(2,1)S(1)}, bf16[16,32,2,128]{3,2,1,0:T(2,128)(2,1)}, u32[]{:S(2)}) copy-start(bf16[16,32,2,128]{3,2,1,0:T(2,128)(2,1)} %param.7) | copy-start | bytes 786436
  105.4 4.9 %collective-permute-start.19 = (f32[8992]{0:T(1024)S(1)}, f32[8992]{0:T(1024)S(1)}, u32[]{:S(2)}, u32[]{:S(2)}) collective-permute-start(f32[8992]{0:T(1024)S(1)} %add.380), channel_id=1, source_target_pairs={{0,8},{4,12},{8,0},{12,4},{1,9},{5,13},{9,1},{13,5},{2,10},{6,14},... | collective-permute-start | bytes 107912 | tf_op jit(solution)/shard_map/ppermute | solution.py:36

commit v6 on v2

--- a/solution.py
+++ b/solution.py
@@ -25,7 +25,9 @@
     return lax.ppermute(block, axis, route)
 
 
-def all_summed(value, axes):
+def all_summed(value, axes, tied=None):
+    if tied is not None:
+        value, _ = lax.optimization_barrier((value, tied))
     for axis in axes:
         count = lax.axis_size(axis)
         if count & (count - 1):
@@ -82,10 +84,12 @@
     h_sorted = hidden_flat[order]
     g_sorted = grad_flat[order]
     h_taps = [h_sorted] * taps
+    h_received = []
     g_taps = [g_sorted] * taps
     for dist in range(1, half + 1):
         for sign in (-1, 1):
             h_far = passed_along(h_sorted, "chan", -sign * dist)
+            h_received.append(h_far)
             g_far = passed_along(g_sorted, "chan", -sign * dist)
             if sign < 0:
                 wrapped = device < dist
@@ -139,7 +143,7 @@
     dirty_grad = (cotangent.astype(jnp.float32) + conv).astype(jnp.bfloat16)
     parts = (kernel_term, mix_term, spec_grad)
     flat = jnp.concatenate([part.reshape(-1) for part in parts]) * scale
-    flat = all_summed(flat, ("sub", "tile", "chan"))
+    flat = all_summed(flat, ("sub", "tile", "chan"), tied=h_received)
     sizes = [part.size for part in parts]
     kgrad, mgrad, sgrad = (
         piece.reshape(part.shape)

time: 87.9 us -> 90.4 us (1.028)
  waiting for transfers between devices: 24 us -> 13.7 us
  local copies, waits for them, and re-layouts: 12.4 us -> 17.9 us
  starting transfers between devices: 29.8 us -> 35.2 us
  matrix products: 5.29 us -> 6.95 us
    ppermute x6, waiting for transfers between devices: 17.7 us -> 10.3 us  [passed_along(): return lax.ppermute(block, axis, route)]
    ppermute x4, starting transfers between devices: 3.11 us -> 10.1 us  [all_summed(): lax.ppermute(value, axis, [(i, i ^ step) for i in range(count)])]
    ppermute x4, waiting for transfers between devices: 6.3 us -> 3.37 us  [all_summed(): lax.ppermute(value, axis, [(i, i ^ step) for i in range(count)])]
    dot_general x1, matrix products: 0.6 us -> 2.29 us  [local(): jnp.einsum('mKp,mfp->Kf', g_stack, h_sorted, preferred_element_type=jnp.f...]
    ppermute x6, starting transfers between devices: 17.2 us -> 15.5 us  [passed_along(): return lax.ppermute(block, axis, route)]
    unnamed x130 -> x142, local copies, waits for them, and re-layouts: 2.38 us -> 4.03 us
    gather x1, local copies, waits for them, and re-layouts: 0.56 us -> 2.2 us  [local(): h_sorted = hidden_flat[order]]
  transfers between devices with their start and end apart: 14 -> 14, of which waited for: 5 -> 6; matrix products, arithmetic and copies ran while one was open for 12% -> 24% of each run, Pallas kernels for 0% -> 0%
where the time goes in v6:
time: 90.4 us; the launch traced here: 89.8 us
  starting transfers between devices  35.2 us (39%)
  local copies, waits for them, and re-layouts  17.9 us (20%)
  other arithmetic  14.2 us (16%)
  waiting for transfers between devices  13.7 us (15%)
  matrix products  6.95 us (8%)
  between operations  1.86 us (2%)
    ppermute x6, starting transfers between devices, passed_along(): return lax.ppermute(block, axis, route)  15.5 us
    ppermute x6, waiting for transfers between devices, passed_along(): return lax.ppermute(block, axis, route)  10.3 us
    ppermute x4, starting transfers between devices, all_summed(): lax.ppermute(value, axis, [(i, i ^ step) for i in range(count)])  10.1 us
    ppermute x2, starting transfers between devices, padded(): lax.ppermute(lax.slice_in_dim(block, block.shape[dim] - width, None, axis...  6.97 us
    unnamed x142, local copies, waits for them, and re-layouts  4.03 us
    ppermute x4, waiting for transfers between devices, all_summed(): lax.ppermute(value, axis, [(i, i ^ step) for i in range(count)])  3.37 us
    dot_general x2, other arithmetic, local(): jnp.einsum('cfhw,cfhw->f', dsmooth, xpad[:, :, i:i + rows, j:j + cols], p...  3.05 us
    convert_element_type x1, other arithmetic, local(): dirty_grad = (cotangent.astype(jnp.float32) + conv).astype(jnp.bfloat16)  3.04 us
  transfers between devices with their start and end apart: 14, of which 6 were waited for; matrix products, arithmetic and copies ran while one was open for 24% of the time, Pallas kernels for 0%

profile of v6, /device:TPU:0, one launch (start us, length us, event | category | flops | bytes accessed | tf_op | source)
XLA Modules:
  0.0 89.8 jit_solution(13082449273565238811)
XLA Ops:
  0.7 0.8 compare_select_fusion.1
  1.4 0.6 scatter_custom_fusion
  2.1 1.1 %reshape.80 = bf16[16,32,256]{2,1,0:T(8,128)(2,1)S(1)} reshape(bf16[16,32,2,128]{3,2,1,0:T(2,128)(2,1)} %param.7) | data formatting | bytes 524288 | tf_op jit(solution)/shard_map/reshape | solution.py:79
  3.2 0.6 gather_fusion.2
  3.8 3.1 %collective-permute-start.7 = (bf16[16,32,256]{2,1,0:T(8,128)(2,1)S(1)}, bf16[16,32,256]{2,1,0:T(8,128)(2,1)S(1)}, u32[]{:S(2)}, u32[]{:S(2)}) collective-permute-start(bf16[16,32,256]{2,1,0:T(8,128)(2,1)S(1)} %gather_fusion.2), channel_id=1, source_target_pairs={{12,0},{0,4},{4,8},{8,12},{13,1},{1,5},{5,9},{9,13},{14,2},{2,6},{... | collective-permute-start | bytes 786440 | tf_op jit(solution)/shard_map/ppermute | solution.py:25
  6.9 2.6 %collective-permute-start.6 = (bf16[16,32,256]{2,1,0:T(8,128)(2,1)S(1)}, bf16[16,32,256]{2,1,0:T(8,128)(2,1)S(1)}, u32[]{:S(2)}, u32[]{:S(2)}) collective-permute-start(bf16[16,32,256]{2,1,0:T(8,128)(2,1)S(1)} %gather_fusion.2), channel_id=1, source_target_pairs={{8,0},{12,4},{0,8},{4,12},{9,1},{13,5},{1,9},{5,13},{10,2},{14,6},... | collective-permute-start | bytes 786440 | tf_op jit(solution)/shard_map/ppermute | solution.py:25
  9.5 1.3 %collective-permute-start.5 = (bf16[16,32,256]{2,1,0:T(8,128)(2,1)S(1)}, bf16[16,32,256]{2,1,0:T(8,128)(2,1)S(1)}, u32[]{:S(2)}, u32[]{:S(2)}) collective-permute-start(bf16[16,32,256]{2,1,0:T(8,128)(2,1)S(1)} %gather_fusion.2), channel_id=1, source_target_pairs={{4,0},{8,4},{12,8},{0,12},{5,1},{9,5},{13,9},{1,13},{6,2},{10,6},{... | collective-permute-start | bytes 786440 | tf_op jit(solution)/shard_map/ppermute | solution.py:25
  10.8 1.0 %copy.27 = bf16[16,32,2,128]{3,1,2,0:T(8,128)(2,1)S(1)} copy(bf16[16,32,2,128]{3,2,1,0:T(2,128)(2,1)} %param.6) | data formatting | bytes 524288 | tf_op args[0]
  11.8 1.3 %collective-permute-start.1 = (bf16[16,32,2,128]{3,1,2,0:T(8,128)(2,1)S(1)}, bf16[16,32,2,128]{3,1,2,0:T(8,128)(2,1)S(1)}, u32[]{:S(2)}, u32[]{:S(2)}) collective-permute-start(bf16[16,32,2,128]{3,1,2,0:T(8,128)(2,1)S(1)} %copy.27), channel_id=1, source_target_pairs={{1,0},{2,1},{3,2},{5,4},{6,5},{7,6},{9,8},{10,9},{11,10},{13,12},{... | collective-permute-start | bytes 786440 | tf_op jit(solution)/shard_map/ppermute | solution.py:17
  13.1 3.7 %collective-permute-start = (bf16[16,32,2,128]{3,1,2,0:T(8,128)(2,1)S(1)}, bf16[16,32,2,128]{3,1,2,0:T(8,128)(2,1)}, u32[]{:S(2)}, u32[]{:S(2)}) collective-permute-start(bf16[16,32,2,128]{3,1,2,0:T(8,128)(2,1)S(1)} %copy.27), channel_id=1, source_target_pairs={{0,1},{1,2},{2,3},{4,5},{5,6},{6,7},{8,9},{9,10},{10,11},{12,13},{... | collective-permute-start | bytes 786440 | tf_op jit(solution)/shard_map/ppermute | solution.py:14
  16.9 1.7 %slice_reduce_fusion.23 = (f32[32]{0:T(128)S(1)}, f32[32]{0:T(128)S(1)}, f32[32]{0:T(128)S(1)}, f32[32]{0:T(128)S(1)}, f32[32]{0:T(128)}, /*index=5*/f32[32]{0:T(128)}) fusion(f32[32,25]{1,0:T(8,128)} %param.8), kind=kLoop, calls=%fused_computation.286 | loop fusion | bytes 1536 | tf_op jit(solution)/shard_map/slice | solution.py:72
  18.6 1.1 %slice_reduce_fusion.24 = (f32[32]{0:T(128)}, f32[32]{0:T(128)}, f32[32]{0:T(128)}, f32[32]{0:T(128)}, f32[32]{0:T(128)}, /*index=5*/f32[32]{0:T(128)}, f32[32]{...) fusion(f32[32,25]{1,0:T(8,128)S(1)} %copy-done.1), kind=kLoop, calls=%fused_computation.287 | loop fusion | bytes 4864 | tf_op jit(solution)/shard_map/slice | solution.py:72
  19.7 4.0 %collective-permute-done.5 = bf16[16,32,256]{2,1,0:T(8,128)(2,1)S(1)} collective-permute-done((bf16[16,32,256]{2,1,0:T(8,128)(2,1)S(1)}, bf16[16,32,256]{2,1,0:T(8,128)(2,1)S(1)}, u32[]{:S(2)}, u32[]{:S(2)}) %collective-permute-start.5) | collective-permute-done | bytes 262176 | tf_op jit(solution)/shard_map/ppermute | solution.py:25
  23.8 2.8 %collective-permute-done.6 = bf16[16,32,256]{2,1,0:T(8,128)(2,1)S(1)} collective-permute-done((bf16[16,32,256]{2,1,0:T(8,128)(2,1)S(1)}, bf16[16,32,256]{2,1,0:T(8,128)(2,1)S(1)}, u32[]{:S(2)}, u32[]{:S(2)}) %collective-permute-start.6) | collective-permute-done | bytes 262176 | tf_op jit(solution)/shard_map/ppermute | solution.py:25
  27.4 1.3 %gather_fusion.3 = bf16[16,32,256]{2,1,0:T(8,128)(2,1)} fusion(bf16[16,32,256]{2,1,0:T(8,128)(2,1)S(1)} %fusion.8, s32[1024]{0:T(1024)S(1)} %pad_clamp_fusion), kind=kCustom, calls=%fused_computation.3 | custom fusion | bytes 524352 | tf_op jit(solution)/shard_map/gather | solution.py:114
  28.8 0.7 copy-done.10
  29.5 1.9 %select_maximum_fusion.2 = (bf16[16,32,6,132]{3,1,2,0:T(8,128)(2,1)S(1)}, f32[16,32,6,132]{3,1,2,0:T(8,128)S(1)}) fusion(bf16[16,32,2,128]{3,1,2,0:T(8,128)(2,1)} %copy-done.10, bf16[16,32,2,128]{3,1,2,0:T(8,128)(2,1)} %copy-done.6, bf16[16,32,2,128]{3,1,2,0:T(8,128)(2,1)} %collective-permute-done), kind=kLoop, calls=%fused_computation.37 | loop fusion | flops 5271552 | bytes 3219456 | tf_op jit(solution)/shard_map/concatenate | solution.py:18
  31.6 3.0 %fusion.64 = bf16[16,32,2,128]{3,1,2,0:T(8,128)(2,1)S(1)} fusion(f32[16,32,6,132]{3,1,2,0:T(8,128)S(1)} %get-tuple-element.71, f32[32]{0:T(128)S(1)} %copy-done.13, f32[32]{0:T(128)S(1)} %copy-done.14, f32[32]{0:T(128)S(1)} %copy-done.16, f32[32]{0:T(128)S(1)} %copy-done.17, f32[32]{0:T(128)S(1)} %copy-done.18, f32[32]{0:T(128)S(1)} %copy-done.19, ...), kind=kLoop, calls=%fused_computation.129 | loop fusion | flops 6553600 | bytes 13372544 | tf_op jit(solution)/shard_map/convert_element_type | solution.py:75
  34.7 1.1 %fusion.36 = (bf16[16,32,2,128]{3,1,2,0:T(8,128)(2,1)}, bf16[16,2,4,8,128]{4,3,2,1,0:T(8,128)(2,1)S(1)}) fusion(bf16[16,32,2,128]{3,1,2,0:T(8,128)(2,1)S(1)} %fusion.64, bf16[32,32]{1,0:T(8,128)(2,1)S(1)} %copy-done, bf16[16,32,256]{2,1,0:T(8,128)(2,1)S(1)} %copy-done.8), kind=kOutput, calls=%fused_computation.75 | convolution fusion | flops 9961472 | bytes 1050624 | tf_op jit(solution)/shard_map/gf,cfhw->cghw/dot_general | solution.py:76
  35.8 0.8 copy.242
  36.6 2.2 %gather_fusion = bf16[16,32,256]{2,1,0:T(8,128)(2,1)} fusion(bf16[16,32,256]{2,1,0:T(8,128)(2,1)} %bitcast.346, s32[1024]{0:T(1024)S(1)} %pad_clamp_fusion.1), kind=kCustom, calls=%fused_computation | custom fusion | bytes 524352 | tf_op jit(solution)/shard_map/gather | solution.py:84
  38.8 2.3 %fusion.9 = f32[7,32,32]{2,1,0:T(8,128)} fusion(bf16[16,7,32,256]{3,2,0,1:T(8,128)(2,1)S(1)} %fusion.123, bf16[16,32,256]{2,1,0:T(8,128)(2,1)} %gather_fusion), kind=kOutput, calls=%fused_computation.48 | convolution fusion | flops 58720256 | bytes 2125824 | tf_op jit(solution)/shard_map/mKp,mfp->Kf/dot_general | solution.py:110
  41.1 6.2 %collective-permute-start.4 = (bf16[16,32,256]{2,1,0:T(8,128)(2,1)}, bf16[16,32,256]{2,1,0:T(8,128)(2,1)S(1)}, u32[]{:S(2)}, u32[]{:S(2)}) collective-permute-start(bf16[16,32,256]{2,1,0:T(8,128)(2,1)} %gather_fusion), channel_id=1, source_target_pairs={{12,0},{0,4},{4,8},{8,12},{13,1},{1,5},{5,9},{9,13},{14,2},{2,6},{... | collective-permute-start | bytes 786440 | tf_op jit(solution)/shard_map/ppermute | solution.py:25
  47.3 1.5 %collective-permute-start.3 = (bf16[16,32,256]{2,1,0:T(8,128)(2,1)}, bf16[16,32,256]{2,1,0:T(8,128)(2,1)S(1)}, u32[]{:S(2)}, u32[]{:S(2)}) collective-permute-start(bf16[16,32,256]{2,1,0:T(8,128)(2,1)} %gather_fusion), channel_id=1, source_target_pairs={{8,0},{12,4},{0,8},{4,12},{9,1},{13,5},{1,9},{5,13},{10,2},{14,6},... | collective-permute-start | bytes 786440 | tf_op jit(solution)/shard_map/ppermute | solution.py:25
  48.8 0.9 collective-permute-start.2
  49.8 2.3 %fusion.34 = (f32[32]{0:T(128)}, f32[32]{0:T(128)}, f32[32]{0:T(128)}, f32[32]{0:T(128)}, f32[32]{0:T(128)}, /*index=5*/f32[32]{0:T(128)}, bf16[16,2,128,32]{2,3,1,0:T(8,128)(2,1)S(1)}) fusion(bf16[16,32,6,132]{3,1,2,0:T(8,128)(2,1)S(1)} %get-tuple-element.70, bf16[16,32,2,128]{3,1,2,0:T(8,128)(2,1)} %collective-permute-done, ...), kind=kOutput, calls=%fused_computation.72 | convolution fusion | flops 11272000 | bytes 1837824 | tf_op jit(solution)/shard_map/gf,cghw->cfhw/dot_general | solution.py:120
  52.1 2.3 %fusion.35 = (f32[32]{0:T(128)}, f32[32]{0:T(128)}, f32[32]{0:T(128)}, f32[32]{0:T(128)}, f32[32]{0:T(128)}, /*index=5*/f32[32]{0:T(128)}, f32[32]{0:T(128)}, f3...) fusion(bf16[16,32,6,132]{3,1,2,0:T(8,128)(2,1)S(1)} %get-tuple-, ...), kind=kLoop, calls=%fused_computation.73 | loop fusion | flops 7208384 | bytes 4983040 | tf_op jit(solution)/shard_map/cfhw,cfhw->f/dot_general | solution.py:135
  54.6 1.3 %collective-permute-start.9 = (bf16[16,32,2,128]{3,1,2,0:T(8,128)(2,1)S(1)}, bf16[16,32,2,128]{3,1,2,0:T(8,128)(2,1)S(1)}, u32[]{:S(2)}, u32[]{:S(2)}) collective-permute-start(bf16[16,32,2,128]{3,1,2,0:T(8,128)(2,1)S(1)} %bitcast.343), channel_id=1, source_target_pairs={{1,0},{2,1},{3,2},{5,4},{6,5},{7,6},{9,8},{10,9},{11,10},{13,12},{... | collective-permute-start | bytes 786440 | tf_op jit(solution)/shard_map/ppermute | solution.py:17
  55.9 3.2 %collective-permute-start.8 = (bf16[16,32,2,128]{3,1,2,0:T(8,128)(2,1)S(1)}, bf16[16,32,2,128]{3,1,2,0:T(8,128)(2,1)S(1)}, u32[]{:S(2)}, u32[]{:S(2)}) collective-permute-start(bf16[16,32,2,128]{3,1,2,0:T(8,128)(2,1)S(1)} %bitcast.344), channel_id=1, source_target_pairs={{0,1},{1,2},{2,3},{4,5},{5,6},{6,7},{8,9},{9,10},{10,11},{12,13},{... | collective-permute-start | bytes 786440 | tf_op jit(solution)/shard_map/ppermute | solution.py:14
  59.3 0.9 %rev.7 = f32[7,32,32]{2,1,0:T(8,128)S(1)} reverse(f32[7,32,32]{2,1,0:T(8,128)} %fusion.9), dimensions={0} | reverse | bytes 57344 | tf_op jit(solution)/shard_map/rev | solution.py:110
  60.3 0.8 multiply_reduce_fusion
  61.7 3.5 %collective-permute-done.3 = bf16[16,32,256]{2,1,0:T(8,128)(2,1)S(1)} collective-permute-done((bf16[16,32,256]{2,1,0:T(8,128)(2,1)}, bf16[16,32,256]{2,1,0:T(8,128)(2,1)S(1)}, u32[]{:S(2)}, u32[]{:S(2)}) %collective-permute-start.3) | collective-permute-done | bytes 262176 | tf_op jit(solution)/shard_map/ppermute | solution.py:25
  65.4 1.0 %bitcast_dynamic-update-slice_fusion = bf16[16,7,32,256]{3,2,1,0:T(8,128)(2,1)S(1)} fusion(bf16[16,7,32,256]{3,2,1,0:T(8,128)(2,1)S(1)} %fusion.96, bf16[16,32,256]{2,1,0:T(8,128)(2,1)} %gather_fusion), kind=kLoop, calls=%fused_computation.255 | loop fusion | bytes 524288
  66.5 0.7 fusion.3
  67.4 3.0 %fusion.39 = bf16[16,32,2,128]{3,1,2,0:T(8,128)(2,1)S(1)} fusion(f32[16,32,6,132]{3,1,2,0:T(8,128)S(1)} %fusion.3, bf16[16,32,2,128]{3,2,1,0:T(2,128)(2,1)S(1)} %copy-done.3, f32[32]{0:T(128)S(1)} %copy-done.13, f32[32]{0:T(128)S(1)} %copy-done.14, f32[32]{0:T(128)S(1)} %copy-done.16, f32[32]{0:T(128)S(1)} %copy-done.17, f32[32]{0:T(128)S(1)} %copy-done.18, ...), kind=kLoop, calls=%fused_computation.79 | loop fusion | flops 6815744 | bytes 13634688 | tf_op jit(solution)/shard_map/convert_element_type | solution.py:143
  70.6 1.6 %collective-permute-start.11 = (f32[8992]{0:T(1024)S(1)}, f32[8992]{0:T(1024)S(1)}, u32[]{:S(2)}, u32[]{:S(2)}) collective-permute-start(f32[8992]{0:T(1024)S(1)} %add.278), channel_id=1, source_target_pairs={{0,2},{2,0},{1,3},{3,1},{4,6},{6,4},{5,7},{7,5},{8,10},{10,8},{9,1... | collective-permute-start | bytes 107912 | tf_op jit(solution)/shard_map/ppermute | solution.py:38
  72.2 2.4 %collective-permute-done.11 = f32[8992]{0:T(1024)S(1)} collective-permute-done((f32[8992]{0:T(1024)S(1)}, f32[8992]{0:T(1024)S(1)}, u32[]{:S(2)}, u32[]{:S(2)}) %collective-permute-start.11) | collective-permute-done | bytes 36000 | tf_op jit(solution)/shard_map/ppermute | solution.py:38
  74.6 6.1 %collective-permute-start.12 = (f32[8992]{0:T(1024)S(1)}, f32[8992]{0:T(1024)S(1)}, u32[]{:S(2)}, u32[]{:S(2)}) collective-permute-start(f32[8992]{0:T(1024)S(1)} %add.279), channel_id=1, source_target_pairs={{0,4},{4,0},{8,12},{12,8},{1,5},{5,1},{9,13},{13,9},{2,6},{6,2},{1... | collective-permute-start | bytes 107912 | tf_op jit(solution)/shard_map/ppermute | solution.py:38
  80.7 0.6 fusion.7
  81.4 0.6 gather_fusion.1
  82.2 0.5 collective-permute-done.12
  82.7 2.4 %collective-permute-start.13 = (f32[8992]{0:T(1024)S(1)}, f32[8992]{0:T(1024)S(1)}, u32[]{:S(2)}, u32[]{:S(2)}) collective-permute-start(f32[8992]{0:T(1024)S(1)} %add.280), channel_id=1, source_target_pairs={{0,8},{4,12},{8,0},{12,4},{1,9},{5,13},{9,1},{13,5},{2,10},{6,14},... | collective-permute-start | bytes 107912 | tf_op jit(solution)/shard_map/ppermute | solution.py:38
  85.1 1.0 %add_convert_fusion = bf16[16,32,2,128]{3,2,1,0:T(2,128)(2,1)} fusion(f32[16,32,2,128]{3,2,1,0:T(2,128)S(1)} %reshape.87, bf16[16,32,2,128]{3,2,1,0:T(2,128)(2,1)S(1)} %copy-done.2), kind=kLoop, calls=%fused_computation.179 | loop fusion | flops 393216 | bytes 1048576 | tf_op jit(solution)/shard_map/convert_element_type | solution.py:117
  86.1 0.9 %copy.48 = bf16[16,32,2,128]{3,2,1,0:T(2,128)(2,1)} copy(bf16[16,32,2,128]{3,1,2,0:T(8,128)(2,1)S(1)} %fusion.39) | data formatting | bytes 524288
  87.0 0.5 collective-permute-done.13
  87.7 0.7 reshape.85
  88.4 0.7 split.13
  89.1 0.7 reshape.86
  (182 shorter events, 2.8 us)
Async XLA Ops:
  0.6 34.0 %copy-start = (bf16[32,32]{1,0:T(8,128)(2,1)S(1)}, bf16[32,32]{1,0:T(8,128)(2,1)}, u32[]{:S(2)}) copy-start(bf16[32,32]{1,0:T(8,128)(2,1)} %param.9) | copy-start | bytes 6148
  0.6 17.9 %copy-start.1 = (f32[32,25]{1,0:T(8,128)S(1)}, f32[32,25]{1,0:T(8,128)}, u32[]{:S(2)}) copy-start(f32[32,25]{1,0:T(8,128)} %param.8) | copy-start | bytes 9604
  0.7 19.0 %copy-start.12 = (bf16[7,32,32]{2,1,0:T(8,128)(2,1)S(1)}, bf16[7,32,32]{2,1,0:T(8,128)(2,1)}, u32[]{:S(2)}) copy-start(bf16[7,32,32]{2,1,0:T(8,128)(2,1)} %param.10) | copy-start | bytes 43012
  3.8 22.8 %collective-permute-start.7 = (bf16[16,32,256]{2,1,0:T(8,128)(2,1)S(1)}, bf16[16,32,256]{2,1,0:T(8,128)(2,1)S(1)}, u32[]{:S(2)}, u32[]{:S(2)}) collective-permute-start(bf16[16,32,256]{2,1,0:T(8,128)(2,1)S(1)} %gather_fusion.2), channel_id=1, source_target_pairs={{12,0},{0,4},{4,8},{8,12},{13,1},{1,5},{5,9},{9,13},{14,2},{2,6},{... | collective-permute-start | bytes 786440 | tf_op jit(solution)/shard_map/ppermute | solution.py:25
  6.9 19.7 %collective-permute-start.6 = (bf16[16,32,256]{2,1,0:T(8,128)(2,1)S(1)}, bf16[16,32,256]{2,1,0:T(8,128)(2,1)S(1)}, u32[]{:S(2)}, u32[]{:S(2)}) collective-permute-start(bf16[16,32,256]{2,1,0:T(8,128)(2,1)S(1)} %gather_fusion.2), channel_id=1, source_target_pairs={{8,0},{12,4},{0,8},{4,12},{9,1},{13,5},{1,9},{5,13},{10,2},{14,6},... | collective-permute-start | bytes 786440 | tf_op jit(solution)/shard_map/ppermute | solution.py:25
  9.5 14.3 %collective-permute-start.5 = (bf16[16,32,256]{2,1,0:T(8,128)(2,1)S(1)}, bf16[16,32,256]{2,1,0:T(8,128)(2,1)S(1)}, u32[]{:S(2)}, u32[]{:S(2)}) collective-permute-start(bf16[16,32,256]{2,1,0:T(8,128)(2,1)S(1)} %gather_fusion.2), channel_id=1, source_target_pairs={{4,0},{8,4},{12,8},{0,12},{5,1},{9,5},{13,9},{1,13},{6,2},{10,6},{... | collective-permute-start | bytes 786440 | tf_op jit(solution)/shard_map/ppermute | solution.py:25
  11.8 15.1 %copy-start.6 = (bf16[16,32,2,128]{3,1,2,0:T(8,128)(2,1)}, bf16[16,32,2,128]{3,1,2,0:T(8,128)(2,1)S(1)}, u32[]{:S(2)}) copy-start(bf16[16,32,2,128]{3,1,2,0:T(8,128)(2,1)S(1)} %copy.27) | copy-start | bytes 786436
  11.8 17.0 %collective-permute-start.1 = (bf16[16,32,2,128]{3,1,2,0:T(8,128)(2,1)S(1)}, bf16[16,32,2,128]{3,1,2,0:T(8,128)(2,1)S(1)}, u32[]{:S(2)}, u32[]{:S(2)}) collective-permute-start(bf16[16,32,2,128]{3,1,2,0:T(8,128)(2,1)S(1)} %copy.27), channel_id=1, source_target_pairs={{1,0},{2,1},{3,2},{5,4},{6,5},{7,6},{9,8},{10,9},{11,10},{13,12},{... | collective-permute-start | bytes 786440 | tf_op jit(solution)/shard_map/ppermute | solution.py:17
  13.1 16.4 %collective-permute-start = (bf16[16,32,2,128]{3,1,2,0:T(8,128)(2,1)S(1)}, bf16[16,32,2,128]{3,1,2,0:T(8,128)(2,1)}, u32[]{:S(2)}, u32[]{:S(2)}) collective-permute-start(bf16[16,32,2,128]{3,1,2,0:T(8,128)(2,1)S(1)} %copy.27), channel_id=1, source_target_pairs={{0,1},{1,2},{2,3},{4,5},{5,6},{6,7},{8,9},{9,10},{10,11},{12,13},{... | collective-permute-start | bytes 786440 | tf_op jit(solution)/shard_map/ppermute | solution.py:14
  31.6 3.1 %copy-start.8 = (bf16[16,32,256]{2,1,0:T(8,128)(2,1)S(1)}, bf16[16,32,256]{2,1,0:T(8,128)(2,1)}, u32[]{:S(2)}) copy-start(bf16[16,32,256]{2,1,0:T(8,128)(2,1)} %gather_fusion.3) | copy-start | bytes 786436
  38.8 10.8 %copy-start.5 = (bf16[16,32,2,128]{3,1,2,0:T(8,128)(2,1)S(1)}, bf16[16,32,2,128]{3,1,2,0:T(8,128)(2,1)}, u32[]{:S(2)}) copy-start(bf16[16,32,2,128]{3,1,2,0:T(8,128)(2,1)} %copy-done.4) | copy-start | bytes 786436
  38.8 10.8 %copy-start.9 = (bf16[16,32,2,128]{3,1,2,0:T(8,128)(2,1)S(1)}, bf16[16,32,2,128]{3,1,2,0:T(8,128)(2,1)}, u32[]{:S(2)}) copy-start(bf16[16,32,2,128]{3,1,2,0:T(8,128)(2,1)} %get-tuple-element.72) | copy-start | bytes 786436
  38.8 11.0 %copy-start.7 = (bf16[16,32,2,128]{3,1,2,0:T(8,128)(2,1)S(1)}, bf16[16,32,2,128]{3,1,2,0:T(8,128)(2,1)}, u32[]{:S(2)}) copy-start(bf16[16,32,2,128]{3,1,2,0:T(8,128)(2,1)} %copy-done.6) | copy-start | bytes 786436
  38.8 11.0 %copy-start.11 = (bf16[16,32,2,128]{3,1,2,0:T(8,128)(2,1)S(1)}, bf16[16,32,2,128]{3,1,2,0:T(8,128)(2,1)}, u32[]{:S(2)}) copy-start(bf16[16,32,2,128]{3,1,2,0:T(8,128)(2,1)} %copy-done.10) | copy-start | bytes 786436
  41.1 20.6 %collective-permute-start.4 = (bf16[16,32,256]{2,1,0:T(8,128)(2,1)}, bf16[16,32,256]{2,1,0:T(8,128)(2,1)S(1)}, u32[]{:S(2)}, u32[]{:S(2)}) collective-permute-start(bf16[16,32,256]{2,1,0:T(8,128)(2,1)} %gather_fusion), channel_id=1, source_target_pairs={{12,0},{0,4},{4,8},{8,12},{13,1},{1,5},{5,9},{9,13},{14,2},{2,6},{... | collective-permute-start | bytes 786440 | tf_op jit(solution)/shard_map/ppermute | solution.py:25
  47.3 18.0 %collective-permute-start.3 = (bf16[16,32,256]{2,1,0:T(8,128)(2,1)}, bf16[16,32,256]{2,1,0:T(8,128)(2,1)S(1)}, u32[]{:S(2)}, u32[]{:S(2)}) collective-permute-start(bf16[16,32,256]{2,1,0:T(8,128)(2,1)} %gather_fusion), channel_id=1, source_target_pairs={{8,0},{12,4},{0,8},{4,12},{9,1},{13,5},{1,9},{5,13},{10,2},{14,6},... | collective-permute-start | bytes 786440 | tf_op jit(solution)/shard_map/ppermute | solution.py:25
  48.8 16.4 %collective-permute-start.2 = (bf16[16,32,256]{2,1,0:T(8,128)(2,1)}, bf16[16,32,256]{2,1,0:T(8,128)(2,1)S(1)}, u32[]{:S(2)}, u32[]{:S(2)}) collective-permute-start(bf16[16,32,256]{2,1,0:T(8,128)(2,1)} %gather_fusion), channel_id=1, source_target_pairs={{4,0},{8,4},{12,8},{0,12},{5,1},{9,5},{13,9},{1,13},{6,2},{10,6},{... | collective-permute-start | bytes 786440 | tf_op jit(solution)/shard_map/ppermute | solution.py:25
  52.1 8.2 %copy-start.2 = (bf16[16,32,2,128]{3,2,1,0:T(2,128)(2,1)S(1)}, bf16[16,32,2,128]{3,2,1,0:T(2,128)(2,1)}, u32[]{:S(2)}) copy-start(bf16[16,32,2,128]{3,2,1,0:T(2,128)(2,1)} %param.6) | copy-start | bytes 786436
  54.4 6.7 %copy-start.45 = (f32[32]{0:T(128)S(1)}, f32[32]{0:T(128)}, u32[]{:S(2)}) copy-start(f32[32]{0:T(128)} %get-tuple-element.17) | copy-start | bytes 388
  54.4 6.7 %copy-start.46 = (f32[32]{0:T(128)S(1)}, f32[32]{0:T(128)}, u32[]{:S(2)}) copy-start(f32[32]{0:T(128)} %get-tuple-element.18) | copy-start | bytes 388
  54.4 6.7 %copy-start.47 = (f32[32]{0:T(128)S(1)}, f32[32]{0:T(128)}, u32[]{:S(2)}) copy-start(f32[32]{0:T(128)} %get-tuple-element.19) | copy-start | bytes 388
  54.4 6.7 %copy-start.48 = (f32[32]{0:T(128)S(1)}, f32[32]{0:T(128)}, u32[]{:S(2)}) copy-start(f32[32]{0:T(128)} %get-tuple-element.20) | copy-start | bytes 388
  54.4 6.7 %copy-start.49 = (f32[32]{0:T(128)S(1)}, f32[32]{0:T(128)}, u32[]{:S(2)}) copy-start(f32[32]{0:T(128)} %get-tuple-element.21) | copy-start | bytes 388
  54.4 6.7 %copy-start.50 = (f32[32]{0:T(128)S(1)}, f32[32]{0:T(128)}, u32[]{:S(2)}) copy-start(f32[32]{0:T(128)} %get-tuple-element.22) | copy-start | bytes 388
  54.4 6.7 %copy-start.51 = (f32[32]{0:T(128)S(1)}, f32[32]{0:T(128)}, u32[]{:S(2)}) copy-start(f32[32]{0:T(128)} %get-tuple-element.23) | copy-start | bytes 388
  54.4 6.7 %copy-start.52 = (f32[32]{0:T(128)S(1)}, f32[32]{0:T(128)}, u32[]{:S(2)}) copy-start(f32[32]{0:T(128)} %get-tuple-element.24) | copy-start | bytes 388
  54.5 6.7 %copy-start.53 = (f32[32]{0:T(128)S(1)}, f32[32]{0:T(128)}, u32[]{:S(2)}) copy-start(f32[32]{0:T(128)} %get-tuple-element.25) | copy-start | bytes 388
  54.5 6.7 %copy-start.54 = (f32[32]{0:T(128)S(1)}, f32[32]{0:T(128)}, u32[]{:S(2)}) copy-start(f32[32]{0:T(128)} %get-tuple-element.26) | copy-start | bytes 388
  54.5 6.7 %copy-start.55 = (f32[32]{0:T(128)S(1)}, f32[32]{0:T(128)}, u32[]{:S(2)}) copy-start(f32[32]{0:T(128)} %get-tuple-element.27) | copy-start | bytes 388
  54.5 6.7 %copy-start.56 = (f32[32]{0:T(128)S(1)}, f32[32]{0:T(128)}, u32[]{:S(2)}) copy-start(f32[32]{0:T(128)} %get-tuple-element.28) | copy-start | bytes 388
  54.5 6.7 %copy-start.57 = (f32[32]{0:T(128)S(1)}, f32[32]{0:T(128)}, u32[]{:S(2)}) copy-start(f32[32]{0:T(128)} %get-tuple-element.29) | copy-start | bytes 388
  54.5 6.7 %copy-start.58 = (f32[32]{0:T(128)S(1)}, f32[32]{0:T(128)}, u32[]{:S(2)}) copy-start(f32[32]{0:T(128)} %get-tuple-element.30) | copy-start | bytes 388
  54.5 6.7 %copy-start.59 = (f32[32]{0:T(128)S(1)}, f32[32]{0:T(128)}, u32[]{:S(2)}) copy-start(f32[32]{0:T(128)} %get-tuple-element.31) | copy-start | bytes 388
  54.5 6.7 %copy-start.60 = (f32[32]{0:T(128)S(1)}, f32[32]{0:T(128)}, u32[]{:S(2)}) copy-start(f32[32]{0:T(128)} %get-tuple-element.32) | copy-start | bytes 388
  54.5 6.7 %copy-start.61 = (f32[32]{0:T(128)S(1)}, f32[32]{0:T(128)}, u32[]{:S(2)}) copy-start(f32[32]{0:T(128)} %get-tuple-element.33) | copy-start | bytes 388
  54.5 6.7 %copy-start.62 = (f32[32]{0:T(128)S(1)}, f32[32]{0:T(128)}, u32[]{:S(2)}) copy-start(f32[32]{0:T(128)} %get-tuple-element.34) | copy-start | bytes 388
  54.6 6.7 %copy-start.63 = (f32[32]{0:T(128)S(1)}, f32[32]{0:T(128)}, u32[]{:S(2)}) copy-start(f32[32]{0:T(128)} %get-tuple-element.35) | copy-start | bytes 388
  54.6 6.7 %copy-start.64 = (f32[32]{0:T(128)S(1)}, f32[32]{0:T(128)}, u32[]{:S(2)}) copy-start(f32[32]{0:T(128)} %get-tuple-element.36) | copy-start | bytes 388
  54.6 6.7 %copy-start.65 = (f32[32]{0:T(128)S(1)}, f32[32]{0:T(128)}, u32[]{:S(2)}) copy-start(f32[32]{0:T(128)} %get-tuple-element.41) | copy-start | bytes 388
  54.6 6.7 %copy-start.66 = (f32[32]{0:T(128)S(1)}, f32[32]{0:T(128)}, u32[]{:S(2)}) copy-start(f32[32]{0:T(128)} %get-tuple-element.42) | copy-start | bytes 388
  54.6 6.7 %copy-start.67 = (f32[32]{0:T(128)S(1)}, f32[32]{0:T(128)}, u32[]{:S(2)}) copy-start(f32[32]{0:T(128)} %get-tuple-element.43) | copy-start | bytes 388
  54.6 6.7 %copy-start.68 = (f32[32]{0:T(128)S(1)}, f32[32]{0:T(128)}, u32[]{:S(2)}) copy-start(f32[32]{0:T(128)} %get-tuple-element.44) | copy-start | bytes 388
  54.6 11.9 %collective-permute-start.9 = (bf16[16,32,2,128]{3,1,2,0:T(8,128)(2,1)S(1)}, bf16[16,32,2,128]{3,1,2,0:T(8,128)(2,1)S(1)}, u32[]{:S(2)}, u32[]{:S(2)}) collective-permute-start(bf16[16,32,2,128]{3,1,2,0:T(8,128)(2,1)S(1)} %bitcast.343), channel_id=1, source_target_pairs={{1,0},{2,1},{3,2},{5,4},{6,5},{7,6},{9,8},{10,9},{11,10},{13,12},{... | collective-permute-start | bytes 786440 | tf_op jit(solution)/shard_map/ppermute | solution.py:17
  55.9 10.6 %collective-permute-start.8 = (bf16[16,32,2,128]{3,1,2,0:T(8,128)(2,1)S(1)}, bf16[16,32,2,128]{3,1,2,0:T(8,128)(2,1)S(1)}, u32[]{:S(2)}, u32[]{:S(2)}) collective-permute-start(bf16[16,32,2,128]{3,1,2,0:T(8,128)(2,1)S(1)} %bitcast.344), channel_id=1, source_target_pairs={{0,1},{1,2},{2,3},{4,5},{5,6},{6,7},{8,9},{9,10},{10,11},{12,13},{... | collective-permute-start | bytes 786440 | tf_op jit(solution)/shard_map/ppermute | solution.py:14
  65.2 5.4 %collective-permute-start.10 = (f32[8992]{0:T(1024)S(1)}, f32[8992]{0:T(1024)S(1)}, u32[]{:S(2)}, u32[]{:S(2)}) collective-permute-start(f32[8992]{0:T(1024)S(1)} %broadcast_multiply_fusion), channel_id=1, source_target_pairs={{0,1},{1,0},{2,3},{3,2},{4,5},{5,4},{6,7},{7,6},{8,9},{9,8},{10,11... | collective-permute-start | bytes 107912 | tf_op jit(solution)/shard_map/ppermute | solution.py:38
  70.6 4.0 %collective-permute-start.11 = (f32[8992]{0:T(1024)S(1)}, f32[8992]{0:T(1024)S(1)}, u32[]{:S(2)}, u32[]{:S(2)}) collective-permute-start(f32[8992]{0:T(1024)S(1)} %add.278), channel_id=1, source_target_pairs={{0,2},{2,0},{1,3},{3,1},{4,6},{6,4},{5,7},{7,5},{8,10},{10,8},{9,1... | collective-permute-start | bytes 107912 | tf_op jit(solution)/shard_map/ppermute | solution.py:38
  74.6 8.0 %collective-permute-start.12 = (f32[8992]{0:T(1024)S(1)}, f32[8992]{0:T(1024)S(1)}, u32[]{:S(2)}, u32[]{:S(2)}) collective-permute-start(f32[8992]{0:T(1024)S(1)} %add.279), channel_id=1, source_target_pairs={{0,4},{4,0},{8,12},{12,8},{1,5},{5,1},{9,13},{13,9},{2,6},{6,2},{1... | collective-permute-start | bytes 107912 | tf_op jit(solution)/shard_map/ppermute | solution.py:38
  82.7 4.9 %collective-permute-start.13 = (f32[8992]{0:T(1024)S(1)}, f32[8992]{0:T(1024)S(1)}, u32[]{:S(2)}, u32[]{:S(2)}) collective-permute-start(f32[8992]{0:T(1024)S(1)} %add.280), channel_id=1, source_target_pairs={{0,8},{4,12},{8,0},{12,4},{1,9},{5,13},{9,1},{13,5},{2,10},{6,14},... | collective-permute-start | bytes 107912 | tf_op jit(solution)/shard_map/ppermute | solution.py:38
  (35 other events, 72.5 us)

commit v7 on v6

--- a/solution.py
+++ b/solution.py
@@ -25,9 +25,8 @@
     return lax.ppermute(block, axis, route)
 
 
-def all_summed(value, axes, tied=None):
-    if tied is not None:
-        value, _ = lax.optimization_barrier((value, tied))
+def all_summed(value, axes, tied=None, tie_at=0):
+    done = 0
     for axis in axes:
         count = lax.axis_size(axis)
         if count & (count - 1):
@@ -35,8 +34,11 @@
             continue
         step = 1
         while step < count:
+            if tied is not None and done == tie_at:
+                value, _ = lax.optimization_barrier((value, tied))
             value = value + lax.ppermute(value, axis, [(i, i ^ step) for i in range(count)])
             step *= 2
+            done += 1
     return value
 
 
@@ -143,7 +145,7 @@
     dirty_grad = (cotangent.astype(jnp.float32) + conv).astype(jnp.bfloat16)
     parts = (kernel_term, mix_term, spec_grad)
     flat = jnp.concatenate([part.reshape(-1) for part in parts]) * scale
-    flat = all_summed(flat, ("sub", "tile", "chan"), tied=h_received)
+    flat = all_summed(flat, ("sub", "tile", "chan"), tied=h_received, tie_at=3)
     sizes = [part.size for part in parts]
     kgrad, mgrad, sgrad = (
         piece.reshape(part.shape)

time: 90.4 us -> 83.5 us (0.924)
  waiting for transfers between devices: 13.7 us -> 20.3 us
  starting transfers between devices: 35.2 us -> 29.1 us
  local copies, waits for them, and re-layouts: 17.9 us -> 12.3 us
  matrix products: 6.95 us -> 5.29 us
    ppermute x4, waiting for transfers between devices: 3.37 us -> 13.5 us  [all_summed(): lax.ppermute(value, axis, [(i, i ^ step) for i in range(count)])]
    ppermute x4, starting transfers between devices: 10.1 us -> 5.03 us  [all_summed(): lax.ppermute(value, axis, [(i, i ^ step) for i in range(count)])]
    ppermute x6, waiting for transfers between devices: 10.3 us -> 6.81 us  [passed_along(): return lax.ppermute(block, axis, route)]
    dot_general x1, matrix products: 2.29 us -> 0.6 us  [local(): jnp.einsum('mKp,mfp->Kf', g_stack, h_sorted, preferred_element_type=jnp.f...]
    unnamed x142 -> x130, local copies, waits for them, and re-layouts: 4.03 us -> 2.36 us
    gather x1, local copies, waits for them, and re-layouts: 2.2 us -> 0.56 us  [local(): h_sorted = hidden_flat[order]]
    ppermute x2, starting transfers between devices: 6.97 us -> 5.84 us  [padded(): lax.ppermute(lax.slice_in_dim(block, block.shape[dim] - width, None, axis...]
  transfers between devices with their start and end apart: 14 -> 14, of which waited for: 6 -> 4; matrix products, arithmetic and copies ran while one was open for 24% -> 15% of each run, Pallas kernels for 0% -> 0%
where the time goes in v7:
time: 83.5 us; the launch traced here: 83 us
  starting transfers between devices  29.1 us (35%)
  waiting for transfers between devices  20.3 us (24%)
  other arithmetic  14.1 us (17%)
  local copies, waits for them, and re-layouts  12.3 us (15%)
  matrix products  5.29 us (6%)
  between operations  1.94 us (2%)
    ppermute x6, starting transfers between devices, passed_along(): return lax.ppermute(block, axis, route)  15.7 us
    ppermute x4, waiting for transfers between devices, all_summed(): lax.ppermute(value, axis, [(i, i ^ step) for i in range(count)])  13.5 us
    ppermute x6, waiting for transfers between devices, passed_along(): return lax.ppermute(block, axis, route)  6.81 us
    ppermute x2, starting transfers between devices, padded(): lax.ppermute(lax.slice_in_dim(block, block.shape[dim] - width, None, axis...  5.84 us
    ppermute x4, starting transfers between devices, all_summed(): lax.ppermute(value, axis, [(i, i ^ step) for i in range(count)])  5.03 us
    dot_general x2, other arithmetic, local(): jnp.einsum('cfhw,cfhw->f', dsmooth, xpad[:, :, i:i + rows, j:j + cols], p...  3.05 us
    convert_element_type x1, other arithmetic, local(): dirty_grad = (cotangent.astype(jnp.float32) + conv).astype(jnp.bfloat16)  3.04 us
    convert_element_type x1, other arithmetic, local(): smooth = total.astype(jnp.bfloat16)  3.03 us
  transfers between devices with their start and end apart: 14, of which 4 were waited for; matrix products, arithmetic and copies ran while one was open for 15% of the time, Pallas kernels for 0%

profile of v7, /device:TPU:0, one launch (start us, length us, event | category | flops | bytes accessed | tf_op | source)
XLA Modules:
  0.0 83.0 jit_solution(16189077797438908705)
XLA Ops:
  0.7 0.8 compare_select_fusion.1
  1.4 0.6 scatter_custom_fusion
  2.1 1.1 %reshape.80 = bf16[16,32,256]{2,1,0:T(8,128)(2,1)S(1)} reshape(bf16[16,32,2,128]{3,2,1,0:T(2,128)(2,1)} %param.7) | data formatting | bytes 524288 | tf_op jit(solution)/shard_map/reshape | solution.py:81
  3.2 0.6 gather_fusion.2
  3.8 3.1 %collective-permute-start.7 = (bf16[16,32,256]{2,1,0:T(8,128)(2,1)S(1)}, bf16[16,32,256]{2,1,0:T(8,128)(2,1)S(1)}, u32[]{:S(2)}, u32[]{:S(2)}) collective-permute-start(bf16[16,32,256]{2,1,0:T(8,128)(2,1)S(1)} %gather_fusion.2), channel_id=1, source_target_pairs={{12,0},{0,4},{4,8},{8,12},{13,1},{1,5},{5,9},{9,13},{14,2},{2,6},{... | collective-permute-start | bytes 786440 | tf_op jit(solution)/shard_map/ppermute | solution.py:25
  6.9 2.6 %collective-permute-start.6 = (bf16[16,32,256]{2,1,0:T(8,128)(2,1)S(1)}, bf16[16,32,256]{2,1,0:T(8,128)(2,1)S(1)}, u32[]{:S(2)}, u32[]{:S(2)}) collective-permute-start(bf16[16,32,256]{2,1,0:T(8,128)(2,1)S(1)} %gather_fusion.2), channel_id=1, source_target_pairs={{8,0},{12,4},{0,8},{4,12},{9,1},{13,5},{1,9},{5,13},{10,2},{14,6},... | collective-permute-start | bytes 786440 | tf_op jit(solution)/shard_map/ppermute | solution.py:25
  9.5 1.3 %collective-permute-start.5 = (bf16[16,32,256]{2,1,0:T(8,128)(2,1)S(1)}, bf16[16,32,256]{2,1,0:T(8,128)(2,1)S(1)}, u32[]{:S(2)}, u32[]{:S(2)}) collective-permute-start(bf16[16,32,256]{2,1,0:T(8,128)(2,1)S(1)} %gather_fusion.2), channel_id=1, source_target_pairs={{4,0},{8,4},{12,8},{0,12},{5,1},{9,5},{13,9},{1,13},{6,2},{10,6},{... | collective-permute-start | bytes 786440 | tf_op jit(solution)/shard_map/ppermute | solution.py:25
  10.8 1.0 %copy.27 = bf16[16,32,2,128]{3,1,2,0:T(8,128)(2,1)S(1)} copy(bf16[16,32,2,128]{3,2,1,0:T(2,128)(2,1)} %param.6) | data formatting | bytes 524288 | tf_op args[0]
  11.8 1.3 %collective-permute-start.1 = (bf16[16,32,2,128]{3,1,2,0:T(8,128)(2,1)S(1)}, bf16[16,32,2,128]{3,1,2,0:T(8,128)(2,1)S(1)}, u32[]{:S(2)}, u32[]{:S(2)}) collective-permute-start(bf16[16,32,2,128]{3,1,2,0:T(8,128)(2,1)S(1)} %copy.27), channel_id=1, source_target_pairs={{1,0},{2,1},{3,2},{5,4},{6,5},{7,6},{9,8},{10,9},{11,10},{13,12},{... | collective-permute-start | bytes 786440 | tf_op jit(solution)/shard_map/ppermute | solution.py:17
  13.1 3.7 %collective-permute-start = (bf16[16,32,2,128]{3,1,2,0:T(8,128)(2,1)S(1)}, bf16[16,32,2,128]{3,1,2,0:T(8,128)(2,1)}, u32[]{:S(2)}, u32[]{:S(2)}) collective-permute-start(bf16[16,32,2,128]{3,1,2,0:T(8,128)(2,1)S(1)} %copy.27), channel_id=1, source_target_pairs={{0,1},{1,2},{2,3},{4,5},{5,6},{6,7},{8,9},{9,10},{10,11},{12,13},{... | collective-permute-start | bytes 786440 | tf_op jit(solution)/shard_map/ppermute | solution.py:14
  16.8 1.7 %slice_reduce_fusion.23 = (f32[32]{0:T(128)S(1)}, f32[32]{0:T(128)S(1)}, f32[32]{0:T(128)S(1)}, f32[32]{0:T(128)S(1)}, f32[32]{0:T(128)}, /*index=5*/f32[32]{0:T(128)}) fusion(f32[32,25]{1,0:T(8,128)} %param.8), kind=kLoop, calls=%fused_computation.286 | loop fusion | bytes 1536 | tf_op jit(solution)/shard_map/slice | solution.py:74
  18.6 1.1 %slice_reduce_fusion.24 = (f32[32]{0:T(128)}, f32[32]{0:T(128)}, f32[32]{0:T(128)}, f32[32]{0:T(128)}, f32[32]{0:T(128)}, /*index=5*/f32[32]{0:T(128)}, f32[32]{...) fusion(f32[32,25]{1,0:T(8,128)S(1)} %copy-done.1), kind=kLoop, calls=%fused_computation.287 | loop fusion | bytes 4864 | tf_op jit(solution)/shard_map/slice | solution.py:74
  19.7 4.0 %collective-permute-done.5 = bf16[16,32,256]{2,1,0:T(8,128)(2,1)S(1)} collective-permute-done((bf16[16,32,256]{2,1,0:T(8,128)(2,1)S(1)}, bf16[16,32,256]{2,1,0:T(8,128)(2,1)S(1)}, u32[]{:S(2)}, u32[]{:S(2)}) %collective-permute-start.5) | collective-permute-done | bytes 262176 | tf_op jit(solution)/shard_map/ppermute | solution.py:25
  23.8 2.8 %collective-permute-done.6 = bf16[16,32,256]{2,1,0:T(8,128)(2,1)S(1)} collective-permute-done((bf16[16,32,256]{2,1,0:T(8,128)(2,1)S(1)}, bf16[16,32,256]{2,1,0:T(8,128)(2,1)S(1)}, u32[]{:S(2)}, u32[]{:S(2)}) %collective-permute-start.6) | collective-permute-done | bytes 262176 | tf_op jit(solution)/shard_map/ppermute | solution.py:25
  26.9 0.5 fusion.8
  27.4 0.6 gather_fusion.3
  28.2 1.7 %select_maximum_fusion.2 = (bf16[16,32,6,132]{3,1,2,0:T(8,128)(2,1)S(1)}, f32[16,32,6,132]{3,1,2,0:T(8,128)S(1)}) fusion(bf16[16,32,2,128]{3,1,2,0:T(8,128)(2,1)S(1)} %collective-permute-done.1, bf16[16,32,2,128]{3,1,2,0:T(8,128)(2,1)S(1)} %copy.27, bf16[16,32,2,128]{3,1,2,0:T(8,128)(2,1)} %collective-permute-done), kind=kLoop, calls=%fused_computation.37 | loop fusion | flops 5271552 | bytes 3219456 | tf_op jit(solution)/shard_map/concatenate | solution.py:18
  30.1 3.0 %fusion.64 = bf16[16,32,2,128]{3,1,2,0:T(8,128)(2,1)S(1)} fusion(f32[16,32,6,132]{3,1,2,0:T(8,128)S(1)} %get-tuple-element.71, f32[32]{0:T(128)S(1)} %copy-done.6, f32[32]{0:T(128)S(1)} %copy-done.7, f32[32]{0:T(128)S(1)} %copy-done.9, f32[32]{0:T(128)S(1)} %copy-done.10, f32[32]{0:T(128)S(1)} %copy-done.11, f32[32]{0:T(128)S(1)} %copy-done.12, ...), kind=kLoop, calls=%fused_computation.129 | loop fusion | flops 6553600 | bytes 13372544 | tf_op jit(solution)/shard_map/convert_element_type | solution.py:77
  33.2 1.1 %fusion.36 = (bf16[16,32,2,128]{3,1,2,0:T(8,128)(2,1)S(1)}, bf16[16,2,4,8,128]{4,3,2,1,0:T(8,128)(2,1)}) fusion(bf16[16,32,2,128]{3,1,2,0:T(8,128)(2,1)S(1)} %fusion.64, bf16[32,32]{1,0:T(8,128)(2,1)S(1)} %copy-done, bf16[16,32,256]{2,1,0:T(8,128)(2,1)S(1)} %gather_fusion.3), kind=kOutput, calls=%fused_computation.75 | convolution fusion | flops 9961472 | bytes 1050624 | tf_op jit(solution)/shard_map/gf,cfhw->cghw/dot_general | solution.py:78
  34.3 0.2 convolution_bitcast_fusion.3
  34.5 2.3 %fusion.34 = (f32[32]{0:T(128)}, f32[32]{0:T(128)}, f32[32]{0:T(128)}, f32[32]{0:T(128)}, f32[32]{0:T(128)}, /*index=5*/f32[32]{0:T(128)}, bf16[16,2,128,32]{2,3,1,0:T(8,128)(2,1)S(1)}) fusion(bf16[16,32,6,132]{3,1,2,0:T(8,128)(2,1)S(1)} %get-tuple-element.70, bf16[16,32,2,128]{3,1,2,0:T(8,128)(2,1)} %collective-permute-done, ...), kind=kOutput, calls=%fused_computation.72 | convolution fusion | flops 11272000 | bytes 1837824 | tf_op jit(solution)/shard_map/gf,cghw->cfhw/dot_general | solution.py:122
  36.8 2.3 %fusion.35 = (f32[32]{0:T(128)}, f32[32]{0:T(128)}, f32[32]{0:T(128)}, f32[32]{0:T(128)}, f32[32]{0:T(128)}, /*index=5*/f32[32]{0:T(128)}, f32[32]{0:T(128)}, f3...) fusion(bf16[16,32,6,132]{3,1,2,0:T(8,128)(2,1)S(1)} %get-tuple-, ...), kind=kLoop, calls=%fused_computation.73 | loop fusion | flops 7208384 | bytes 4983040 | tf_op jit(solution)/shard_map/cfhw,cfhw->f/dot_general | solution.py:137
  39.3 0.6 gather_fusion
  40.1 0.6 fusion.9
  40.8 0.8 multiply_reduce_fusion
  41.8 0.1 stack.167
  42.0 0.1 reshape.81
  42.3 6.2 %collective-permute-start.4 = (bf16[16,32,256]{2,1,0:T(8,128)(2,1)S(1)}, bf16[16,32,256]{2,1,0:T(8,128)(2,1)S(1)}, u32[]{:S(2)}, u32[]{:S(2)}) collective-permute-start(bf16[16,32,256]{2,1,0:T(8,128)(2,1)S(1)} %gather_fusion), channel_id=1, source_target_pairs={{12,0},{0,4},{4,8},{8,12},{13,1},{1,5},{5,9},{9,13},{14,2},{2,6},{... | collective-permute-start | bytes 786440 | tf_op jit(solution)/shard_map/ppermute | solution.py:25
  48.5 1.5 %collective-permute-start.3 = (bf16[16,32,256]{2,1,0:T(8,128)(2,1)S(1)}, bf16[16,32,256]{2,1,0:T(8,128)(2,1)S(1)}, u32[]{:S(2)}, u32[]{:S(2)}) collective-permute-start(bf16[16,32,256]{2,1,0:T(8,128)(2,1)S(1)} %gather_fusion), channel_id=1, source_target_pairs={{8,0},{12,4},{0,8},{4,12},{9,1},{13,5},{1,9},{5,13},{10,2},{14,6},... | collective-permute-start | bytes 786440 | tf_op jit(solution)/shard_map/ppermute | solution.py:25
  50.0 0.9 %collective-permute-start.2 = (bf16[16,32,256]{2,1,0:T(8,128)(2,1)S(1)}, bf16[16,32,256]{2,1,0:T(8,128)(2,1)S(1)}, u32[]{:S(2)}, u32[]{:S(2)}) collective-permute-start(bf16[16,32,256]{2,1,0:T(8,128)(2,1)S(1)} %gather_fusion), channel_id=1, source_target_pairs={{4,0},{8,4},{12,8},{0,12},{5,1},{9,5},{13,9},{1,13},{6,2},{10,6},{... | collective-permute-start | bytes 786440 | tf_op jit(solution)/shard_map/ppermute | solution.py:25
  51.0 1.6 %collective-permute-start.11 = (f32[8992]{0:T(1024)S(1)}, f32[8992]{0:T(1024)S(1)}, u32[]{:S(2)}, u32[]{:S(2)}) collective-permute-start(f32[8992]{0:T(1024)S(1)} %fusion.134), channel_id=1, source_target_pairs={{0,2},{2,0},{1,3},{3,1},{4,6},{6,4},{5,7},{7,5},{8,10},{10,8},{9,1... | collective-permute-start | bytes 107912 | tf_op jit(solution)/shard_map/ppermute | solution.py:39
  52.5 2.5 %collective-permute-done.11 = f32[8992]{0:T(1024)S(1)} collective-permute-done((f32[8992]{0:T(1024)S(1)}, f32[8992]{0:T(1024)S(1)}, u32[]{:S(2)}, u32[]{:S(2)}) %collective-permute-start.11) | collective-permute-done | bytes 36000 | tf_op jit(solution)/shard_map/ppermute | solution.py:39
  55.0 1.1 %collective-permute-start.12 = (f32[8992]{0:T(1024)S(1)}, f32[8992]{0:T(1024)S(1)}, u32[]{:S(2)}, u32[]{:S(2)}) collective-permute-start(f32[8992]{0:T(1024)S(1)} %add.279), channel_id=1, source_target_pairs={{0,4},{4,0},{8,12},{12,8},{1,5},{5,1},{9,13},{13,9},{2,6},{6,2},{1... | collective-permute-start | bytes 107912 | tf_op jit(solution)/shard_map/ppermute | solution.py:39
  56.1 1.3 %collective-permute-start.9 = (bf16[16,32,2,128]{3,1,2,0:T(8,128)(2,1)S(1)}, bf16[16,32,2,128]{3,1,2,0:T(8,128)(2,1)S(1)}, u32[]{:S(2)}, u32[]{:S(2)}) collective-permute-start(bf16[16,32,2,128]{3,1,2,0:T(8,128)(2,1)S(1)} %bitcast.343), channel_id=1, source_target_pairs={{1,0},{2,1},{3,2},{5,4},{6,5},{7,6},{9,8},{10,9},{11,10},{13,12},{... | collective-permute-start | bytes 786440 | tf_op jit(solution)/shard_map/ppermute | solution.py:17
  57.4 11.0 %collective-permute-done.12 = f32[8992]{0:T(1024)S(1)} collective-permute-done((f32[8992]{0:T(1024)S(1)}, f32[8992]{0:T(1024)S(1)}, u32[]{:S(2)}, u32[]{:S(2)}) %collective-permute-start.12) | collective-permute-done | bytes 36000 | tf_op jit(solution)/shard_map/ppermute | solution.py:39
  68.4 2.1 %collective-permute-start.8 = (bf16[16,32,2,128]{3,1,2,0:T(8,128)(2,1)S(1)}, bf16[16,32,2,128]{3,1,2,0:T(8,128)(2,1)S(1)}, u32[]{:S(2)}, u32[]{:S(2)}) collective-permute-start(bf16[16,32,2,128]{3,1,2,0:T(8,128)(2,1)S(1)} %bitcast.344), channel_id=1, source_target_pairs={{0,1},{1,2},{2,3},{4,5},{5,6},{6,7},{8,9},{9,10},{10,11},{12,13},{... | collective-permute-start | bytes 786440 | tf_op jit(solution)/shard_map/ppermute | solution.py:14
  70.5 2.3 %collective-permute-start.13 = (f32[8992]{0:T(1024)S(1)}, f32[8992]{0:T(1024)S(1)}, u32[]{:S(2)}, u32[]{:S(2)}) collective-permute-start(f32[8992]{0:T(1024)S(1)} %add.280), channel_id=1, source_target_pairs={{0,8},{4,12},{8,0},{12,4},{1,9},{5,13},{9,1},{13,5},{2,10},{6,14},... | collective-permute-start | bytes 107912 | tf_op jit(solution)/shard_map/ppermute | solution.py:39
  73.3 0.6 fusion.7
  73.9 0.6 gather_fusion.1
  74.5 0.3 reshape.87
  74.9 0.7 fusion.3
  75.6 0.1 copy-done.3
  75.8 3.0 %fusion.39 = bf16[16,32,2,128]{3,1,2,0:T(8,128)(2,1)S(1)} fusion(f32[16,32,6,132]{3,1,2,0:T(8,128)S(1)} %fusion.3, bf16[16,32,2,128]{3,2,1,0:T(2,128)(2,1)S(1)} %copy-done.3, f32[32]{0:T(128)S(1)} %copy-done.6, f32[32]{0:T(128)S(1)} %copy-done.7, f32[32]{0:T(128)S(1)} %copy-done.9, f32[32]{0:T(128)S(1)} %copy-done.10, f32[32]{0:T(128)S(1)} %copy-done.11, ...), kind=kLoop, calls=%fused_computation.79 | loop fusion | flops 6815744 | bytes 13634688 | tf_op jit(solution)/shard_map/convert_element_type | solution.py:145
  78.8 1.0 %add_convert_fusion = bf16[16,32,2,128]{3,2,1,0:T(2,128)(2,1)} fusion(f32[16,32,2,128]{3,2,1,0:T(2,128)S(1)} %reshape.87, bf16[16,32,2,128]{3,2,1,0:T(2,128)(2,1)S(1)} %copy-done.2), kind=kLoop, calls=%fused_computation.179 | loop fusion | flops 393216 | bytes 1048576 | tf_op jit(solution)/shard_map/convert_element_type | solution.py:119
  79.8 0.9 %copy.48 = bf16[16,32,2,128]{3,2,1,0:T(2,128)(2,1)} copy(bf16[16,32,2,128]{3,1,2,0:T(8,128)(2,1)S(1)} %fusion.39) | data formatting | bytes 524288
  80.9 0.7 reshape.85
  81.6 0.7 split.13
  82.3 0.7 reshape.86
  (170 shorter events, 1.7 us)
Async XLA Ops:
  0.6 32.5 %copy-start = (bf16[32,32]{1,0:T(8,128)(2,1)S(1)}, bf16[32,32]{1,0:T(8,128)(2,1)}, u32[]{:S(2)}) copy-start(bf16[32,32]{1,0:T(8,128)(2,1)} %param.9) | copy-start | bytes 6148
  0.6 17.9 %copy-start.1 = (f32[32,25]{1,0:T(8,128)S(1)}, f32[32,25]{1,0:T(8,128)}, u32[]{:S(2)}) copy-start(f32[32,25]{1,0:T(8,128)} %param.8) | copy-start | bytes 9604
  0.7 19.0 %copy-start.5 = (bf16[7,32,32]{2,1,0:T(8,128)(2,1)S(1)}, bf16[7,32,32]{2,1,0:T(8,128)(2,1)}, u32[]{:S(2)}) copy-start(bf16[7,32,32]{2,1,0:T(8,128)(2,1)} %param.10) | copy-start | bytes 43012
  3.8 22.8 %collective-permute-start.7 = (bf16[16,32,256]{2,1,0:T(8,128)(2,1)S(1)}, bf16[16,32,256]{2,1,0:T(8,128)(2,1)S(1)}, u32[]{:S(2)}, u32[]{:S(2)}) collective-permute-start(bf16[16,32,256]{2,1,0:T(8,128)(2,1)S(1)} %gather_fusion.2), channel_id=1, source_target_pairs={{12,0},{0,4},{4,8},{8,12},{13,1},{1,5},{5,9},{9,13},{14,2},{2,6},{... | collective-permute-start | bytes 786440 | tf_op jit(solution)/shard_map/ppermute | solution.py:25
  6.9 19.7 %collective-permute-start.6 = (bf16[16,32,256]{2,1,0:T(8,128)(2,1)S(1)}, bf16[16,32,256]{2,1,0:T(8,128)(2,1)S(1)}, u32[]{:S(2)}, u32[]{:S(2)}) collective-permute-start(bf16[16,32,256]{2,1,0:T(8,128)(2,1)S(1)} %gather_fusion.2), channel_id=1, source_target_pairs={{8,0},{12,4},{0,8},{4,12},{9,1},{13,5},{1,9},{5,13},{10,2},{14,6},... | collective-permute-start | bytes 786440 | tf_op jit(solution)/shard_map/ppermute | solution.py:25
  9.5 14.3 %collective-permute-start.5 = (bf16[16,32,256]{2,1,0:T(8,128)(2,1)S(1)}, bf16[16,32,256]{2,1,0:T(8,128)(2,1)S(1)}, u32[]{:S(2)}, u32[]{:S(2)}) collective-permute-start(bf16[16,32,256]{2,1,0:T(8,128)(2,1)S(1)} %gather_fusion.2), channel_id=1, source_target_pairs={{4,0},{8,4},{12,8},{0,12},{5,1},{9,5},{13,9},{1,13},{6,2},{10,6},{... | collective-permute-start | bytes 786440 | tf_op jit(solution)/shard_map/ppermute | solution.py:25
  11.8 16.4 %collective-permute-start.1 = (bf16[16,32,2,128]{3,1,2,0:T(8,128)(2,1)S(1)}, bf16[16,32,2,128]{3,1,2,0:T(8,128)(2,1)S(1)}, u32[]{:S(2)}, u32[]{:S(2)}) collective-permute-start(bf16[16,32,2,128]{3,1,2,0:T(8,128)(2,1)S(1)} %copy.27), channel_id=1, source_target_pairs={{1,0},{2,1},{3,2},{5,4},{6,5},{7,6},{9,8},{10,9},{11,10},{13,12},{... | collective-permute-start | bytes 786440 | tf_op jit(solution)/shard_map/ppermute | solution.py:17
  13.1 15.1 %collective-permute-start = (bf16[16,32,2,128]{3,1,2,0:T(8,128)(2,1)S(1)}, bf16[16,32,2,128]{3,1,2,0:T(8,128)(2,1)}, u32[]{:S(2)}, u32[]{:S(2)}) collective-permute-start(bf16[16,32,2,128]{3,1,2,0:T(8,128)(2,1)S(1)} %copy.27), channel_id=1, source_target_pairs={{0,1},{1,2},{2,3},{4,5},{5,6},{6,7},{8,9},{9,10},{10,11},{12,13},{... | collective-permute-start | bytes 786440 | tf_op jit(solution)/shard_map/ppermute | solution.py:14
  28.0 2.0 %copy-start.6 = (f32[32]{0:T(128)S(1)}, f32[32]{0:T(128)}, u32[]{:S(2)}) copy-start(f32[32]{0:T(128)} %get-tuple-element.68) | copy-start | bytes 388
  28.0 2.0 %copy-start.7 = (f32[32]{0:T(128)S(1)}, f32[32]{0:T(128)}, u32[]{:S(2)}) copy-start(f32[32]{0:T(128)} %get-tuple-element.69) | copy-start | bytes 388
  28.0 2.0 %copy-start.8 = (f32[32]{0:T(128)S(1)}, f32[32]{0:T(128)}, u32[]{:S(2)}) copy-start(f32[32]{0:T(128)} %get-tuple-element.45) | copy-start | bytes 388
  28.0 2.0 %copy-start.9 = (f32[32]{0:T(128)S(1)}, f32[32]{0:T(128)}, u32[]{:S(2)}) copy-start(f32[32]{0:T(128)} %get-tuple-element.46) | copy-start | bytes 388
  28.0 2.0 %copy-start.10 = (f32[32]{0:T(128)S(1)}, f32[32]{0:T(128)}, u32[]{:S(2)}) copy-start(f32[32]{0:T(128)} %get-tuple-element.47) | copy-start | bytes 388
  28.0 2.0 %copy-start.11 = (f32[32]{0:T(128)S(1)}, f32[32]{0:T(128)}, u32[]{:S(2)}) copy-start(f32[32]{0:T(128)} %get-tuple-element.48) | copy-start | bytes 388
  28.0 2.0 %copy-start.12 = (f32[32]{0:T(128)S(1)}, f32[32]{0:T(128)}, u32[]{:S(2)}) copy-start(f32[32]{0:T(128)} %get-tuple-element.49) | copy-start | bytes 388
  28.0 2.0 %copy-start.13 = (f32[32]{0:T(128)S(1)}, f32[32]{0:T(128)}, u32[]{:S(2)}) copy-start(f32[32]{0:T(128)} %get-tuple-element.50) | copy-start | bytes 388
  28.0 2.0 %copy-start.14 = (f32[32]{0:T(128)S(1)}, f32[32]{0:T(128)}, u32[]{:S(2)}) copy-start(f32[32]{0:T(128)} %get-tuple-element.51) | copy-start | bytes 388
  28.1 2.0 %copy-start.15 = (f32[32]{0:T(128)S(1)}, f32[32]{0:T(128)}, u32[]{:S(2)}) copy-start(f32[32]{0:T(128)} %get-tuple-element.52) | copy-start | bytes 388
  28.1 2.0 %copy-start.17 = (f32[32]{0:T(128)S(1)}, f32[32]{0:T(128)}, u32[]{:S(2)}) copy-start(f32[32]{0:T(128)} %get-tuple-element.53) | copy-start | bytes 388
  28.1 2.0 %copy-start.19 = (f32[32]{0:T(128)S(1)}, f32[32]{0:T(128)}, u32[]{:S(2)}) copy-start(f32[32]{0:T(128)} %get-tuple-element.54) | copy-start | bytes 388
  28.1 2.0 %copy-start.21 = (f32[32]{0:T(128)S(1)}, f32[32]{0:T(128)}, u32[]{:S(2)}) copy-start(f32[32]{0:T(128)} %get-tuple-element.55) | copy-start | bytes 388
  28.1 2.0 %copy-start.23 = (f32[32]{0:T(128)S(1)}, f32[32]{0:T(128)}, u32[]{:S(2)}) copy-start(f32[32]{0:T(128)} %get-tuple-element.56) | copy-start | bytes 388
  28.1 2.0 %copy-start.25 = (f32[32]{0:T(128)S(1)}, f32[32]{0:T(128)}, u32[]{:S(2)}) copy-start(f32[32]{0:T(128)} %get-tuple-element.57) | copy-start | bytes 388
  28.1 2.0 %copy-start.27 = (f32[32]{0:T(128)S(1)}, f32[32]{0:T(128)}, u32[]{:S(2)}) copy-start(f32[32]{0:T(128)} %get-tuple-element.58) | copy-start | bytes 388
  28.1 2.0 %copy-start.29 = (f32[32]{0:T(128)S(1)}, f32[32]{0:T(128)}, u32[]{:S(2)}) copy-start(f32[32]{0:T(128)} %get-tuple-element.59) | copy-start | bytes 388
  28.1 2.0 %copy-start.31 = (f32[32]{0:T(128)S(1)}, f32[32]{0:T(128)}, u32[]{:S(2)}) copy-start(f32[32]{0:T(128)} %get-tuple-element.60) | copy-start | bytes 388
  28.1 2.0 %copy-start.33 = (f32[32]{0:T(128)S(1)}, f32[32]{0:T(128)}, u32[]{:S(2)}) copy-start(f32[32]{0:T(128)} %get-tuple-element.61) | copy-start | bytes 388
  28.2 2.0 %copy-start.35 = (f32[32]{0:T(128)S(1)}, f32[32]{0:T(128)}, u32[]{:S(2)}) copy-start(f32[32]{0:T(128)} %get-tuple-element.62) | copy-start | bytes 388
  28.2 2.0 %copy-start.37 = (f32[32]{0:T(128)S(1)}, f32[32]{0:T(128)}, u32[]{:S(2)}) copy-start(f32[32]{0:T(128)} %get-tuple-element.63) | copy-start | bytes 388
  36.8 2.4 %copy-start.4 = (bf16[16,2,4,8,128]{4,3,2,1,0:T(8,128)(2,1)S(1)}, bf16[16,2,4,8,128]{4,3,2,1,0:T(8,128)(2,1)}, u32[]{:S(2)}) copy-start(bf16[16,2,4,8,128]{4,3,2,1,0:T(8,128)(2,1)} %get-tuple-element.73) | copy-start | bytes 786436
  39.9 1.7 %copy-start.39 = (f32[32]{0:T(128)S(1)}, f32[32]{0:T(128)}, u32[]{:S(2)}) copy-start(f32[32]{0:T(128)} %get-tuple-element.17) | copy-start | bytes 388
  39.9 1.7 %copy-start.40 = (f32[32]{0:T(128)S(1)}, f32[32]{0:T(128)}, u32[]{:S(2)}) copy-start(f32[32]{0:T(128)} %get-tuple-element.18) | copy-start | bytes 388
  39.9 1.7 %copy-start.41 = (f32[32]{0:T(128)S(1)}, f32[32]{0:T(128)}, u32[]{:S(2)}) copy-start(f32[32]{0:T(128)} %get-tuple-element.19) | copy-start | bytes 388
  39.9 1.7 %copy-start.42 = (f32[32]{0:T(128)S(1)}, f32[32]{0:T(128)}, u32[]{:S(2)}) copy-start(f32[32]{0:T(128)} %get-tuple-element.20) | copy-start | bytes 388
  39.9 1.7 %copy-start.43 = (f32[32]{0:T(128)S(1)}, f32[32]{0:T(128)}, u32[]{:S(2)}) copy-start(f32[32]{0:T(128)} %get-tuple-element.21) | copy-start | bytes 388
  39.9 1.7 %copy-start.44 = (f32[32]{0:T(128)S(1)}, f32[32]{0:T(128)}, u32[]{:S(2)}) copy-start(f32[32]{0:T(128)} %get-tuple-element.22) | copy-start | bytes 388
  39.9 1.7 %copy-start.45 = (f32[32]{0:T(128)S(1)}, f32[32]{0:T(128)}, u32[]{:S(2)}) copy-start(f32[32]{0:T(128)} %get-tuple-element.23) | copy-start | bytes 388
  39.9 1.7 %copy-start.46 = (f32[32]{0:T(128)S(1)}, f32[32]{0:T(128)}, u32[]{:S(2)}) copy-start(f32[32]{0:T(128)} %get-tuple-element.24) | copy-start | bytes 388
  39.9 1.7 %copy-start.47 = (f32[32]{0:T(128)S(1)}, f32[32]{0:T(128)}, u32[]{:S(2)}) copy-start(f32[32]{0:T(128)} %get-tuple-element.25) | copy-start | bytes 388
  42.2 8.7 %collective-permute-start.10 = (f32[8992]{0:T(1024)S(1)}, f32[8992]{0:T(1024)S(1)}, u32[]{:S(2)}, u32[]{:S(2)}) collective-permute-start(f32[8992]{0:T(1024)S(1)} %broadcast_multiply_fusion), channel_id=1, source_target_pairs={{0,1},{1,0},{2,3},{3,2},{4,5},{5,4},{6,7},{7,6},{8,9},{9,8},{10,11... | collective-permute-start | bytes 107912 | tf_op jit(solution)/shard_map/ppermute | solution.py:39
  42.3 28.2 %collective-permute-start.4 = (bf16[16,32,256]{2,1,0:T(8,128)(2,1)S(1)}, bf16[16,32,256]{2,1,0:T(8,128)(2,1)S(1)}, u32[]{:S(2)}, u32[]{:S(2)}) collective-permute-start(bf16[16,32,256]{2,1,0:T(8,128)(2,1)S(1)} %gather_fusion), channel_id=1, source_target_pairs={{12,0},{0,4},{4,8},{8,12},{13,1},{1,5},{5,9},{9,13},{14,2},{2,6},{... | collective-permute-start | bytes 786440 | tf_op jit(solution)/shard_map/ppermute | solution.py:25
  48.5 22.0 %collective-permute-start.3 = (bf16[16,32,256]{2,1,0:T(8,128)(2,1)S(1)}, bf16[16,32,256]{2,1,0:T(8,128)(2,1)S(1)}, u32[]{:S(2)}, u32[]{:S(2)}) collective-permute-start(bf16[16,32,256]{2,1,0:T(8,128)(2,1)S(1)} %gather_fusion), channel_id=1, source_target_pairs={{8,0},{12,4},{0,8},{4,12},{9,1},{13,5},{1,9},{5,13},{10,2},{14,6},... | collective-permute-start | bytes 786440 | tf_op jit(solution)/shard_map/ppermute | solution.py:25
  50.0 20.5 %collective-permute-start.2 = (bf16[16,32,256]{2,1,0:T(8,128)(2,1)S(1)}, bf16[16,32,256]{2,1,0:T(8,128)(2,1)S(1)}, u32[]{:S(2)}, u32[]{:S(2)}) collective-permute-start(bf16[16,32,256]{2,1,0:T(8,128)(2,1)S(1)} %gather_fusion), channel_id=1, source_target_pairs={{4,0},{8,4},{12,8},{0,12},{5,1},{9,5},{13,9},{1,13},{6,2},{10,6},{... | collective-permute-start | bytes 786440 | tf_op jit(solution)/shard_map/ppermute | solution.py:25
  51.0 4.0 %collective-permute-start.11 = (f32[8992]{0:T(1024)S(1)}, f32[8992]{0:T(1024)S(1)}, u32[]{:S(2)}, u32[]{:S(2)}) collective-permute-start(f32[8992]{0:T(1024)S(1)} %fusion.134), channel_id=1, source_target_pairs={{0,2},{2,0},{1,3},{3,1},{4,6},{6,4},{5,7},{7,5},{8,10},{10,8},{9,1... | collective-permute-start | bytes 107912 | tf_op jit(solution)/shard_map/ppermute | solution.py:39
  55.0 13.4 %collective-permute-start.12 = (f32[8992]{0:T(1024)S(1)}, f32[8992]{0:T(1024)S(1)}, u32[]{:S(2)}, u32[]{:S(2)}) collective-permute-start(f32[8992]{0:T(1024)S(1)} %add.279), channel_id=1, source_target_pairs={{0,4},{4,0},{8,12},{12,8},{1,5},{5,1},{9,13},{13,9},{2,6},{6,2},{1... | collective-permute-start | bytes 107912 | tf_op jit(solution)/shard_map/ppermute | solution.py:39
  56.1 18.8 %collective-permute-start.9 = (bf16[16,32,2,128]{3,1,2,0:T(8,128)(2,1)S(1)}, bf16[16,32,2,128]{3,1,2,0:T(8,128)(2,1)S(1)}, u32[]{:S(2)}, u32[]{:S(2)}) collective-permute-start(bf16[16,32,2,128]{3,1,2,0:T(8,128)(2,1)S(1)} %bitcast.343), channel_id=1, source_target_pairs={{1,0},{2,1},{3,2},{5,4},{6,5},{7,6},{9,8},{10,9},{11,10},{13,12},{... | collective-permute-start | bytes 786440 | tf_op jit(solution)/shard_map/ppermute | solution.py:17
  68.4 6.5 %collective-permute-start.8 = (bf16[16,32,2,128]{3,1,2,0:T(8,128)(2,1)S(1)}, bf16[16,32,2,128]{3,1,2,0:T(8,128)(2,1)S(1)}, u32[]{:S(2)}, u32[]{:S(2)}) collective-permute-start(bf16[16,32,2,128]{3,1,2,0:T(8,128)(2,1)S(1)} %bitcast.344), channel_id=1, source_target_pairs={{0,1},{1,2},{2,3},{4,5},{5,6},{6,7},{8,9},{9,10},{10,11},{12,13},{... | collective-permute-start | bytes 786440 | tf_op jit(solution)/shard_map/ppermute | solution.py:14
  70.5 10.2 %collective-permute-start.13 = (f32[8992]{0:T(1024)S(1)}, f32[8992]{0:T(1024)S(1)}, u32[]{:S(2)}, u32[]{:S(2)}) collective-permute-start(f32[8992]{0:T(1024)S(1)} %add.280), channel_id=1, source_target_pairs={{0,8},{4,12},{8,0},{12,4},{1,9},{5,13},{9,1},{13,5},{2,10},{6,14},... | collective-permute-start | bytes 107912 | tf_op jit(solution)/shard_map/ppermute | solution.py:39
  (29 other events, 39.3 us)

commit v8 on v7

--- a/solution.py
+++ b/solution.py
@@ -145,7 +145,7 @@
     dirty_grad = (cotangent.astype(jnp.float32) + conv).astype(jnp.bfloat16)
     parts = (kernel_term, mix_term, spec_grad)
     flat = jnp.concatenate([part.reshape(-1) for part in parts]) * scale
-    flat = all_summed(flat, ("sub", "tile", "chan"), tied=h_received, tie_at=3)
+    flat = all_summed(flat, ("sub", "tile", "chan"), tied=h_received, tie_at=2)
     sizes = [part.size for part in parts]
     kgrad, mgrad, sgrad = (
         piece.reshape(part.shape)

time: 83.5 us -> 87.4 us (1.047)
  starting transfers between devices: 29.1 us -> 33.2 us
    ppermute x4, waiting for transfers between devices: 13.5 us -> 2.73 us  [all_summed(): lax.ppermute(value, axis, [(i, i ^ step) for i in range(count)])]
    ppermute x6, waiting for transfers between devices: 6.81 us -> 17.4 us  [passed_along(): return lax.ppermute(block, axis, route)]
    ppermute x4, starting transfers between devices: 5.03 us -> 9.18 us  [all_summed(): lax.ppermute(value, axis, [(i, i ^ step) for i in range(count)])]
  transfers between devices with their start and end apart: 14 -> 14, of which waited for: 4 -> 5; matrix products, arithmetic and copies ran while one was open for 15% -> 15% of each run, Pallas kernels for 0% -> 0%
where the time goes in v8:
time: 87.4 us; the launch traced here: 87 us
  starting transfers between devices  33.2 us (38%)
  waiting for transfers between devices  20.2 us (23%)
  other arithmetic  14.1 us (16%)
  local copies, waits for them, and re-layouts  12.3 us (14%)
  matrix products  5.29 us (6%)
  between operations  1.93 us (2%)
    ppermute x6, waiting for transfers between devices, passed_along(): return lax.ppermute(block, axis, route)  17.4 us
    ppermute x6, starting transfers between devices, passed_along(): return lax.ppermute(block, axis, route)  15.7 us
    ppermute x4, starting transfers between devices, all_summed(): lax.ppermute(value, axis, [(i, i ^ step) for i in range(count)])  9.18 us
    ppermute x2, starting transfers between devices, padded(): lax.ppermute(lax.slice_in_dim(block, block.shape[dim] - width, None, axis...  5.79 us
    dot_general x2, other arithmetic, local(): jnp.einsum('cfhw,cfhw->f', dsmooth, xpad[:, :, i:i + rows, j:j + cols], p...  3.05 us
    convert_element_type x1, other arithmetic, local(): dirty_grad = (cotangent.astype(jnp.float32) + conv).astype(jnp.bfloat16)  3.04 us
    convert_element_type x1, other arithmetic, local(): smooth = total.astype(jnp.bfloat16)  3.03 us
    slice x2, local copies, waits for them, and re-layouts, local(): spatial_kernel[:, i * 5 + j][None, :, None, None]  2.85 us
  transfers between devices with their start and end apart: 14, of which 5 were waited for; matrix products, arithmetic and copies ran while one was open for 15% of the time, Pallas kernels for 0%

profile of v8, /device:TPU:0, one launch (start us, length us, event | category | flops | bytes accessed | tf_op | source)
XLA Modules:
  0.0 87.0 jit_solution(6764712753799961700)
XLA Ops:
  0.7 0.8 compare_select_fusion.1
  1.4 0.6 scatter_custom_fusion
  2.1 1.1 %reshape.80 = bf16[16,32,256]{2,1,0:T(8,128)(2,1)S(1)} reshape(bf16[16,32,2,128]{3,2,1,0:T(2,128)(2,1)} %param.7) | data formatting | bytes 524288 | tf_op jit(solution)/shard_map/reshape | solution.py:81
  3.2 0.6 gather_fusion.2
  3.8 3.1 %collective-permute-start.7 = (bf16[16,32,256]{2,1,0:T(8,128)(2,1)S(1)}, bf16[16,32,256]{2,1,0:T(8,128)(2,1)S(1)}, u32[]{:S(2)}, u32[]{:S(2)}) collective-permute-start(bf16[16,32,256]{2,1,0:T(8,128)(2,1)S(1)} %gather_fusion.2), channel_id=1, source_target_pairs={{12,0},{0,4},{4,8},{8,12},{13,1},{1,5},{5,9},{9,13},{14,2},{2,6},{... | collective-permute-start | bytes 786440 | tf_op jit(solution)/shard_map/ppermute | solution.py:25
  6.9 2.6 %collective-permute-start.6 = (bf16[16,32,256]{2,1,0:T(8,128)(2,1)S(1)}, bf16[16,32,256]{2,1,0:T(8,128)(2,1)S(1)}, u32[]{:S(2)}, u32[]{:S(2)}) collective-permute-start(bf16[16,32,256]{2,1,0:T(8,128)(2,1)S(1)} %gather_fusion.2), channel_id=1, source_target_pairs={{8,0},{12,4},{0,8},{4,12},{9,1},{13,5},{1,9},{5,13},{10,2},{14,6},... | collective-permute-start | bytes 786440 | tf_op jit(solution)/shard_map/ppermute | solution.py:25
  9.5 1.3 %collective-permute-start.5 = (bf16[16,32,256]{2,1,0:T(8,128)(2,1)S(1)}, bf16[16,32,256]{2,1,0:T(8,128)(2,1)S(1)}, u32[]{:S(2)}, u32[]{:S(2)}) collective-permute-start(bf16[16,32,256]{2,1,0:T(8,128)(2,1)S(1)} %gather_fusion.2), channel_id=1, source_target_pairs={{4,0},{8,4},{12,8},{0,12},{5,1},{9,5},{13,9},{1,13},{6,2},{10,6},{... | collective-permute-start | bytes 786440 | tf_op jit(solution)/shard_map/ppermute | solution.py:25
  10.8 1.0 %copy.27 = bf16[16,32,2,128]{3,1,2,0:T(8,128)(2,1)S(1)} copy(bf16[16,32,2,128]{3,2,1,0:T(2,128)(2,1)} %param.6) | data formatting | bytes 524288 | tf_op args[0]
  11.8 1.3 %collective-permute-start.1 = (bf16[16,32,2,128]{3,1,2,0:T(8,128)(2,1)S(1)}, bf16[16,32,2,128]{3,1,2,0:T(8,128)(2,1)S(1)}, u32[]{:S(2)}, u32[]{:S(2)}) collective-permute-start(bf16[16,32,2,128]{3,1,2,0:T(8,128)(2,1)S(1)} %copy.27), channel_id=1, source_target_pairs={{1,0},{2,1},{3,2},{5,4},{6,5},{7,6},{9,8},{10,9},{11,10},{13,12},{... | collective-permute-start | bytes 786440 | tf_op jit(solution)/shard_map/ppermute | solution.py:17
  13.1 3.7 %collective-permute-start = (bf16[16,32,2,128]{3,1,2,0:T(8,128)(2,1)S(1)}, bf16[16,32,2,128]{3,1,2,0:T(8,128)(2,1)}, u32[]{:S(2)}, u32[]{:S(2)}) collective-permute-start(bf16[16,32,2,128]{3,1,2,0:T(8,128)(2,1)S(1)} %copy.27), channel_id=1, source_target_pairs={{0,1},{1,2},{2,3},{4,5},{5,6},{6,7},{8,9},{9,10},{10,11},{12,13},{... | collective-permute-start | bytes 786440 | tf_op jit(solution)/shard_map/ppermute | solution.py:14
  16.8 1.7 %slice_reduce_fusion.23 = (f32[32]{0:T(128)S(1)}, f32[32]{0:T(128)S(1)}, f32[32]{0:T(128)S(1)}, f32[32]{0:T(128)S(1)}, f32[32]{0:T(128)}, /*index=5*/f32[32]{0:T(128)}) fusion(f32[32,25]{1,0:T(8,128)} %param.8), kind=kLoop, calls=%fused_computation.286 | loop fusion | bytes 1536 | tf_op jit(solution)/shard_map/slice | solution.py:74
  18.6 1.1 %slice_reduce_fusion.24 = (f32[32]{0:T(128)}, f32[32]{0:T(128)}, f32[32]{0:T(128)}, f32[32]{0:T(128)}, f32[32]{0:T(128)}, /*index=5*/f32[32]{0:T(128)}, f32[32]{...) fusion(f32[32,25]{1,0:T(8,128)S(1)} %copy-done.1), kind=kLoop, calls=%fused_computation.287 | loop fusion | bytes 4864 | tf_op jit(solution)/shard_map/slice | solution.py:74
  19.7 4.0 %collective-permute-done.5 = bf16[16,32,256]{2,1,0:T(8,128)(2,1)S(1)} collective-permute-done((bf16[16,32,256]{2,1,0:T(8,128)(2,1)S(1)}, bf16[16,32,256]{2,1,0:T(8,128)(2,1)S(1)}, u32[]{:S(2)}, u32[]{:S(2)}) %collective-permute-start.5) | collective-permute-done | bytes 262176 | tf_op jit(solution)/shard_map/ppermute | solution.py:25
  23.8 2.8 %collective-permute-done.6 = bf16[16,32,256]{2,1,0:T(8,128)(2,1)S(1)} collective-permute-done((bf16[16,32,256]{2,1,0:T(8,128)(2,1)S(1)}, bf16[16,32,256]{2,1,0:T(8,128)(2,1)S(1)}, u32[]{:S(2)}, u32[]{:S(2)}) %collective-permute-start.6) | collective-permute-done | bytes 262176 | tf_op jit(solution)/shard_map/ppermute | solution.py:25
  26.9 0.5 fusion.8
  27.4 0.6 gather_fusion.3
  28.2 1.7 %select_maximum_fusion.2 = (bf16[16,32,6,132]{3,1,2,0:T(8,128)(2,1)S(1)}, f32[16,32,6,132]{3,1,2,0:T(8,128)S(1)}) fusion(bf16[16,32,2,128]{3,1,2,0:T(8,128)(2,1)S(1)} %collective-permute-done.1, bf16[16,32,2,128]{3,1,2,0:T(8,128)(2,1)S(1)} %copy.27, bf16[16,32,2,128]{3,1,2,0:T(8,128)(2,1)} %collective-permute-done), kind=kLoop, calls=%fused_computation.37 | loop fusion | flops 5271552 | bytes 3219456 | tf_op jit(solution)/shard_map/concatenate | solution.py:18
  30.1 3.0 %fusion.64 = bf16[16,32,2,128]{3,1,2,0:T(8,128)(2,1)S(1)} fusion(f32[16,32,6,132]{3,1,2,0:T(8,128)S(1)} %get-tuple-element.71, f32[32]{0:T(128)S(1)} %copy-done.6, f32[32]{0:T(128)S(1)} %copy-done.7, f32[32]{0:T(128)S(1)} %copy-done.9, f32[32]{0:T(128)S(1)} %copy-done.10, f32[32]{0:T(128)S(1)} %copy-done.11, f32[32]{0:T(128)S(1)} %copy-done.12, ...), kind=kLoop, calls=%fused_computation.129 | loop fusion | flops 6553600 | bytes 13372544 | tf_op jit(solution)/shard_map/convert_element_type | solution.py:77
  33.2 1.1 %fusion.36 = (bf16[16,32,2,128]{3,1,2,0:T(8,128)(2,1)S(1)}, bf16[16,2,4,8,128]{4,3,2,1,0:T(8,128)(2,1)}) fusion(bf16[16,32,2,128]{3,1,2,0:T(8,128)(2,1)S(1)} %fusion.64, bf16[32,32]{1,0:T(8,128)(2,1)S(1)} %copy-done, bf16[16,32,256]{2,1,0:T(8,128)(2,1)S(1)} %gather_fusion.3), kind=kOutput, calls=%fused_computation.75 | convolution fusion | flops 9961472 | bytes 1050624 | tf_op jit(solution)/shard_map/gf,cfhw->cghw/dot_general | solution.py:78
  34.3 0.2 convolution_bitcast_fusion.3
  34.5 2.3 %fusion.34 = (f32[32]{0:T(128)}, f32[32]{0:T(128)}, f32[32]{0:T(128)}, f32[32]{0:T(128)}, f32[32]{0:T(128)}, /*index=5*/f32[32]{0:T(128)}, bf16[16,2,128,32]{2,3,1,0:T(8,128)(2,1)S(1)}) fusion(bf16[16,32,6,132]{3,1,2,0:T(8,128)(2,1)S(1)} %get-tuple-element.70, bf16[16,32,2,128]{3,1,2,0:T(8,128)(2,1)} %collective-permute-done, ...), kind=kOutput, calls=%fused_computation.72 | convolution fusion | flops 11272000 | bytes 1837824 | tf_op jit(solution)/shard_map/gf,cghw->cfhw/dot_general | solution.py:122
  36.8 2.3 %fusion.35 = (f32[32]{0:T(128)}, f32[32]{0:T(128)}, f32[32]{0:T(128)}, f32[32]{0:T(128)}, f32[32]{0:T(128)}, /*index=5*/f32[32]{0:T(128)}, f32[32]{0:T(128)}, f3...) fusion(bf16[16,32,6,132]{3,1,2,0:T(8,128)(2,1)S(1)} %get-tuple-, ...), kind=kLoop, calls=%fused_computation.73 | loop fusion | flops 7208384 | bytes 4983040 | tf_op jit(solution)/shard_map/cfhw,cfhw->f/dot_general | solution.py:137
  39.3 0.6 gather_fusion
  40.1 0.6 fusion.9
  40.8 0.8 multiply_reduce_fusion
  42.0 0.1 reshape.81
  42.3 6.2 %collective-permute-start.4 = (bf16[16,32,256]{2,1,0:T(8,128)(2,1)S(1)}, bf16[16,32,256]{2,1,0:T(8,128)(2,1)S(1)}, u32[]{:S(2)}, u32[]{:S(2)}) collective-permute-start(bf16[16,32,256]{2,1,0:T(8,128)(2,1)S(1)} %gather_fusion), channel_id=1, source_target_pairs={{12,0},{0,4},{4,8},{8,12},{13,1},{1,5},{5,9},{9,13},{14,2},{2,6},{... | collective-permute-start | bytes 786440 | tf_op jit(solution)/shard_map/ppermute | solution.py:25
  48.5 1.5 %collective-permute-start.3 = (bf16[16,32,256]{2,1,0:T(8,128)(2,1)S(1)}, bf16[16,32,256]{2,1,0:T(8,128)(2,1)S(1)}, u32[]{:S(2)}, u32[]{:S(2)}) collective-permute-start(bf16[16,32,256]{2,1,0:T(8,128)(2,1)S(1)} %gather_fusion), channel_id=1, source_target_pairs={{8,0},{12,4},{0,8},{4,12},{9,1},{13,5},{1,9},{5,13},{10,2},{14,6},... | collective-permute-start | bytes 786440 | tf_op jit(solution)/shard_map/ppermute | solution.py:25
  50.0 0.9 %collective-permute-start.2 = (bf16[16,32,256]{2,1,0:T(8,128)(2,1)S(1)}, bf16[16,32,256]{2,1,0:T(8,128)(2,1)S(1)}, u32[]{:S(2)}, u32[]{:S(2)}) collective-permute-start(bf16[16,32,256]{2,1,0:T(8,128)(2,1)S(1)} %gather_fusion), channel_id=1, source_target_pairs={{4,0},{8,4},{12,8},{0,12},{5,1},{9,5},{13,9},{1,13},{6,2},{10,6},{... | collective-permute-start | bytes 786440 | tf_op jit(solution)/shard_map/ppermute | solution.py:25
  51.0 1.6 %collective-permute-start.11 = (f32[8992]{0:T(1024)S(1)}, f32[8992]{0:T(1024)S(1)}, u32[]{:S(2)}, u32[]{:S(2)}) collective-permute-start(f32[8992]{0:T(1024)S(1)} %fusion.134), channel_id=1, source_target_pairs={{0,2},{2,0},{1,3},{3,1},{4,6},{6,4},{5,7},{7,5},{8,10},{10,8},{9,1... | collective-permute-start | bytes 107912 | tf_op jit(solution)/shard_map/ppermute | solution.py:39
  52.5 1.3 %collective-permute-start.9 = (bf16[16,32,2,128]{3,1,2,0:T(8,128)(2,1)S(1)}, bf16[16,32,2,128]{3,1,2,0:T(8,128)(2,1)S(1)}, u32[]{:S(2)}, u32[]{:S(2)}) collective-permute-start(bf16[16,32,2,128]{3,1,2,0:T(8,128)(2,1)S(1)} %bitcast.343), channel_id=1, source_target_pairs={{1,0},{2,1},{3,2},{5,4},{6,5},{7,6},{9,8},{10,9},{11,10},{13,12},{... | collective-permute-start | bytes 786440 | tf_op jit(solution)/shard_map/ppermute | solution.py:17
  53.8 1.2 %collective-permute-done.11 = f32[8992]{0:T(1024)S(1)} collective-permute-done((f32[8992]{0:T(1024)S(1)}, f32[8992]{0:T(1024)S(1)}, u32[]{:S(2)}, u32[]{:S(2)}) %collective-permute-start.11) | collective-permute-done | bytes 36000 | tf_op jit(solution)/shard_map/ppermute | solution.py:39
  55.0 2.1 %collective-permute-start.8 = (bf16[16,32,2,128]{3,1,2,0:T(8,128)(2,1)S(1)}, bf16[16,32,2,128]{3,1,2,0:T(8,128)(2,1)S(1)}, u32[]{:S(2)}, u32[]{:S(2)}) collective-permute-start(bf16[16,32,2,128]{3,1,2,0:T(8,128)(2,1)S(1)} %bitcast.344), channel_id=1, source_target_pairs={{0,1},{1,2},{2,3},{4,5},{5,6},{6,7},{8,9},{9,10},{10,11},{12,13},{... | collective-permute-start | bytes 786440 | tf_op jit(solution)/shard_map/ppermute | solution.py:14
  57.1 10.6 %collective-permute-done.3 = bf16[16,32,256]{2,1,0:T(8,128)(2,1)S(1)} collective-permute-done((bf16[16,32,256]{2,1,0:T(8,128)(2,1)S(1)}, bf16[16,32,256]{2,1,0:T(8,128)(2,1)S(1)}, u32[]{:S(2)}, u32[]{:S(2)}) %collective-permute-start.3) | collective-permute-done | bytes 262176 | tf_op jit(solution)/shard_map/ppermute | solution.py:25
  67.7 6.1 %collective-permute-start.12 = (f32[8992]{0:T(1024)S(1)}, f32[8992]{0:T(1024)S(1)}, u32[]{:S(2)}, u32[]{:S(2)}) collective-permute-start(f32[8992]{0:T(1024)S(1)} %add.279), channel_id=1, source_target_pairs={{0,4},{4,0},{8,12},{12,8},{1,5},{5,1},{9,13},{13,9},{2,6},{6,2},{1... | collective-permute-start | bytes 107912 | tf_op jit(solution)/shard_map/ppermute | solution.py:39
  74.2 0.7 fusion.3
  74.9 0.1 copy-done.3
  75.1 3.0 %fusion.39 = bf16[16,32,2,128]{3,1,2,0:T(8,128)(2,1)S(1)} fusion(f32[16,32,6,132]{3,1,2,0:T(8,128)S(1)} %fusion.3, bf16[16,32,2,128]{3,2,1,0:T(2,128)(2,1)S(1)} %copy-done.3, f32[32]{0:T(128)S(1)} %copy-done.6, f32[32]{0:T(128)S(1)} %copy-done.7, f32[32]{0:T(128)S(1)} %copy-done.9, f32[32]{0:T(128)S(1)} %copy-done.10, f32[32]{0:T(128)S(1)} %copy-done.11, ...), kind=kLoop, calls=%fused_computation.79 | loop fusion | flops 6815744 | bytes 13634688 | tf_op jit(solution)/shard_map/convert_element_type | solution.py:145
  78.3 0.6 fusion.7
  78.9 0.6 gather_fusion.1
  79.5 0.3 reshape.87
  79.8 1.4 %collective-permute-start.13 = (f32[8992]{0:T(1024)S(1)}, f32[8992]{0:T(1024)S(1)}, u32[]{:S(2)}, u32[]{:S(2)}) collective-permute-start(f32[8992]{0:T(1024)S(1)} %add.280), channel_id=1, source_target_pairs={{0,8},{4,12},{8,0},{12,4},{1,9},{5,13},{9,1},{13,5},{2,10},{6,14},... | collective-permute-start | bytes 107912 | tf_op jit(solution)/shard_map/ppermute | solution.py:39
  81.2 1.0 %add_convert_fusion = bf16[16,32,2,128]{3,2,1,0:T(2,128)(2,1)} fusion(f32[16,32,2,128]{3,2,1,0:T(2,128)S(1)} %reshape.87, bf16[16,32,2,128]{3,2,1,0:T(2,128)(2,1)S(1)} %copy-done.2), kind=kLoop, calls=%fused_computation.179 | loop fusion | flops 393216 | bytes 1048576 | tf_op jit(solution)/shard_map/convert_element_type | solution.py:119
  82.2 0.9 %copy.48 = bf16[16,32,2,128]{3,2,1,0:T(2,128)(2,1)} copy(bf16[16,32,2,128]{3,1,2,0:T(8,128)(2,1)S(1)} %fusion.39) | data formatting | bytes 524288
  83.2 1.6 %collective-permute-done.13 = f32[8992]{0:T(1024)S(1)} collective-permute-done((f32[8992]{0:T(1024)S(1)}, f32[8992]{0:T(1024)S(1)}, u32[]{:S(2)}, u32[]{:S(2)}) %collective-permute-start.13) | collective-permute-done | bytes 36000 | tf_op jit(solution)/shard_map/ppermute | solution.py:39
  84.9 0.7 reshape.85
  85.6 0.7 split.13
  86.3 0.7 reshape.86
  (170 shorter events, 1.8 us)
Async XLA Ops:
  0.6 32.5 %copy-start = (bf16[32,32]{1,0:T(8,128)(2,1)S(1)}, bf16[32,32]{1,0:T(8,128)(2,1)}, u32[]{:S(2)}) copy-start(bf16[32,32]{1,0:T(8,128)(2,1)} %param.9) | copy-start | bytes 6148
  0.6 17.9 %copy-start.1 = (f32[32,25]{1,0:T(8,128)S(1)}, f32[32,25]{1,0:T(8,128)}, u32[]{:S(2)}) copy-start(f32[32,25]{1,0:T(8,128)} %param.8) | copy-start | bytes 9604
  0.7 19.0 %copy-start.5 = (bf16[7,32,32]{2,1,0:T(8,128)(2,1)S(1)}, bf16[7,32,32]{2,1,0:T(8,128)(2,1)}, u32[]{:S(2)}) copy-start(bf16[7,32,32]{2,1,0:T(8,128)(2,1)} %param.10) | copy-start | bytes 43012
  3.8 22.8 %collective-permute-start.7 = (bf16[16,32,256]{2,1,0:T(8,128)(2,1)S(1)}, bf16[16,32,256]{2,1,0:T(8,128)(2,1)S(1)}, u32[]{:S(2)}, u32[]{:S(2)}) collective-permute-start(bf16[16,32,256]{2,1,0:T(8,128)(2,1)S(1)} %gather_fusion.2), channel_id=1, source_target_pairs={{12,0},{0,4},{4,8},{8,12},{13,1},{1,5},{5,9},{9,13},{14,2},{2,6},{... | collective-permute-start | bytes 786440 | tf_op jit(solution)/shard_map/ppermute | solution.py:25
  6.9 19.7 %collective-permute-start.6 = (bf16[16,32,256]{2,1,0:T(8,128)(2,1)S(1)}, bf16[16,32,256]{2,1,0:T(8,128)(2,1)S(1)}, u32[]{:S(2)}, u32[]{:S(2)}) collective-permute-start(bf16[16,32,256]{2,1,0:T(8,128)(2,1)S(1)} %gather_fusion.2), channel_id=1, source_target_pairs={{8,0},{12,4},{0,8},{4,12},{9,1},{13,5},{1,9},{5,13},{10,2},{14,6},... | collective-permute-start | bytes 786440 | tf_op jit(solution)/shard_map/ppermute | solution.py:25
  9.5 14.3 %collective-permute-start.5 = (bf16[16,32,256]{2,1,0:T(8,128)(2,1)S(1)}, bf16[16,32,256]{2,1,0:T(8,128)(2,1)S(1)}, u32[]{:S(2)}, u32[]{:S(2)}) collective-permute-start(bf16[16,32,256]{2,1,0:T(8,128)(2,1)S(1)} %gather_fusion.2), channel_id=1, source_target_pairs={{4,0},{8,4},{12,8},{0,12},{5,1},{9,5},{13,9},{1,13},{6,2},{10,6},{... | collective-permute-start | bytes 786440 | tf_op jit(solution)/shard_map/ppermute | solution.py:25
  11.8 16.4 %collective-permute-start.1 = (bf16[16,32,2,128]{3,1,2,0:T(8,128)(2,1)S(1)}, bf16[16,32,2,128]{3,1,2,0:T(8,128)(2,1)S(1)}, u32[]{:S(2)}, u32[]{:S(2)}) collective-permute-start(bf16[16,32,2,128]{3,1,2,0:T(8,128)(2,1)S(1)} %copy.27), channel_id=1, source_target_pairs={{1,0},{2,1},{3,2},{5,4},{6,5},{7,6},{9,8},{10,9},{11,10},{13,12},{... | collective-permute-start | bytes 786440 | tf_op jit(solution)/shard_map/ppermute | solution.py:17
  13.1 15.1 %collective-permute-start = (bf16[16,32,2,128]{3,1,2,0:T(8,128)(2,1)S(1)}, bf16[16,32,2,128]{3,1,2,0:T(8,128)(2,1)}, u32[]{:S(2)}, u32[]{:S(2)}) collective-permute-start(bf16[16,32,2,128]{3,1,2,0:T(8,128)(2,1)S(1)} %copy.27), channel_id=1, source_target_pairs={{0,1},{1,2},{2,3},{4,5},{5,6},{6,7},{8,9},{9,10},{10,11},{12,13},{... | collective-permute-start | bytes 786440 | tf_op jit(solution)/shard_map/ppermute | solution.py:14
  28.0 2.0 %copy-start.6 = (f32[32]{0:T(128)S(1)}, f32[32]{0:T(128)}, u32[]{:S(2)}) copy-start(f32[32]{0:T(128)} %get-tuple-element.68) | copy-start | bytes 388
  28.0 2.0 %copy-start.7 = (f32[32]{0:T(128)S(1)}, f32[32]{0:T(128)}, u32[]{:S(2)}) copy-start(f32[32]{0:T(128)} %get-tuple-element.69) | copy-start | bytes 388
  28.0 2.0 %copy-start.8 = (f32[32]{0:T(128)S(1)}, f32[32]{0:T(128)}, u32[]{:S(2)}) copy-start(f32[32]{0:T(128)} %get-tuple-element.45) | copy-start | bytes 388
  28.0 2.0 %copy-start.9 = (f32[32]{0:T(128)S(1)}, f32[32]{0:T(128)}, u32[]{:S(2)}) copy-start(f32[32]{0:T(128)} %get-tuple-element.46) | copy-start | bytes 388
  28.0 2.0 %copy-start.10 = (f32[32]{0:T(128)S(1)}, f32[32]{0:T(128)}, u32[]{:S(2)}) copy-start(f32[32]{0:T(128)} %get-tuple-element.47) | copy-start | bytes 388
  28.0 2.0 %copy-start.11 = (f32[32]{0:T(128)S(1)}, f32[32]{0:T(128)}, u32[]{:S(2)}) copy-start(f32[32]{0:T(128)} %get-tuple-element.48) | copy-start | bytes 388
  28.0 2.0 %copy-start.12 = (f32[32]{0:T(128)S(1)}, f32[32]{0:T(128)}, u32[]{:S(2)}) copy-start(f32[32]{0:T(128)} %get-tuple-element.49) | copy-start | bytes 388
  28.0 2.0 %copy-start.13 = (f32[32]{0:T(128)S(1)}, f32[32]{0:T(128)}, u32[]{:S(2)}) copy-start(f32[32]{0:T(128)} %get-tuple-element.50) | copy-start | bytes 388
  28.0 2.0 %copy-start.14 = (f32[32]{0:T(128)S(1)}, f32[32]{0:T(128)}, u32[]{:S(2)}) copy-start(f32[32]{0:T(128)} %get-tuple-element.51) | copy-start | bytes 388
  28.1 2.0 %copy-start.15 = (f32[32]{0:T(128)S(1)}, f32[32]{0:T(128)}, u32[]{:S(2)}) copy-start(f32[32]{0:T(128)} %get-tuple-element.52) | copy-start | bytes 388
  28.1 2.0 %copy-start.17 = (f32[32]{0:T(128)S(1)}, f32[32]{0:T(128)}, u32[]{:S(2)}) copy-start(f32[32]{0:T(128)} %get-tuple-element.53) | copy-start | bytes 388
  28.1 2.0 %copy-start.19 = (f32[32]{0:T(128)S(1)}, f32[32]{0:T(128)}, u32[]{:S(2)}) copy-start(f32[32]{0:T(128)} %get-tuple-element.54) | copy-start | bytes 388
  28.1 2.0 %copy-start.21 = (f32[32]{0:T(128)S(1)}, f32[32]{0:T(128)}, u32[]{:S(2)}) copy-start(f32[32]{0:T(128)} %get-tuple-element.55) | copy-start | bytes 388
  28.1 2.0 %copy-start.23 = (f32[32]{0:T(128)S(1)}, f32[32]{0:T(128)}, u32[]{:S(2)}) copy-start(f32[32]{0:T(128)} %get-tuple-element.56) | copy-start | bytes 388
  28.1 2.0 %copy-start.25 = (f32[32]{0:T(128)S(1)}, f32[32]{0:T(128)}, u32[]{:S(2)}) copy-start(f32[32]{0:T(128)} %get-tuple-element.57) | copy-start | bytes 388
  28.1 2.0 %copy-start.27 = (f32[32]{0:T(128)S(1)}, f32[32]{0:T(128)}, u32[]{:S(2)}) copy-start(f32[32]{0:T(128)} %get-tuple-element.58) | copy-start | bytes 388
  28.1 2.0 %copy-start.29 = (f32[32]{0:T(128)S(1)}, f32[32]{0:T(128)}, u32[]{:S(2)}) copy-start(f32[32]{0:T(128)} %get-tuple-element.59) | copy-start | bytes 388
  28.1 2.0 %copy-start.31 = (f32[32]{0:T(128)S(1)}, f32[32]{0:T(128)}, u32[]{:S(2)}) copy-start(f32[32]{0:T(128)} %get-tuple-element.60) | copy-start | bytes 388
  28.1 2.0 %copy-start.33 = (f32[32]{0:T(128)S(1)}, f32[32]{0:T(128)}, u32[]{:S(2)}) copy-start(f32[32]{0:T(128)} %get-tuple-element.61) | copy-start | bytes 388
  28.2 2.0 %copy-start.35 = (f32[32]{0:T(128)S(1)}, f32[32]{0:T(128)}, u32[]{:S(2)}) copy-start(f32[32]{0:T(128)} %get-tuple-element.62) | copy-start | bytes 388
  28.2 2.0 %copy-start.37 = (f32[32]{0:T(128)S(1)}, f32[32]{0:T(128)}, u32[]{:S(2)}) copy-start(f32[32]{0:T(128)} %get-tuple-element.63) | copy-start | bytes 388
  36.8 2.4 %copy-start.4 = (bf16[16,2,4,8,128]{4,3,2,1,0:T(8,128)(2,1)S(1)}, bf16[16,2,4,8,128]{4,3,2,1,0:T(8,128)(2,1)}, u32[]{:S(2)}) copy-start(bf16[16,2,4,8,128]{4,3,2,1,0:T(8,128)(2,1)} %get-tuple-element.73) | copy-start | bytes 786436
  39.9 1.7 %copy-start.39 = (f32[32]{0:T(128)S(1)}, f32[32]{0:T(128)}, u32[]{:S(2)}) copy-start(f32[32]{0:T(128)} %get-tuple-element.17) | copy-start | bytes 388
  39.9 1.7 %copy-start.40 = (f32[32]{0:T(128)S(1)}, f32[32]{0:T(128)}, u32[]{:S(2)}) copy-start(f32[32]{0:T(128)} %get-tuple-element.18) | copy-start | bytes 388
  39.9 1.7 %copy-start.41 = (f32[32]{0:T(128)S(1)}, f32[32]{0:T(128)}, u32[]{:S(2)}) copy-start(f32[32]{0:T(128)} %get-tuple-element.19) | copy-start | bytes 388
  39.9 1.7 %copy-start.42 = (f32[32]{0:T(128)S(1)}, f32[32]{0:T(128)}, u32[]{:S(2)}) copy-start(f32[32]{0:T(128)} %get-tuple-element.20) | copy-start | bytes 388
  39.9 1.7 %copy-start.43 = (f32[32]{0:T(128)S(1)}, f32[32]{0:T(128)}, u32[]{:S(2)}) copy-start(f32[32]{0:T(128)} %get-tuple-element.21) | copy-start | bytes 388
  39.9 1.7 %copy-start.44 = (f32[32]{0:T(128)S(1)}, f32[32]{0:T(128)}, u32[]{:S(2)}) copy-start(f32[32]{0:T(128)} %get-tuple-element.22) | copy-start | bytes 388
  39.9 1.7 %copy-start.45 = (f32[32]{0:T(128)S(1)}, f32[32]{0:T(128)}, u32[]{:S(2)}) copy-start(f32[32]{0:T(128)} %get-tuple-element.23) | copy-start | bytes 388
  39.9 1.7 %copy-start.46 = (f32[32]{0:T(128)S(1)}, f32[32]{0:T(128)}, u32[]{:S(2)}) copy-start(f32[32]{0:T(128)} %get-tuple-element.24) | copy-start | bytes 388
  39.9 1.7 %copy-start.47 = (f32[32]{0:T(128)S(1)}, f32[32]{0:T(128)}, u32[]{:S(2)}) copy-start(f32[32]{0:T(128)} %get-tuple-element.25) | copy-start | bytes 388
  42.2 8.7 %collective-permute-start.10 = (f32[8992]{0:T(1024)S(1)}, f32[8992]{0:T(1024)S(1)}, u32[]{:S(2)}, u32[]{:S(2)}) collective-permute-start(f32[8992]{0:T(1024)S(1)} %broadcast_multiply_fusion), channel_id=1, source_target_pairs={{0,1},{1,0},{2,3},{3,2},{4,5},{5,4},{6,7},{7,6},{8,9},{9,8},{10,11... | collective-permute-start | bytes 107912 | tf_op jit(solution)/shard_map/ppermute | solution.py:39
  42.3 14.8 %collective-permute-start.4 = (bf16[16,32,256]{2,1,0:T(8,128)(2,1)S(1)}, bf16[16,32,256]{2,1,0:T(8,128)(2,1)S(1)}, u32[]{:S(2)}, u32[]{:S(2)}) collective-permute-start(bf16[16,32,256]{2,1,0:T(8,128)(2,1)S(1)} %gather_fusion), channel_id=1, source_target_pairs={{12,0},{0,4},{4,8},{8,12},{13,1},{1,5},{5,9},{9,13},{14,2},{2,6},{... | collective-permute-start | bytes 786440 | tf_op jit(solution)/shard_map/ppermute | solution.py:25
  48.5 19.2 %collective-permute-start.3 = (bf16[16,32,256]{2,1,0:T(8,128)(2,1)S(1)}, bf16[16,32,256]{2,1,0:T(8,128)(2,1)S(1)}, u32[]{:S(2)}, u32[]{:S(2)}) collective-permute-start(bf16[16,32,256]{2,1,0:T(8,128)(2,1)S(1)} %gather_fusion), channel_id=1, source_target_pairs={{8,0},{12,4},{0,8},{4,12},{9,1},{13,5},{1,9},{5,13},{10,2},{14,6},... | collective-permute-start | bytes 786440 | tf_op jit(solution)/shard_map/ppermute | solution.py:25
  50.0 17.7 %collective-permute-start.2 = (bf16[16,32,256]{2,1,0:T(8,128)(2,1)S(1)}, bf16[16,32,256]{2,1,0:T(8,128)(2,1)S(1)}, u32[]{:S(2)}, u32[]{:S(2)}) collective-permute-start(bf16[16,32,256]{2,1,0:T(8,128)(2,1)S(1)} %gather_fusion), channel_id=1, source_target_pairs={{4,0},{8,4},{12,8},{0,12},{5,1},{9,5},{13,9},{1,13},{6,2},{10,6},{... | collective-permute-start | bytes 786440 | tf_op jit(solution)/shard_map/ppermute | solution.py:25
  51.0 4.0 %collective-permute-start.11 = (f32[8992]{0:T(1024)S(1)}, f32[8992]{0:T(1024)S(1)}, u32[]{:S(2)}, u32[]{:S(2)}) collective-permute-start(f32[8992]{0:T(1024)S(1)} %fusion.134), channel_id=1, source_target_pairs={{0,2},{2,0},{1,3},{3,1},{4,6},{6,4},{5,7},{7,5},{8,10},{10,8},{9,1... | collective-permute-start | bytes 107912 | tf_op jit(solution)/shard_map/ppermute | solution.py:39
  52.5 21.6 %collective-permute-start.9 = (bf16[16,32,2,128]{3,1,2,0:T(8,128)(2,1)S(1)}, bf16[16,32,2,128]{3,1,2,0:T(8,128)(2,1)S(1)}, u32[]{:S(2)}, u32[]{:S(2)}) collective-permute-start(bf16[16,32,2,128]{3,1,2,0:T(8,128)(2,1)S(1)} %bitcast.343), channel_id=1, source_target_pairs={{1,0},{2,1},{3,2},{5,4},{6,5},{7,6},{9,8},{10,9},{11,10},{13,12},{... | collective-permute-start | bytes 786440 | tf_op jit(solution)/shard_map/ppermute | solution.py:17
  55.0 19.2 %collective-permute-start.8 = (bf16[16,32,2,128]{3,1,2,0:T(8,128)(2,1)S(1)}, bf16[16,32,2,128]{3,1,2,0:T(8,128)(2,1)S(1)}, u32[]{:S(2)}, u32[]{:S(2)}) collective-permute-start(bf16[16,32,2,128]{3,1,2,0:T(8,128)(2,1)S(1)} %bitcast.344), channel_id=1, source_target_pairs={{0,1},{1,2},{2,3},{4,5},{5,6},{6,7},{8,9},{9,10},{10,11},{12,13},{... | collective-permute-start | bytes 786440 | tf_op jit(solution)/shard_map/ppermute | solution.py:14
  67.7 12.1 %collective-permute-start.12 = (f32[8992]{0:T(1024)S(1)}, f32[8992]{0:T(1024)S(1)}, u32[]{:S(2)}, u32[]{:S(2)}) collective-permute-start(f32[8992]{0:T(1024)S(1)} %add.279), channel_id=1, source_target_pairs={{0,4},{4,0},{8,12},{12,8},{1,5},{5,1},{9,13},{13,9},{2,6},{6,2},{1... | collective-permute-start | bytes 107912 | tf_op jit(solution)/shard_map/ppermute | solution.py:39
  79.8 4.9 %collective-permute-start.13 = (f32[8992]{0:T(1024)S(1)}, f32[8992]{0:T(1024)S(1)}, u32[]{:S(2)}, u32[]{:S(2)}) collective-permute-start(f32[8992]{0:T(1024)S(1)} %add.280), channel_id=1, source_target_pairs={{0,8},{4,12},{8,0},{12,4},{1,9},{5,13},{9,1},{13,5},{2,10},{6,14},... | collective-permute-start | bytes 107912 | tf_op jit(solution)/shard_map/ppermute | solution.py:39
  (29 other events, 39.3 us)

commit v9 on v8

--- a/solution.py
+++ b/solution.py
@@ -47,6 +47,11 @@
     return sig * (1.0 + value * (1.0 - sig))
 
 
+def order_of(inverse, source, chans, n_chan):
+    table = inverse.reshape(chans, n_chan)
+    return lax.dynamic_index_in_dim(table, source, 1, keepdims=False) - source * chans
+
+
 def move_down(array):
     return jnp.pad(array, ((1, 0), (0, 0), (0, 0)))[:-1]
 
@@ -82,27 +87,29 @@
     device = lax.axis_index("chan")
     start = device * chans
     own = lax.dynamic_slice_in_dim(freq_table, start, chans) // n_chan
-    order = jnp.zeros((chans,), jnp.int32).at[own].set(jnp.arange(chans, dtype=jnp.int32))
+    total_chans = freq_table.shape[0]
+    inverse = jnp.zeros((total_chans,), jnp.int32).at[freq_table].set(
+        jnp.arange(total_chans, dtype=jnp.int32)
+    )
+    order = order_of(inverse, device, chans, n_chan)
     h_sorted = hidden_flat[order]
     g_sorted = grad_flat[order]
     h_taps = [h_sorted] * taps
-    h_received = []
     g_taps = [g_sorted] * taps
-    for dist in range(1, half + 1):
-        for sign in (-1, 1):
-            h_far = passed_along(h_sorted, "chan", -sign * dist)
-            h_received.append(h_far)
-            g_far = passed_along(g_sorted, "chan", -sign * dist)
-            if sign < 0:
-                wrapped = device < dist
-                h_near = jnp.where(wrapped, move_down(h_far), h_far)
-                g_near = jnp.where(wrapped, move_down(g_far), g_far)
-            else:
-                wrapped = device + dist >= n_chan
-                h_near = jnp.where(wrapped, move_up(h_far), h_far)
-                g_near = jnp.where(wrapped, move_up(g_far), g_far)
-            h_taps[half + sign * dist] = h_near
-            g_taps[half + sign * dist] = g_near
+    offsets = [(dist, sign) for dist in range(1, half + 1) for sign in (-1, 1)]
+    h_received = [passed_along(h_sorted, "chan", -sign * dist) for dist, sign in offsets]
+    g_received = [passed_along(grad_flat, "chan", -sign * dist) for dist, sign in offsets]
+    g_received, _ = lax.optimization_barrier((g_received, h_received))
+    for (dist, sign), h_far, g_far in zip(offsets, h_received, g_received):
+        g_far = g_far[order_of(inverse, (device + sign * dist) % n_chan, chans, n_chan)]
+        if sign < 0:
+            wrapped = device < dist
+            shift = move_down
+        else:
+            wrapped = device + dist >= n_chan
+            shift = move_up
+        h_taps[half + sign * dist] = jnp.where(wrapped, shift(h_far), h_far)
+        g_taps[half + sign * dist] = jnp.where(wrapped, shift(g_far), g_far)
     h_stack = jnp.stack(h_taps, 1).reshape(chans, taps * feats, pixels)
     g_stack = jnp.stack(g_taps, 1).reshape(chans, taps * feats, pixels)
     fwd_weight = spectral_kernel.transpose(1, 0, 2).reshape(feats, taps * feats)
@@ -145,7 +152,7 @@
     dirty_grad = (cotangent.astype(jnp.float32) + conv).astype(jnp.bfloat16)
     parts = (kernel_term, mix_term, spec_grad)
     flat = jnp.concatenate([part.reshape(-1) for part in parts]) * scale
-    flat = all_summed(flat, ("sub", "tile", "chan"), tied=h_received, tie_at=2)
+    flat = all_summed(flat, ("sub", "tile", "chan"), tied=None)
     sizes = [part.size for part in parts]
     kgrad, mgrad, sgrad = (
         piece.reshape(part.shape)

time: 87.4 us -> 117 us (1.34)
  waiting for transfers between devices: 20.2 us -> 35.5 us
  other arithmetic: 14.1 us -> 28.1 us
  starting transfers between devices: 33.2 us -> 21.3 us
  local copies, waits for them, and re-layouts: 12.3 us -> 23.1 us
    unnamed x11, other arithmetic: 0.6 us -> 11.8 us
    ppermute x6, waiting for transfers between devices: 17.4 us -> 26.1 us  [passed_along(): return lax.ppermute(block, axis, route)]
    ppermute x4, starting transfers between devices: 9.18 us -> 2.28 us  [all_summed(): lax.ppermute(value, axis, [(i, i ^ step) for i in range(count)])]
    ppermute x4, waiting for transfers between devices: 2.73 us -> 9.38 us  [all_summed(): lax.ppermute(value, axis, [(i, i ^ step) for i in range(count)])]
    ppermute x6, starting transfers between devices: 15.7 us -> 10 us  [passed_along(): return lax.ppermute(block, axis, route)]
    gather x0 -> x6, local copies, waits for them, and re-layouts: none -> 5.61 us  [local(): g_far[order_of(inverse, (device + sign * dist) % n_chan, chans, n_chan)]]
    gather x1, local copies, waits for them, and re-layouts: 0.56 us -> 2.23 us  [local(): g_sorted = grad_flat[order]]
    unnamed x130 -> x146, local copies, waits for them, and re-layouts: 2.36 us -> 3.96 us
  transfers between devices with their start and end apart: 14 -> 14, of which waited for: 5 -> 6; matrix products, arithmetic and copies ran while one was open for 15% -> 27% of each run, Pallas kernels for 0% -> 0%
where the time goes in v9:
time: 117 us; the launch traced here: 116 us
  waiting for transfers between devices  35.5 us (30%)
  other arithmetic  28.1 us (24%)
  local copies, waits for them, and re-layouts  23.1 us (20%)
  starting transfers between devices  21.3 us (18%)
  matrix products  6.07 us (5%)
  between operations  1.99 us (2%)
    ppermute x6, waiting for transfers between devices, passed_along(): return lax.ppermute(block, axis, route)  26.1 us
    unnamed x11, other arithmetic  11.8 us
    ppermute x6, starting transfers between devices, passed_along(): return lax.ppermute(block, axis, route)  10 us
    ppermute x4, waiting for transfers between devices, all_summed(): lax.ppermute(value, axis, [(i, i ^ step) for i in range(count)])  9.38 us
    ppermute x2, starting transfers between devices, padded(): lax.ppermute(lax.slice_in_dim(block, block.shape[dim] - width, None, axis...  6.27 us
    gather x6, local copies, waits for them, and re-layouts, local(): g_far[order_of(inverse, (device + sign * dist) % n_chan, chans, n_chan)]  5.61 us
    unnamed x146, local copies, waits for them, and re-layouts  3.96 us
    slice x2, local copies, waits for them, and re-layouts, local(): spatial_kernel[:, i * 5 + j][None, :, None, None]  3.2 us
  transfers between devices with their start and end apart: 14, of which 6 were waited for; matrix products, arithmetic and copies ran while one was open for 27% of the time, Pallas kernels for 0%

profile of v9, /device:TPU:0, one launch (start us, length us, event | category | flops | bytes accessed | tf_op | source)
XLA Modules:
  0.0 116.1 jit_solution(11473866578122877157)
XLA Ops:
  0.6 1.0 copy.27
  1.7 1.3 %collective-permute-start.1 = (bf16[16,32,2,128]{3,1,2,0:T(8,128)(2,1)S(1)}, bf16[16,32,2,128]{3,1,2,0:T(8,128)(2,1)S(1)}, u32[]{:S(2)}, u32[]{:S(2)}) collective-permute-start(bf16[16,32,2,128]{3,1,2,0:T(8,128)(2,1)S(1)} %copy.27), channel_id=1, source_target_pairs={{1,0},{2,1},{3,2},{5,4},{6,5},{7,6},{9,8},{10,9},{11,10},{13,12},{... | collective-permute-start | bytes 786440 | tf_op jit(solution)/shard_map/ppermute | solution.py:17
  3.0 3.0 %collective-permute-start = (bf16[16,32,2,128]{3,1,2,0:T(8,128)(2,1)S(1)}, bf16[16,32,2,128]{3,1,2,0:T(8,128)(2,1)S(1)}, u32[]{:S(2)}, u32[]{:S(2)}) collective-permute-start(bf16[16,32,2,128]{3,1,2,0:T(8,128)(2,1)S(1)} %copy.27), channel_id=1, source_target_pairs={{0,1},{1,2},{2,3},{4,5},{5,6},{6,7},{8,9},{9,10},{10,11},{12,13},{... | collective-permute-start | bytes 786440 | tf_op jit(solution)/shard_map/ppermute | solution.py:14
  6.0 1.8 %reshape.90 = bf16[16,32,256]{2,1,0:T(8,128)(2,1)} reshape(bf16[16,32,2,128]{3,2,1,0:T(2,128)(2,1)} %param.7) | data formatting | bytes 524288 | tf_op jit(solution)/shard_map/reshape | solution.py:86
  7.8 3.0 %collective-permute-start.5 = (bf16[16,32,256]{2,1,0:T(8,128)(2,1)}, bf16[16,32,256]{2,1,0:T(8,128)(2,1)S(1)}, u32[]{:S(2)}, u32[]{:S(2)}) collective-permute-start(bf16[16,32,256]{2,1,0:T(8,128)(2,1)} %reshape.90), channel_id=1, source_target_pairs={{12,0},{0,4},{4,8},{8,12},{13,1},{1,5},{5,9},{9,13},{14,2},{2,6},{... | collective-permute-start | bytes 786440 | tf_op jit(solution)/shard_map/ppermute | solution.py:25
  10.9 2.0 %collective-permute-start.6 = (bf16[16,32,256]{2,1,0:T(8,128)(2,1)}, bf16[16,32,256]{2,1,0:T(8,128)(2,1)S(1)}, u32[]{:S(2)}, u32[]{:S(2)}) collective-permute-start(bf16[16,32,256]{2,1,0:T(8,128)(2,1)} %reshape.90), channel_id=1, source_target_pairs={{4,0},{8,4},{12,8},{0,12},{5,1},{9,5},{13,9},{1,13},{6,2},{10,6},{... | collective-permute-start | bytes 786440 | tf_op jit(solution)/shard_map/ppermute | solution.py:25
  12.9 1.0 collective-permute-start.7
  14.6 0.8 scatter_custom_fusion
  15.4 0.8 fusion.136
  16.9 1.2 %slice_reduce_fusion.23 = (f32[32]{0:T(128)S(1)}, f32[32]{0:T(128)S(1)}, f32[32]{0:T(128)S(1)}, f32[32]{0:T(128)S(1)}, f32[32]{0:T(128)S(1)}, /*index=5*/f32[32]{0:T(128)S(1)}) fusion(f32[32,25]{1,0:T(8,128)} %param.8), kind=kLoop, calls=%fused_computation.299 | loop fusion | bytes 1536 | tf_op jit(solution)/shard_map/slice | solution.py:79
  18.2 2.0 %slice_reduce_fusion.24 = (f32[32]{0:T(128)S(1)}, f32[32]{0:T(128)S(1)}, f32[32]{0:T(128)S(1)}, f32[32]{0:T(128)S(1)}, f32[32]{0:T(128)S(1)}, /*index=5*/f32[32]...) fusion(f32[32,25]{1,0:T(8,128)} %param.8), kind=kLoop, calls=%fused_computation.300 | loop fusion | bytes 4864 | tf_op jit(solution)/shard_map/slice | solution.py:79
  20.4 0.8 select_maximum_fusion.2
  21.5 3.0 %fusion.64 = bf16[16,32,2,128]{3,1,2,0:T(8,128)(2,1)S(1)} fusion(f32[16,32,6,132]{3,1,2,0:T(8,128)S(1)} %get-tuple-element.88, f32[32]{0:T(128)S(1)} %get-tuple-element.78, f32[32]{0:T(128)S(1)} %get-tuple-element.79, f32[32]{0:T(128)S(1)} %get-tuple-element.56, f32[32]{0:T(128)S(1)} %get-tuple-element.57, f32[32]{0:T(128)S(1)} %get-tuple-element.58, ...), kind=kLoop, calls=%fused_computation.135 | loop fusion | flops 6553600 | bytes 13372544 | tf_op jit(solution)/shard_map/convert_element_type | solution.py:82
  24.9 1.3 %gather_fusion = bf16[16,32,256]{2,1,0:T(8,128)(2,1)} fusion(bf16[16,32,256]{2,1,0:T(8,128)(2,1)S(1)} %copy_bitcast_fusion, s32[1024]{0:T(1024)S(1)} %pad_clamp_fusion.7), kind=kCustom, calls=%fused_computation | custom fusion | bytes 524352 | tf_op jit(solution)/shard_map/gather | solution.py:95
  26.2 1.3 %collective-permute-start.2 = (bf16[16,32,256]{2,1,0:T(8,128)(2,1)}, bf16[16,32,256]{2,1,0:T(8,128)(2,1)}, u32[]{:S(2)}, u32[]{:S(2)}) collective-permute-start(bf16[16,32,256]{2,1,0:T(8,128)(2,1)} %gather_fusion), channel_id=1, source_target_pairs={{4,0},{8,4},{12,8},{0,12},{5,1},{9,5},{13,9},{1,13},{6,2},{10,6},{... | collective-permute-start | bytes 786440 | tf_op jit(solution)/shard_map/ppermute | solution.py:25
  27.5 1.7 %collective-permute-start.3 = (bf16[16,32,256]{2,1,0:T(8,128)(2,1)}, bf16[16,32,256]{2,1,0:T(8,128)(2,1)}, u32[]{:S(2)}, u32[]{:S(2)}) collective-permute-start(bf16[16,32,256]{2,1,0:T(8,128)(2,1)} %gather_fusion), channel_id=1, source_target_pairs={{8,0},{12,4},{0,8},{4,12},{9,1},{13,5},{1,9},{5,13},{10,2},{14,6},... | collective-permute-start | bytes 786440 | tf_op jit(solution)/shard_map/ppermute | solution.py:25
  29.2 0.9 collective-permute-start.4
  30.1 2.2 %gather_fusion.5 = bf16[16,32,256]{2,1,0:T(8,128)(2,1)} fusion(bf16[16,32,256]{2,1,0:T(8,128)(2,1)} %reshape.90, s32[1024]{0:T(1024)S(1)} %pad_clamp_fusion.7), kind=kCustom, calls=%fused_computation.5 | custom fusion | bytes 524352 | tf_op jit(solution)/shard_map/gather | solution.py:96
  33.6 3.8 %collective-permute-done.7 = bf16[16,32,256]{2,1,0:T(8,128)(2,1)S(1)} collective-permute-done((bf16[16,32,256]{2,1,0:T(8,128)(2,1)}, bf16[16,32,256]{2,1,0:T(8,128)(2,1)S(1)}, u32[]{:S(2)}, u32[]{:S(2)}) %collective-permute-start.7) | collective-permute-done | bytes 262176 | tf_op jit(solution)/shard_map/ppermute | solution.py:25
  37.4 3.0 %collective-permute-done.2 = bf16[16,32,256]{2,1,0:T(8,128)(2,1)} collective-permute-done((bf16[16,32,256]{2,1,0:T(8,128)(2,1)}, bf16[16,32,256]{2,1,0:T(8,128)(2,1)}, u32[]{:S(2)}, u32[]{:S(2)}) %collective-permute-start.2) | collective-permute-done | bytes 262176 | tf_op jit(solution)/shard_map/ppermute | solution.py:25
  40.4 19.3 %collective-permute-done.3 = bf16[16,32,256]{2,1,0:T(8,128)(2,1)} collective-permute-done((bf16[16,32,256]{2,1,0:T(8,128)(2,1)}, bf16[16,32,256]{2,1,0:T(8,128)(2,1)}, u32[]{:S(2)}, u32[]{:S(2)}) %collective-permute-start.3) | collective-permute-done | bytes 262176 | tf_op jit(solution)/shard_map/ppermute | solution.py:25
  59.7 1.3 %gather_fusion.2 = bf16[16,32,256]{2,1,0:T(8,128)(2,1)} fusion(bf16[16,32,256]{2,1,0:T(8,128)(2,1)S(1)} %collective-permute-done.6, s32[1024]{0:T(1024)S(1)} %get-tuple-element.95), kind=kCustom, calls=%fused_computation.2 | custom fusion | bytes 524352 | tf_op jit(solution)/shard_map/gather | solution.py:104
  61.0 1.9 %fusion.108 = bf16[16,7,32,256]{3,2,0,1:T(8,128)(2,1)} fusion(bf16[16,32,256]{2,1,0:T(8,128)(2,1)} %gather_fusion.2, pred[]{:T(512)S(6)} %lt.96), kind=kLoop, calls=%fused_computation.220 | loop fusion | flops 131071 | bytes 524289
  62.9 1.3 %gather_fusion.3 = bf16[16,32,256]{2,1,0:T(8,128)(2,1)} fusion(bf16[16,32,256]{2,1,0:T(8,128)(2,1)S(1)} %collective-permute-done.7, s32[1024]{0:T(1024)S(1)} %get-tuple-element.94), kind=kCustom, calls=%fused_computation.3 | custom fusion | bytes 524352 | tf_op jit(solution)/shard_map/gather | solution.py:104
  64.1 1.4 %gather_fusion.4 = bf16[16,32,256]{2,1,0:T(8,128)(2,1)} fusion(bf16[16,32,256]{2,1,0:T(8,128)(2,1)S(1)} %collective-permute-done.5, s32[1024]{0:T(1024)} %get-tuple-element.93), kind=kCustom, calls=%fused_computation.4 | custom fusion | bytes 524352 | tf_op jit(solution)/shard_map/gather | solution.py:104
  65.5 1.9 %fusion.111 = bf16[16,7,32,256]{3,2,0,1:T(8,128)(2,1)} fusion(bf16[16,7,32,256]{3,2,0,1:T(8,128)(2,1)} %fusion.108, bf16[16,32,256]{2,1,0:T(8,128)(2,1)} %gather_fusion.3, pred[]{:T(512)S(6)} %lt.100), kind=kLoop, calls=%fused_computation.223 | loop fusion | flops 131072 | bytes 524289
  67.4 1.9 %fusion.114 = bf16[16,7,32,256]{3,2,0,1:T(8,128)(2,1)} fusion(bf16[16,7,32,256]{3,2,0,1:T(8,128)(2,1)} %fusion.111, bf16[16,32,256]{2,1,0:T(8,128)(2,1)} %gather_fusion.4, pred[]{:T(512)S(6)} %lt.101), kind=kLoop, calls=%fused_computation.226 | loop fusion | flops 131072 | bytes 524289
  69.2 1.7 %bitcast_dynamic-update-slice_fusion.1 = bf16[16,7,32,256]{3,2,0,1:T(8,128)(2,1)} fusion(bf16[16,7,32,256]{3,2,0,1:T(8,128)(2,1)} %fusion.114, bf16[16,32,256]{2,1,0:T(8,128)(2,1)} %gather_fusion.5), kind=kLoop, calls=%fused_computation.264 | loop fusion | bytes 524288
  72.6 0.8 fusion.117
  73.4 0.8 fusion.120
  74.9 2.0 %fusion.8 = bf16[16,32,256]{2,1,0:T(8,128)(2,1)S(1)} fusion(bf16[16,7,32,256]{3,2,0,1:T(8,128)(2,1)} %fusion.123, bf16[7,32,32]{2,1,0:T(8,128)(2,1)S(1)} %rev.6), kind=kOutput, calls=%fused_computation.53 | convolution fusion | flops 58851328 | bytes 2111488 | tf_op jit(solution)/shard_map/fK,mKp->mfp/dot_general | solution.py:118
  77.7 2.5 %fusion.34 = (f32[32]{0:T(128)}, f32[32]{0:T(128)}, f32[32]{0:T(128)}, f32[32]{0:T(128)}, f32[32]{0:T(128)}, /*index=5*/f32[32]{0:T(128)}, bf16[16,2,128,32]{2,3,1,0:T(8,128)(2,1)S(1)}) fusion(bf16[16,32,6,132]{3,1,2,0:T(8,128)(2,1)S(1)} %get-tuple-element.87, bf16[16,32,2,128]{3,1,2,0:T(8,128)(2,1)} %copy-done.10, ...), kind=kOutput, calls=%fused_computation.78 | convolution fusion | flops 11272000 | bytes 1837824 | tf_op jit(solution)/shard_map/gf,cghw->cfhw/dot_general | solution.py:129
  80.2 1.4 %collective-permute-start.9 = (bf16[16,32,2,128]{3,1,2,0:T(8,128)(2,1)S(1)}, bf16[16,32,2,128]{3,1,2,0:T(8,128)(2,1)S(1)}, u32[]{:S(2)}, u32[]{:S(2)}) collective-permute-start(bf16[16,32,2,128]{3,1,2,0:T(8,128)(2,1)S(1)} %bitcast.338), channel_id=1, source_target_pairs={{1,0},{2,1},{3,2},{5,4},{6,5},{7,6},{9,8},{10,9},{11,10},{13,12},{... | collective-permute-start | bytes 786440 | tf_op jit(solution)/shard_map/ppermute | solution.py:17
  81.6 3.2 %collective-permute-start.8 = (bf16[16,32,2,128]{3,1,2,0:T(8,128)(2,1)S(1)}, bf16[16,32,2,128]{3,1,2,0:T(8,128)(2,1)S(1)}, u32[]{:S(2)}, u32[]{:S(2)}) collective-permute-start(bf16[16,32,2,128]{3,1,2,0:T(8,128)(2,1)S(1)} %bitcast.339), channel_id=1, source_target_pairs={{0,1},{1,2},{2,3},{4,5},{5,6},{6,7},{8,9},{9,10},{10,11},{12,13},{... | collective-permute-start | bytes 786440 | tf_op jit(solution)/shard_map/ppermute | solution.py:14
  84.9 2.4 %fusion.35 = (f32[32]{0:T(128)S(1)}, f32[32]{0:T(128)S(1)}, f32[32]{0:T(128)S(1)}, f32[32]{0:T(128)S(1)}, f32[32]{0:T(128)S(1)}, /*index=5*/f32[32]{0:T(128)S(1)...) fusion(bf16[16,32,6,132]{3,1,2,0:T(8,128)(2,1)S(1)} %get-tuple-, ...), kind=kLoop, calls=%fused_computation.79 | loop fusion | flops 7208384 | bytes 4983040 | tf_op jit(solution)/shard_map/cfhw,cfhw->f/dot_general | solution.py:144
  88.2 1.2 fusion.90
  89.4 1.2 fusion.93
  90.7 0.8 multiply_reduce_fusion
  92.1 1.4 %collective-permute-start.10 = (f32[8992]{0:T(1024)S(1)}, f32[8992]{0:T(1024)S(1)}, u32[]{:S(2)}, u32[]{:S(2)}) collective-permute-start(f32[8992]{0:T(1024)S(1)} %broadcast_multiply_fusion), channel_id=1, source_target_pairs={{0,1},{1,0},{2,3},{3,2},{4,5},{5,4},{6,7},{7,6},{8,9},{9,8},{10,11... | collective-permute-start | bytes 107912 | tf_op jit(solution)/shard_map/ppermute | solution.py:39
  93.4 1.2 fusion.99
  94.6 1.2 fusion.102
  95.9 3.9 %collective-permute-done.11 = f32[8992]{0:T(1024)S(1)} collective-permute-done((f32[8992]{0:T(1024)S(1)}, f32[8992]{0:T(1024)S(1)}, u32[]{:S(2)}, u32[]{:S(2)}) %collective-permute-start.11) | collective-permute-done | bytes 36000 | tf_op jit(solution)/shard_map/ppermute | solution.py:39
  101.3 2.5 %collective-permute-done.12 = f32[8992]{0:T(1024)S(1)} collective-permute-done((f32[8992]{0:T(1024)S(1)}, f32[8992]{0:T(1024)S(1)}, u32[]{:S(2)}, u32[]{:S(2)}) %collective-permute-start.12) | collective-permute-done | bytes 36000 | tf_op jit(solution)/shard_map/ppermute | solution.py:39
  103.8 0.9 collective-permute-start.13
  104.6 1.0 add_convert_fusion
  105.6 3.0 %collective-permute-done.13 = f32[8992]{0:T(1024)S(1)} collective-permute-done((f32[8992]{0:T(1024)S(1)}, f32[8992]{0:T(1024)S(1)}, u32[]{:S(2)}, u32[]{:S(2)}) %collective-permute-start.13) | collective-permute-done | bytes 36000 | tf_op jit(solution)/shard_map/ppermute | solution.py:39
  112.1 3.0 %fusion.39 = bf16[16,32,2,128]{3,1,2,0:T(8,128)(2,1)S(1)} fusion(f32[16,32,6,132]{3,1,2,0:T(8,128)S(1)} %fusion.3, bf16[16,32,2,128]{3,2,1,0:T(2,128)(2,1)S(1)} %copy-done.3, f32[32]{0:T(128)S(1)} %copy-done.21, f32[32]{0:T(128)S(1)} %copy-done.23, f32[32]{0:T(128)S(1)} %copy-done.27, f32[32]{0:T(128)S(1)} %copy-done.29, f32[32]{0:T(128)S(1)} %copy-done.31, ...), kind=kLoop, calls=%fused_computation.85 | loop fusion | flops 6815744 | bytes 13634688 | tf_op jit(solution)/shard_map/convert_element_type | solution.py:152
  115.2 0.9 copy.48
  (198 shorter events, 12.7 us)
Async XLA Ops:
  0.6 23.9 %copy-start = (bf16[32,32]{1,0:T(8,128)(2,1)S(1)}, bf16[32,32]{1,0:T(8,128)(2,1)}, u32[]{:S(2)}) copy-start(bf16[32,32]{1,0:T(8,128)(2,1)} %param.9) | copy-start | bytes 6148
  1.7 19.6 %copy-start.7 = (bf16[16,32,2,128]{3,1,2,0:T(8,128)(2,1)}, bf16[16,32,2,128]{3,1,2,0:T(8,128)(2,1)S(1)}, u32[]{:S(2)}) copy-start(bf16[16,32,2,128]{3,1,2,0:T(8,128)(2,1)S(1)} %copy.27) | copy-start | bytes 786436
  1.7 18.7 %collective-permute-start.1 = (bf16[16,32,2,128]{3,1,2,0:T(8,128)(2,1)S(1)}, bf16[16,32,2,128]{3,1,2,0:T(8,128)(2,1)S(1)}, u32[]{:S(2)}, u32[]{:S(2)}) collective-permute-start(bf16[16,32,2,128]{3,1,2,0:T(8,128)(2,1)S(1)} %copy.27), channel_id=1, source_target_pairs={{1,0},{2,1},{3,2},{5,4},{6,5},{7,6},{9,8},{10,9},{11,10},{13,12},{... | collective-permute-start | bytes 786440 | tf_op jit(solution)/shard_map/ppermute | solution.py:17
  3.0 17.5 %collective-permute-start = (bf16[16,32,2,128]{3,1,2,0:T(8,128)(2,1)S(1)}, bf16[16,32,2,128]{3,1,2,0:T(8,128)(2,1)S(1)}, u32[]{:S(2)}, u32[]{:S(2)}) collective-permute-start(bf16[16,32,2,128]{3,1,2,0:T(8,128)(2,1)S(1)} %copy.27), channel_id=1, source_target_pairs={{0,1},{1,2},{2,3},{4,5},{5,6},{6,7},{8,9},{9,10},{10,11},{12,13},{... | collective-permute-start | bytes 786440 | tf_op jit(solution)/shard_map/ppermute | solution.py:14
  7.8 21.4 %collective-permute-start.5 = (bf16[16,32,256]{2,1,0:T(8,128)(2,1)}, bf16[16,32,256]{2,1,0:T(8,128)(2,1)S(1)}, u32[]{:S(2)}, u32[]{:S(2)}) collective-permute-start(bf16[16,32,256]{2,1,0:T(8,128)(2,1)} %reshape.90), channel_id=1, source_target_pairs={{12,0},{0,4},{4,8},{8,12},{13,1},{1,5},{5,9},{9,13},{14,2},{2,6},{... | collective-permute-start | bytes 786440 | tf_op jit(solution)/shard_map/ppermute | solution.py:25
  10.9 22.8 %collective-permute-start.6 = (bf16[16,32,256]{2,1,0:T(8,128)(2,1)}, bf16[16,32,256]{2,1,0:T(8,128)(2,1)S(1)}, u32[]{:S(2)}, u32[]{:S(2)}) collective-permute-start(bf16[16,32,256]{2,1,0:T(8,128)(2,1)} %reshape.90), channel_id=1, source_target_pairs={{4,0},{8,4},{12,8},{0,12},{5,1},{9,5},{13,9},{1,13},{6,2},{10,6},{... | collective-permute-start | bytes 786440 | tf_op jit(solution)/shard_map/ppermute | solution.py:25
  12.9 24.5 %collective-permute-start.7 = (bf16[16,32,256]{2,1,0:T(8,128)(2,1)}, bf16[16,32,256]{2,1,0:T(8,128)(2,1)S(1)}, u32[]{:S(2)}, u32[]{:S(2)}) collective-permute-start(bf16[16,32,256]{2,1,0:T(8,128)(2,1)} %reshape.90), channel_id=1, source_target_pairs={{8,0},{12,4},{0,8},{4,12},{9,1},{13,5},{1,9},{5,13},{10,2},{14,6},... | collective-permute-start | bytes 786440 | tf_op jit(solution)/shard_map/ppermute | solution.py:25
  18.2 3.1 %copy-start.12 = (f32[32]{0:T(128)}, f32[32]{0:T(128)S(1)}, u32[]{:S(2)}) copy-start(f32[32]{0:T(128)S(1)} %get-tuple-element.74) | copy-start | bytes 388
  18.2 3.1 %copy-start.14 = (f32[32]{0:T(128)}, f32[32]{0:T(128)S(1)}, u32[]{:S(2)}) copy-start(f32[32]{0:T(128)S(1)} %get-tuple-element.75) | copy-start | bytes 388
  18.2 3.1 %copy-start.16 = (f32[32]{0:T(128)}, f32[32]{0:T(128)S(1)}, u32[]{:S(2)}) copy-start(f32[32]{0:T(128)S(1)} %get-tuple-element.76) | copy-start | bytes 388
  18.2 3.1 %copy-start.18 = (f32[32]{0:T(128)}, f32[32]{0:T(128)S(1)}, u32[]{:S(2)}) copy-start(f32[32]{0:T(128)S(1)} %get-tuple-element.77) | copy-start | bytes 388
  18.2 3.1 %copy-start.20 = (f32[32]{0:T(128)}, f32[32]{0:T(128)S(1)}, u32[]{:S(2)}) copy-start(f32[32]{0:T(128)S(1)} %get-tuple-element.78) | copy-start | bytes 388
  18.2 3.1 %copy-start.22 = (f32[32]{0:T(128)}, f32[32]{0:T(128)S(1)}, u32[]{:S(2)}) copy-start(f32[32]{0:T(128)S(1)} %get-tuple-element.79) | copy-start | bytes 388
  20.2 1.1 copy-start.26
  20.2 1.1 copy-start.28
  20.2 1.1 copy-start.30
  20.2 1.1 copy-start.32
  20.3 1.1 copy-start.34
  20.3 1.1 copy-start.36
  20.3 1.1 copy-start.38
  20.3 1.1 copy-start.40
  20.3 1.1 copy-start.42
  20.3 1.1 copy-start.44
  24.5 7.8 %copy-start.11 = (bf16[7,32,32]{2,1,0:T(8,128)(2,1)S(1)}, bf16[7,32,32]{2,1,0:T(8,128)(2,1)}, u32[]{:S(2)}) copy-start(bf16[7,32,32]{2,1,0:T(8,128)(2,1)} %param.10) | copy-start | bytes 43012
  26.2 14.3 %collective-permute-start.2 = (bf16[16,32,256]{2,1,0:T(8,128)(2,1)}, bf16[16,32,256]{2,1,0:T(8,128)(2,1)}, u32[]{:S(2)}, u32[]{:S(2)}) collective-permute-start(bf16[16,32,256]{2,1,0:T(8,128)(2,1)} %gather_fusion), channel_id=1, source_target_pairs={{4,0},{8,4},{12,8},{0,12},{5,1},{9,5},{13,9},{1,13},{6,2},{10,6},{... | collective-permute-start | bytes 786440 | tf_op jit(solution)/shard_map/ppermute | solution.py:25
  27.5 32.2 %collective-permute-start.3 = (bf16[16,32,256]{2,1,0:T(8,128)(2,1)}, bf16[16,32,256]{2,1,0:T(8,128)(2,1)}, u32[]{:S(2)}, u32[]{:S(2)}) collective-permute-start(bf16[16,32,256]{2,1,0:T(8,128)(2,1)} %gather_fusion), channel_id=1, source_target_pairs={{8,0},{12,4},{0,8},{4,12},{9,1},{13,5},{1,9},{5,13},{10,2},{14,6},... | collective-permute-start | bytes 786440 | tf_op jit(solution)/shard_map/ppermute | solution.py:25
  29.2 30.5 %collective-permute-start.4 = (bf16[16,32,256]{2,1,0:T(8,128)(2,1)}, bf16[16,32,256]{2,1,0:T(8,128)(2,1)S(1)}, u32[]{:S(2)}, u32[]{:S(2)}) collective-permute-start(bf16[16,32,256]{2,1,0:T(8,128)(2,1)} %gather_fusion), channel_id=1, source_target_pairs={{12,0},{0,4},{4,8},{8,12},{13,1},{1,5},{5,9},{9,13},{14,2},{2,6},{... | collective-permute-start | bytes 786440 | tf_op jit(solution)/shard_map/ppermute | solution.py:25
  59.7 11.2 %copy-start.4 = (bf16[16,32,256]{2,1,0:T(8,128)(2,1)}, bf16[16,32,256]{2,1,0:T(8,128)(2,1)S(1)}, u32[]{:S(2)}) copy-start(bf16[16,32,256]{2,1,0:T(8,128)(2,1)S(1)} %collective-permute-done.4) | copy-start | bytes 786436
  74.9 2.8 %copy-start.8 = (bf16[16,32,2,128]{3,1,2,0:T(8,128)(2,1)S(1)}, bf16[16,32,2,128]{3,1,2,0:T(8,128)(2,1)}, u32[]{:S(2)}) copy-start(bf16[16,32,2,128]{3,1,2,0:T(8,128)(2,1)} %copy-done.7) | copy-start | bytes 786436
  80.2 7.3 %copy-start.1 = (bf16[16,7,32,256]{3,2,0,1:T(8,128)(2,1)S(1)}, bf16[16,7,32,256]{3,2,0,1:T(8,128)(2,1)}, u32[]{:S(2)}) copy-start(bf16[16,7,32,256]{3,2,0,1:T(8,128)(2,1)} %fusion.123) | copy-start | bytes 5505028
  80.2 7.3 %copy-start.6 = (bf16[16,32,256]{2,1,0:T(8,128)(2,1)S(1)}, bf16[16,32,256]{2,1,0:T(8,128)(2,1)}, u32[]{:S(2)}) copy-start(bf16[16,32,256]{2,1,0:T(8,128)(2,1)} %gather_fusion) | copy-start | bytes 786436
  80.2 30.9 %collective-permute-start.9 = (bf16[16,32,2,128]{3,1,2,0:T(8,128)(2,1)S(1)}, bf16[16,32,2,128]{3,1,2,0:T(8,128)(2,1)S(1)}, u32[]{:S(2)}, u32[]{:S(2)}) collective-permute-start(bf16[16,32,2,128]{3,1,2,0:T(8,128)(2,1)S(1)} %bitcast.338), channel_id=1, source_target_pairs={{1,0},{2,1},{3,2},{5,4},{6,5},{7,6},{9,8},{10,9},{11,10},{13,12},{... | collective-permute-start | bytes 786440 | tf_op jit(solution)/shard_map/ppermute | solution.py:17
  81.6 29.5 %collective-permute-start.8 = (bf16[16,32,2,128]{3,1,2,0:T(8,128)(2,1)S(1)}, bf16[16,32,2,128]{3,1,2,0:T(8,128)(2,1)S(1)}, u32[]{:S(2)}, u32[]{:S(2)}) collective-permute-start(bf16[16,32,2,128]{3,1,2,0:T(8,128)(2,1)S(1)} %bitcast.339), channel_id=1, source_target_pairs={{0,1},{1,2},{2,3},{4,5},{5,6},{6,7},{8,9},{9,10},{10,11},{12,13},{... | collective-permute-start | bytes 786440 | tf_op jit(solution)/shard_map/ppermute | solution.py:14
  87.3 3.3 %copy-start.5 = (bf16[16,32,256]{2,1,0:T(8,128)(2,1)S(1)}, bf16[16,32,256]{2,1,0:T(8,128)(2,1)}, u32[]{:S(2)}) copy-start(bf16[16,32,256]{2,1,0:T(8,128)(2,1)} %copy-done.4) | copy-start | bytes 786436
  87.5 3.1 %copy-start.2 = (bf16[16,32,2,128]{3,2,1,0:T(2,128)(2,1)S(1)}, bf16[16,32,2,128]{3,2,1,0:T(2,128)(2,1)}, u32[]{:S(2)}) copy-start(bf16[16,32,2,128]{3,2,1,0:T(2,128)(2,1)} %param.6) | copy-start | bytes 786436
  88.1 3.3 %copy-start.62 = (f32[32]{0:T(128)S(1)}, f32[32]{0:T(128)}, u32[]{:S(2)}) copy-start(f32[32]{0:T(128)} %get-tuple-element.42) | copy-start | bytes 388
  88.1 3.3 %copy-start.63 = (f32[32]{0:T(128)S(1)}, f32[32]{0:T(128)}, u32[]{:S(2)}) copy-start(f32[32]{0:T(128)} %get-tuple-element.43) | copy-start | bytes 388
  88.1 3.3 %copy-start.64 = (f32[32]{0:T(128)S(1)}, f32[32]{0:T(128)}, u32[]{:S(2)}) copy-start(f32[32]{0:T(128)} %get-tuple-element.44) | copy-start | bytes 388
  88.2 3.3 %copy-start.65 = (f32[32]{0:T(128)S(1)}, f32[32]{0:T(128)}, u32[]{:S(2)}) copy-start(f32[32]{0:T(128)} %get-tuple-element.45) | copy-start | bytes 388
  88.2 3.3 %copy-start.66 = (f32[32]{0:T(128)S(1)}, f32[32]{0:T(128)}, u32[]{:S(2)}) copy-start(f32[32]{0:T(128)} %get-tuple-element.46) | copy-start | bytes 388
  88.2 3.3 %copy-start.67 = (f32[32]{0:T(128)S(1)}, f32[32]{0:T(128)}, u32[]{:S(2)}) copy-start(f32[32]{0:T(128)} %get-tuple-element.51) | copy-start | bytes 388
  88.2 3.3 %copy-start.68 = (f32[32]{0:T(128)S(1)}, f32[32]{0:T(128)}, u32[]{:S(2)}) copy-start(f32[32]{0:T(128)} %get-tuple-element.52) | copy-start | bytes 388
  88.2 3.3 %copy-start.69 = (f32[32]{0:T(128)S(1)}, f32[32]{0:T(128)}, u32[]{:S(2)}) copy-start(f32[32]{0:T(128)} %get-tuple-element.53) | copy-start | bytes 388
  88.2 3.3 %copy-start.70 = (f32[32]{0:T(128)S(1)}, f32[32]{0:T(128)}, u32[]{:S(2)}) copy-start(f32[32]{0:T(128)} %get-tuple-element.54) | copy-start | bytes 388
  92.1 3.7 %collective-permute-start.10 = (f32[8992]{0:T(1024)S(1)}, f32[8992]{0:T(1024)S(1)}, u32[]{:S(2)}, u32[]{:S(2)}) collective-permute-start(f32[8992]{0:T(1024)S(1)} %broadcast_multiply_fusion), channel_id=1, source_target_pairs={{0,1},{1,0},{2,3},{3,2},{4,5},{5,4},{6,7},{7,6},{8,9},{9,8},{10,11... | collective-permute-start | bytes 107912 | tf_op jit(solution)/shard_map/ppermute | solution.py:39
  95.8 4.0 %collective-permute-start.11 = (f32[8992]{0:T(1024)S(1)}, f32[8992]{0:T(1024)S(1)}, u32[]{:S(2)}, u32[]{:S(2)}) collective-permute-start(f32[8992]{0:T(1024)S(1)} %fusion.141), channel_id=1, source_target_pairs={{0,2},{2,0},{1,3},{3,1},{4,6},{6,4},{5,7},{7,5},{8,10},{10,8},{9,1... | collective-permute-start | bytes 107912 | tf_op jit(solution)/shard_map/ppermute | solution.py:39
  99.8 4.0 %collective-permute-start.12 = (f32[8992]{0:T(1024)S(1)}, f32[8992]{0:T(1024)S(1)}, u32[]{:S(2)}, u32[]{:S(2)}) collective-permute-start(f32[8992]{0:T(1024)S(1)} %add.386), channel_id=1, source_target_pairs={{0,4},{4,0},{8,12},{12,8},{1,5},{5,1},{9,13},{13,9},{2,6},{6,2},{1... | collective-permute-start | bytes 107912 | tf_op jit(solution)/shard_map/ppermute | solution.py:39
  103.8 4.9 %collective-permute-start.13 = (f32[8992]{0:T(1024)S(1)}, f32[8992]{0:T(1024)S(1)}, u32[]{:S(2)}, u32[]{:S(2)}) collective-permute-start(f32[8992]{0:T(1024)S(1)} %add.387), channel_id=1, source_target_pairs={{0,8},{4,12},{8,0},{12,4},{1,9},{5,13},{9,1},{13,5},{2,10},{6,14},... | collective-permute-start | bytes 107912 | tf_op jit(solution)/shard_map/ppermute | solution.py:39
  (37 other events, 37.0 us)

commit v10 on v8

--- a/solution.py
+++ b/solution.py
@@ -25,7 +25,7 @@
     return lax.ppermute(block, axis, route)
 
 
-def all_summed(value, axes, tied=None, tie_at=0):
+def all_summed(value, axes, ties=()):
     done = 0
     for axis in axes:
         count = lax.axis_size(axis)
@@ -34,8 +34,9 @@
             continue
         step = 1
         while step < count:
-            if tied is not None and done == tie_at:
-                value, _ = lax.optimization_barrier((value, tied))
+            for position, tied in ties:
+                if done == position:
+                    value, _ = lax.optimization_barrier((value, tied))
             value = value + lax.ppermute(value, axis, [(i, i ^ step) for i in range(count)])
             step *= 2
             done += 1
@@ -145,7 +146,7 @@
     dirty_grad = (cotangent.astype(jnp.float32) + conv).astype(jnp.bfloat16)
     parts = (kernel_term, mix_term, spec_grad)
     flat = jnp.concatenate([part.reshape(-1) for part in parts]) * scale
-    flat = all_summed(flat, ("sub", "tile", "chan"), tied=h_received, tie_at=2)
+    flat = all_summed(flat, ("sub", "tile", "chan"), ties=((2, grad_ext), (3, h_received)))
     sizes = [part.size for part in parts]
     kgrad, mgrad, sgrad = (
         piece.reshape(part.shape)

time: 87.4 us -> 89.3 us (1.022); the launches traced: 87 us -> 87.9 us
  waiting for transfers between devices: 20.2 us -> 21.3 us
    ppermute x6, waiting for transfers between devices: 17.4 us -> 21.3 us  [passed_along(): return lax.ppermute(block, axis, route)]
    ppermute x4, waiting for transfers between devices: 2.73 us -> 0.01 us  [all_summed(): lax.ppermute(value, axis, [(i, i ^ step) for i in range(count)])]
    ppermute x4, starting transfers between devices: 9.18 us -> 7.02 us  [all_summed(): lax.ppermute(value, axis, [(i, i ^ step) for i in range(count)])]
    convert_element_type x0 -> x1, other arithmetic: none -> 1.72 us  [local(): xpad32 = xpad.astype(jnp.float32)]
    concatenate x1, other arithmetic: 1.72 us -> 0.09 us  [padded(): block = jnp.concatenate([low, block, high], axis=dim)]
    ppermute x6, starting transfers between devices: 15.7 us -> 16.8 us  [passed_along(): return lax.ppermute(block, axis, route)]
    ppermute x2, starting transfers between devices: 5.79 us -> 6.78 us  [padded(): lax.ppermute(lax.slice_in_dim(block, block.shape[dim] - width, None, axis...]
    unnamed x130 -> x122, local copies, waits for them, and re-layouts: 2.36 us -> 2.24 us
  transfers between devices with their start and end apart: 14 -> 14, of which waited for: 5 -> 4; matrix products, arithmetic and copies ran while one was open for 15% -> 14% of each run, Pallas kernels for 0% -> 0%
where the time goes in v10:
time: 89.3 us; the launch traced here: 87.9 us
  starting transfers between devices  33.2 us (37%)
  waiting for transfers between devices  21.3 us (24%)
  other arithmetic  14 us (16%)
  local copies, waits for them, and re-layouts  12.2 us (14%)
  matrix products  5.31 us (6%)
  between operations  1.92 us (2%)
    ppermute x6, waiting for transfers between devices, passed_along(): return lax.ppermute(block, axis, route)  21.3 us
    ppermute x6, starting transfers between devices, passed_along(): return lax.ppermute(block, axis, route)  16.8 us
    ppermute x4, starting transfers between devices, all_summed(): lax.ppermute(value, axis, [(i, i ^ step) for i in range(count)])  7.02 us
    ppermute x2, starting transfers between devices, padded(): lax.ppermute(lax.slice_in_dim(block, block.shape[dim] - width, None, axis...  6.78 us
    dot_general x2, other arithmetic, local(): jnp.einsum('cfhw,cfhw->f', dsmooth, xpad[:, :, i:i + rows, j:j + cols], p...  3.07 us
    convert_element_type x1, other arithmetic, local(): dirty_grad = (cotangent.astype(jnp.float32) + conv).astype(jnp.bfloat16)  3.04 us
    convert_element_type x1, other arithmetic, local(): smooth = total.astype(jnp.bfloat16)  3.03 us
    slice x2, local copies, waits for them, and re-layouts, local(): spatial_kernel[:, i * 5 + j][None, :, None, None]  2.81 us
  transfers between devices with their start and end apart: 14, of which 4 were waited for; matrix products, arithmetic and copies ran while one was open for 14% of the time, Pallas kernels for 0%

profile of v10, /device:TPU:0, one launch (start us, length us, event | category | flops | bytes accessed | tf_op | source)
XLA Modules:
  0.0 87.9 jit_solution(5767425018560110208)
XLA Ops:
  0.7 0.8 compare_select_fusion.1
  1.4 0.6 scatter_custom_fusion
  2.1 1.1 %reshape.80 = bf16[16,32,256]{2,1,0:T(8,128)(2,1)S(1)} reshape(bf16[16,32,2,128]{3,2,1,0:T(2,128)(2,1)} %param.7) | data formatting | bytes 524288 | tf_op jit(solution)/shard_map/reshape | solution.py:82
  3.2 0.6 gather_fusion.2
  3.8 3.1 %collective-permute-start.7 = (bf16[16,32,256]{2,1,0:T(8,128)(2,1)S(1)}, bf16[16,32,256]{2,1,0:T(8,128)(2,1)S(1)}, u32[]{:S(2)}, u32[]{:S(2)}) collective-permute-start(bf16[16,32,256]{2,1,0:T(8,128)(2,1)S(1)} %gather_fusion.2), channel_id=1, source_target_pairs={{12,0},{0,4},{4,8},{8,12},{13,1},{1,5},{5,9},{9,13},{14,2},{2,6},{... | collective-permute-start | bytes 786440 | tf_op jit(solution)/shard_map/ppermute | solution.py:25
  6.9 2.6 %collective-permute-start.6 = (bf16[16,32,256]{2,1,0:T(8,128)(2,1)S(1)}, bf16[16,32,256]{2,1,0:T(8,128)(2,1)S(1)}, u32[]{:S(2)}, u32[]{:S(2)}) collective-permute-start(bf16[16,32,256]{2,1,0:T(8,128)(2,1)S(1)} %gather_fusion.2), channel_id=1, source_target_pairs={{8,0},{12,4},{0,8},{4,12},{9,1},{13,5},{1,9},{5,13},{10,2},{14,6},... | collective-permute-start | bytes 786440 | tf_op jit(solution)/shard_map/ppermute | solution.py:25
  9.5 1.3 %collective-permute-start.5 = (bf16[16,32,256]{2,1,0:T(8,128)(2,1)S(1)}, bf16[16,32,256]{2,1,0:T(8,128)(2,1)S(1)}, u32[]{:S(2)}, u32[]{:S(2)}) collective-permute-start(bf16[16,32,256]{2,1,0:T(8,128)(2,1)S(1)} %gather_fusion.2), channel_id=1, source_target_pairs={{4,0},{8,4},{12,8},{0,12},{5,1},{9,5},{13,9},{1,13},{6,2},{10,6},{... | collective-permute-start | bytes 786440 | tf_op jit(solution)/shard_map/ppermute | solution.py:25
  10.8 1.0 %copy.27 = bf16[16,32,2,128]{3,1,2,0:T(8,128)(2,1)S(1)} copy(bf16[16,32,2,128]{3,2,1,0:T(2,128)(2,1)} %param.6) | data formatting | bytes 524288 | tf_op args[0]
  11.8 1.3 %collective-permute-start.1 = (bf16[16,32,2,128]{3,1,2,0:T(8,128)(2,1)S(1)}, bf16[16,32,2,128]{3,1,2,0:T(8,128)(2,1)S(1)}, u32[]{:S(2)}, u32[]{:S(2)}) collective-permute-start(bf16[16,32,2,128]{3,1,2,0:T(8,128)(2,1)S(1)} %copy.27), channel_id=1, source_target_pairs={{1,0},{2,1},{3,2},{5,4},{6,5},{7,6},{9,8},{10,9},{11,10},{13,12},{... | collective-permute-start | bytes 786440 | tf_op jit(solution)/shard_map/ppermute | solution.py:17
  13.1 3.7 %collective-permute-start = (bf16[16,32,2,128]{3,1,2,0:T(8,128)(2,1)S(1)}, bf16[16,32,2,128]{3,1,2,0:T(8,128)(2,1)}, u32[]{:S(2)}, u32[]{:S(2)}) collective-permute-start(bf16[16,32,2,128]{3,1,2,0:T(8,128)(2,1)S(1)} %copy.27), channel_id=1, source_target_pairs={{0,1},{1,2},{2,3},{4,5},{5,6},{6,7},{8,9},{9,10},{10,11},{12,13},{... | collective-permute-start | bytes 786440 | tf_op jit(solution)/shard_map/ppermute | solution.py:14
  16.8 1.7 %slice_reduce_fusion.23 = (f32[32]{0:T(128)S(1)}, f32[32]{0:T(128)S(1)}, f32[32]{0:T(128)S(1)}, f32[32]{0:T(128)S(1)}, f32[32]{0:T(128)}, /*index=5*/f32[32]{0:T(128)}) fusion(f32[32,25]{1,0:T(8,128)} %param.8), kind=kLoop, calls=%fused_computation.287 | loop fusion | bytes 1536 | tf_op jit(solution)/shard_map/slice | solution.py:75
  18.6 1.1 %slice_reduce_fusion.24 = (f32[32]{0:T(128)}, f32[32]{0:T(128)}, f32[32]{0:T(128)}, f32[32]{0:T(128)}, f32[32]{0:T(128)}, /*index=5*/f32[32]{0:T(128)}, f32[32]{...) fusion(f32[32,25]{1,0:T(8,128)S(1)} %copy-done.1), kind=kLoop, calls=%fused_computation.288 | loop fusion | bytes 4864 | tf_op jit(solution)/shard_map/slice | solution.py:75
  19.7 4.0 %collective-permute-done.5 = bf16[16,32,256]{2,1,0:T(8,128)(2,1)S(1)} collective-permute-done((bf16[16,32,256]{2,1,0:T(8,128)(2,1)S(1)}, bf16[16,32,256]{2,1,0:T(8,128)(2,1)S(1)}, u32[]{:S(2)}, u32[]{:S(2)}) %collective-permute-start.5) | collective-permute-done | bytes 262176 | tf_op jit(solution)/shard_map/ppermute | solution.py:25
  23.8 2.8 %collective-permute-done.6 = bf16[16,32,256]{2,1,0:T(8,128)(2,1)S(1)} collective-permute-done((bf16[16,32,256]{2,1,0:T(8,128)(2,1)S(1)}, bf16[16,32,256]{2,1,0:T(8,128)(2,1)S(1)}, u32[]{:S(2)}, u32[]{:S(2)}) %collective-permute-start.6) | collective-permute-done | bytes 262176 | tf_op jit(solution)/shard_map/ppermute | solution.py:25
  26.9 0.5 fusion.11
  27.4 0.6 gather_fusion.3
  28.2 1.7 %fusion.138 = (f32[16,32,6,132]{3,1,2,0:T(8,128)S(1)}, bf16[16,32,6,132]{3,1,2,0:T(8,128)(2,1)S(1)}) fusion(bf16[16,32,2,128]{3,1,2,0:T(8,128)(2,1)S(1)} %collective-permute-done.1, bf16[16,32,2,128]{3,1,2,0:T(8,128)(2,1)S(1)} %copy.27, bf16[16,32,2,128]{3,1,2,0:T(8,128)(2,1)} %collective-permute-done), kind=kLoop, calls=%fused_computation.302 | loop fusion | flops 5271552 | bytes 3219456 | tf_op jit(solution)/shard_map/convert_element_type | solution.py:69
  30.1 3.0 %fusion.67 = bf16[16,32,2,128]{3,1,2,0:T(8,128)(2,1)S(1)} fusion(f32[16,32,6,132]{3,1,2,0:T(8,128)S(1)} %get-tuple-element.70, f32[32]{0:T(128)S(1)} %copy-done.6, f32[32]{0:T(128)S(1)} %copy-done.7, f32[32]{0:T(128)S(1)} %copy-done.9, f32[32]{0:T(128)S(1)} %copy-done.10, f32[32]{0:T(128)S(1)} %copy-done.11, f32[32]{0:T(128)S(1)} %copy-done.12, ...), kind=kLoop, calls=%fused_computation.130 | loop fusion | flops 6553600 | bytes 13372544 | tf_op jit(solution)/shard_map/convert_element_type | solution.py:78
  33.2 1.1 %fusion.39 = (bf16[16,32,2,128]{3,1,2,0:T(8,128)(2,1)S(1)}, bf16[16,2,4,8,128]{4,3,2,1,0:T(8,128)(2,1)}) fusion(bf16[16,32,2,128]{3,1,2,0:T(8,128)(2,1)S(1)} %fusion.67, bf16[32,32]{1,0:T(8,128)(2,1)S(1)} %copy-done, bf16[16,32,256]{2,1,0:T(8,128)(2,1)S(1)} %gather_fusion.3), kind=kOutput, calls=%fused_computation.76 | convolution fusion | flops 9961472 | bytes 1050624 | tf_op jit(solution)/shard_map/gf,cfhw->cghw/dot_general | solution.py:79
  34.3 0.2 convolution_bitcast_fusion.3
  34.5 2.3 %fusion.36 = (f32[32]{0:T(128)}, f32[32]{0:T(128)}, f32[32]{0:T(128)}, f32[32]{0:T(128)}, f32[32]{0:T(128)}, /*index=5*/f32[32]{0:T(128)}, bf16[16,2,128,32]{2,3,1,0:T(8,128)(2,1)S(1)}) fusion(bf16[16,32,2,128]{3,1,2,0:T(8,128)(2,1)S(1)} %collective-permute-done.1, bf16[16,32,2,128]{3,1,2,0:T(8,128)(2,1)S(1)} %copy.27, ...), kind=kOutput, calls=%fused_computation.72 | convolution fusion | flops 11272000 | bytes 1837824 | tf_op jit(solution)/shard_map/gf,cghw->cfhw/dot_general | solution.py:123
  36.8 2.3 %fusion.38 = (f32[32]{0:T(128)}, f32[32]{0:T(128)}, f32[32]{0:T(128)}, f32[32]{0:T(128)}, f32[32]{0:T(128)}, /*index=5*/f32[32]{0:T(128)}, f32[32]{0:T(128)}, f3...) fusion(bf16[16,32,6,132]{3,1,2,0:T(8,128)(2,1)S(1)} %get-tuple-, ...), kind=kLoop, calls=%fused_computation.74 | loop fusion | flops 7208384 | bytes 4983040 | tf_op jit(solution)/shard_map/cfhw,cfhw->f/dot_general | solution.py:138
  39.3 0.6 gather_fusion
  40.1 0.6 fusion.12
  40.9 0.8 multiply_reduce_fusion
  41.9 0.1 stack.167
  42.0 0.1 reshape.81
  42.1 0.1 concatenate.19
  42.3 1.3 %collective-permute-start.9 = (bf16[16,32,2,128]{3,1,2,0:T(8,128)(2,1)S(1)}, bf16[16,32,2,128]{3,1,2,0:T(8,128)(2,1)S(1)}, u32[]{:S(2)}, u32[]{:S(2)}) collective-permute-start(bf16[16,32,2,128]{3,1,2,0:T(8,128)(2,1)S(1)} %bitcast.343), channel_id=1, source_target_pairs={{1,0},{2,1},{3,2},{5,4},{6,5},{7,6},{9,8},{10,9},{11,10},{13,12},{... | collective-permute-start | bytes 786440 | tf_op jit(solution)/shard_map/ppermute | solution.py:17
  43.6 3.0 %collective-permute-start.8 = (bf16[16,32,2,128]{3,1,2,0:T(8,128)(2,1)S(1)}, bf16[16,32,2,128]{3,1,2,0:T(8,128)(2,1)S(1)}, u32[]{:S(2)}, u32[]{:S(2)}) collective-permute-start(bf16[16,32,2,128]{3,1,2,0:T(8,128)(2,1)S(1)} %bitcast.344), channel_id=1, source_target_pairs={{0,1},{1,2},{2,3},{4,5},{5,6},{6,7},{8,9},{9,10},{10,11},{12,13},{... | collective-permute-start | bytes 786440 | tf_op jit(solution)/shard_map/ppermute | solution.py:14
  46.7 1.7 %collective-permute-start.11 = (f32[8992]{0:T(1024)S(1)}, f32[8992]{0:T(1024)S(1)}, u32[]{:S(2)}, u32[]{:S(2)}) collective-permute-start(f32[8992]{0:T(1024)S(1)} %fusion.137), channel_id=1, source_target_pairs={{0,2},{2,0},{1,3},{3,1},{4,6},{6,4},{5,7},{7,5},{8,10},{10,8},{9,1... | collective-permute-start | bytes 107912 | tf_op jit(solution)/shard_map/ppermute | solution.py:40
  48.4 6.2 %collective-permute-start.4 = (bf16[16,32,256]{2,1,0:T(8,128)(2,1)S(1)}, bf16[16,32,256]{2,1,0:T(8,128)(2,1)S(1)}, u32[]{:S(2)}, u32[]{:S(2)}) collective-permute-start(bf16[16,32,256]{2,1,0:T(8,128)(2,1)S(1)} %gather_fusion), channel_id=1, source_target_pairs={{12,0},{0,4},{4,8},{8,12},{13,1},{1,5},{5,9},{9,13},{14,2},{2,6},{... | collective-permute-start | bytes 786440 | tf_op jit(solution)/shard_map/ppermute | solution.py:25
  54.5 1.5 %collective-permute-start.3 = (bf16[16,32,256]{2,1,0:T(8,128)(2,1)S(1)}, bf16[16,32,256]{2,1,0:T(8,128)(2,1)S(1)}, u32[]{:S(2)}, u32[]{:S(2)}) collective-permute-start(bf16[16,32,256]{2,1,0:T(8,128)(2,1)S(1)} %gather_fusion), channel_id=1, source_target_pairs={{8,0},{12,4},{0,8},{4,12},{9,1},{13,5},{1,9},{5,13},{10,2},{14,6},... | collective-permute-start | bytes 786440 | tf_op jit(solution)/shard_map/ppermute | solution.py:25
  56.0 2.1 %collective-permute-start.2 = (bf16[16,32,256]{2,1,0:T(8,128)(2,1)S(1)}, bf16[16,32,256]{2,1,0:T(8,128)(2,1)S(1)}, u32[]{:S(2)}, u32[]{:S(2)}) collective-permute-start(bf16[16,32,256]{2,1,0:T(8,128)(2,1)S(1)} %gather_fusion), channel_id=1, source_target_pairs={{4,0},{8,4},{12,8},{0,12},{5,1},{9,5},{13,9},{1,13},{6,2},{10,6},{... | collective-permute-start | bytes 786440 | tf_op jit(solution)/shard_map/ppermute | solution.py:25
  58.2 0.1 pad_maximum_fusion
  58.3 0.6 pad_convert_fusion
  59.0 13.1 %collective-permute-done.2 = bf16[16,32,256]{2,1,0:T(8,128)(2,1)S(1)} collective-permute-done((bf16[16,32,256]{2,1,0:T(8,128)(2,1)S(1)}, bf16[16,32,256]{2,1,0:T(8,128)(2,1)S(1)}, u32[]{:S(2)}, u32[]{:S(2)}) %collective-permute-start.2) | collective-permute-done | bytes 262176 | tf_op jit(solution)/shard_map/ppermute | solution.py:25
  72.2 1.4 %collective-permute-done.3 = bf16[16,32,256]{2,1,0:T(8,128)(2,1)S(1)} collective-permute-done((bf16[16,32,256]{2,1,0:T(8,128)(2,1)S(1)}, bf16[16,32,256]{2,1,0:T(8,128)(2,1)S(1)}, u32[]{:S(2)}, u32[]{:S(2)}) %collective-permute-start.3) | collective-permute-done | bytes 262176 | tf_op jit(solution)/shard_map/ppermute | solution.py:25
  73.8 3.0 %fusion.42 = bf16[16,32,2,128]{3,1,2,0:T(8,128)(2,1)S(1)} fusion(f32[16,32,6,132]{3,1,2,0:T(8,128)S(1)} %pad_convert_fusion, bf16[16,32,2,128]{3,2,1,0:T(2,128)(2,1)S(1)} %copy-done.3, f32[32]{0:T(128)S(1)} %copy-done.6, f32[32]{0:T(128)S(1)} %copy-done.7, f32[32]{0:T(128)S(1)} %copy-done.9, f32[32]{0:T(128)S(1)} %copy-done.10, f32[32]{0:T(128)S(1)} %copy-done.11, ...), kind=kLoop, calls=%fused_computation.80 | loop fusion | flops 6815744 | bytes 13634688 | tf_op jit(solution)/shard_map/convert_element_type | solution.py:146
  77.0 0.6 fusion.10
  77.6 0.6 gather_fusion.1
  78.2 0.3 reshape.87
  78.5 5.2 %collective-permute-start.13 = (f32[8992]{0:T(1024)S(1)}, f32[8992]{0:T(1024)S(1)}, u32[]{:S(2)}, u32[]{:S(2)}) collective-permute-start(f32[8992]{0:T(1024)S(1)} %add.280), channel_id=1, source_target_pairs={{0,8},{4,12},{8,0},{12,4},{1,9},{5,13},{9,1},{13,5},{2,10},{6,14},... | collective-permute-start | bytes 107912 | tf_op jit(solution)/shard_map/ppermute | solution.py:40
  83.7 1.0 %add_convert_fusion = bf16[16,32,2,128]{3,2,1,0:T(2,128)(2,1)} fusion(f32[16,32,2,128]{3,2,1,0:T(2,128)S(1)} %reshape.87, bf16[16,32,2,128]{3,2,1,0:T(2,128)(2,1)S(1)} %copy-done.2), kind=kLoop, calls=%fused_computation.180 | loop fusion | flops 393216 | bytes 1048576 | tf_op jit(solution)/shard_map/convert_element_type | solution.py:120
  84.7 0.9 %copy.48 = bf16[16,32,2,128]{3,2,1,0:T(2,128)(2,1)} copy(bf16[16,32,2,128]{3,1,2,0:T(8,128)(2,1)S(1)} %fusion.42) | data formatting | bytes 524288
  85.8 0.7 reshape.85
  86.5 0.7 split.13
  87.2 0.7 reshape.86
  (163 shorter events, 1.7 us)
Async XLA Ops:
  0.6 32.5 %copy-start = (bf16[32,32]{1,0:T(8,128)(2,1)S(1)}, bf16[32,32]{1,0:T(8,128)(2,1)}, u32[]{:S(2)}) copy-start(bf16[32,32]{1,0:T(8,128)(2,1)} %param.9) | copy-start | bytes 6148
  0.6 17.9 %copy-start.1 = (f32[32,25]{1,0:T(8,128)S(1)}, f32[32,25]{1,0:T(8,128)}, u32[]{:S(2)}) copy-start(f32[32,25]{1,0:T(8,128)} %param.8) | copy-start | bytes 9604
  0.7 19.0 %copy-start.5 = (bf16[7,32,32]{2,1,0:T(8,128)(2,1)S(1)}, bf16[7,32,32]{2,1,0:T(8,128)(2,1)}, u32[]{:S(2)}) copy-start(bf16[7,32,32]{2,1,0:T(8,128)(2,1)} %param.10) | copy-start | bytes 43012
  3.8 22.8 %collective-permute-start.7 = (bf16[16,32,256]{2,1,0:T(8,128)(2,1)S(1)}, bf16[16,32,256]{2,1,0:T(8,128)(2,1)S(1)}, u32[]{:S(2)}, u32[]{:S(2)}) collective-permute-start(bf16[16,32,256]{2,1,0:T(8,128)(2,1)S(1)} %gather_fusion.2), channel_id=1, source_target_pairs={{12,0},{0,4},{4,8},{8,12},{13,1},{1,5},{5,9},{9,13},{14,2},{2,6},{... | collective-permute-start | bytes 786440 | tf_op jit(solution)/shard_map/ppermute | solution.py:25
  6.9 19.7 %collective-permute-start.6 = (bf16[16,32,256]{2,1,0:T(8,128)(2,1)S(1)}, bf16[16,32,256]{2,1,0:T(8,128)(2,1)S(1)}, u32[]{:S(2)}, u32[]{:S(2)}) collective-permute-start(bf16[16,32,256]{2,1,0:T(8,128)(2,1)S(1)} %gather_fusion.2), channel_id=1, source_target_pairs={{8,0},{12,4},{0,8},{4,12},{9,1},{13,5},{1,9},{5,13},{10,2},{14,6},... | collective-permute-start | bytes 786440 | tf_op jit(solution)/shard_map/ppermute | solution.py:25
  9.5 14.3 %collective-permute-start.5 = (bf16[16,32,256]{2,1,0:T(8,128)(2,1)S(1)}, bf16[16,32,256]{2,1,0:T(8,128)(2,1)S(1)}, u32[]{:S(2)}, u32[]{:S(2)}) collective-permute-start(bf16[16,32,256]{2,1,0:T(8,128)(2,1)S(1)} %gather_fusion.2), channel_id=1, source_target_pairs={{4,0},{8,4},{12,8},{0,12},{5,1},{9,5},{13,9},{1,13},{6,2},{10,6},{... | collective-permute-start | bytes 786440 | tf_op jit(solution)/shard_map/ppermute | solution.py:25
  11.8 16.4 %collective-permute-start.1 = (bf16[16,32,2,128]{3,1,2,0:T(8,128)(2,1)S(1)}, bf16[16,32,2,128]{3,1,2,0:T(8,128)(2,1)S(1)}, u32[]{:S(2)}, u32[]{:S(2)}) collective-permute-start(bf16[16,32,2,128]{3,1,2,0:T(8,128)(2,1)S(1)} %copy.27), channel_id=1, source_target_pairs={{1,0},{2,1},{3,2},{5,4},{6,5},{7,6},{9,8},{10,9},{11,10},{13,12},{... | collective-permute-start | bytes 786440 | tf_op jit(solution)/shard_map/ppermute | solution.py:17
  13.1 15.1 %collective-permute-start = (bf16[16,32,2,128]{3,1,2,0:T(8,128)(2,1)S(1)}, bf16[16,32,2,128]{3,1,2,0:T(8,128)(2,1)}, u32[]{:S(2)}, u32[]{:S(2)}) collective-permute-start(bf16[16,32,2,128]{3,1,2,0:T(8,128)(2,1)S(1)} %copy.27), channel_id=1, source_target_pairs={{0,1},{1,2},{2,3},{4,5},{5,6},{6,7},{8,9},{9,10},{10,11},{12,13},{... | collective-permute-start | bytes 786440 | tf_op jit(solution)/shard_map/ppermute | solution.py:14
  28.0 2.0 %copy-start.6 = (f32[32]{0:T(128)S(1)}, f32[32]{0:T(128)}, u32[]{:S(2)}) copy-start(f32[32]{0:T(128)} %get-tuple-element.68) | copy-start | bytes 388
  28.0 2.0 %copy-start.7 = (f32[32]{0:T(128)S(1)}, f32[32]{0:T(128)}, u32[]{:S(2)}) copy-start(f32[32]{0:T(128)} %get-tuple-element.69) | copy-start | bytes 388
  28.0 2.0 %copy-start.8 = (f32[32]{0:T(128)S(1)}, f32[32]{0:T(128)}, u32[]{:S(2)}) copy-start(f32[32]{0:T(128)} %get-tuple-element.45) | copy-start | bytes 388
  28.0 2.0 %copy-start.9 = (f32[32]{0:T(128)S(1)}, f32[32]{0:T(128)}, u32[]{:S(2)}) copy-start(f32[32]{0:T(128)} %get-tuple-element.46) | copy-start | bytes 388
  28.0 2.0 %copy-start.10 = (f32[32]{0:T(128)S(1)}, f32[32]{0:T(128)}, u32[]{:S(2)}) copy-start(f32[32]{0:T(128)} %get-tuple-element.47) | copy-start | bytes 388
  28.0 2.0 %copy-start.11 = (f32[32]{0:T(128)S(1)}, f32[32]{0:T(128)}, u32[]{:S(2)}) copy-start(f32[32]{0:T(128)} %get-tuple-element.48) | copy-start | bytes 388
  28.0 2.0 %copy-start.12 = (f32[32]{0:T(128)S(1)}, f32[32]{0:T(128)}, u32[]{:S(2)}) copy-start(f32[32]{0:T(128)} %get-tuple-element.49) | copy-start | bytes 388
  28.0 2.0 %copy-start.13 = (f32[32]{0:T(128)S(1)}, f32[32]{0:T(128)}, u32[]{:S(2)}) copy-start(f32[32]{0:T(128)} %get-tuple-element.50) | copy-start | bytes 388
  28.0 2.0 %copy-start.14 = (f32[32]{0:T(128)S(1)}, f32[32]{0:T(128)}, u32[]{:S(2)}) copy-start(f32[32]{0:T(128)} %get-tuple-element.51) | copy-start | bytes 388
  28.1 2.0 %copy-start.15 = (f32[32]{0:T(128)S(1)}, f32[32]{0:T(128)}, u32[]{:S(2)}) copy-start(f32[32]{0:T(128)} %get-tuple-element.52) | copy-start | bytes 388
  28.1 2.0 %copy-start.16 = (f32[32]{0:T(128)S(1)}, f32[32]{0:T(128)}, u32[]{:S(2)}) copy-start(f32[32]{0:T(128)} %get-tuple-element.53) | copy-start | bytes 388
  28.1 2.0 %copy-start.17 = (f32[32]{0:T(128)S(1)}, f32[32]{0:T(128)}, u32[]{:S(2)}) copy-start(f32[32]{0:T(128)} %get-tuple-element.54) | copy-start | bytes 388
  28.1 2.0 %copy-start.18 = (f32[32]{0:T(128)S(1)}, f32[32]{0:T(128)}, u32[]{:S(2)}) copy-start(f32[32]{0:T(128)} %get-tuple-element.55) | copy-start | bytes 388
  28.1 2.0 %copy-start.19 = (f32[32]{0:T(128)S(1)}, f32[32]{0:T(128)}, u32[]{:S(2)}) copy-start(f32[32]{0:T(128)} %get-tuple-element.56) | copy-start | bytes 388
  28.1 2.0 %copy-start.21 = (f32[32]{0:T(128)S(1)}, f32[32]{0:T(128)}, u32[]{:S(2)}) copy-start(f32[32]{0:T(128)} %get-tuple-element.57) | copy-start | bytes 388
  28.1 2.0 %copy-start.23 = (f32[32]{0:T(128)S(1)}, f32[32]{0:T(128)}, u32[]{:S(2)}) copy-start(f32[32]{0:T(128)} %get-tuple-element.58) | copy-start | bytes 388
  28.1 2.0 %copy-start.25 = (f32[32]{0:T(128)S(1)}, f32[32]{0:T(128)}, u32[]{:S(2)}) copy-start(f32[32]{0:T(128)} %get-tuple-element.59) | copy-start | bytes 388
  28.1 2.0 %copy-start.27 = (f32[32]{0:T(128)S(1)}, f32[32]{0:T(128)}, u32[]{:S(2)}) copy-start(f32[32]{0:T(128)} %get-tuple-element.60) | copy-start | bytes 388
  28.1 2.0 %copy-start.29 = (f32[32]{0:T(128)S(1)}, f32[32]{0:T(128)}, u32[]{:S(2)}) copy-start(f32[32]{0:T(128)} %get-tuple-element.61) | copy-start | bytes 388
  28.2 2.0 %copy-start.31 = (f32[32]{0:T(128)S(1)}, f32[32]{0:T(128)}, u32[]{:S(2)}) copy-start(f32[32]{0:T(128)} %get-tuple-element.62) | copy-start | bytes 388
  28.2 2.0 %copy-start.33 = (f32[32]{0:T(128)S(1)}, f32[32]{0:T(128)}, u32[]{:S(2)}) copy-start(f32[32]{0:T(128)} %get-tuple-element.63) | copy-start | bytes 388
  36.8 2.4 %copy-start.4 = (bf16[16,2,4,8,128]{4,3,2,1,0:T(8,128)(2,1)S(1)}, bf16[16,2,4,8,128]{4,3,2,1,0:T(8,128)(2,1)}, u32[]{:S(2)}) copy-start(bf16[16,2,4,8,128]{4,3,2,1,0:T(8,128)(2,1)} %get-tuple-element.73) | copy-start | bytes 786436
  42.2 4.4 %collective-permute-start.10 = (f32[8992]{0:T(1024)S(1)}, f32[8992]{0:T(1024)S(1)}, u32[]{:S(2)}, u32[]{:S(2)}) collective-permute-start(f32[8992]{0:T(1024)S(1)} %broadcast_multiply_fusion), channel_id=1, source_target_pairs={{0,1},{1,0},{2,3},{3,2},{4,5},{5,4},{6,7},{7,6},{8,9},{9,8},{10,11... | collective-permute-start | bytes 107912 | tf_op jit(solution)/shard_map/ppermute | solution.py:40
  42.3 15.9 %collective-permute-start.9 = (bf16[16,32,2,128]{3,1,2,0:T(8,128)(2,1)S(1)}, bf16[16,32,2,128]{3,1,2,0:T(8,128)(2,1)S(1)}, u32[]{:S(2)}, u32[]{:S(2)}) collective-permute-start(bf16[16,32,2,128]{3,1,2,0:T(8,128)(2,1)S(1)} %bitcast.343), channel_id=1, source_target_pairs={{1,0},{2,1},{3,2},{5,4},{6,5},{7,6},{9,8},{10,9},{11,10},{13,12},{... | collective-permute-start | bytes 786440 | tf_op jit(solution)/shard_map/ppermute | solution.py:17
  43.6 14.6 %collective-permute-start.8 = (bf16[16,32,2,128]{3,1,2,0:T(8,128)(2,1)S(1)}, bf16[16,32,2,128]{3,1,2,0:T(8,128)(2,1)S(1)}, u32[]{:S(2)}, u32[]{:S(2)}) collective-permute-start(bf16[16,32,2,128]{3,1,2,0:T(8,128)(2,1)S(1)} %bitcast.344), channel_id=1, source_target_pairs={{0,1},{1,2},{2,3},{4,5},{5,6},{6,7},{8,9},{9,10},{10,11},{12,13},{... | collective-permute-start | bytes 786440 | tf_op jit(solution)/shard_map/ppermute | solution.py:14
  46.7 9.3 %collective-permute-start.11 = (f32[8992]{0:T(1024)S(1)}, f32[8992]{0:T(1024)S(1)}, u32[]{:S(2)}, u32[]{:S(2)}) collective-permute-start(f32[8992]{0:T(1024)S(1)} %fusion.137), channel_id=1, source_target_pairs={{0,2},{2,0},{1,3},{3,1},{4,6},{6,4},{5,7},{7,5},{8,10},{10,8},{9,1... | collective-permute-start | bytes 107912 | tf_op jit(solution)/shard_map/ppermute | solution.py:40
  48.4 25.2 %collective-permute-start.4 = (bf16[16,32,256]{2,1,0:T(8,128)(2,1)S(1)}, bf16[16,32,256]{2,1,0:T(8,128)(2,1)S(1)}, u32[]{:S(2)}, u32[]{:S(2)}) collective-permute-start(bf16[16,32,256]{2,1,0:T(8,128)(2,1)S(1)} %gather_fusion), channel_id=1, source_target_pairs={{12,0},{0,4},{4,8},{8,12},{13,1},{1,5},{5,9},{9,13},{14,2},{2,6},{... | collective-permute-start | bytes 786440 | tf_op jit(solution)/shard_map/ppermute | solution.py:25
  54.5 19.0 %collective-permute-start.3 = (bf16[16,32,256]{2,1,0:T(8,128)(2,1)S(1)}, bf16[16,32,256]{2,1,0:T(8,128)(2,1)S(1)}, u32[]{:S(2)}, u32[]{:S(2)}) collective-permute-start(bf16[16,32,256]{2,1,0:T(8,128)(2,1)S(1)} %gather_fusion), channel_id=1, source_target_pairs={{8,0},{12,4},{0,8},{4,12},{9,1},{13,5},{1,9},{5,13},{10,2},{14,6},... | collective-permute-start | bytes 786440 | tf_op jit(solution)/shard_map/ppermute | solution.py:25
  56.0 16.1 %collective-permute-start.2 = (bf16[16,32,256]{2,1,0:T(8,128)(2,1)S(1)}, bf16[16,32,256]{2,1,0:T(8,128)(2,1)S(1)}, u32[]{:S(2)}, u32[]{:S(2)}) collective-permute-start(bf16[16,32,256]{2,1,0:T(8,128)(2,1)S(1)} %gather_fusion), channel_id=1, source_target_pairs={{4,0},{8,4},{12,8},{0,12},{5,1},{9,5},{13,9},{1,13},{6,2},{10,6},{... | collective-permute-start | bytes 786440 | tf_op jit(solution)/shard_map/ppermute | solution.py:25
  58.9 14.8 %copy-start.3 = (bf16[16,32,2,128]{3,2,1,0:T(2,128)(2,1)S(1)}, bf16[16,32,2,128]{3,2,1,0:T(2,128)(2,1)}, u32[]{:S(2)}) copy-start(bf16[16,32,2,128]{3,2,1,0:T(2,128)(2,1)} %param.7) | copy-start | bytes 786436
  58.9 14.8 %copy-start.20 = (f32[32]{0:T(128)S(1)}, f32[32]{0:T(128)}, u32[]{:S(2)}) copy-start(f32[32]{0:T(128)} %get-tuple-element.56) | copy-start | bytes 388
  58.9 14.8 %copy-start.22 = (f32[32]{0:T(128)S(1)}, f32[32]{0:T(128)}, u32[]{:S(2)}) copy-start(f32[32]{0:T(128)} %get-tuple-element.57) | copy-start | bytes 388
  58.9 14.8 %copy-start.24 = (f32[32]{0:T(128)S(1)}, f32[32]{0:T(128)}, u32[]{:S(2)}) copy-start(f32[32]{0:T(128)} %get-tuple-element.58) | copy-start | bytes 388
  58.9 14.8 %copy-start.26 = (f32[32]{0:T(128)S(1)}, f32[32]{0:T(128)}, u32[]{:S(2)}) copy-start(f32[32]{0:T(128)} %get-tuple-element.59) | copy-start | bytes 388
  58.9 14.8 %copy-start.28 = (f32[32]{0:T(128)S(1)}, f32[32]{0:T(128)}, u32[]{:S(2)}) copy-start(f32[32]{0:T(128)} %get-tuple-element.60) | copy-start | bytes 388
  58.9 14.8 %copy-start.30 = (f32[32]{0:T(128)S(1)}, f32[32]{0:T(128)}, u32[]{:S(2)}) copy-start(f32[32]{0:T(128)} %get-tuple-element.61) | copy-start | bytes 388
  58.9 14.8 %copy-start.32 = (f32[32]{0:T(128)S(1)}, f32[32]{0:T(128)}, u32[]{:S(2)}) copy-start(f32[32]{0:T(128)} %get-tuple-element.62) | copy-start | bytes 388
  58.9 14.8 %copy-start.34 = (f32[32]{0:T(128)S(1)}, f32[32]{0:T(128)}, u32[]{:S(2)}) copy-start(f32[32]{0:T(128)} %get-tuple-element.63) | copy-start | bytes 388
  59.0 19.5 %collective-permute-start.12 = (f32[8992]{0:T(1024)S(1)}, f32[8992]{0:T(1024)S(1)}, u32[]{:S(2)}, u32[]{:S(2)}) collective-permute-start(f32[8992]{0:T(1024)S(1)} %add.279), channel_id=1, source_target_pairs={{0,4},{4,0},{8,12},{12,8},{1,5},{5,1},{9,13},{13,9},{2,6},{6,2},{1... | collective-permute-start | bytes 107912 | tf_op jit(solution)/shard_map/ppermute | solution.py:40
  78.5 7.1 %collective-permute-start.13 = (f32[8992]{0:T(1024)S(1)}, f32[8992]{0:T(1024)S(1)}, u32[]{:S(2)}, u32[]{:S(2)}) collective-permute-start(f32[8992]{0:T(1024)S(1)} %add.280), channel_id=1, source_target_pairs={{0,8},{4,12},{8,0},{12,4},{1,9},{5,13},{9,1},{13,5},{2,10},{6,14},... | collective-permute-start | bytes 107912 | tf_op jit(solution)/shard_map/ppermute | solution.py:40
  (25 other events, 43.0 us)

commit v11 on v6

--- a/solution.py
+++ b/solution.py
@@ -25,19 +25,32 @@
     return lax.ppermute(block, axis, route)
 
 
-def all_summed(value, axes, tied=None):
-    if tied is not None:
-        value, _ = lax.optimization_barrier((value, tied))
+def all_summed(value, axes, pieces, tied=None, tie_at=0):
+    rounds = []
     for axis in axes:
         count = lax.axis_size(axis)
         if count & (count - 1):
+            rounds.append((axis, 0))
+        else:
+            rounds.extend((axis, 1 << bit) for bit in range(count.bit_length() - 1))
+    received = None
+    for done, (axis, step) in enumerate(rounds):
+        if received is not None:
+            value = value + received
+            received = None
+        if tied is not None and done == tie_at:
+            value, _ = lax.optimization_barrier((value, tied))
+        if step == 0:
             value = lax.psum(value, axis)
-            continue
-        step = 1
-        while step < count:
-            value = value + lax.ppermute(value, axis, [(i, i ^ step) for i in range(count)])
-            step *= 2
-    return value
+        else:
+            count = lax.axis_size(axis)
+            received = lax.ppermute(value, axis, [(i, i ^ step) for i in range(count)])
+    if received is not None:
+        return tuple(
+            (value[lo : lo + size] + received[lo : lo + size]).reshape(shape)
+            for lo, size, shape in pieces
+        )
+    return tuple(value[lo : lo + size].reshape(shape) for lo, size, shape in pieces)
 
 
 def silu_slope(value):
@@ -143,11 +156,10 @@
     dirty_grad = (cotangent.astype(jnp.float32) + conv).astype(jnp.bfloat16)
     parts = (kernel_term, mix_term, spec_grad)
     flat = jnp.concatenate([part.reshape(-1) for part in parts]) * scale
-    flat = all_summed(flat, ("sub", "tile", "chan"), tied=h_received)
-    sizes = [part.size for part in parts]
-    kgrad, mgrad, sgrad = (
-        piece.reshape(part.shape)
-        for piece, part in zip(jnp.split(flat, [sizes[0], sizes[0] + sizes[1]]), parts)
+    starts = [0, parts[0].size, parts[0].size + parts[1].size]
+    pieces = [(lo, part.size, part.shape) for lo, part in zip(starts, parts)]
+    kgrad, mgrad, sgrad = all_summed(
+        flat, ("sub", "tile", "chan"), pieces, tied=h_received, tie_at=3
     )
     return (restored, dirty_grad, kgrad, mgrad, sgrad)
 

time: 90.4 us -> 83.5 us (0.924)
  waiting for transfers between devices: 13.7 us -> 20.3 us
  starting transfers between devices: 35.2 us -> 29.1 us
  local copies, waits for them, and re-layouts: 17.9 us -> 12.2 us
  matrix products: 6.95 us -> 5.29 us
    ppermute x4, waiting for transfers between devices: 3.37 us -> 13.5 us  [all_summed(): received = lax.ppermute(value, axis, [(i, i ^ step) for i in range(count)])]
    ppermute x4, starting transfers between devices: 10.1 us -> 5.03 us  [all_summed(): received = lax.ppermute(value, axis, [(i, i ^ step) for i in range(count)])]
    ppermute x6, waiting for transfers between devices: 10.3 us -> 6.81 us  [passed_along(): return lax.ppermute(block, axis, route)]
    add x0 -> x3, local copies, waits for them, and re-layouts: none -> 2.13 us  [all_summed(): value[lo:lo + size] + received[lo:lo + size]]
    dot_general x1, matrix products: 2.29 us -> 0.6 us  [local(): jnp.einsum('mKp,mfp->Kf', g_stack, h_sorted, preferred_element_type=jnp.f...]
    unnamed x142 -> x130, local copies, waits for them, and re-layouts: 4.03 us -> 2.36 us
    gather x1, local copies, waits for them, and re-layouts: 2.2 us -> 0.56 us  [local(): h_sorted = hidden_flat[order]]
    reshape x2 -> x0, local copies, waits for them, and re-layouts: 1.44 us -> none  [local(): piece.reshape(part.shape)]
  transfers between devices with their start and end apart: 14 -> 14, of which waited for: 6 -> 4; matrix products, arithmetic and copies ran while one was open for 24% -> 15% of each run, Pallas kernels for 0% -> 0%
where the time goes in v11:
time: 83.5 us; the launch traced here: 83 us
  starting transfers between devices  29.1 us (35%)
  waiting for transfers between devices  20.3 us (24%)
  other arithmetic  14.2 us (17%)
  local copies, waits for them, and re-layouts  12.2 us (15%)
  matrix products  5.29 us (6%)
  between operations  1.94 us (2%)
    ppermute x6, starting transfers between devices, passed_along(): return lax.ppermute(block, axis, route)  15.7 us
    ppermute x4, waiting for transfers between devices, all_summed(): received = lax.ppermute(value, axis, [(i, i ^ step) for i in range(count)])  13.5 us
    ppermute x6, waiting for transfers between devices, passed_along(): return lax.ppermute(block, axis, route)  6.81 us
    ppermute x2, starting transfers between devices, padded(): lax.ppermute(lax.slice_in_dim(block, block.shape[dim] - width, None, axis...  5.84 us
    ppermute x4, starting transfers between devices, all_summed(): received = lax.ppermute(value, axis, [(i, i ^ step) for i in range(count)])  5.03 us
    dot_general x2, other arithmetic, local(): jnp.einsum('cfhw,cfhw->f', dsmooth, xpad[:, :, i:i + rows, j:j + cols], p...  3.05 us
    convert_element_type x1, other arithmetic, local(): dirty_grad = (cotangent.astype(jnp.float32) + conv).astype(jnp.bfloat16)  3.04 us
    convert_element_type x1, other arithmetic, local(): smooth = total.astype(jnp.bfloat16)  3.03 us
  transfers between devices with their start and end apart: 14, of which 4 were waited for; matrix products, arithmetic and copies ran while one was open for 15% of the time, Pallas kernels for 0%

profile of v11, /device:TPU:0, one launch (start us, length us, event | category | flops | bytes accessed | tf_op | source)
XLA Modules:
  0.0 83.0 jit_solution(16137867151931670381)
XLA Ops:
  0.7 0.8 compare_select_fusion.1
  1.4 0.6 scatter_custom_fusion
  2.1 1.1 %reshape.91 = bf16[16,32,256]{2,1,0:T(8,128)(2,1)S(1)} reshape(bf16[16,32,2,128]{3,2,1,0:T(2,128)(2,1)} %param.7) | data formatting | bytes 524288 | tf_op jit(solution)/shard_map/reshape | solution.py:92
  3.2 0.6 gather_fusion.2
  3.8 3.1 %collective-permute-start.7 = (bf16[16,32,256]{2,1,0:T(8,128)(2,1)S(1)}, bf16[16,32,256]{2,1,0:T(8,128)(2,1)S(1)}, u32[]{:S(2)}, u32[]{:S(2)}) collective-permute-start(bf16[16,32,256]{2,1,0:T(8,128)(2,1)S(1)} %gather_fusion.2), channel_id=1, source_target_pairs={{12,0},{0,4},{4,8},{8,12},{13,1},{1,5},{5,9},{9,13},{14,2},{2,6},{... | collective-permute-start | bytes 786440 | tf_op jit(solution)/shard_map/ppermute | solution.py:25
  6.9 2.6 %collective-permute-start.6 = (bf16[16,32,256]{2,1,0:T(8,128)(2,1)S(1)}, bf16[16,32,256]{2,1,0:T(8,128)(2,1)S(1)}, u32[]{:S(2)}, u32[]{:S(2)}) collective-permute-start(bf16[16,32,256]{2,1,0:T(8,128)(2,1)S(1)} %gather_fusion.2), channel_id=1, source_target_pairs={{8,0},{12,4},{0,8},{4,12},{9,1},{13,5},{1,9},{5,13},{10,2},{14,6},... | collective-permute-start | bytes 786440 | tf_op jit(solution)/shard_map/ppermute | solution.py:25
  9.5 1.3 %collective-permute-start.5 = (bf16[16,32,256]{2,1,0:T(8,128)(2,1)S(1)}, bf16[16,32,256]{2,1,0:T(8,128)(2,1)S(1)}, u32[]{:S(2)}, u32[]{:S(2)}) collective-permute-start(bf16[16,32,256]{2,1,0:T(8,128)(2,1)S(1)} %gather_fusion.2), channel_id=1, source_target_pairs={{4,0},{8,4},{12,8},{0,12},{5,1},{9,5},{13,9},{1,13},{6,2},{10,6},{... | collective-permute-start | bytes 786440 | tf_op jit(solution)/shard_map/ppermute | solution.py:25
  10.8 1.0 %copy.27 = bf16[16,32,2,128]{3,1,2,0:T(8,128)(2,1)S(1)} copy(bf16[16,32,2,128]{3,2,1,0:T(2,128)(2,1)} %param.6) | data formatting | bytes 524288 | tf_op args[0]
  11.8 1.3 %collective-permute-start.1 = (bf16[16,32,2,128]{3,1,2,0:T(8,128)(2,1)S(1)}, bf16[16,32,2,128]{3,1,2,0:T(8,128)(2,1)S(1)}, u32[]{:S(2)}, u32[]{:S(2)}) collective-permute-start(bf16[16,32,2,128]{3,1,2,0:T(8,128)(2,1)S(1)} %copy.27), channel_id=1, source_target_pairs={{1,0},{2,1},{3,2},{5,4},{6,5},{7,6},{9,8},{10,9},{11,10},{13,12},{... | collective-permute-start | bytes 786440 | tf_op jit(solution)/shard_map/ppermute | solution.py:17
  13.1 3.7 %collective-permute-start = (bf16[16,32,2,128]{3,1,2,0:T(8,128)(2,1)S(1)}, bf16[16,32,2,128]{3,1,2,0:T(8,128)(2,1)}, u32[]{:S(2)}, u32[]{:S(2)}) collective-permute-start(bf16[16,32,2,128]{3,1,2,0:T(8,128)(2,1)S(1)} %copy.27), channel_id=1, source_target_pairs={{0,1},{1,2},{2,3},{4,5},{5,6},{6,7},{8,9},{9,10},{10,11},{12,13},{... | collective-permute-start | bytes 786440 | tf_op jit(solution)/shard_map/ppermute | solution.py:14
  16.8 1.7 %slice_reduce_fusion.23 = (f32[32]{0:T(128)S(1)}, f32[32]{0:T(128)S(1)}, f32[32]{0:T(128)S(1)}, f32[32]{0:T(128)S(1)}, f32[32]{0:T(128)}, /*index=5*/f32[32]{0:T(128)}) fusion(f32[32,25]{1,0:T(8,128)} %param.8), kind=kLoop, calls=%fused_computation.287 | loop fusion | bytes 1536 | tf_op jit(solution)/shard_map/slice | solution.py:85
  18.6 1.1 %slice_reduce_fusion.24 = (f32[32]{0:T(128)}, f32[32]{0:T(128)}, f32[32]{0:T(128)}, f32[32]{0:T(128)}, f32[32]{0:T(128)}, /*index=5*/f32[32]{0:T(128)}, f32[32]{...) fusion(f32[32,25]{1,0:T(8,128)S(1)} %copy-done.1), kind=kLoop, calls=%fused_computation.288 | loop fusion | bytes 4864 | tf_op jit(solution)/shard_map/slice | solution.py:85
  19.7 4.0 %collective-permute-done.5 = bf16[16,32,256]{2,1,0:T(8,128)(2,1)S(1)} collective-permute-done((bf16[16,32,256]{2,1,0:T(8,128)(2,1)S(1)}, bf16[16,32,256]{2,1,0:T(8,128)(2,1)S(1)}, u32[]{:S(2)}, u32[]{:S(2)}) %collective-permute-start.5) | collective-permute-done | bytes 262176 | tf_op jit(solution)/shard_map/ppermute | solution.py:25
  23.8 2.8 %collective-permute-done.6 = bf16[16,32,256]{2,1,0:T(8,128)(2,1)S(1)} collective-permute-done((bf16[16,32,256]{2,1,0:T(8,128)(2,1)S(1)}, bf16[16,32,256]{2,1,0:T(8,128)(2,1)S(1)}, u32[]{:S(2)}, u32[]{:S(2)}) %collective-permute-start.6) | collective-permute-done | bytes 262176 | tf_op jit(solution)/shard_map/ppermute | solution.py:25
  26.9 0.5 fusion.8
  27.4 0.6 gather_fusion.3
  28.2 1.7 %select_maximum_fusion.2 = (bf16[16,32,6,132]{3,1,2,0:T(8,128)(2,1)S(1)}, f32[16,32,6,132]{3,1,2,0:T(8,128)S(1)}) fusion(bf16[16,32,2,128]{3,1,2,0:T(8,128)(2,1)S(1)} %collective-permute-done.1, bf16[16,32,2,128]{3,1,2,0:T(8,128)(2,1)S(1)} %copy.27, bf16[16,32,2,128]{3,1,2,0:T(8,128)(2,1)} %collective-permute-done), kind=kLoop, calls=%fused_computation.37 | loop fusion | flops 5271552 | bytes 3219456 | tf_op jit(solution)/shard_map/concatenate | solution.py:18
  30.1 3.0 %fusion.64 = bf16[16,32,2,128]{3,1,2,0:T(8,128)(2,1)S(1)} fusion(f32[16,32,6,132]{3,1,2,0:T(8,128)S(1)} %get-tuple-element.71, f32[32]{0:T(128)S(1)} %copy-done.6, f32[32]{0:T(128)S(1)} %copy-done.7, f32[32]{0:T(128)S(1)} %copy-done.9, f32[32]{0:T(128)S(1)} %copy-done.10, f32[32]{0:T(128)S(1)} %copy-done.11, f32[32]{0:T(128)S(1)} %copy-done.12, ...), kind=kLoop, calls=%fused_computation.129 | loop fusion | flops 6553600 | bytes 13372544 | tf_op jit(solution)/shard_map/convert_element_type | solution.py:88
  33.2 1.1 %fusion.36 = (bf16[16,32,2,128]{3,1,2,0:T(8,128)(2,1)S(1)}, bf16[16,2,4,8,128]{4,3,2,1,0:T(8,128)(2,1)}) fusion(bf16[16,32,2,128]{3,1,2,0:T(8,128)(2,1)S(1)} %fusion.64, bf16[32,32]{1,0:T(8,128)(2,1)S(1)} %copy-done, bf16[16,32,256]{2,1,0:T(8,128)(2,1)S(1)} %gather_fusion.3), kind=kOutput, calls=%fused_computation.75 | convolution fusion | flops 9961472 | bytes 1050624 | tf_op jit(solution)/shard_map/gf,cfhw->cghw/dot_general | solution.py:89
  34.3 0.2 convolution_bitcast_fusion.3
  34.5 2.3 %fusion.34 = (f32[32]{0:T(128)}, f32[32]{0:T(128)}, f32[32]{0:T(128)}, f32[32]{0:T(128)}, f32[32]{0:T(128)}, /*index=5*/f32[32]{0:T(128)}, bf16[16,2,128,32]{2,3,1,0:T(8,128)(2,1)S(1)}) fusion(bf16[16,32,6,132]{3,1,2,0:T(8,128)(2,1)S(1)} %get-tuple-element.70, bf16[16,32,2,128]{3,1,2,0:T(8,128)(2,1)} %collective-permute-done, ...), kind=kOutput, calls=%fused_computation.72 | convolution fusion | flops 11272000 | bytes 1837824 | tf_op jit(solution)/shard_map/gf,cghw->cfhw/dot_general | solution.py:133
  36.8 2.3 %fusion.35 = (f32[32]{0:T(128)}, f32[32]{0:T(128)}, f32[32]{0:T(128)}, f32[32]{0:T(128)}, f32[32]{0:T(128)}, /*index=5*/f32[32]{0:T(128)}, f32[32]{0:T(128)}, f3...) fusion(bf16[16,32,6,132]{3,1,2,0:T(8,128)(2,1)S(1)} %get-tuple-, ...), kind=kLoop, calls=%fused_computation.73 | loop fusion | flops 7208384 | bytes 4983040 | tf_op jit(solution)/shard_map/cfhw,cfhw->f/dot_general | solution.py:148
  39.3 0.6 gather_fusion
  40.1 0.6 fusion.9
  40.8 0.8 multiply_reduce_fusion
  41.8 0.1 stack.167
  42.0 0.1 reshape.92
  42.3 6.2 %collective-permute-start.4 = (bf16[16,32,256]{2,1,0:T(8,128)(2,1)S(1)}, bf16[16,32,256]{2,1,0:T(8,128)(2,1)S(1)}, u32[]{:S(2)}, u32[]{:S(2)}) collective-permute-start(bf16[16,32,256]{2,1,0:T(8,128)(2,1)S(1)} %gather_fusion), channel_id=1, source_target_pairs={{12,0},{0,4},{4,8},{8,12},{13,1},{1,5},{5,9},{9,13},{14,2},{2,6},{... | collective-permute-start | bytes 786440 | tf_op jit(solution)/shard_map/ppermute | solution.py:25
  48.5 1.5 %collective-permute-start.3 = (bf16[16,32,256]{2,1,0:T(8,128)(2,1)S(1)}, bf16[16,32,256]{2,1,0:T(8,128)(2,1)S(1)}, u32[]{:S(2)}, u32[]{:S(2)}) collective-permute-start(bf16[16,32,256]{2,1,0:T(8,128)(2,1)S(1)} %gather_fusion), channel_id=1, source_target_pairs={{8,0},{12,4},{0,8},{4,12},{9,1},{13,5},{1,9},{5,13},{10,2},{14,6},... | collective-permute-start | bytes 786440 | tf_op jit(solution)/shard_map/ppermute | solution.py:25
  50.0 0.9 %collective-permute-start.2 = (bf16[16,32,256]{2,1,0:T(8,128)(2,1)S(1)}, bf16[16,32,256]{2,1,0:T(8,128)(2,1)S(1)}, u32[]{:S(2)}, u32[]{:S(2)}) collective-permute-start(bf16[16,32,256]{2,1,0:T(8,128)(2,1)S(1)} %gather_fusion), channel_id=1, source_target_pairs={{4,0},{8,4},{12,8},{0,12},{5,1},{9,5},{13,9},{1,13},{6,2},{10,6},{... | collective-permute-start | bytes 786440 | tf_op jit(solution)/shard_map/ppermute | solution.py:25
  51.0 1.6 %collective-permute-start.11 = (f32[8992]{0:T(1024)S(1)}, f32[8992]{0:T(1024)S(1)}, u32[]{:S(2)}, u32[]{:S(2)}) collective-permute-start(f32[8992]{0:T(1024)S(1)} %fusion.134), channel_id=1, source_target_pairs={{0,2},{2,0},{1,3},{3,1},{4,6},{6,4},{5,7},{7,5},{8,10},{10,8},{9,1... | collective-permute-start | bytes 107912 | tf_op jit(solution)/shard_map/ppermute | solution.py:47
  52.5 2.5 %collective-permute-done.11 = f32[8992]{0:T(1024)S(1)} collective-permute-done((f32[8992]{0:T(1024)S(1)}, f32[8992]{0:T(1024)S(1)}, u32[]{:S(2)}, u32[]{:S(2)}) %collective-permute-start.11) | collective-permute-done | bytes 36000 | tf_op jit(solution)/shard_map/ppermute | solution.py:47
  55.0 1.1 %collective-permute-start.12 = (f32[8992]{0:T(1024)S(1)}, f32[8992]{0:T(1024)S(1)}, u32[]{:S(2)}, u32[]{:S(2)}) collective-permute-start(f32[8992]{0:T(1024)S(1)} %add.297), channel_id=1, source_target_pairs={{0,4},{4,0},{8,12},{12,8},{1,5},{5,1},{9,13},{13,9},{2,6},{6,2},{1... | collective-permute-start | bytes 107912 | tf_op jit(solution)/shard_map/ppermute | solution.py:47
  56.1 1.3 %collective-permute-start.9 = (bf16[16,32,2,128]{3,1,2,0:T(8,128)(2,1)S(1)}, bf16[16,32,2,128]{3,1,2,0:T(8,128)(2,1)S(1)}, u32[]{:S(2)}, u32[]{:S(2)}) collective-permute-start(bf16[16,32,2,128]{3,1,2,0:T(8,128)(2,1)S(1)} %bitcast.343), channel_id=1, source_target_pairs={{1,0},{2,1},{3,2},{5,4},{6,5},{7,6},{9,8},{10,9},{11,10},{13,12},{... | collective-permute-start | bytes 786440 | tf_op jit(solution)/shard_map/ppermute | solution.py:17
  57.4 11.0 %collective-permute-done.12 = f32[8992]{0:T(1024)S(1)} collective-permute-done((f32[8992]{0:T(1024)S(1)}, f32[8992]{0:T(1024)S(1)}, u32[]{:S(2)}, u32[]{:S(2)}) %collective-permute-start.12) | collective-permute-done | bytes 36000 | tf_op jit(solution)/shard_map/ppermute | solution.py:47
  68.4 2.1 %collective-permute-start.8 = (bf16[16,32,2,128]{3,1,2,0:T(8,128)(2,1)S(1)}, bf16[16,32,2,128]{3,1,2,0:T(8,128)(2,1)S(1)}, u32[]{:S(2)}, u32[]{:S(2)}) collective-permute-start(bf16[16,32,2,128]{3,1,2,0:T(8,128)(2,1)S(1)} %bitcast.344), channel_id=1, source_target_pairs={{0,1},{1,2},{2,3},{4,5},{5,6},{6,7},{8,9},{9,10},{10,11},{12,13},{... | collective-permute-start | bytes 786440 | tf_op jit(solution)/shard_map/ppermute | solution.py:14
  70.5 2.3 %collective-permute-start.13 = (f32[8992]{0:T(1024)S(1)}, f32[8992]{0:T(1024)S(1)}, u32[]{:S(2)}, u32[]{:S(2)}) collective-permute-start(f32[8992]{0:T(1024)S(1)} %add.298), channel_id=1, source_target_pairs={{0,8},{4,12},{8,0},{12,4},{1,9},{5,13},{9,1},{13,5},{2,10},{6,14},... | collective-permute-start | bytes 107912 | tf_op jit(solution)/shard_map/ppermute | solution.py:47
  73.3 0.6 fusion.7
  73.9 0.6 gather_fusion.1
  74.5 0.3 reshape.96
  74.9 0.7 fusion.3
  75.6 0.1 copy-done.3
  75.8 3.0 %fusion.39 = bf16[16,32,2,128]{3,1,2,0:T(8,128)(2,1)S(1)} fusion(f32[16,32,6,132]{3,1,2,0:T(8,128)S(1)} %fusion.3, bf16[16,32,2,128]{3,2,1,0:T(2,128)(2,1)S(1)} %copy-done.3, f32[32]{0:T(128)S(1)} %copy-done.6, f32[32]{0:T(128)S(1)} %copy-done.7, f32[32]{0:T(128)S(1)} %copy-done.9, f32[32]{0:T(128)S(1)} %copy-done.10, f32[32]{0:T(128)S(1)} %copy-done.11, ...), kind=kLoop, calls=%fused_computation.79 | loop fusion | flops 6815744 | bytes 13634688 | tf_op jit(solution)/shard_map/convert_element_type | solution.py:156
  78.8 1.0 %add_convert_fusion = bf16[16,32,2,128]{3,2,1,0:T(2,128)(2,1)} fusion(f32[16,32,2,128]{3,2,1,0:T(2,128)S(1)} %reshape.96, bf16[16,32,2,128]{3,2,1,0:T(2,128)(2,1)S(1)} %copy-done.2), kind=kLoop, calls=%fused_computation.179 | loop fusion | flops 393216 | bytes 1048576 | tf_op jit(solution)/shard_map/convert_element_type | solution.py:130
  79.8 0.9 %copy.48 = bf16[16,32,2,128]{3,2,1,0:T(2,128)(2,1)} copy(bf16[16,32,2,128]{3,1,2,0:T(8,128)(2,1)S(1)} %fusion.39) | data formatting | bytes 524288
  80.8 0.7 add.300
  81.5 0.7 add.302
  82.3 0.7 add.304
  (169 shorter events, 1.7 us)
Async XLA Ops:
  0.6 32.5 %copy-start = (bf16[32,32]{1,0:T(8,128)(2,1)S(1)}, bf16[32,32]{1,0:T(8,128)(2,1)}, u32[]{:S(2)}) copy-start(bf16[32,32]{1,0:T(8,128)(2,1)} %param.9) | copy-start | bytes 6148
  0.6 17.9 %copy-start.1 = (f32[32,25]{1,0:T(8,128)S(1)}, f32[32,25]{1,0:T(8,128)}, u32[]{:S(2)}) copy-start(f32[32,25]{1,0:T(8,128)} %param.8) | copy-start | bytes 9604
  0.7 19.0 %copy-start.5 = (bf16[7,32,32]{2,1,0:T(8,128)(2,1)S(1)}, bf16[7,32,32]{2,1,0:T(8,128)(2,1)}, u32[]{:S(2)}) copy-start(bf16[7,32,32]{2,1,0:T(8,128)(2,1)} %param.10) | copy-start | bytes 43012
  3.8 22.8 %collective-permute-start.7 = (bf16[16,32,256]{2,1,0:T(8,128)(2,1)S(1)}, bf16[16,32,256]{2,1,0:T(8,128)(2,1)S(1)}, u32[]{:S(2)}, u32[]{:S(2)}) collective-permute-start(bf16[16,32,256]{2,1,0:T(8,128)(2,1)S(1)} %gather_fusion.2), channel_id=1, source_target_pairs={{12,0},{0,4},{4,8},{8,12},{13,1},{1,5},{5,9},{9,13},{14,2},{2,6},{... | collective-permute-start | bytes 786440 | tf_op jit(solution)/shard_map/ppermute | solution.py:25
  6.9 19.7 %collective-permute-start.6 = (bf16[16,32,256]{2,1,0:T(8,128)(2,1)S(1)}, bf16[16,32,256]{2,1,0:T(8,128)(2,1)S(1)}, u32[]{:S(2)}, u32[]{:S(2)}) collective-permute-start(bf16[16,32,256]{2,1,0:T(8,128)(2,1)S(1)} %gather_fusion.2), channel_id=1, source_target_pairs={{8,0},{12,4},{0,8},{4,12},{9,1},{13,5},{1,9},{5,13},{10,2},{14,6},... | collective-permute-start | bytes 786440 | tf_op jit(solution)/shard_map/ppermute | solution.py:25
  9.5 14.3 %collective-permute-start.5 = (bf16[16,32,256]{2,1,0:T(8,128)(2,1)S(1)}, bf16[16,32,256]{2,1,0:T(8,128)(2,1)S(1)}, u32[]{:S(2)}, u32[]{:S(2)}) collective-permute-start(bf16[16,32,256]{2,1,0:T(8,128)(2,1)S(1)} %gather_fusion.2), channel_id=1, source_target_pairs={{4,0},{8,4},{12,8},{0,12},{5,1},{9,5},{13,9},{1,13},{6,2},{10,6},{... | collective-permute-start | bytes 786440 | tf_op jit(solution)/shard_map/ppermute | solution.py:25
  11.8 16.4 %collective-permute-start.1 = (bf16[16,32,2,128]{3,1,2,0:T(8,128)(2,1)S(1)}, bf16[16,32,2,128]{3,1,2,0:T(8,128)(2,1)S(1)}, u32[]{:S(2)}, u32[]{:S(2)}) collective-permute-start(bf16[16,32,2,128]{3,1,2,0:T(8,128)(2,1)S(1)} %copy.27), channel_id=1, source_target_pairs={{1,0},{2,1},{3,2},{5,4},{6,5},{7,6},{9,8},{10,9},{11,10},{13,12},{... | collective-permute-start | bytes 786440 | tf_op jit(solution)/shard_map/ppermute | solution.py:17
  13.1 15.1 %collective-permute-start = (bf16[16,32,2,128]{3,1,2,0:T(8,128)(2,1)S(1)}, bf16[16,32,2,128]{3,1,2,0:T(8,128)(2,1)}, u32[]{:S(2)}, u32[]{:S(2)}) collective-permute-start(bf16[16,32,2,128]{3,1,2,0:T(8,128)(2,1)S(1)} %copy.27), channel_id=1, source_target_pairs={{0,1},{1,2},{2,3},{4,5},{5,6},{6,7},{8,9},{9,10},{10,11},{12,13},{... | collective-permute-start | bytes 786440 | tf_op jit(solution)/shard_map/ppermute | solution.py:14
  28.0 2.0 %copy-start.6 = (f32[32]{0:T(128)S(1)}, f32[32]{0:T(128)}, u32[]{:S(2)}) copy-start(f32[32]{0:T(128)} %get-tuple-element.68) | copy-start | bytes 388
  28.0 2.0 %copy-start.7 = (f32[32]{0:T(128)S(1)}, f32[32]{0:T(128)}, u32[]{:S(2)}) copy-start(f32[32]{0:T(128)} %get-tuple-element.69) | copy-start | bytes 388
  28.0 2.0 %copy-start.8 = (f32[32]{0:T(128)S(1)}, f32[32]{0:T(128)}, u32[]{:S(2)}) copy-start(f32[32]{0:T(128)} %get-tuple-element.45) | copy-start | bytes 388
  28.0 2.0 %copy-start.9 = (f32[32]{0:T(128)S(1)}, f32[32]{0:T(128)}, u32[]{:S(2)}) copy-start(f32[32]{0:T(128)} %get-tuple-element.46) | copy-start | bytes 388
  28.0 2.0 %copy-start.10 = (f32[32]{0:T(128)S(1)}, f32[32]{0:T(128)}, u32[]{:S(2)}) copy-start(f32[32]{0:T(128)} %get-tuple-element.47) | copy-start | bytes 388
  28.0 2.0 %copy-start.11 = (f32[32]{0:T(128)S(1)}, f32[32]{0:T(128)}, u32[]{:S(2)}) copy-start(f32[32]{0:T(128)} %get-tuple-element.48) | copy-start | bytes 388
  28.0 2.0 %copy-start.12 = (f32[32]{0:T(128)S(1)}, f32[32]{0:T(128)}, u32[]{:S(2)}) copy-start(f32[32]{0:T(128)} %get-tuple-element.49) | copy-start | bytes 388
  28.0 2.0 %copy-start.13 = (f32[32]{0:T(128)S(1)}, f32[32]{0:T(128)}, u32[]{:S(2)}) copy-start(f32[32]{0:T(128)} %get-tuple-element.50) | copy-start | bytes 388
  28.0 2.0 %copy-start.14 = (f32[32]{0:T(128)S(1)}, f32[32]{0:T(128)}, u32[]{:S(2)}) copy-start(f32[32]{0:T(128)} %get-tuple-element.51) | copy-start | bytes 388
  28.1 2.0 %copy-start.15 = (f32[32]{0:T(128)S(1)}, f32[32]{0:T(128)}, u32[]{:S(2)}) copy-start(f32[32]{0:T(128)} %get-tuple-element.52) | copy-start | bytes 388
  28.1 2.0 %copy-start.17 = (f32[32]{0:T(128)S(1)}, f32[32]{0:T(128)}, u32[]{:S(2)}) copy-start(f32[32]{0:T(128)} %get-tuple-element.53) | copy-start | bytes 388
  28.1 2.0 %copy-start.19 = (f32[32]{0:T(128)S(1)}, f32[32]{0:T(128)}, u32[]{:S(2)}) copy-start(f32[32]{0:T(128)} %get-tuple-element.54) | copy-start | bytes 388
  28.1 2.0 %copy-start.21 = (f32[32]{0:T(128)S(1)}, f32[32]{0:T(128)}, u32[]{:S(2)}) copy-start(f32[32]{0:T(128)} %get-tuple-element.55) | copy-start | bytes 388
  28.1 2.0 %copy-start.23 = (f32[32]{0:T(128)S(1)}, f32[32]{0:T(128)}, u32[]{:S(2)}) copy-start(f32[32]{0:T(128)} %get-tuple-element.56) | copy-start | bytes 388
  28.1 2.0 %copy-start.25 = (f32[32]{0:T(128)S(1)}, f32[32]{0:T(128)}, u32[]{:S(2)}) copy-start(f32[32]{0:T(128)} %get-tuple-element.57) | copy-start | bytes 388
  28.1 2.0 %copy-start.27 = (f32[32]{0:T(128)S(1)}, f32[32]{0:T(128)}, u32[]{:S(2)}) copy-start(f32[32]{0:T(128)} %get-tuple-element.58) | copy-start | bytes 388
  28.1 2.0 %copy-start.29 = (f32[32]{0:T(128)S(1)}, f32[32]{0:T(128)}, u32[]{:S(2)}) copy-start(f32[32]{0:T(128)} %get-tuple-element.59) | copy-start | bytes 388
  28.1 2.0 %copy-start.31 = (f32[32]{0:T(128)S(1)}, f32[32]{0:T(128)}, u32[]{:S(2)}) copy-start(f32[32]{0:T(128)} %get-tuple-element.60) | copy-start | bytes 388
  28.1 2.0 %copy-start.33 = (f32[32]{0:T(128)S(1)}, f32[32]{0:T(128)}, u32[]{:S(2)}) copy-start(f32[32]{0:T(128)} %get-tuple-element.61) | copy-start | bytes 388
  28.2 2.0 %copy-start.35 = (f32[32]{0:T(128)S(1)}, f32[32]{0:T(128)}, u32[]{:S(2)}) copy-start(f32[32]{0:T(128)} %get-tuple-element.62) | copy-start | bytes 388
  28.2 2.0 %copy-start.37 = (f32[32]{0:T(128)S(1)}, f32[32]{0:T(128)}, u32[]{:S(2)}) copy-start(f32[32]{0:T(128)} %get-tuple-element.63) | copy-start | bytes 388
  36.8 2.4 %copy-start.4 = (bf16[16,2,4,8,128]{4,3,2,1,0:T(8,128)(2,1)S(1)}, bf16[16,2,4,8,128]{4,3,2,1,0:T(8,128)(2,1)}, u32[]{:S(2)}) copy-start(bf16[16,2,4,8,128]{4,3,2,1,0:T(8,128)(2,1)} %get-tuple-element.73) | copy-start | bytes 786436
  39.9 1.7 %copy-start.39 = (f32[32]{0:T(128)S(1)}, f32[32]{0:T(128)}, u32[]{:S(2)}) copy-start(f32[32]{0:T(128)} %get-tuple-element.17) | copy-start | bytes 388
  39.9 1.7 %copy-start.40 = (f32[32]{0:T(128)S(1)}, f32[32]{0:T(128)}, u32[]{:S(2)}) copy-start(f32[32]{0:T(128)} %get-tuple-element.18) | copy-start | bytes 388
  39.9 1.7 %copy-start.41 = (f32[32]{0:T(128)S(1)}, f32[32]{0:T(128)}, u32[]{:S(2)}) copy-start(f32[32]{0:T(128)} %get-tuple-element.19) | copy-start | bytes 388
  39.9 1.7 %copy-start.42 = (f32[32]{0:T(128)S(1)}, f32[32]{0:T(128)}, u32[]{:S(2)}) copy-start(f32[32]{0:T(128)} %get-tuple-element.20) | copy-start | bytes 388
  39.9 1.7 %copy-start.43 = (f32[32]{0:T(128)S(1)}, f32[32]{0:T(128)}, u32[]{:S(2)}) copy-start(f32[32]{0:T(128)} %get-tuple-element.21) | copy-start | bytes 388
  39.9 1.7 %copy-start.44 = (f32[32]{0:T(128)S(1)}, f32[32]{0:T(128)}, u32[]{:S(2)}) copy-start(f32[32]{0:T(128)} %get-tuple-element.22) | copy-start | bytes 388
  39.9 1.7 %copy-start.45 = (f32[32]{0:T(128)S(1)}, f32[32]{0:T(128)}, u32[]{:S(2)}) copy-start(f32[32]{0:T(128)} %get-tuple-element.23) | copy-start | bytes 388
  39.9 1.7 %copy-start.46 = (f32[32]{0:T(128)S(1)}, f32[32]{0:T(128)}, u32[]{:S(2)}) copy-start(f32[32]{0:T(128)} %get-tuple-element.24) | copy-start | bytes 388
  39.9 1.7 %copy-start.47 = (f32[32]{0:T(128)S(1)}, f32[32]{0:T(128)}, u32[]{:S(2)}) copy-start(f32[32]{0:T(128)} %get-tuple-element.25) | copy-start | bytes 388
  42.2 8.7 %collective-permute-start.10 = (f32[8992]{0:T(1024)S(1)}, f32[8992]{0:T(1024)S(1)}, u32[]{:S(2)}, u32[]{:S(2)}) collective-permute-start(f32[8992]{0:T(1024)S(1)} %broadcast_multiply_fusion), channel_id=1, source_target_pairs={{0,1},{1,0},{2,3},{3,2},{4,5},{5,4},{6,7},{7,6},{8,9},{9,8},{10,11... | collective-permute-start | bytes 107912 | tf_op jit(solution)/shard_map/ppermute | solution.py:47
  42.3 28.2 %collective-permute-start.4 = (bf16[16,32,256]{2,1,0:T(8,128)(2,1)S(1)}, bf16[16,32,256]{2,1,0:T(8,128)(2,1)S(1)}, u32[]{:S(2)}, u32[]{:S(2)}) collective-permute-start(bf16[16,32,256]{2,1,0:T(8,128)(2,1)S(1)} %gather_fusion), channel_id=1, source_target_pairs={{12,0},{0,4},{4,8},{8,12},{13,1},{1,5},{5,9},{9,13},{14,2},{2,6},{... | collective-permute-start | bytes 786440 | tf_op jit(solution)/shard_map/ppermute | solution.py:25
  48.5 22.0 %collective-permute-start.3 = (bf16[16,32,256]{2,1,0:T(8,128)(2,1)S(1)}, bf16[16,32,256]{2,1,0:T(8,128)(2,1)S(1)}, u32[]{:S(2)}, u32[]{:S(2)}) collective-permute-start(bf16[16,32,256]{2,1,0:T(8,128)(2,1)S(1)} %gather_fusion), channel_id=1, source_target_pairs={{8,0},{12,4},{0,8},{4,12},{9,1},{13,5},{1,9},{5,13},{10,2},{14,6},... | collective-permute-start | bytes 786440 | tf_op jit(solution)/shard_map/ppermute | solution.py:25
  50.0 20.5 %collective-permute-start.2 = (bf16[16,32,256]{2,1,0:T(8,128)(2,1)S(1)}, bf16[16,32,256]{2,1,0:T(8,128)(2,1)S(1)}, u32[]{:S(2)}, u32[]{:S(2)}) collective-permute-start(bf16[16,32,256]{2,1,0:T(8,128)(2,1)S(1)} %gather_fusion), channel_id=1, source_target_pairs={{4,0},{8,4},{12,8},{0,12},{5,1},{9,5},{13,9},{1,13},{6,2},{10,6},{... | collective-permute-start | bytes 786440 | tf_op jit(solution)/shard_map/ppermute | solution.py:25
  51.0 4.0 %collective-permute-start.11 = (f32[8992]{0:T(1024)S(1)}, f32[8992]{0:T(1024)S(1)}, u32[]{:S(2)}, u32[]{:S(2)}) collective-permute-start(f32[8992]{0:T(1024)S(1)} %fusion.134), channel_id=1, source_target_pairs={{0,2},{2,0},{1,3},{3,1},{4,6},{6,4},{5,7},{7,5},{8,10},{10,8},{9,1... | collective-permute-start | bytes 107912 | tf_op jit(solution)/shard_map/ppermute | solution.py:47
  55.0 13.4 %collective-permute-start.12 = (f32[8992]{0:T(1024)S(1)}, f32[8992]{0:T(1024)S(1)}, u32[]{:S(2)}, u32[]{:S(2)}) collective-permute-start(f32[8992]{0:T(1024)S(1)} %add.297), channel_id=1, source_target_pairs={{0,4},{4,0},{8,12},{12,8},{1,5},{5,1},{9,13},{13,9},{2,6},{6,2},{1... | collective-permute-start | bytes 107912 | tf_op jit(solution)/shard_map/ppermute | solution.py:47
  56.1 18.8 %collective-permute-start.9 = (bf16[16,32,2,128]{3,1,2,0:T(8,128)(2,1)S(1)}, bf16[16,32,2,128]{3,1,2,0:T(8,128)(2,1)S(1)}, u32[]{:S(2)}, u32[]{:S(2)}) collective-permute-start(bf16[16,32,2,128]{3,1,2,0:T(8,128)(2,1)S(1)} %bitcast.343), channel_id=1, source_target_pairs={{1,0},{2,1},{3,2},{5,4},{6,5},{7,6},{9,8},{10,9},{11,10},{13,12},{... | collective-permute-start | bytes 786440 | tf_op jit(solution)/shard_map/ppermute | solution.py:17
  68.4 6.5 %collective-permute-start.8 = (bf16[16,32,2,128]{3,1,2,0:T(8,128)(2,1)S(1)}, bf16[16,32,2,128]{3,1,2,0:T(8,128)(2,1)S(1)}, u32[]{:S(2)}, u32[]{:S(2)}) collective-permute-start(bf16[16,32,2,128]{3,1,2,0:T(8,128)(2,1)S(1)} %bitcast.344), channel_id=1, source_target_pairs={{0,1},{1,2},{2,3},{4,5},{5,6},{6,7},{8,9},{9,10},{10,11},{12,13},{... | collective-permute-start | bytes 786440 | tf_op jit(solution)/shard_map/ppermute | solution.py:14
  70.5 10.2 %collective-permute-start.13 = (f32[8992]{0:T(1024)S(1)}, f32[8992]{0:T(1024)S(1)}, u32[]{:S(2)}, u32[]{:S(2)}) collective-permute-start(f32[8992]{0:T(1024)S(1)} %add.298), channel_id=1, source_target_pairs={{0,8},{4,12},{8,0},{12,4},{1,9},{5,13},{9,1},{13,5},{2,10},{6,14},... | collective-permute-start | bytes 107912 | tf_op jit(solution)/shard_map/ppermute | solution.py:47
  (29 other events, 39.3 us)

commit v12 on v8

--- a/solution.py
+++ b/solution.py
@@ -92,7 +92,7 @@
         for sign in (-1, 1):
             h_far = passed_along(h_sorted, "chan", -sign * dist)
             h_received.append(h_far)
-            g_far = passed_along(g_sorted, "chan", -sign * dist)
+            g_far, _ = lax.optimization_barrier((passed_along(g_sorted, "chan", -sign * dist), mixed))
             if sign < 0:
                 wrapped = device < dist
                 h_near = jnp.where(wrapped, move_down(h_far), h_far)
@@ -145,7 +145,7 @@
     dirty_grad = (cotangent.astype(jnp.float32) + conv).astype(jnp.bfloat16)
     parts = (kernel_term, mix_term, spec_grad)
     flat = jnp.concatenate([part.reshape(-1) for part in parts]) * scale
-    flat = all_summed(flat, ("sub", "tile", "chan"), tied=h_received, tie_at=2)
+    flat = all_summed(flat, ("sub", "tile", "chan"), tied=h_received, tie_at=1)
     sizes = [part.size for part in parts]
     kgrad, mgrad, sgrad = (
         piece.reshape(part.shape)

time: 87.4 us -> 99.8 us (1.14)
  waiting for transfers between devices: 20.2 us -> 36.2 us
  starting transfers between devices: 33.2 us -> 20.8 us
  other arithmetic: 14.1 us -> 18.9 us
  local copies, waits for them, and re-layouts: 12.3 us -> 15.9 us
    ppermute x6, waiting for transfers between devices: 17.4 us -> 31.8 us  [passed_along(): return lax.ppermute(block, axis, route)]
    ppermute x6, starting transfers between devices: 15.7 us -> 10 us  [passed_along(): return lax.ppermute(block, axis, route)]
    ppermute x4, starting transfers between devices: 9.18 us -> 4.31 us  [all_summed(): lax.ppermute(value, axis, [(i, i ^ step) for i in range(count)])]
    unnamed x11, other arithmetic: 0.6 us -> 3.95 us
    ppermute x2, starting transfers between devices: 5.79 us -> 3.67 us  [padded(): lax.ppermute(lax.slice_in_dim(block, block.shape[dim] - width, None, axis...]
    gather x1, local copies, waits for them, and re-layouts: 0.58 us -> 2.21 us  [local(): back_flat = bwd_acc.astype(jnp.bfloat16)[own]]
    ppermute x4, waiting for transfers between devices: 2.73 us -> 4.33 us  [all_summed(): lax.ppermute(value, axis, [(i, i ^ step) for i in range(count)])]
    another operation x2, local copies, waits for them, and re-layouts: 0.18 us -> 1.56 us  [local(): kernel_term = jnp.stack(terms, 1)]
  transfers between devices with their start and end apart: 14 -> 14, of which waited for: 5 -> 5; matrix products, arithmetic and copies ran while one was open for 15% -> 18% of each run, Pallas kernels for 0% -> 0%
where the time goes in v12:
time: 99.8 us; the launch traced here: 99.2 us
  waiting for transfers between devices  36.2 us (36%)
  starting transfers between devices  20.8 us (21%)
  other arithmetic  18.9 us (19%)
  local copies, waits for them, and re-layouts  15.9 us (16%)
  matrix products  6.12 us (6%)
  between operations  1.42 us (1%)
    ppermute x6, waiting for transfers between devices, passed_along(): return lax.ppermute(block, axis, route)  31.8 us
    ppermute x6, starting transfers between devices, passed_along(): return lax.ppermute(block, axis, route)  10 us
    ppermute x4, waiting for transfers between devices, all_summed(): lax.ppermute(value, axis, [(i, i ^ step) for i in range(count)])  4.33 us
    ppermute x4, starting transfers between devices, all_summed(): lax.ppermute(value, axis, [(i, i ^ step) for i in range(count)])  4.31 us
    unnamed x11, other arithmetic  3.95 us
    ppermute x2, starting transfers between devices, padded(): lax.ppermute(lax.slice_in_dim(block, block.shape[dim] - width, None, axis...  3.67 us
    unnamed x68, local copies, waits for them, and re-layouts  3.12 us
    dot_general x2, other arithmetic, local(): jnp.einsum('cfhw,cfhw->f', dsmooth, xpad[:, :, i:i + rows, j:j + cols], p...  3.08 us
  transfers between devices with their start and end apart: 14, of which 5 were waited for; matrix products, arithmetic and copies ran while one was open for 18% of the time, Pallas kernels for 0%

profile of v12, /device:TPU:0, one launch (start us, length us, event | category | flops | bytes accessed | tf_op | source)
XLA Modules:
  0.0 99.2 jit_solution(16223437316153969011)
XLA Ops:
  0.7 1.0 %copy.27 = bf16[16,32,2,128]{3,1,2,0:T(8,128)(2,1)S(1)} copy(bf16[16,32,2,128]{3,2,1,0:T(2,128)(2,1)} %param.6) | data formatting | bytes 524288 | tf_op args[0]
  1.7 2.4 %collective-permute-start = (bf16[16,32,2,128]{3,1,2,0:T(8,128)(2,1)S(1)}, bf16[16,32,2,128]{3,1,2,0:T(8,128)(2,1)S(1)}, u32[]{:S(2)}, u32[]{:S(2)}) collective-permute-start(bf16[16,32,2,128]{3,1,2,0:T(8,128)(2,1)S(1)} %copy.27), channel_id=1, source_target_pairs={{0,1},{1,2},{2,3},{4,5},{5,6},{6,7},{8,9},{9,10},{10,11},{12,13},{... | collective-permute-start | bytes 786440 | tf_op jit(solution)/shard_map/ppermute | solution.py:14
  4.1 1.3 %collective-permute-start.1 = (bf16[16,32,2,128]{3,1,2,0:T(8,128)(2,1)S(1)}, bf16[16,32,2,128]{3,1,2,0:T(8,128)(2,1)S(1)}, u32[]{:S(2)}, u32[]{:S(2)}) collective-permute-start(bf16[16,32,2,128]{3,1,2,0:T(8,128)(2,1)S(1)} %copy.27), channel_id=1, source_target_pairs={{1,0},{2,1},{3,2},{5,4},{6,5},{7,6},{9,8},{10,9},{11,10},{13,12},{... | collective-permute-start | bytes 786440 | tf_op jit(solution)/shard_map/ppermute | solution.py:17
  5.4 0.7 compare_select_fusion.1
  6.1 0.6 scatter_custom_fusion
  6.8 1.1 %reshape.80 = bf16[16,32,256]{2,1,0:T(8,128)(2,1)S(1)} reshape(bf16[16,32,2,128]{3,2,1,0:T(2,128)(2,1)} %param.7) | data formatting | bytes 524288 | tf_op jit(solution)/shard_map/reshape | solution.py:81
  7.9 0.6 gather_fusion.2
  8.5 4.5 %collective-permute-start.5 = (bf16[16,32,256]{2,1,0:T(8,128)(2,1)S(1)}, bf16[16,32,256]{2,1,0:T(8,128)(2,1)S(1)}, u32[]{:S(2)}, u32[]{:S(2)}) collective-permute-start(bf16[16,32,256]{2,1,0:T(8,128)(2,1)S(1)} %gather_fusion.2), channel_id=1, source_target_pairs={{4,0},{8,4},{12,8},{0,12},{5,1},{9,5},{13,9},{1,13},{6,2},{10,6},{... | collective-permute-start | bytes 786440 | tf_op jit(solution)/shard_map/ppermute | solution.py:25
  13.0 1.0 %collective-permute-start.7 = (bf16[16,32,256]{2,1,0:T(8,128)(2,1)S(1)}, bf16[16,32,256]{2,1,0:T(8,128)(2,1)}, u32[]{:S(2)}, u32[]{:S(2)}) collective-permute-start(bf16[16,32,256]{2,1,0:T(8,128)(2,1)S(1)} %gather_fusion.2), channel_id=1, source_target_pairs={{12,0},{0,4},{4,8},{8,12},{13,1},{1,5},{5,9},{9,13},{14,2},{2,6},{... | collective-permute-start | bytes 786440 | tf_op jit(solution)/shard_map/ppermute | solution.py:25
  14.0 0.8 rev.6
  14.8 1.2 %slice_reduce_fusion.23 = (f32[32]{0:T(128)S(1)}, f32[32]{0:T(128)S(1)}, f32[32]{0:T(128)S(1)}, f32[32]{0:T(128)S(1)}, f32[32]{0:T(128)S(1)}, /*index=5*/f32[32]{0:T(128)S(1)}) fusion(f32[32,25]{1,0:T(8,128)} %param.8), kind=kLoop, calls=%fused_computation.286 | loop fusion | bytes 1536 | tf_op jit(solution)/shard_map/slice | solution.py:74
  16.7 0.8 select_maximum_fusion.2
  17.5 3.0 %fusion.64 = bf16[16,32,2,128]{3,1,2,0:T(8,128)(2,1)S(1)} fusion(f32[16,32,6,132]{3,1,2,0:T(8,128)S(1)} %get-tuple-element.77, f32[32]{0:T(128)S(1)} %get-tuple-element.74, f32[32]{0:T(128)S(1)} %get-tuple-element.75, f32[32]{0:T(128)S(1)} %get-tuple-element.52, f32[32]{0:T(128)S(1)} %get-tuple-element.53, f32[32]{0:T(128)S(1)} %get-tuple-element.54, ...), kind=kLoop, calls=%fused_computation.129 | loop fusion | flops 6553600 | bytes 13372544 | tf_op jit(solution)/shard_map/convert_element_type | solution.py:77
  20.6 1.0 %convolution_bitcast_fusion.2 = f32[16,32,2,128]{3,1,2,0:T(8,128)} fusion(bf16[16,32,2,128]{3,1,2,0:T(8,128)(2,1)S(1)} %fusion.64, bf16[32,32]{1,0:T(8,128)(2,1)S(1)} %copy-done), kind=kOutput, calls=%fused_computation.42 | convolution fusion | flops 8388608 | bytes 788480 | tf_op jit(solution)/shard_map/gf,cfhw->cghw/dot_general | solution.py:78
  21.6 13.3 %collective-permute-done.6 = bf16[16,32,256]{2,1,0:T(8,128)(2,1)S(1)} collective-permute-done((bf16[16,32,256]{2,1,0:T(8,128)(2,1)S(1)}, bf16[16,32,256]{2,1,0:T(8,128)(2,1)S(1)}, u32[]{:S(2)}, u32[]{:S(2)}) %collective-permute-start.6) | collective-permute-done | bytes 262176 | tf_op jit(solution)/shard_map/ppermute | solution.py:25
  34.9 0.7 copy-done.10
  35.6 1.2 %fusion.108 = bf16[16,7,32,256]{3,2,0,1:T(8,128)(2,1)S(1)} fusion(bf16[16,32,256]{2,1,0:T(8,128)(2,1)} %copy-done.8, pred[]{:T(512)S(6)} %lt.21), kind=kLoop, calls=%fused_computation.214 | loop fusion | flops 131071 | bytes 524289
  36.8 1.2 %fusion.111 = bf16[16,7,32,256]{3,2,0,1:T(8,128)(2,1)S(1)} fusion(bf16[16,7,32,256]{3,2,0,1:T(8,128)(2,1)S(1)} %fusion.108, bf16[16,32,256]{2,1,0:T(8,128)(2,1)} %copy-done.10, pred[]{:T(512)S(6)} %lt.25), kind=kLoop, calls=%fused_computation.217 | loop fusion | flops 131072 | bytes 524289
  38.0 1.2 %fusion.114 = bf16[16,7,32,256]{3,2,0,1:T(8,128)(2,1)S(1)} fusion(bf16[16,7,32,256]{3,2,0,1:T(8,128)(2,1)S(1)} %fusion.111, bf16[16,32,256]{2,1,0:T(8,128)(2,1)} %collective-permute-done.7, pred[]{:T(512)S(6)} %lt.26), kind=kLoop, calls=%fused_computation.220 | loop fusion | flops 131072 | bytes 524289
  39.4 1.2 %fusion.123 = bf16[16,7,32,256]{3,2,0,1:T(8,128)(2,1)S(1)} fusion(bf16[16,7,32,256]{3,2,0,1:T(8,128)(2,1)S(1)} %fusion.120, bf16[16,32,256]{2,1,0:T(8,128)(2,1)} %collective-permute-done.7, pred[]{:T(512)S(6)} %ge.11), kind=kLoop, calls=%fused_computation.229 | loop fusion | flops 131072 | bytes 524289 | tf_op jit(solution)/shard_map/stack | solution.py:107
  40.5 1.2 %fusion.8 = bf16[16,32,256]{2,1,0:T(8,128)(2,1)} fusion(bf16[16,7,32,256]{3,2,0,1:T(8,128)(2,1)S(1)} %fusion.123, bf16[7,32,32]{2,1,0:T(8,128)(2,1)S(1)} %rev.6), kind=kOutput, calls=%fused_computation.47 | convolution fusion | flops 58851328 | bytes 2111488 | tf_op jit(solution)/shard_map/fK,mKp->mfp/dot_general | solution.py:111
  41.7 2.2 %gather_fusion.3 = bf16[16,32,256]{2,1,0:T(8,128)(2,1)} fusion(bf16[16,32,256]{2,1,0:T(8,128)(2,1)} %fusion.8, s32[1024]{0:T(1024)S(1)} %get-tuple-element.81), kind=kCustom, calls=%fused_computation.3 | custom fusion | bytes 524352 | tf_op jit(solution)/shard_map/gather | solution.py:116
  43.9 1.4 %fusion.36 = (bf16[16,32,2,128]{3,1,2,0:T(8,128)(2,1)S(1)}, bf16[16,2,4,8,128]{4,3,2,1,0:T(8,128)(2,1)S(1)}) fusion(f32[16,32,2,128]{3,1,2,0:T(8,128)} %convolution_bitcast_fusion.2, bf16[16,32,256]{2,1,0:T(8,128)(2,1)} %gather_fusion.3), kind=kLoop, calls=%fused_computation.75 | loop fusion | flops 1572864 | bytes 1310720 | tf_op jit(solution)/shard_map/convert_element_type | solution.py:120
  45.3 2.5 %fusion.34 = (f32[32]{0:T(128)}, f32[32]{0:T(128)}, f32[32]{0:T(128)}, f32[32]{0:T(128)}, f32[32]{0:T(128)}, /*index=5*/f32[32]{0:T(128)}, bf16[16,2,128,32]{2,3,1,0:T(8,128)(2,1)S(1)}) fusion(bf16[16,32,6,132]{3,1,2,0:T(8,128)(2,1)S(1)} %get-tuple-element.76, bf16[16,32,2,128]{3,1,2,0:T(8,128)(2,1)} %copy-done.15, bf16[16,32,2,128]{3,1,2,0:T(8,128)(2,1)} %copy-done.14, ...), kind=kOutput, calls=%fused_computation.72 | convolution fusion | flops 11272000 | bytes 1837824 | tf_op jit(solution)/shard_map/gf,cghw->cfhw/dot_general | solution.py:122
  47.8 2.3 %fusion.35 = (f32[32]{0:T(128)S(1)}, f32[32]{0:T(128)S(1)}, f32[32]{0:T(128)S(1)}, f32[32]{0:T(128)S(1)}, f32[32]{0:T(128)S(1)}, /*index=5*/f32[32]{0:T(128)S(1)...) fusion(bf16[16,32,6,132]{3,1,2,0:T(8,128)(2,1)S(1)} %get-tuple-, ...), kind=kLoop, calls=%fused_computation.73 | loop fusion | flops 7208384 | bytes 4983040 | tf_op jit(solution)/shard_map/cfhw,cfhw->f/dot_general | solution.py:137
  51.1 0.6 fusion.9
  51.8 0.8 multiply_reduce_fusion
  52.6 1.5 %stack.167 = f32[32,25]{0,1:T(8,128)S(1)} concatenate(f32[32,1]{0,1:T(1,128)} %bitcast.362, f32[32,1]{0,1:T(1,128)} %bitcast.360, f32[32,1]{0,1:T(1,128)} %bitcast.363, f32[32,1]{0,1:T(1,128)} %bitcast.359, f32[32,1]{0,1:T(1,128)} %bitcast.358, f32[32,1]{0,1:T(1,128)} %bitcast.357, f32[32,1]{0,1:T(1,128)S(1)} %bitcast.356, f32[32,1]{0,1:T(1,128)} %bitcast.364, ...), dimensions={1} | concatenate | bytes 6400 | tf_op jit(solution)/shard_map/stack | solution.py:144
  54.4 1.4 %collective-permute-start.10 = (f32[8992]{0:T(1024)S(1)}, f32[8992]{0:T(1024)S(1)}, u32[]{:S(2)}, u32[]{:S(2)}) collective-permute-start(f32[8992]{0:T(1024)S(1)} %broadcast_multiply_fusion), channel_id=1, source_target_pairs={{0,1},{1,0},{2,3},{3,2},{4,5},{5,4},{6,7},{7,6},{8,9},{9,8},{10,11... | collective-permute-start | bytes 107912 | tf_op jit(solution)/shard_map/ppermute | solution.py:39
  55.7 2.5 %collective-permute-start.3 = (bf16[16,32,256]{2,1,0:T(8,128)(2,1)S(1)}, bf16[16,32,256]{2,1,0:T(8,128)(2,1)S(1)}, u32[]{:S(2)}, u32[]{:S(2)}) collective-permute-start(bf16[16,32,256]{2,1,0:T(8,128)(2,1)S(1)} %gather_fusion), channel_id=1, source_target_pairs={{8,0},{12,4},{0,8},{4,12},{9,1},{13,5},{1,9},{5,13},{10,2},{14,6},... | collective-permute-start | bytes 786440 | tf_op jit(solution)/shard_map/ppermute | solution.py:25
  58.2 2.0 %collective-permute-start.4 = (bf16[16,32,256]{2,1,0:T(8,128)(2,1)S(1)}, bf16[16,32,256]{2,1,0:T(8,128)(2,1)S(1)}, u32[]{:S(2)}, u32[]{:S(2)}) collective-permute-start(bf16[16,32,256]{2,1,0:T(8,128)(2,1)S(1)} %gather_fusion), channel_id=1, source_target_pairs={{12,0},{0,4},{4,8},{8,12},{13,1},{1,5},{5,9},{9,13},{14,2},{2,6},{... | collective-permute-start | bytes 786440 | tf_op jit(solution)/shard_map/ppermute | solution.py:25
  60.3 1.3 %collective-permute-start.8 = (bf16[16,32,2,128]{3,1,2,0:T(8,128)(2,1)S(1)}, bf16[16,32,2,128]{3,1,2,0:T(8,128)(2,1)S(1)}, u32[]{:S(2)}, u32[]{:S(2)}) collective-permute-start(bf16[16,32,2,128]{3,1,2,0:T(8,128)(2,1)S(1)} %bitcast.338), channel_id=1, source_target_pairs={{0,1},{1,2},{2,3},{4,5},{5,6},{6,7},{8,9},{9,10},{10,11},{12,13},{... | collective-permute-start | bytes 786440 | tf_op jit(solution)/shard_map/ppermute | solution.py:14
  61.6 1.5 %collective-permute-start.9 = (bf16[16,32,2,128]{3,1,2,0:T(8,128)(2,1)S(1)}, bf16[16,32,2,128]{3,1,2,0:T(8,128)(2,1)S(1)}, u32[]{:S(2)}, u32[]{:S(2)}) collective-permute-start(bf16[16,32,2,128]{3,1,2,0:T(8,128)(2,1)S(1)} %bitcast.339), channel_id=1, source_target_pairs={{1,0},{2,1},{3,2},{5,4},{6,5},{7,6},{9,8},{10,9},{11,10},{13,12},{... | collective-permute-start | bytes 786440 | tf_op jit(solution)/shard_map/ppermute | solution.py:17
  63.2 0.9 collective-permute-done.2
  64.0 17.6 %collective-permute-done.3 = bf16[16,32,256]{2,1,0:T(8,128)(2,1)S(1)} collective-permute-done((bf16[16,32,256]{2,1,0:T(8,128)(2,1)S(1)}, bf16[16,32,256]{2,1,0:T(8,128)(2,1)S(1)}, u32[]{:S(2)}, u32[]{:S(2)}) %collective-permute-start.3) | collective-permute-done | bytes 262176 | tf_op jit(solution)/shard_map/ppermute | solution.py:25
  81.7 2.1 %collective-permute-start.11 = (f32[8992]{0:T(1024)S(1)}, f32[8992]{0:T(1024)S(1)}, u32[]{:S(2)}, u32[]{:S(2)}) collective-permute-start(f32[8992]{0:T(1024)S(1)} %fusion.134), channel_id=1, source_target_pairs={{0,2},{2,0},{1,3},{3,1},{4,6},{6,4},{5,7},{7,5},{8,10},{10,8},{9,1... | collective-permute-start | bytes 107912 | tf_op jit(solution)/shard_map/ppermute | solution.py:39
  83.8 0.7 fusion.3
  84.6 3.0 %fusion.39 = bf16[16,32,2,128]{3,1,2,0:T(8,128)(2,1)S(1)} fusion(f32[16,32,6,132]{3,1,2,0:T(8,128)S(1)} %fusion.3, bf16[16,32,2,128]{3,2,1,0:T(2,128)(2,1)S(1)} %copy-done.7, f32[32]{0:T(128)S(1)} %get-tuple-element.74, f32[32]{0:T(128)S(1)} %get-tuple-element.75, f32[32]{0:T(128)S(1)} %get-tuple-element.52, f32[32]{0:T(128)S(1)} %get-tuple-element.53, ...), kind=kLoop, calls=%fused_computation.79 | loop fusion | flops 6815744 | bytes 13634688 | tf_op jit(solution)/shard_map/convert_element_type | solution.py:145
  88.4 0.6 fusion.7
  89.1 0.6 gather_fusion.1
  89.9 2.2 %collective-permute-done.12 = f32[8992]{0:T(1024)S(1)} collective-permute-done((f32[8992]{0:T(1024)S(1)}, f32[8992]{0:T(1024)S(1)}, u32[]{:S(2)}, u32[]{:S(2)}) %collective-permute-start.12) | collective-permute-done | bytes 36000 | tf_op jit(solution)/shard_map/ppermute | solution.py:39
  92.1 0.8 collective-permute-start.13
  92.9 1.0 add_convert_fusion
  93.9 0.9 copy.48
  94.8 2.2 %collective-permute-done.13 = f32[8992]{0:T(1024)S(1)} collective-permute-done((f32[8992]{0:T(1024)S(1)}, f32[8992]{0:T(1024)S(1)}, u32[]{:S(2)}, u32[]{:S(2)}) %collective-permute-start.13) | collective-permute-done | bytes 36000 | tf_op jit(solution)/shard_map/ppermute | solution.py:39
  97.1 0.7 reshape.86
  97.8 0.7 reshape.85
  98.6 0.7 split.13
  (108 shorter events, 3.3 us)
Async XLA Ops:
  0.6 20.0 %copy-start = (bf16[32,32]{1,0:T(8,128)(2,1)S(1)}, bf16[32,32]{1,0:T(8,128)(2,1)}, u32[]{:S(2)}) copy-start(bf16[32,32]{1,0:T(8,128)(2,1)} %param.9) | copy-start | bytes 6148
  0.6 15.4 %copy-start.1 = (f32[32,25]{1,0:T(8,128)S(1)}, f32[32,25]{1,0:T(8,128)}, u32[]{:S(2)}) copy-start(f32[32,25]{1,0:T(8,128)} %param.8) | copy-start | bytes 9604
  1.7 15.8 %copy-start.14 = (bf16[16,32,2,128]{3,1,2,0:T(8,128)(2,1)}, bf16[16,32,2,128]{3,1,2,0:T(8,128)(2,1)S(1)}, u32[]{:S(2)}) copy-start(bf16[16,32,2,128]{3,1,2,0:T(8,128)(2,1)S(1)} %copy.27) | copy-start | bytes 786436
  1.7 14.9 %collective-permute-start = (bf16[16,32,2,128]{3,1,2,0:T(8,128)(2,1)S(1)}, bf16[16,32,2,128]{3,1,2,0:T(8,128)(2,1)S(1)}, u32[]{:S(2)}, u32[]{:S(2)}) collective-permute-start(bf16[16,32,2,128]{3,1,2,0:T(8,128)(2,1)S(1)} %copy.27), channel_id=1, source_target_pairs={{0,1},{1,2},{2,3},{4,5},{5,6},{6,7},{8,9},{9,10},{10,11},{12,13},{... | collective-permute-start | bytes 786440 | tf_op jit(solution)/shard_map/ppermute | solution.py:14
  4.1 12.6 %collective-permute-start.1 = (bf16[16,32,2,128]{3,1,2,0:T(8,128)(2,1)S(1)}, bf16[16,32,2,128]{3,1,2,0:T(8,128)(2,1)S(1)}, u32[]{:S(2)}, u32[]{:S(2)}) collective-permute-start(bf16[16,32,2,128]{3,1,2,0:T(8,128)(2,1)S(1)} %copy.27), channel_id=1, source_target_pairs={{1,0},{2,1},{3,2},{5,4},{6,5},{7,6},{9,8},{10,9},{11,10},{13,12},{... | collective-permute-start | bytes 786440 | tf_op jit(solution)/shard_map/ppermute | solution.py:17
  8.5 9.0 %copy-start.12 = (bf16[16,32,256]{2,1,0:T(8,128)(2,1)}, bf16[16,32,256]{2,1,0:T(8,128)(2,1)S(1)}, u32[]{:S(2)}) copy-start(bf16[16,32,256]{2,1,0:T(8,128)(2,1)S(1)} %gather_fusion.2) | copy-start | bytes 786436
  8.5 13.1 %collective-permute-start.5 = (bf16[16,32,256]{2,1,0:T(8,128)(2,1)S(1)}, bf16[16,32,256]{2,1,0:T(8,128)(2,1)S(1)}, u32[]{:S(2)}, u32[]{:S(2)}) collective-permute-start(bf16[16,32,256]{2,1,0:T(8,128)(2,1)S(1)} %gather_fusion.2), channel_id=1, source_target_pairs={{4,0},{8,4},{12,8},{0,12},{5,1},{9,5},{13,9},{1,13},{6,2},{10,6},{... | collective-permute-start | bytes 786440 | tf_op jit(solution)/shard_map/ppermute | solution.py:25
  13.0 22.0 %collective-permute-start.6 = (bf16[16,32,256]{2,1,0:T(8,128)(2,1)S(1)}, bf16[16,32,256]{2,1,0:T(8,128)(2,1)S(1)}, u32[]{:S(2)}, u32[]{:S(2)}) collective-permute-start(bf16[16,32,256]{2,1,0:T(8,128)(2,1)S(1)} %gather_fusion.2), channel_id=1, source_target_pairs={{8,0},{12,4},{0,8},{4,12},{9,1},{13,5},{1,9},{5,13},{10,2},{14,6},... | collective-permute-start | bytes 786440 | tf_op jit(solution)/shard_map/ppermute | solution.py:25
  13.0 22.7 %collective-permute-start.7 = (bf16[16,32,256]{2,1,0:T(8,128)(2,1)S(1)}, bf16[16,32,256]{2,1,0:T(8,128)(2,1)}, u32[]{:S(2)}, u32[]{:S(2)}) collective-permute-start(bf16[16,32,256]{2,1,0:T(8,128)(2,1)S(1)} %gather_fusion.2), channel_id=1, source_target_pairs={{12,0},{0,4},{4,8},{8,12},{13,1},{1,5},{5,9},{9,13},{14,2},{2,6},{... | collective-permute-start | bytes 786440 | tf_op jit(solution)/shard_map/ppermute | solution.py:25
  16.6 0.9 copy-start.18
  16.6 0.9 copy-start.20
  16.6 0.9 copy-start.22
  16.6 0.9 copy-start.24
  16.6 0.9 copy-start.26
  16.6 0.9 copy-start.28
  16.6 0.9 copy-start.30
  16.6 0.8 copy-start.15
  16.7 0.8 copy-start.16
  20.6 18.8 %copy-start.2 = (bf16[16,32,2,128]{3,1,2,0:T(8,128)(2,1)}, bf16[16,32,2,128]{3,1,2,0:T(8,128)(2,1)S(1)}, u32[]{:S(2)}) copy-start(bf16[16,32,2,128]{3,1,2,0:T(8,128)(2,1)S(1)} %fusion.64) | copy-start | bytes 786436
  20.6 18.6 %copy-start.13 = (bf16[16,32,256]{2,1,0:T(8,128)(2,1)S(1)}, bf16[16,32,256]{2,1,0:T(8,128)(2,1)}, u32[]{:S(2)}) copy-start(bf16[16,32,256]{2,1,0:T(8,128)(2,1)} %copy-done.12) | copy-start | bytes 786436
  21.6 13.3 %copy-start.8 = (bf16[16,32,256]{2,1,0:T(8,128)(2,1)}, bf16[16,32,256]{2,1,0:T(8,128)(2,1)S(1)}, u32[]{:S(2)}) copy-start(bf16[16,32,256]{2,1,0:T(8,128)(2,1)S(1)} %collective-permute-done.5) | copy-start | bytes 786436
  34.9 0.7 copy-start.10
  35.6 3.6 %copy-start.9 = (bf16[16,32,256]{2,1,0:T(8,128)(2,1)S(1)}, bf16[16,32,256]{2,1,0:T(8,128)(2,1)}, u32[]{:S(2)}) copy-start(bf16[16,32,256]{2,1,0:T(8,128)(2,1)} %copy-done.8) | copy-start | bytes 786436
  35.6 3.6 %copy-start.11 = (bf16[16,32,256]{2,1,0:T(8,128)(2,1)S(1)}, bf16[16,32,256]{2,1,0:T(8,128)(2,1)}, u32[]{:S(2)}) copy-start(bf16[16,32,256]{2,1,0:T(8,128)(2,1)} %copy-done.10) | copy-start | bytes 786436
  47.8 2.3 %copy-start.5 = (bf16[16,2,128,32]{2,3,1,0:T(8,128)(2,1)}, bf16[16,2,128,32]{2,3,1,0:T(8,128)(2,1)S(1)}, u32[]{:S(2)}) copy-start(bf16[16,2,128,32]{2,3,1,0:T(8,128)(2,1)S(1)} %get-tuple-element.80) | copy-start | bytes 786436
  47.8 2.4 %copy-start.3 = (bf16[16,32,2,128]{3,1,2,0:T(8,128)(2,1)S(1)}, bf16[16,32,2,128]{3,1,2,0:T(8,128)(2,1)}, u32[]{:S(2)}) copy-start(bf16[16,32,2,128]{3,1,2,0:T(8,128)(2,1)} %copy-done.2) | copy-start | bytes 786436
  50.4 1.4 %copy-start.4 = (bf16[16,32,2,128]{3,2,1,0:T(2,128)(2,1)S(1)}, bf16[16,32,2,128]{3,2,1,0:T(2,128)(2,1)}, u32[]{:S(2)}) copy-start(bf16[16,32,2,128]{3,2,1,0:T(2,128)(2,1)} %param.6) | copy-start | bytes 786436
  51.0 9.2 %copy-start.6 = (bf16[16,2,128,32]{2,3,1,0:T(8,128)(2,1)S(1)}, bf16[16,2,128,32]{2,3,1,0:T(8,128)(2,1)}, u32[]{:S(2)}) copy-start(bf16[16,2,128,32]{2,3,1,0:T(8,128)(2,1)} %copy-done.5) | copy-start | bytes 786436
  54.4 7.2 %collective-permute-start.10 = (f32[8992]{0:T(1024)S(1)}, f32[8992]{0:T(1024)S(1)}, u32[]{:S(2)}, u32[]{:S(2)}) collective-permute-start(f32[8992]{0:T(1024)S(1)} %broadcast_multiply_fusion), channel_id=1, source_target_pairs={{0,1},{1,0},{2,3},{3,2},{4,5},{5,4},{6,7},{7,6},{8,9},{9,8},{10,11... | collective-permute-start | bytes 107912 | tf_op jit(solution)/shard_map/ppermute | solution.py:39
  55.7 8.3 %collective-permute-start.2 = (bf16[16,32,256]{2,1,0:T(8,128)(2,1)S(1)}, bf16[16,32,256]{2,1,0:T(8,128)(2,1)S(1)}, u32[]{:S(2)}, u32[]{:S(2)}) collective-permute-start(bf16[16,32,256]{2,1,0:T(8,128)(2,1)S(1)} %gather_fusion), channel_id=1, source_target_pairs={{4,0},{8,4},{12,8},{0,12},{5,1},{9,5},{13,9},{1,13},{6,2},{10,6},{... | collective-permute-start | bytes 786440 | tf_op jit(solution)/shard_map/ppermute | solution.py:25
  55.7 25.9 %collective-permute-start.3 = (bf16[16,32,256]{2,1,0:T(8,128)(2,1)S(1)}, bf16[16,32,256]{2,1,0:T(8,128)(2,1)S(1)}, u32[]{:S(2)}, u32[]{:S(2)}) collective-permute-start(bf16[16,32,256]{2,1,0:T(8,128)(2,1)S(1)} %gather_fusion), channel_id=1, source_target_pairs={{8,0},{12,4},{0,8},{4,12},{9,1},{13,5},{1,9},{5,13},{10,2},{14,6},... | collective-permute-start | bytes 786440 | tf_op jit(solution)/shard_map/ppermute | solution.py:25
  58.2 23.4 %collective-permute-start.4 = (bf16[16,32,256]{2,1,0:T(8,128)(2,1)S(1)}, bf16[16,32,256]{2,1,0:T(8,128)(2,1)S(1)}, u32[]{:S(2)}, u32[]{:S(2)}) collective-permute-start(bf16[16,32,256]{2,1,0:T(8,128)(2,1)S(1)} %gather_fusion), channel_id=1, source_target_pairs={{12,0},{0,4},{4,8},{8,12},{13,1},{1,5},{5,9},{9,13},{14,2},{2,6},{... | collective-permute-start | bytes 786440 | tf_op jit(solution)/shard_map/ppermute | solution.py:25
  60.3 23.5 %collective-permute-start.8 = (bf16[16,32,2,128]{3,1,2,0:T(8,128)(2,1)S(1)}, bf16[16,32,2,128]{3,1,2,0:T(8,128)(2,1)S(1)}, u32[]{:S(2)}, u32[]{:S(2)}) collective-permute-start(bf16[16,32,2,128]{3,1,2,0:T(8,128)(2,1)S(1)} %bitcast.338), channel_id=1, source_target_pairs={{0,1},{1,2},{2,3},{4,5},{5,6},{6,7},{8,9},{9,10},{10,11},{12,13},{... | collective-permute-start | bytes 786440 | tf_op jit(solution)/shard_map/ppermute | solution.py:14
  61.6 22.2 %collective-permute-start.9 = (bf16[16,32,2,128]{3,1,2,0:T(8,128)(2,1)S(1)}, bf16[16,32,2,128]{3,1,2,0:T(8,128)(2,1)S(1)}, u32[]{:S(2)}, u32[]{:S(2)}) collective-permute-start(bf16[16,32,2,128]{3,1,2,0:T(8,128)(2,1)S(1)} %bitcast.339), channel_id=1, source_target_pairs={{1,0},{2,1},{3,2},{5,4},{6,5},{7,6},{9,8},{10,9},{11,10},{13,12},{... | collective-permute-start | bytes 786440 | tf_op jit(solution)/shard_map/ppermute | solution.py:17
  63.1 21.4 %copy-start.7 = (bf16[16,32,2,128]{3,2,1,0:T(2,128)(2,1)S(1)}, bf16[16,32,2,128]{3,2,1,0:T(2,128)(2,1)}, u32[]{:S(2)}) copy-start(bf16[16,32,2,128]{3,2,1,0:T(2,128)(2,1)} %param.7) | copy-start | bytes 786436
  63.1 21.4 %copy-start.19 = (f32[32]{0:T(128)S(1)}, f32[32]{0:T(128)}, u32[]{:S(2)}) copy-start(f32[32]{0:T(128)} %copy-done.18) | copy-start | bytes 388
  63.1 21.4 %copy-start.21 = (f32[32]{0:T(128)S(1)}, f32[32]{0:T(128)}, u32[]{:S(2)}) copy-start(f32[32]{0:T(128)} %copy-done.20) | copy-start | bytes 388
  63.1 21.4 %copy-start.23 = (f32[32]{0:T(128)S(1)}, f32[32]{0:T(128)}, u32[]{:S(2)}) copy-start(f32[32]{0:T(128)} %copy-done.22) | copy-start | bytes 388
  63.1 21.4 %copy-start.25 = (f32[32]{0:T(128)S(1)}, f32[32]{0:T(128)}, u32[]{:S(2)}) copy-start(f32[32]{0:T(128)} %copy-done.24) | copy-start | bytes 388
  63.1 21.4 %copy-start.27 = (f32[32]{0:T(128)S(1)}, f32[32]{0:T(128)}, u32[]{:S(2)}) copy-start(f32[32]{0:T(128)} %copy-done.26) | copy-start | bytes 388
  63.1 21.4 %copy-start.29 = (f32[32]{0:T(128)S(1)}, f32[32]{0:T(128)}, u32[]{:S(2)}) copy-start(f32[32]{0:T(128)} %copy-done.28) | copy-start | bytes 388
  63.1 21.4 %copy-start.31 = (f32[32]{0:T(128)S(1)}, f32[32]{0:T(128)}, u32[]{:S(2)}) copy-start(f32[32]{0:T(128)} %copy-done.30) | copy-start | bytes 388
  81.7 6.4 %collective-permute-start.11 = (f32[8992]{0:T(1024)S(1)}, f32[8992]{0:T(1024)S(1)}, u32[]{:S(2)}, u32[]{:S(2)}) collective-permute-start(f32[8992]{0:T(1024)S(1)} %fusion.134), channel_id=1, source_target_pairs={{0,2},{2,0},{1,3},{3,1},{4,6},{6,4},{5,7},{7,5},{8,10},{10,8},{9,1... | collective-permute-start | bytes 107912 | tf_op jit(solution)/shard_map/ppermute | solution.py:39
  87.6 0.8 copy-start.17
  88.1 4.0 %collective-permute-start.12 = (f32[8992]{0:T(1024)S(1)}, f32[8992]{0:T(1024)S(1)}, u32[]{:S(2)}, u32[]{:S(2)}) collective-permute-start(f32[8992]{0:T(1024)S(1)} %add.279), channel_id=1, source_target_pairs={{0,4},{4,0},{8,12},{12,8},{1,5},{5,1},{9,13},{13,9},{2,6},{6,2},{1... | collective-permute-start | bytes 107912 | tf_op jit(solution)/shard_map/ppermute | solution.py:39
  92.1 4.9 %collective-permute-start.13 = (f32[8992]{0:T(1024)S(1)}, f32[8992]{0:T(1024)S(1)}, u32[]{:S(2)}, u32[]{:S(2)}) collective-permute-start(f32[8992]{0:T(1024)S(1)} %add.280), channel_id=1, source_target_pairs={{0,8},{4,12},{8,0},{12,4},{1,9},{5,13},{9,1},{13,5},{2,10},{6,14},... | collective-permute-start | bytes 107912 | tf_op jit(solution)/shard_map/ppermute | solution.py:39

commit v13 on v8

--- a/solution.py
+++ b/solution.py
@@ -143,14 +143,13 @@
             )
     kernel_term = jnp.stack(terms, 1)
     dirty_grad = (cotangent.astype(jnp.float32) + conv).astype(jnp.bfloat16)
-    parts = (kernel_term, mix_term, spec_grad)
-    flat = jnp.concatenate([part.reshape(-1) for part in parts]) * scale
-    flat = all_summed(flat, ("sub", "tile", "chan"), tied=h_received, tie_at=2)
-    sizes = [part.size for part in parts]
-    kgrad, mgrad, sgrad = (
-        piece.reshape(part.shape)
-        for piece, part in zip(jnp.split(flat, [sizes[0], sizes[0] + sizes[1]]), parts)
-    )
+    late = all_summed(kernel_term.reshape(-1) * scale, ("sub", "tile"))
+    early = jnp.concatenate([mix_term.reshape(-1), spec_grad.reshape(-1)]) * scale
+    early = all_summed(early, ("sub", "tile"))
+    flat = all_summed(jnp.concatenate([late, early]), ("chan",), tied=h_received, tie_at=0)
+    kgrad = flat[: kernel_term.size].reshape(kernel_term.shape)
+    mgrad = flat[kernel_term.size : kernel_term.size + mix_term.size].reshape(mix_term.shape)
+    sgrad = flat[kernel_term.size + mix_term.size :].reshape(spec_grad.shape)
     return (restored, dirty_grad, kgrad, mgrad, sgrad)
 
 

time: 87.4 us -> 85.9 us (0.983)
  waiting for transfers between devices: 20.2 us -> 11.5 us
  local copies, waits for them, and re-layouts: 12.3 us -> 17.9 us
  matrix products: 5.29 us -> 6.95 us
    ppermute x6, waiting for transfers between devices: 17.4 us -> 6.81 us  [passed_along(): return lax.ppermute(block, axis, route)]
    ppermute x4 -> x6, waiting for transfers between devices: 2.73 us -> 4.69 us  [all_summed(): lax.ppermute(value, axis, [(i, i ^ step) for i in range(count)])]
    unnamed x130 -> x134, local copies, waits for them, and re-layouts: 2.36 us -> 4.05 us
    dot_general x1, matrix products: 0.6 us -> 2.29 us  [local(): jnp.einsum('mKp,mfp->Kf', g_stack, h_sorted, preferred_element_type=jnp.f...]
    gather x1, local copies, waits for them, and re-layouts: 0.56 us -> 2.2 us  [local(): h_sorted = hidden_flat[order]]
    ppermute x4 -> x6, starting transfers between devices: 9.18 us -> 7.86 us  [all_summed(): lax.ppermute(value, axis, [(i, i ^ step) for i in range(count)])]
    ppermute x2, starting transfers between devices: 5.79 us -> 6.97 us  [padded(): lax.ppermute(lax.slice_in_dim(block, block.shape[dim] - width, None, axis...]
    rev x1, local copies, waits for them, and re-layouts: 0.01 us -> 0.91 us  [local(): jnp.einsum('mKp,mfp->Kf', g_stack, h_sorted, preferred_element_type=jnp.f...]
  transfers between devices with their start and end apart: 14 -> 16, of which waited for: 5 -> 6; matrix products, arithmetic and copies ran while one was open for 15% -> 25% of each run, Pallas kernels for 0% -> 0%
where the time goes in v13:
time: 85.9 us; the launch traced here: 85.4 us
  starting transfers between devices  32.9 us (38%)
  local copies, waits for them, and re-layouts  17.9 us (21%)
  other arithmetic  14.3 us (17%)
  waiting for transfers between devices  11.5 us (13%)
  matrix products  6.95 us (8%)
  between operations  1.83 us (2%)
    ppermute x6, starting transfers between devices, passed_along(): return lax.ppermute(block, axis, route)  15.5 us
    ppermute x6, starting transfers between devices, all_summed(): lax.ppermute(value, axis, [(i, i ^ step) for i in range(count)])  7.86 us
    ppermute x2, starting transfers between devices, padded(): lax.ppermute(lax.slice_in_dim(block, block.shape[dim] - width, None, axis...  6.97 us
    ppermute x6, waiting for transfers between devices, passed_along(): return lax.ppermute(block, axis, route)  6.81 us
    ppermute x6, waiting for transfers between devices, all_summed(): lax.ppermute(value, axis, [(i, i ^ step) for i in range(count)])  4.69 us
    unnamed x134, local copies, waits for them, and re-layouts  4.05 us
    dot_general x2, other arithmetic, local(): jnp.einsum('cfhw,cfhw->f', dsmooth, xpad[:, :, i:i + rows, j:j + cols], p...  3.05 us
    convert_element_type x1, other arithmetic, local(): dirty_grad = (cotangent.astype(jnp.float32) + conv).astype(jnp.bfloat16)  3.03 us
  transfers between devices with their start and end apart: 16, of which 6 were waited for; matrix products, arithmetic and copies ran while one was open for 25% of the time, Pallas kernels for 0%

profile of v13, /device:TPU:0, one launch (start us, length us, event | category | flops | bytes accessed | tf_op | source)
XLA Modules:
  0.0 85.4 jit_solution(9311303861627448891)
XLA Ops:
  0.7 0.8 compare_select_fusion.1
  1.4 0.6 scatter_custom_fusion
  2.1 1.1 %reshape.80 = bf16[16,32,256]{2,1,0:T(8,128)(2,1)S(1)} reshape(bf16[16,32,2,128]{3,2,1,0:T(2,128)(2,1)} %param.7) | data formatting | bytes 524288 | tf_op jit(solution)/shard_map/reshape | solution.py:81
  3.2 0.6 gather_fusion.2
  3.8 3.1 %collective-permute-start.7 = (bf16[16,32,256]{2,1,0:T(8,128)(2,1)S(1)}, bf16[16,32,256]{2,1,0:T(8,128)(2,1)S(1)}, u32[]{:S(2)}, u32[]{:S(2)}) collective-permute-start(bf16[16,32,256]{2,1,0:T(8,128)(2,1)S(1)} %gather_fusion.2), channel_id=1, source_target_pairs={{12,0},{0,4},{4,8},{8,12},{13,1},{1,5},{5,9},{9,13},{14,2},{2,6},{... | collective-permute-start | bytes 786440 | tf_op jit(solution)/shard_map/ppermute | solution.py:25
  6.9 2.6 %collective-permute-start.6 = (bf16[16,32,256]{2,1,0:T(8,128)(2,1)S(1)}, bf16[16,32,256]{2,1,0:T(8,128)(2,1)S(1)}, u32[]{:S(2)}, u32[]{:S(2)}) collective-permute-start(bf16[16,32,256]{2,1,0:T(8,128)(2,1)S(1)} %gather_fusion.2), channel_id=1, source_target_pairs={{8,0},{12,4},{0,8},{4,12},{9,1},{13,5},{1,9},{5,13},{10,2},{14,6},... | collective-permute-start | bytes 786440 | tf_op jit(solution)/shard_map/ppermute | solution.py:25
  9.5 1.3 %collective-permute-start.5 = (bf16[16,32,256]{2,1,0:T(8,128)(2,1)S(1)}, bf16[16,32,256]{2,1,0:T(8,128)(2,1)S(1)}, u32[]{:S(2)}, u32[]{:S(2)}) collective-permute-start(bf16[16,32,256]{2,1,0:T(8,128)(2,1)S(1)} %gather_fusion.2), channel_id=1, source_target_pairs={{4,0},{8,4},{12,8},{0,12},{5,1},{9,5},{13,9},{1,13},{6,2},{10,6},{... | collective-permute-start | bytes 786440 | tf_op jit(solution)/shard_map/ppermute | solution.py:25
  10.8 1.0 %copy.27 = bf16[16,32,2,128]{3,1,2,0:T(8,128)(2,1)S(1)} copy(bf16[16,32,2,128]{3,2,1,0:T(2,128)(2,1)} %param.6) | data formatting | bytes 524288 | tf_op args[0]
  11.8 1.3 %collective-permute-start.1 = (bf16[16,32,2,128]{3,1,2,0:T(8,128)(2,1)S(1)}, bf16[16,32,2,128]{3,1,2,0:T(8,128)(2,1)S(1)}, u32[]{:S(2)}, u32[]{:S(2)}) collective-permute-start(bf16[16,32,2,128]{3,1,2,0:T(8,128)(2,1)S(1)} %copy.27), channel_id=1, source_target_pairs={{1,0},{2,1},{3,2},{5,4},{6,5},{7,6},{9,8},{10,9},{11,10},{13,12},{... | collective-permute-start | bytes 786440 | tf_op jit(solution)/shard_map/ppermute | solution.py:17
  13.1 3.7 %collective-permute-start = (bf16[16,32,2,128]{3,1,2,0:T(8,128)(2,1)S(1)}, bf16[16,32,2,128]{3,1,2,0:T(8,128)(2,1)}, u32[]{:S(2)}, u32[]{:S(2)}) collective-permute-start(bf16[16,32,2,128]{3,1,2,0:T(8,128)(2,1)S(1)} %copy.27), channel_id=1, source_target_pairs={{0,1},{1,2},{2,3},{4,5},{5,6},{6,7},{8,9},{9,10},{10,11},{12,13},{... | collective-permute-start | bytes 786440 | tf_op jit(solution)/shard_map/ppermute | solution.py:14
  16.9 1.7 %slice_reduce_fusion.23 = (f32[32]{0:T(128)S(1)}, f32[32]{0:T(128)S(1)}, f32[32]{0:T(128)S(1)}, f32[32]{0:T(128)S(1)}, f32[32]{0:T(128)}, /*index=5*/f32[32]{0:T(128)}) fusion(f32[32,25]{1,0:T(8,128)} %param.8), kind=kLoop, calls=%fused_computation.287 | loop fusion | bytes 1536 | tf_op jit(solution)/shard_map/slice | solution.py:74
  18.6 1.1 %slice_reduce_fusion.24 = (f32[32]{0:T(128)}, f32[32]{0:T(128)}, f32[32]{0:T(128)}, f32[32]{0:T(128)}, f32[32]{0:T(128)}, /*index=5*/f32[32]{0:T(128)}, f32[32]{...) fusion(f32[32,25]{1,0:T(8,128)S(1)} %copy-done.1), kind=kLoop, calls=%fused_computation.288 | loop fusion | bytes 4864 | tf_op jit(solution)/shard_map/slice | solution.py:74
  19.7 4.0 %collective-permute-done.5 = bf16[16,32,256]{2,1,0:T(8,128)(2,1)S(1)} collective-permute-done((bf16[16,32,256]{2,1,0:T(8,128)(2,1)S(1)}, bf16[16,32,256]{2,1,0:T(8,128)(2,1)S(1)}, u32[]{:S(2)}, u32[]{:S(2)}) %collective-permute-start.5) | collective-permute-done | bytes 262176 | tf_op jit(solution)/shard_map/ppermute | solution.py:25
  23.8 2.8 %collective-permute-done.6 = bf16[16,32,256]{2,1,0:T(8,128)(2,1)S(1)} collective-permute-done((bf16[16,32,256]{2,1,0:T(8,128)(2,1)S(1)}, bf16[16,32,256]{2,1,0:T(8,128)(2,1)S(1)}, u32[]{:S(2)}, u32[]{:S(2)}) %collective-permute-start.6) | collective-permute-done | bytes 262176 | tf_op jit(solution)/shard_map/ppermute | solution.py:25
  27.4 1.3 %gather_fusion.3 = bf16[16,32,256]{2,1,0:T(8,128)(2,1)} fusion(bf16[16,32,256]{2,1,0:T(8,128)(2,1)S(1)} %fusion.8, s32[1024]{0:T(1024)S(1)} %pad_clamp_fusion), kind=kCustom, calls=%fused_computation.3 | custom fusion | bytes 524352 | tf_op jit(solution)/shard_map/gather | solution.py:116
  28.8 0.7 copy-done.10
  29.5 1.9 %select_maximum_fusion.2 = (bf16[16,32,6,132]{3,1,2,0:T(8,128)(2,1)S(1)}, f32[16,32,6,132]{3,1,2,0:T(8,128)S(1)}) fusion(bf16[16,32,2,128]{3,1,2,0:T(8,128)(2,1)} %copy-done.10, bf16[16,32,2,128]{3,1,2,0:T(8,128)(2,1)} %copy-done.6, bf16[16,32,2,128]{3,1,2,0:T(8,128)(2,1)} %collective-permute-done), kind=kLoop, calls=%fused_computation.37 | loop fusion | flops 5271552 | bytes 3219456 | tf_op jit(solution)/shard_map/concatenate | solution.py:18
  31.6 3.0 %fusion.64 = bf16[16,32,2,128]{3,1,2,0:T(8,128)(2,1)S(1)} fusion(f32[16,32,6,132]{3,1,2,0:T(8,128)S(1)} %get-tuple-element.71, f32[32]{0:T(128)S(1)} %copy-done.13, f32[32]{0:T(128)S(1)} %copy-done.14, f32[32]{0:T(128)S(1)} %copy-done.16, f32[32]{0:T(128)S(1)} %copy-done.17, f32[32]{0:T(128)S(1)} %copy-done.18, f32[32]{0:T(128)S(1)} %copy-done.19, ...), kind=kLoop, calls=%fused_computation.129 | loop fusion | flops 6553600 | bytes 13372544 | tf_op jit(solution)/shard_map/convert_element_type | solution.py:77
  34.7 1.1 %fusion.36 = (bf16[16,32,2,128]{3,1,2,0:T(8,128)(2,1)}, bf16[16,2,4,8,128]{4,3,2,1,0:T(8,128)(2,1)S(1)}) fusion(bf16[16,32,2,128]{3,1,2,0:T(8,128)(2,1)S(1)} %fusion.64, bf16[32,32]{1,0:T(8,128)(2,1)S(1)} %copy-done, bf16[16,32,256]{2,1,0:T(8,128)(2,1)S(1)} %copy-done.8), kind=kOutput, calls=%fused_computation.75 | convolution fusion | flops 9961472 | bytes 1050624 | tf_op jit(solution)/shard_map/gf,cfhw->cghw/dot_general | solution.py:78
  35.8 0.8 copy.242
  36.6 2.2 %gather_fusion = bf16[16,32,256]{2,1,0:T(8,128)(2,1)} fusion(bf16[16,32,256]{2,1,0:T(8,128)(2,1)} %bitcast.346, s32[1024]{0:T(1024)S(1)} %pad_clamp_fusion.1), kind=kCustom, calls=%fused_computation | custom fusion | bytes 524352 | tf_op jit(solution)/shard_map/gather | solution.py:86
  38.8 2.3 %fusion.9 = f32[7,32,32]{2,1,0:T(8,128)} fusion(bf16[16,7,32,256]{3,2,0,1:T(8,128)(2,1)S(1)} %fusion.123, bf16[16,32,256]{2,1,0:T(8,128)(2,1)} %gather_fusion), kind=kOutput, calls=%fused_computation.48 | convolution fusion | flops 58720256 | bytes 2125824 | tf_op jit(solution)/shard_map/mKp,mfp->Kf/dot_general | solution.py:112
  41.1 6.2 %collective-permute-start.4 = (bf16[16,32,256]{2,1,0:T(8,128)(2,1)}, bf16[16,32,256]{2,1,0:T(8,128)(2,1)S(1)}, u32[]{:S(2)}, u32[]{:S(2)}) collective-permute-start(bf16[16,32,256]{2,1,0:T(8,128)(2,1)} %gather_fusion), channel_id=1, source_target_pairs={{12,0},{0,4},{4,8},{8,12},{13,1},{1,5},{5,9},{9,13},{14,2},{2,6},{... | collective-permute-start | bytes 786440 | tf_op jit(solution)/shard_map/ppermute | solution.py:25
  47.3 1.5 %collective-permute-start.3 = (bf16[16,32,256]{2,1,0:T(8,128)(2,1)}, bf16[16,32,256]{2,1,0:T(8,128)(2,1)S(1)}, u32[]{:S(2)}, u32[]{:S(2)}) collective-permute-start(bf16[16,32,256]{2,1,0:T(8,128)(2,1)} %gather_fusion), channel_id=1, source_target_pairs={{8,0},{12,4},{0,8},{4,12},{9,1},{13,5},{1,9},{5,13},{10,2},{14,6},... | collective-permute-start | bytes 786440 | tf_op jit(solution)/shard_map/ppermute | solution.py:25
  48.8 0.9 collective-permute-start.2
  49.8 2.3 %fusion.34 = (f32[32]{0:T(128)}, f32[32]{0:T(128)}, f32[32]{0:T(128)}, f32[32]{0:T(128)}, f32[32]{0:T(128)}, /*index=5*/f32[32]{0:T(128)}, bf16[16,2,128,32]{2,3,1,0:T(8,128)(2,1)S(1)}) fusion(bf16[16,32,6,132]{3,1,2,0:T(8,128)(2,1)S(1)} %get-tuple-element.70, bf16[16,32,2,128]{3,1,2,0:T(8,128)(2,1)} %collective-permute-done, ...), kind=kOutput, calls=%fused_computation.72 | convolution fusion | flops 11272000 | bytes 1837824 | tf_op jit(solution)/shard_map/gf,cghw->cfhw/dot_general | solution.py:122
  52.1 2.3 %fusion.35 = (f32[32]{0:T(128)}, f32[32]{0:T(128)}, f32[32]{0:T(128)}, f32[32]{0:T(128)}, f32[32]{0:T(128)}, /*index=5*/f32[32]{0:T(128)}, f32[32]{0:T(128)}, f3...) fusion(bf16[16,32,6,132]{3,1,2,0:T(8,128)(2,1)S(1)} %get-tuple-, ...), kind=kLoop, calls=%fused_computation.73 | loop fusion | flops 7208384 | bytes 4983040 | tf_op jit(solution)/shard_map/cfhw,cfhw->f/dot_general | solution.py:137
  54.8 0.9 %rev.7 = f32[7,32,32]{2,1,0:T(8,128)S(1)} reverse(f32[7,32,32]{2,1,0:T(8,128)} %fusion.9), dimensions={0} | reverse | bytes 57344 | tf_op jit(solution)/shard_map/rev | solution.py:112
  55.9 0.8 multiply_reduce_fusion
  57.1 1.5 %collective-permute-start.13 = (f32[8192]{0:T(1024)S(1)}, f32[8192]{0:T(1024)S(1)}, u32[]{:S(2)}, u32[]{:S(2)}) collective-permute-start(f32[8192]{0:T(1024)S(1)} %fusion.134), channel_id=1, source_target_pairs={{0,2},{2,0},{1,3},{3,1},{4,6},{6,4},{5,7},{7,5},{8,10},{10,8},{9,1... | collective-permute-start | bytes 98312 | tf_op jit(solution)/shard_map/ppermute | solution.py:39
  59.0 1.0 %collective-permute-done.10 = f32[800]{0:T(1024)S(1)} collective-permute-done((f32[800]{0:T(1024)S(1)}, f32[800]{0:T(1024)S(1)}, u32[]{:S(2)}, u32[]{:S(2)}) %collective-permute-start.10) | collective-permute-done | bytes 3232 | tf_op jit(solution)/shard_map/ppermute | solution.py:39
  60.0 0.5 collective-permute-start.11
  60.5 3.1 %collective-permute-done.11 = f32[800]{0:T(1024)S(1)} collective-permute-done((f32[800]{0:T(1024)S(1)}, f32[800]{0:T(1024)S(1)}, u32[]{:S(2)}, u32[]{:S(2)}) %collective-permute-start.11) | collective-permute-done | bytes 3232 | tf_op jit(solution)/shard_map/ppermute | solution.py:39
  63.6 1.3 %collective-permute-start.9 = (bf16[16,32,2,128]{3,1,2,0:T(8,128)(2,1)S(1)}, bf16[16,32,2,128]{3,1,2,0:T(8,128)(2,1)S(1)}, u32[]{:S(2)}, u32[]{:S(2)}) collective-permute-start(bf16[16,32,2,128]{3,1,2,0:T(8,128)(2,1)S(1)} %bitcast.343), channel_id=1, source_target_pairs={{1,0},{2,1},{3,2},{5,4},{6,5},{7,6},{9,8},{10,9},{11,10},{13,12},{... | collective-permute-start | bytes 786440 | tf_op jit(solution)/shard_map/ppermute | solution.py:17
  64.9 3.2 %collective-permute-start.8 = (bf16[16,32,2,128]{3,1,2,0:T(8,128)(2,1)S(1)}, bf16[16,32,2,128]{3,1,2,0:T(8,128)(2,1)S(1)}, u32[]{:S(2)}, u32[]{:S(2)}) collective-permute-start(bf16[16,32,2,128]{3,1,2,0:T(8,128)(2,1)S(1)} %bitcast.344), channel_id=1, source_target_pairs={{0,1},{1,2},{2,3},{4,5},{5,6},{6,7},{8,9},{9,10},{10,11},{12,13},{... | collective-permute-start | bytes 786440 | tf_op jit(solution)/shard_map/ppermute | solution.py:14
  68.3 3.0 %collective-permute-start.14 = (f32[8992]{0:T(1024)S(1)}, f32[8992]{0:T(1024)S(1)}, u32[]{:S(2)}, u32[]{:S(2)}) collective-permute-start(f32[8992]{0:T(1024)S(1)} %pad_maximum_fusion.2), channel_id=1, source_target_pairs={{0,4},{4,0},{8,12},{12,8},{1,5},{5,1},{9,13},{13,9},{2,6},{6,2},{1... | collective-permute-start | bytes 107912 | tf_op jit(solution)/shard_map/ppermute | solution.py:39
  71.5 1.0 %bitcast_dynamic-update-slice_fusion = bf16[16,7,32,256]{3,2,1,0:T(8,128)(2,1)S(1)} fusion(bf16[16,7,32,256]{3,2,1,0:T(8,128)(2,1)S(1)} %fusion.96, bf16[16,32,256]{2,1,0:T(8,128)(2,1)} %gather_fusion), kind=kLoop, calls=%fused_computation.255 | loop fusion | bytes 524288
  72.6 0.7 fusion.3
  73.5 3.0 %fusion.39 = bf16[16,32,2,128]{3,1,2,0:T(8,128)(2,1)S(1)} fusion(f32[16,32,6,132]{3,1,2,0:T(8,128)S(1)} %fusion.3, bf16[16,32,2,128]{3,2,1,0:T(2,128)(2,1)S(1)} %copy-done.3, f32[32]{0:T(128)S(1)} %copy-done.13, f32[32]{0:T(128)S(1)} %copy-done.14, f32[32]{0:T(128)S(1)} %copy-done.16, f32[32]{0:T(128)S(1)} %copy-done.17, f32[32]{0:T(128)S(1)} %copy-done.18, ...), kind=kLoop, calls=%fused_computation.79 | loop fusion | flops 6815744 | bytes 13634688 | tf_op jit(solution)/shard_map/convert_element_type | solution.py:145
  76.7 0.6 fusion.7
  77.3 0.6 gather_fusion.1
  78.2 2.5 %collective-permute-start.15 = (f32[8992]{0:T(1024)S(1)}, f32[8992]{0:T(1024)S(1)}, u32[]{:S(2)}, u32[]{:S(2)}) collective-permute-start(f32[8992]{0:T(1024)S(1)} %add.288), channel_id=1, source_target_pairs={{0,8},{4,12},{8,0},{12,4},{1,9},{5,13},{9,1},{13,5},{2,10},{6,14},... | collective-permute-start | bytes 107912 | tf_op jit(solution)/shard_map/ppermute | solution.py:39
  80.7 1.0 %add_convert_fusion = bf16[16,32,2,128]{3,2,1,0:T(2,128)(2,1)} fusion(f32[16,32,2,128]{3,2,1,0:T(2,128)S(1)} %reshape.86, bf16[16,32,2,128]{3,2,1,0:T(2,128)(2,1)S(1)} %copy-done.2), kind=kLoop, calls=%fused_computation.179 | loop fusion | flops 393216 | bytes 1048576 | tf_op jit(solution)/shard_map/convert_element_type | solution.py:119
  81.7 0.9 %copy.48 = bf16[16,32,2,128]{3,2,1,0:T(2,128)(2,1)} copy(bf16[16,32,2,128]{3,1,2,0:T(8,128)(2,1)S(1)} %fusion.39) | data formatting | bytes 524288
  82.6 0.5 collective-permute-done.15
  83.3 0.7 reshape.84
  84.0 0.7 slice.492
  84.7 0.7 reshape.85
  (181 shorter events, 3.2 us)
Async XLA Ops:
  0.6 34.0 %copy-start = (bf16[32,32]{1,0:T(8,128)(2,1)S(1)}, bf16[32,32]{1,0:T(8,128)(2,1)}, u32[]{:S(2)}) copy-start(bf16[32,32]{1,0:T(8,128)(2,1)} %param.9) | copy-start | bytes 6148
  0.6 17.9 %copy-start.1 = (f32[32,25]{1,0:T(8,128)S(1)}, f32[32,25]{1,0:T(8,128)}, u32[]{:S(2)}) copy-start(f32[32,25]{1,0:T(8,128)} %param.8) | copy-start | bytes 9604
  0.7 19.0 %copy-start.12 = (bf16[7,32,32]{2,1,0:T(8,128)(2,1)S(1)}, bf16[7,32,32]{2,1,0:T(8,128)(2,1)}, u32[]{:S(2)}) copy-start(bf16[7,32,32]{2,1,0:T(8,128)(2,1)} %param.10) | copy-start | bytes 43012
  3.8 22.8 %collective-permute-start.7 = (bf16[16,32,256]{2,1,0:T(8,128)(2,1)S(1)}, bf16[16,32,256]{2,1,0:T(8,128)(2,1)S(1)}, u32[]{:S(2)}, u32[]{:S(2)}) collective-permute-start(bf16[16,32,256]{2,1,0:T(8,128)(2,1)S(1)} %gather_fusion.2), channel_id=1, source_target_pairs={{12,0},{0,4},{4,8},{8,12},{13,1},{1,5},{5,9},{9,13},{14,2},{2,6},{... | collective-permute-start | bytes 786440 | tf_op jit(solution)/shard_map/ppermute | solution.py:25
  6.9 19.7 %collective-permute-start.6 = (bf16[16,32,256]{2,1,0:T(8,128)(2,1)S(1)}, bf16[16,32,256]{2,1,0:T(8,128)(2,1)S(1)}, u32[]{:S(2)}, u32[]{:S(2)}) collective-permute-start(bf16[16,32,256]{2,1,0:T(8,128)(2,1)S(1)} %gather_fusion.2), channel_id=1, source_target_pairs={{8,0},{12,4},{0,8},{4,12},{9,1},{13,5},{1,9},{5,13},{10,2},{14,6},... | collective-permute-start | bytes 786440 | tf_op jit(solution)/shard_map/ppermute | solution.py:25
  9.5 14.3 %collective-permute-start.5 = (bf16[16,32,256]{2,1,0:T(8,128)(2,1)S(1)}, bf16[16,32,256]{2,1,0:T(8,128)(2,1)S(1)}, u32[]{:S(2)}, u32[]{:S(2)}) collective-permute-start(bf16[16,32,256]{2,1,0:T(8,128)(2,1)S(1)} %gather_fusion.2), channel_id=1, source_target_pairs={{4,0},{8,4},{12,8},{0,12},{5,1},{9,5},{13,9},{1,13},{6,2},{10,6},{... | collective-permute-start | bytes 786440 | tf_op jit(solution)/shard_map/ppermute | solution.py:25
  11.8 15.1 %copy-start.6 = (bf16[16,32,2,128]{3,1,2,0:T(8,128)(2,1)}, bf16[16,32,2,128]{3,1,2,0:T(8,128)(2,1)S(1)}, u32[]{:S(2)}) copy-start(bf16[16,32,2,128]{3,1,2,0:T(8,128)(2,1)S(1)} %copy.27) | copy-start | bytes 786436
  11.8 17.0 %collective-permute-start.1 = (bf16[16,32,2,128]{3,1,2,0:T(8,128)(2,1)S(1)}, bf16[16,32,2,128]{3,1,2,0:T(8,128)(2,1)S(1)}, u32[]{:S(2)}, u32[]{:S(2)}) collective-permute-start(bf16[16,32,2,128]{3,1,2,0:T(8,128)(2,1)S(1)} %copy.27), channel_id=1, source_target_pairs={{1,0},{2,1},{3,2},{5,4},{6,5},{7,6},{9,8},{10,9},{11,10},{13,12},{... | collective-permute-start | bytes 786440 | tf_op jit(solution)/shard_map/ppermute | solution.py:17
  13.1 16.4 %collective-permute-start = (bf16[16,32,2,128]{3,1,2,0:T(8,128)(2,1)S(1)}, bf16[16,32,2,128]{3,1,2,0:T(8,128)(2,1)}, u32[]{:S(2)}, u32[]{:S(2)}) collective-permute-start(bf16[16,32,2,128]{3,1,2,0:T(8,128)(2,1)S(1)} %copy.27), channel_id=1, source_target_pairs={{0,1},{1,2},{2,3},{4,5},{5,6},{6,7},{8,9},{9,10},{10,11},{12,13},{... | collective-permute-start | bytes 786440 | tf_op jit(solution)/shard_map/ppermute | solution.py:14
  28.6 2.8 %copy-start.13 = (f32[32]{0:T(128)S(1)}, f32[32]{0:T(128)}, u32[]{:S(2)}) copy-start(f32[32]{0:T(128)} %get-tuple-element.68) | copy-start | bytes 388
  28.6 2.8 %copy-start.14 = (f32[32]{0:T(128)S(1)}, f32[32]{0:T(128)}, u32[]{:S(2)}) copy-start(f32[32]{0:T(128)} %get-tuple-element.69) | copy-start | bytes 388
  28.6 2.8 %copy-start.15 = (f32[32]{0:T(128)S(1)}, f32[32]{0:T(128)}, u32[]{:S(2)}) copy-start(f32[32]{0:T(128)} %get-tuple-element.45) | copy-start | bytes 388
  28.7 2.8 %copy-start.16 = (f32[32]{0:T(128)S(1)}, f32[32]{0:T(128)}, u32[]{:S(2)}) copy-start(f32[32]{0:T(128)} %get-tuple-element.46) | copy-start | bytes 388
  28.7 2.8 %copy-start.17 = (f32[32]{0:T(128)S(1)}, f32[32]{0:T(128)}, u32[]{:S(2)}) copy-start(f32[32]{0:T(128)} %get-tuple-element.47) | copy-start | bytes 388
  28.7 2.8 %copy-start.18 = (f32[32]{0:T(128)S(1)}, f32[32]{0:T(128)}, u32[]{:S(2)}) copy-start(f32[32]{0:T(128)} %get-tuple-element.48) | copy-start | bytes 388
  28.7 2.8 %copy-start.19 = (f32[32]{0:T(128)S(1)}, f32[32]{0:T(128)}, u32[]{:S(2)}) copy-start(f32[32]{0:T(128)} %get-tuple-element.49) | copy-start | bytes 388
  28.7 2.8 %copy-start.20 = (f32[32]{0:T(128)S(1)}, f32[32]{0:T(128)}, u32[]{:S(2)}) copy-start(f32[32]{0:T(128)} %get-tuple-element.50) | copy-start | bytes 388
  28.7 2.8 %copy-start.21 = (f32[32]{0:T(128)S(1)}, f32[32]{0:T(128)}, u32[]{:S(2)}) copy-start(f32[32]{0:T(128)} %get-tuple-element.51) | copy-start | bytes 388
  28.7 2.8 %copy-start.22 = (f32[32]{0:T(128)S(1)}, f32[32]{0:T(128)}, u32[]{:S(2)}) copy-start(f32[32]{0:T(128)} %get-tuple-element.52) | copy-start | bytes 388
  28.7 2.8 %copy-start.23 = (f32[32]{0:T(128)S(1)}, f32[32]{0:T(128)}, u32[]{:S(2)}) copy-start(f32[32]{0:T(128)} %get-tuple-element.53) | copy-start | bytes 388
  28.7 2.8 %copy-start.24 = (f32[32]{0:T(128)S(1)}, f32[32]{0:T(128)}, u32[]{:S(2)}) copy-start(f32[32]{0:T(128)} %get-tuple-element.54) | copy-start | bytes 388
  28.7 2.8 %copy-start.25 = (f32[32]{0:T(128)S(1)}, f32[32]{0:T(128)}, u32[]{:S(2)}) copy-start(f32[32]{0:T(128)} %get-tuple-element.55) | copy-start | bytes 388
  28.7 2.8 %copy-start.26 = (f32[32]{0:T(128)S(1)}, f32[32]{0:T(128)}, u32[]{:S(2)}) copy-start(f32[32]{0:T(128)} %get-tuple-element.56) | copy-start | bytes 388
  28.8 2.8 %copy-start.27 = (f32[32]{0:T(128)S(1)}, f32[32]{0:T(128)}, u32[]{:S(2)}) copy-start(f32[32]{0:T(128)} %get-tuple-element.57) | copy-start | bytes 388
  28.8 2.8 %copy-start.29 = (f32[32]{0:T(128)S(1)}, f32[32]{0:T(128)}, u32[]{:S(2)}) copy-start(f32[32]{0:T(128)} %get-tuple-element.58) | copy-start | bytes 388
  28.8 2.8 %copy-start.31 = (f32[32]{0:T(128)S(1)}, f32[32]{0:T(128)}, u32[]{:S(2)}) copy-start(f32[32]{0:T(128)} %get-tuple-element.59) | copy-start | bytes 388
  28.8 2.8 %copy-start.33 = (f32[32]{0:T(128)S(1)}, f32[32]{0:T(128)}, u32[]{:S(2)}) copy-start(f32[32]{0:T(128)} %get-tuple-element.60) | copy-start | bytes 388
  28.8 2.8 %copy-start.35 = (f32[32]{0:T(128)S(1)}, f32[32]{0:T(128)}, u32[]{:S(2)}) copy-start(f32[32]{0:T(128)} %get-tuple-element.61) | copy-start | bytes 388
  28.8 2.8 %copy-start.37 = (f32[32]{0:T(128)S(1)}, f32[32]{0:T(128)}, u32[]{:S(2)}) copy-start(f32[32]{0:T(128)} %get-tuple-element.62) | copy-start | bytes 388
  28.8 2.8 %copy-start.39 = (f32[32]{0:T(128)S(1)}, f32[32]{0:T(128)}, u32[]{:S(2)}) copy-start(f32[32]{0:T(128)} %get-tuple-element.63) | copy-start | bytes 388
  31.6 3.1 %copy-start.8 = (bf16[16,32,256]{2,1,0:T(8,128)(2,1)S(1)}, bf16[16,32,256]{2,1,0:T(8,128)(2,1)}, u32[]{:S(2)}) copy-start(bf16[16,32,256]{2,1,0:T(8,128)(2,1)} %gather_fusion.3) | copy-start | bytes 786436
  38.8 10.8 %copy-start.5 = (bf16[16,32,2,128]{3,1,2,0:T(8,128)(2,1)S(1)}, bf16[16,32,2,128]{3,1,2,0:T(8,128)(2,1)}, u32[]{:S(2)}) copy-start(bf16[16,32,2,128]{3,1,2,0:T(8,128)(2,1)} %copy-done.4) | copy-start | bytes 786436
  38.8 10.8 %copy-start.9 = (bf16[16,32,2,128]{3,1,2,0:T(8,128)(2,1)S(1)}, bf16[16,32,2,128]{3,1,2,0:T(8,128)(2,1)}, u32[]{:S(2)}) copy-start(bf16[16,32,2,128]{3,1,2,0:T(8,128)(2,1)} %get-tuple-element.72) | copy-start | bytes 786436
  38.8 11.0 %copy-start.7 = (bf16[16,32,2,128]{3,1,2,0:T(8,128)(2,1)S(1)}, bf16[16,32,2,128]{3,1,2,0:T(8,128)(2,1)}, u32[]{:S(2)}) copy-start(bf16[16,32,2,128]{3,1,2,0:T(8,128)(2,1)} %copy-done.6) | copy-start | bytes 786436
  38.8 11.0 %copy-start.11 = (bf16[16,32,2,128]{3,1,2,0:T(8,128)(2,1)S(1)}, bf16[16,32,2,128]{3,1,2,0:T(8,128)(2,1)}, u32[]{:S(2)}) copy-start(bf16[16,32,2,128]{3,1,2,0:T(8,128)(2,1)} %copy-done.10) | copy-start | bytes 786436
  41.1 27.2 %collective-permute-start.4 = (bf16[16,32,256]{2,1,0:T(8,128)(2,1)}, bf16[16,32,256]{2,1,0:T(8,128)(2,1)S(1)}, u32[]{:S(2)}, u32[]{:S(2)}) collective-permute-start(bf16[16,32,256]{2,1,0:T(8,128)(2,1)} %gather_fusion), channel_id=1, source_target_pairs={{12,0},{0,4},{4,8},{8,12},{13,1},{1,5},{5,9},{9,13},{14,2},{2,6},{... | collective-permute-start | bytes 786440 | tf_op jit(solution)/shard_map/ppermute | solution.py:25
  47.3 21.0 %collective-permute-start.3 = (bf16[16,32,256]{2,1,0:T(8,128)(2,1)}, bf16[16,32,256]{2,1,0:T(8,128)(2,1)S(1)}, u32[]{:S(2)}, u32[]{:S(2)}) collective-permute-start(bf16[16,32,256]{2,1,0:T(8,128)(2,1)} %gather_fusion), channel_id=1, source_target_pairs={{8,0},{12,4},{0,8},{4,12},{9,1},{13,5},{1,9},{5,13},{10,2},{14,6},... | collective-permute-start | bytes 786440 | tf_op jit(solution)/shard_map/ppermute | solution.py:25
  48.8 19.5 %collective-permute-start.2 = (bf16[16,32,256]{2,1,0:T(8,128)(2,1)}, bf16[16,32,256]{2,1,0:T(8,128)(2,1)S(1)}, u32[]{:S(2)}, u32[]{:S(2)}) collective-permute-start(bf16[16,32,256]{2,1,0:T(8,128)(2,1)} %gather_fusion), channel_id=1, source_target_pairs={{4,0},{8,4},{12,8},{0,12},{5,1},{9,5},{13,9},{1,13},{6,2},{10,6},{... | collective-permute-start | bytes 786440 | tf_op jit(solution)/shard_map/ppermute | solution.py:25
  52.1 3.7 %copy-start.2 = (bf16[16,32,2,128]{3,2,1,0:T(2,128)(2,1)S(1)}, bf16[16,32,2,128]{3,2,1,0:T(2,128)(2,1)}, u32[]{:S(2)}) copy-start(bf16[16,32,2,128]{3,2,1,0:T(2,128)(2,1)} %param.6) | copy-start | bytes 786436
  54.4 2.2 %copy-start.46 = (f32[32]{0:T(128)S(1)}, f32[32]{0:T(128)}, u32[]{:S(2)}) copy-start(f32[32]{0:T(128)} %get-tuple-element.22) | copy-start | bytes 388
  55.8 1.3 %collective-permute-start.12 = (f32[8192]{0:T(1024)S(1)}, f32[8192]{0:T(1024)S(1)}, u32[]{:S(2)}, u32[]{:S(2)}) collective-permute-start(f32[8192]{0:T(1024)S(1)} %maximum_multiply_fusion), channel_id=1, source_target_pairs={{0,1},{1,0},{2,3},{3,2},{4,5},{5,4},{6,7},{7,6},{8,9},{9,8},{10,11... | collective-permute-start | bytes 98312 | tf_op jit(solution)/shard_map/ppermute | solution.py:39
  57.1 7.9 %collective-permute-start.13 = (f32[8192]{0:T(1024)S(1)}, f32[8192]{0:T(1024)S(1)}, u32[]{:S(2)}, u32[]{:S(2)}) collective-permute-start(f32[8192]{0:T(1024)S(1)} %fusion.134), channel_id=1, source_target_pairs={{0,2},{2,0},{1,3},{3,1},{4,6},{6,4},{5,7},{7,5},{8,10},{10,8},{9,1... | collective-permute-start | bytes 98312 | tf_op jit(solution)/shard_map/ppermute | solution.py:39
  58.8 1.2 %collective-permute-start.10 = (f32[800]{0:T(1024)S(1)}, f32[800]{0:T(1024)S(1)}, u32[]{:S(2)}, u32[]{:S(2)}) collective-permute-start(f32[800]{0:T(1024)S(1)} %mul.538), channel_id=1, source_target_pairs={{0,1},{1,0},{2,3},{3,2},{4,5},{5,4},{6,7},{7,6},{8,9},{9,8},{10,11... | collective-permute-start | bytes 9608 | tf_op jit(solution)/shard_map/ppermute | solution.py:39
  60.0 3.6 %collective-permute-start.11 = (f32[800]{0:T(1024)S(1)}, f32[800]{0:T(1024)S(1)}, u32[]{:S(2)}, u32[]{:S(2)}) collective-permute-start(f32[800]{0:T(1024)S(1)} %add.284), channel_id=1, source_target_pairs={{0,2},{2,0},{1,3},{3,1},{4,6},{6,4},{5,7},{7,5},{8,10},{10,8},{9,1... | collective-permute-start | bytes 9608 | tf_op jit(solution)/shard_map/ppermute | solution.py:39
  63.6 8.9 %collective-permute-start.9 = (bf16[16,32,2,128]{3,1,2,0:T(8,128)(2,1)S(1)}, bf16[16,32,2,128]{3,1,2,0:T(8,128)(2,1)S(1)}, u32[]{:S(2)}, u32[]{:S(2)}) collective-permute-start(bf16[16,32,2,128]{3,1,2,0:T(8,128)(2,1)S(1)} %bitcast.343), channel_id=1, source_target_pairs={{1,0},{2,1},{3,2},{5,4},{6,5},{7,6},{9,8},{10,9},{11,10},{13,12},{... | collective-permute-start | bytes 786440 | tf_op jit(solution)/shard_map/ppermute | solution.py:17
  64.9 7.6 %collective-permute-start.8 = (bf16[16,32,2,128]{3,1,2,0:T(8,128)(2,1)S(1)}, bf16[16,32,2,128]{3,1,2,0:T(8,128)(2,1)S(1)}, u32[]{:S(2)}, u32[]{:S(2)}) collective-permute-start(bf16[16,32,2,128]{3,1,2,0:T(8,128)(2,1)S(1)} %bitcast.344), channel_id=1, source_target_pairs={{0,1},{1,2},{2,3},{4,5},{5,6},{6,7},{8,9},{9,10},{10,11},{12,13},{... | collective-permute-start | bytes 786440 | tf_op jit(solution)/shard_map/ppermute | solution.py:14
  68.3 9.9 %collective-permute-start.14 = (f32[8992]{0:T(1024)S(1)}, f32[8992]{0:T(1024)S(1)}, u32[]{:S(2)}, u32[]{:S(2)}) collective-permute-start(f32[8992]{0:T(1024)S(1)} %pad_maximum_fusion.2), channel_id=1, source_target_pairs={{0,4},{4,0},{8,12},{12,8},{1,5},{5,1},{9,13},{13,9},{2,6},{6,2},{1... | collective-permute-start | bytes 107912 | tf_op jit(solution)/shard_map/ppermute | solution.py:39
  78.2 4.9 %collective-permute-start.15 = (f32[8992]{0:T(1024)S(1)}, f32[8992]{0:T(1024)S(1)}, u32[]{:S(2)}, u32[]{:S(2)}) collective-permute-start(f32[8992]{0:T(1024)S(1)} %add.288), channel_id=1, source_target_pairs={{0,8},{4,12},{8,0},{12,4},{1,9},{5,13},{9,1},{13,5},{2,10},{6,14},... | collective-permute-start | bytes 107912 | tf_op jit(solution)/shard_map/ppermute | solution.py:39
  (33 other events, 61.2 us)

commit v14 on v7

--- a/solution.py
+++ b/solution.py
@@ -47,6 +47,11 @@
     return sig * (1.0 + value * (1.0 - sig))
 
 
+def order_of(inverse, source, chans, n_chan):
+    table = inverse.reshape(chans, n_chan)
+    return lax.dynamic_index_in_dim(table, source, 1, keepdims=False) - source * chans
+
+
 def move_down(array):
     return jnp.pad(array, ((1, 0), (0, 0), (0, 0)))[:-1]
 
@@ -82,7 +87,11 @@
     device = lax.axis_index("chan")
     start = device * chans
     own = lax.dynamic_slice_in_dim(freq_table, start, chans) // n_chan
-    order = jnp.zeros((chans,), jnp.int32).at[own].set(jnp.arange(chans, dtype=jnp.int32))
+    total_chans = freq_table.shape[0]
+    inverse = jnp.zeros((total_chans,), jnp.int32).at[freq_table].set(
+        jnp.arange(total_chans, dtype=jnp.int32)
+    )
+    order = order_of(inverse, device, chans, n_chan)
     h_sorted = hidden_flat[order]
     g_sorted = grad_flat[order]
     h_taps = [h_sorted] * taps
@@ -92,7 +101,8 @@
         for sign in (-1, 1):
             h_far = passed_along(h_sorted, "chan", -sign * dist)
             h_received.append(h_far)
-            g_far = passed_along(g_sorted, "chan", -sign * dist)
+            g_far = passed_along(grad_flat, "chan", -sign * dist)
+            g_far = g_far[order_of(inverse, (device + sign * dist) % n_chan, chans, n_chan)]
             if sign < 0:
                 wrapped = device < dist
                 h_near = jnp.where(wrapped, move_down(h_far), h_far)

time: 83.5 us -> 91.6 us (1.097)
  local copies, waits for them, and re-layouts: 12.3 us -> 18.3 us
  waiting for transfers between devices: 20.3 us -> 22.1 us
  other arithmetic: 14.1 us -> 15.8 us
  starting transfers between devices: 29.1 us -> 28.1 us
    gather x0 -> x6, local copies, waits for them, and re-layouts: none -> 3.5 us  [local(): g_far[order_of(inverse, (device + sign * dist) % n_chan, chans, n_chan)]]
    ppermute x4, starting transfers between devices: 5.03 us -> 3.42 us  [all_summed(): lax.ppermute(value, axis, [(i, i ^ step) for i in range(count)])]
    slice x2, local copies, waits for them, and re-layouts: 2.85 us -> 4.31 us  [local(): spatial_kernel[:, i * 5 + j][None, :, None, None]]
    ppermute x4, waiting for transfers between devices: 13.5 us -> 14.5 us  [all_summed(): lax.ppermute(value, axis, [(i, i ^ step) for i in range(count)])]
    select_n x2 -> x3, other arithmetic: 0.76 us -> 1.71 us  [the longest x1 0.74 us: local(): spec_flat = fwd_acc.astype(jnp.bfloat16)[own]]
    unnamed x130 -> x126, local copies, waits for them, and re-layouts: 2.36 us -> 3.12 us
  transfers between devices with their start and end apart: 14 -> 14, of which waited for: 4 -> 4; matrix products, arithmetic and copies ran while one was open for 15% -> 24% of each run, Pallas kernels for 0% -> 0%
where the time goes in v14:
time: 91.6 us; the launch traced here: 91.1 us
  starting transfers between devices  28.1 us (31%)
  waiting for transfers between devices  22.1 us (24%)
  local copies, waits for them, and re-layouts  18.3 us (20%)
  other arithmetic  15.8 us (17%)
  matrix products  4.82 us (5%)
  between operations  1.96 us (2%)
    ppermute x6, starting transfers between devices, passed_along(): return lax.ppermute(block, axis, route)  16.3 us
    ppermute x4, waiting for transfers between devices, all_summed(): lax.ppermute(value, axis, [(i, i ^ step) for i in range(count)])  14.5 us
    ppermute x6, waiting for transfers between devices, passed_along(): return lax.ppermute(block, axis, route)  7.59 us
    ppermute x2, starting transfers between devices, padded(): lax.ppermute(lax.slice_in_dim(block, block.shape[dim] - width, None, axis...  5.85 us
    slice x2, local copies, waits for them, and re-layouts, local(): spatial_kernel[:, i * 5 + j][None, :, None, None]  4.31 us
    gather x6, local copies, waits for them, and re-layouts, local(): g_far[order_of(inverse, (device + sign * dist) % n_chan, chans, n_chan)]  3.5 us
    ppermute x4, starting transfers between devices, all_summed(): lax.ppermute(value, axis, [(i, i ^ step) for i in range(count)])  3.42 us
    unnamed x126, local copies, waits for them, and re-layouts  3.12 us
  transfers between devices with their start and end apart: 14, of which 4 were waited for; matrix products, arithmetic and copies ran while one was open for 24% of the time, Pallas kernels for 0%

profile of v14, /device:TPU:0, one launch (start us, length us, event | category | flops | bytes accessed | tf_op | source)
XLA Modules:
  0.0 91.1 jit_solution(11820419113812637834)
XLA Ops:
  0.7 1.7 %copy.27 = bf16[16,32,2,128]{3,1,2,0:T(8,128)(2,1)} copy(bf16[16,32,2,128]{3,2,1,0:T(2,128)(2,1)} %param.6) | data formatting | bytes 524288 | tf_op args[0]
  2.4 1.3 %collective-permute-start.1 = (bf16[16,32,2,128]{3,1,2,0:T(8,128)(2,1)}, bf16[16,32,2,128]{3,1,2,0:T(8,128)(2,1)}, u32[]{:S(2)}, u32[]{:S(2)}) collective-permute-start(bf16[16,32,2,128]{3,1,2,0:T(8,128)(2,1)} %copy.27), channel_id=1, source_target_pairs={{1,0},{2,1},{3,2},{5,4},{6,5},{7,6},{9,8},{10,9},{11,10},{13,12},{... | collective-permute-start | bytes 786440 | tf_op jit(solution)/shard_map/ppermute | solution.py:17
  3.7 3.7 %collective-permute-start = (bf16[16,32,2,128]{3,1,2,0:T(8,128)(2,1)}, bf16[16,32,2,128]{3,1,2,0:T(8,128)(2,1)}, u32[]{:S(2)}, u32[]{:S(2)}) collective-permute-start(bf16[16,32,2,128]{3,1,2,0:T(8,128)(2,1)} %copy.27), channel_id=1, source_target_pairs={{0,1},{1,2},{2,3},{4,5},{5,6},{6,7},{8,9},{9,10},{10,11},{12,13},{... | collective-permute-start | bytes 786440 | tf_op jit(solution)/shard_map/ppermute | solution.py:14
  7.4 1.1 %reshape.90 = bf16[16,32,256]{2,1,0:T(8,128)(2,1)S(1)} reshape(bf16[16,32,2,128]{3,2,1,0:T(2,128)(2,1)} %param.7) | data formatting | bytes 524288 | tf_op jit(solution)/shard_map/reshape | solution.py:86
  8.5 3.1 %collective-permute-start.7 = (bf16[16,32,256]{2,1,0:T(8,128)(2,1)S(1)}, bf16[16,32,256]{2,1,0:T(8,128)(2,1)S(1)}, u32[]{:S(2)}, u32[]{:S(2)}) collective-permute-start(bf16[16,32,256]{2,1,0:T(8,128)(2,1)S(1)} %reshape.90), channel_id=1, source_target_pairs={{12,0},{0,4},{4,8},{8,12},{13,1},{1,5},{5,9},{9,13},{14,2},{2,6},{... | collective-permute-start | bytes 786440 | tf_op jit(solution)/shard_map/ppermute | solution.py:25
  11.6 2.6 %collective-permute-start.6 = (bf16[16,32,256]{2,1,0:T(8,128)(2,1)S(1)}, bf16[16,32,256]{2,1,0:T(8,128)(2,1)S(1)}, u32[]{:S(2)}, u32[]{:S(2)}) collective-permute-start(bf16[16,32,256]{2,1,0:T(8,128)(2,1)S(1)} %reshape.90), channel_id=1, source_target_pairs={{8,0},{12,4},{0,8},{4,12},{9,1},{13,5},{1,9},{5,13},{10,2},{14,6},... | collective-permute-start | bytes 786440 | tf_op jit(solution)/shard_map/ppermute | solution.py:25
  14.2 1.3 %collective-permute-start.5 = (bf16[16,32,256]{2,1,0:T(8,128)(2,1)S(1)}, bf16[16,32,256]{2,1,0:T(8,128)(2,1)S(1)}, u32[]{:S(2)}, u32[]{:S(2)}) collective-permute-start(bf16[16,32,256]{2,1,0:T(8,128)(2,1)S(1)} %reshape.90), channel_id=1, source_target_pairs={{4,0},{8,4},{12,8},{0,12},{5,1},{9,5},{13,9},{1,13},{6,2},{10,6},{... | collective-permute-start | bytes 786440 | tf_op jit(solution)/shard_map/ppermute | solution.py:25
  15.5 0.7 compare_select_fusion.8
  16.2 0.7 compare_select_fusion.7
  16.9 1.8 %slice_reduce_fusion.23 = (f32[32]{0:T(128)}, f32[32]{0:T(128)}, f32[32]{0:T(128)}, f32[32]{0:T(128)}, f32[32]{0:T(128)}, /*index=5*/f32[32]{0:T(128)}) fusion(f32[32,25]{1,0:T(8,128)} %param.8), kind=kLoop, calls=%fused_computation.299 | loop fusion | bytes 1536 | tf_op jit(solution)/shard_map/slice | solution.py:79
  18.7 0.8 scatter_custom_fusion
  19.9 0.6 pad_clamp_fusion.1
  20.5 2.5 %slice_reduce_fusion.24 = (f32[32]{0:T(128)}, f32[32]{0:T(128)}, f32[32]{0:T(128)}, f32[32]{0:T(128)}, f32[32]{0:T(128)}, /*index=5*/f32[32]{0:T(128)}, f32[32]{...) fusion(f32[32,25]{1,0:T(8,128)} %param.8), kind=kLoop, calls=%fused_computation.300 | loop fusion | bytes 4864 | tf_op jit(solution)/shard_map/slice | solution.py:79
  23.1 0.6 gather_fusion.5
  23.7 5.4 %collective-permute-done.5 = bf16[16,32,256]{2,1,0:T(8,128)(2,1)S(1)} collective-permute-done((bf16[16,32,256]{2,1,0:T(8,128)(2,1)S(1)}, bf16[16,32,256]{2,1,0:T(8,128)(2,1)S(1)}, u32[]{:S(2)}, u32[]{:S(2)}) %collective-permute-start.5) | collective-permute-done | bytes 262176 | tf_op jit(solution)/shard_map/ppermute | solution.py:25
  29.1 0.6 gather_fusion.2
  29.7 2.2 %collective-permute-done.6 = bf16[16,32,256]{2,1,0:T(8,128)(2,1)S(1)} collective-permute-done((bf16[16,32,256]{2,1,0:T(8,128)(2,1)S(1)}, bf16[16,32,256]{2,1,0:T(8,128)(2,1)S(1)}, u32[]{:S(2)}, u32[]{:S(2)}) %collective-permute-start.6) | collective-permute-done | bytes 262176 | tf_op jit(solution)/shard_map/ppermute | solution.py:25
  31.9 0.7 gather_fusion.3
  32.6 0.6 gather_fusion.4
  33.3 0.6 gather_fusion.6
  33.9 0.6 gather_fusion.7
  34.6 0.6 gather_fusion.8
  35.7 0.6 gather_fusion.9
  36.5 1.9 %select_maximum_fusion.2 = (bf16[16,32,6,132]{3,1,2,0:T(8,128)(2,1)S(1)}, f32[16,32,6,132]{3,1,2,0:T(8,128)S(1)}) fusion(bf16[16,32,2,128]{3,1,2,0:T(8,128)(2,1)} %collective-permute-done.1, bf16[16,32,2,128]{3,1,2,0:T(8,128)(2,1)} %copy.27, bf16[16,32,2,128]{3,1,2,0:T(8,128)(2,1)} %collective-permute-done), kind=kLoop, calls=%fused_computation.43 | loop fusion | flops 5271552 | bytes 3219456 | tf_op jit(solution)/shard_map/concatenate | solution.py:18
  38.7 3.0 %fusion.64 = bf16[16,32,2,128]{3,1,2,0:T(8,128)(2,1)S(1)} fusion(f32[16,32,6,132]{3,1,2,0:T(8,128)S(1)} %get-tuple-element.78, f32[32]{0:T(128)S(1)} %copy-done.8, f32[32]{0:T(128)S(1)} %copy-done.9, f32[32]{0:T(128)S(1)} %copy-done.11, f32[32]{0:T(128)S(1)} %copy-done.12, f32[32]{0:T(128)S(1)} %copy-done.13, f32[32]{0:T(128)S(1)} %copy-done.14, ...), kind=kLoop, calls=%fused_computation.135 | loop fusion | flops 6553600 | bytes 13372544 | tf_op jit(solution)/shard_map/convert_element_type | solution.py:82
  42.3 2.5 %fusion.34 = (f32[32]{0:T(128)}, f32[32]{0:T(128)}, f32[32]{0:T(128)}, f32[32]{0:T(128)}, f32[32]{0:T(128)}, /*index=5*/f32[32]{0:T(128)}, bf16[16,2,128,32]{2,3,1,0:T(8,128)(2,1)S(1)}) fusion(bf16[16,32,6,132]{3,1,2,0:T(8,128)(2,1)S(1)} %get-tuple-element.77, bf16[16,32,2,128]{3,1,2,0:T(8,128)(2,1)} %collective-permute-done, ...), kind=kOutput, calls=%fused_computation.78 | convolution fusion | flops 11272000 | bytes 1837824 | tf_op jit(solution)/shard_map/gf,cghw->cfhw/dot_general | solution.py:132
  44.9 2.3 %fusion.35 = (f32[32]{0:T(128)}, f32[32]{0:T(128)}, f32[32]{0:T(128)}, f32[32]{0:T(128)}, f32[32]{0:T(128)}, /*index=5*/f32[32]{0:T(128)}, f32[32]{0:T(128)}, f3...) fusion(bf16[16,32,6,132]{3,1,2,0:T(8,128)(2,1)S(1)} %get-tuple-, ...), kind=kLoop, calls=%fused_computation.79 | loop fusion | flops 7208384 | bytes 4983040 | tf_op jit(solution)/shard_map/cfhw,cfhw->f/dot_general | solution.py:147
  47.4 0.6 gather_fusion
  48.2 0.6 fusion.9
  48.9 0.8 multiply_reduce_fusion
  50.4 6.8 %collective-permute-start.4 = (bf16[16,32,256]{2,1,0:T(8,128)(2,1)S(1)}, bf16[16,32,256]{2,1,0:T(8,128)(2,1)S(1)}, u32[]{:S(2)}, u32[]{:S(2)}) collective-permute-start(bf16[16,32,256]{2,1,0:T(8,128)(2,1)S(1)} %gather_fusion), channel_id=1, source_target_pairs={{12,0},{0,4},{4,8},{8,12},{13,1},{1,5},{5,9},{9,13},{14,2},{2,6},{... | collective-permute-start | bytes 786440 | tf_op jit(solution)/shard_map/ppermute | solution.py:25
  57.2 1.0 %collective-permute-start.3 = (bf16[16,32,256]{2,1,0:T(8,128)(2,1)S(1)}, bf16[16,32,256]{2,1,0:T(8,128)(2,1)S(1)}, u32[]{:S(2)}, u32[]{:S(2)}) collective-permute-start(bf16[16,32,256]{2,1,0:T(8,128)(2,1)S(1)} %gather_fusion), channel_id=1, source_target_pairs={{8,0},{12,4},{0,8},{4,12},{9,1},{13,5},{1,9},{5,13},{10,2},{14,6},... | collective-permute-start | bytes 786440 | tf_op jit(solution)/shard_map/ppermute | solution.py:25
  58.1 1.5 %collective-permute-start.2 = (bf16[16,32,256]{2,1,0:T(8,128)(2,1)S(1)}, bf16[16,32,256]{2,1,0:T(8,128)(2,1)S(1)}, u32[]{:S(2)}, u32[]{:S(2)}) collective-permute-start(bf16[16,32,256]{2,1,0:T(8,128)(2,1)S(1)} %gather_fusion), channel_id=1, source_target_pairs={{4,0},{8,4},{12,8},{0,12},{5,1},{9,5},{13,9},{1,13},{6,2},{10,6},{... | collective-permute-start | bytes 786440 | tf_op jit(solution)/shard_map/ppermute | solution.py:25
  60.1 3.5 %collective-permute-done.11 = f32[8992]{0:T(1024)S(1)} collective-permute-done((f32[8992]{0:T(1024)S(1)}, f32[8992]{0:T(1024)S(1)}, u32[]{:S(2)}, u32[]{:S(2)}) %collective-permute-start.11) | collective-permute-done | bytes 36000 | tf_op jit(solution)/shard_map/ppermute | solution.py:39
  63.7 0.5 collective-permute-start.12
  64.2 1.3 %collective-permute-start.9 = (bf16[16,32,2,128]{3,1,2,0:T(8,128)(2,1)S(1)}, bf16[16,32,2,128]{3,1,2,0:T(8,128)(2,1)S(1)}, u32[]{:S(2)}, u32[]{:S(2)}) collective-permute-start(bf16[16,32,2,128]{3,1,2,0:T(8,128)(2,1)S(1)} %bitcast.343), channel_id=1, source_target_pairs={{1,0},{2,1},{3,2},{5,4},{6,5},{7,6},{9,8},{10,9},{11,10},{13,12},{... | collective-permute-start | bytes 786440 | tf_op jit(solution)/shard_map/ppermute | solution.py:17
  65.5 11.0 %collective-permute-done.12 = f32[8992]{0:T(1024)S(1)} collective-permute-done((f32[8992]{0:T(1024)S(1)}, f32[8992]{0:T(1024)S(1)}, u32[]{:S(2)}, u32[]{:S(2)}) %collective-permute-start.12) | collective-permute-done | bytes 36000 | tf_op jit(solution)/shard_map/ppermute | solution.py:39
  76.5 2.1 %collective-permute-start.8 = (bf16[16,32,2,128]{3,1,2,0:T(8,128)(2,1)S(1)}, bf16[16,32,2,128]{3,1,2,0:T(8,128)(2,1)S(1)}, u32[]{:S(2)}, u32[]{:S(2)}) collective-permute-start(bf16[16,32,2,128]{3,1,2,0:T(8,128)(2,1)S(1)} %bitcast.344), channel_id=1, source_target_pairs={{0,1},{1,2},{2,3},{4,5},{5,6},{6,7},{8,9},{9,10},{10,11},{12,13},{... | collective-permute-start | bytes 786440 | tf_op jit(solution)/shard_map/ppermute | solution.py:14
  78.7 2.3 %collective-permute-start.13 = (f32[8992]{0:T(1024)S(1)}, f32[8992]{0:T(1024)S(1)}, u32[]{:S(2)}, u32[]{:S(2)}) collective-permute-start(f32[8992]{0:T(1024)S(1)} %add.387), channel_id=1, source_target_pairs={{0,8},{4,12},{8,0},{12,4},{1,9},{5,13},{9,1},{13,5},{2,10},{6,14},... | collective-permute-start | bytes 107912 | tf_op jit(solution)/shard_map/ppermute | solution.py:39
  81.4 0.6 fusion.7
  82.0 0.6 gather_fusion.1
  83.0 0.7 fusion.3
  83.9 3.0 %fusion.39 = bf16[16,32,2,128]{3,1,2,0:T(8,128)(2,1)S(1)} fusion(f32[16,32,6,132]{3,1,2,0:T(8,128)S(1)} %fusion.3, bf16[16,32,2,128]{3,2,1,0:T(2,128)(2,1)S(1)} %copy-done.2, f32[32]{0:T(128)S(1)} %copy-done.8, f32[32]{0:T(128)S(1)} %copy-done.9, f32[32]{0:T(128)S(1)} %copy-done.11, f32[32]{0:T(128)S(1)} %copy-done.12, f32[32]{0:T(128)S(1)} %copy-done.13, ...), kind=kLoop, calls=%fused_computation.85 | loop fusion | flops 6815744 | bytes 13634688 | tf_op jit(solution)/shard_map/convert_element_type | solution.py:155
  86.9 1.0 %add_convert_fusion = bf16[16,32,2,128]{3,2,1,0:T(2,128)(2,1)} fusion(f32[16,32,2,128]{3,2,1,0:T(2,128)S(1)} %reshape.97, bf16[16,32,2,128]{3,2,1,0:T(2,128)(2,1)S(1)} %copy-done.1), kind=kLoop, calls=%fused_computation.185 | loop fusion | flops 393216 | bytes 1048576 | tf_op jit(solution)/shard_map/convert_element_type | solution.py:129
  87.9 0.9 %copy.48 = bf16[16,32,2,128]{3,2,1,0:T(2,128)(2,1)} copy(bf16[16,32,2,128]{3,1,2,0:T(8,128)(2,1)S(1)} %fusion.39) | data formatting | bytes 524288
  89.0 0.7 reshape.95
  89.7 0.7 split.13
  90.4 0.7 reshape.96
  (178 shorter events, 4.3 us)
Async XLA Ops:
  0.6 41.1 %copy-start = (bf16[32,32]{1,0:T(8,128)(2,1)S(1)}, bf16[32,32]{1,0:T(8,128)(2,1)}, u32[]{:S(2)}) copy-start(bf16[32,32]{1,0:T(8,128)(2,1)} %param.9) | copy-start | bytes 6148
  0.6 22.4 %copy-start.3 = (bf16[7,32,32]{2,1,0:T(8,128)(2,1)S(1)}, bf16[7,32,32]{2,1,0:T(8,128)(2,1)}, u32[]{:S(2)}) copy-start(bf16[7,32,32]{2,1,0:T(8,128)(2,1)} %param.10) | copy-start | bytes 43012
  2.4 34.1 %collective-permute-start.1 = (bf16[16,32,2,128]{3,1,2,0:T(8,128)(2,1)}, bf16[16,32,2,128]{3,1,2,0:T(8,128)(2,1)}, u32[]{:S(2)}, u32[]{:S(2)}) collective-permute-start(bf16[16,32,2,128]{3,1,2,0:T(8,128)(2,1)} %copy.27), channel_id=1, source_target_pairs={{1,0},{2,1},{3,2},{5,4},{6,5},{7,6},{9,8},{10,9},{11,10},{13,12},{... | collective-permute-start | bytes 786440 | tf_op jit(solution)/shard_map/ppermute | solution.py:17
  3.7 32.8 %collective-permute-start = (bf16[16,32,2,128]{3,1,2,0:T(8,128)(2,1)}, bf16[16,32,2,128]{3,1,2,0:T(8,128)(2,1)}, u32[]{:S(2)}, u32[]{:S(2)}) collective-permute-start(bf16[16,32,2,128]{3,1,2,0:T(8,128)(2,1)} %copy.27), channel_id=1, source_target_pairs={{0,1},{1,2},{2,3},{4,5},{5,6},{6,7},{8,9},{9,10},{10,11},{12,13},{... | collective-permute-start | bytes 786440 | tf_op jit(solution)/shard_map/ppermute | solution.py:14
  8.5 24.1 %collective-permute-start.7 = (bf16[16,32,256]{2,1,0:T(8,128)(2,1)S(1)}, bf16[16,32,256]{2,1,0:T(8,128)(2,1)S(1)}, u32[]{:S(2)}, u32[]{:S(2)}) collective-permute-start(bf16[16,32,256]{2,1,0:T(8,128)(2,1)S(1)} %reshape.90), channel_id=1, source_target_pairs={{12,0},{0,4},{4,8},{8,12},{13,1},{1,5},{5,9},{9,13},{14,2},{2,6},{... | collective-permute-start | bytes 786440 | tf_op jit(solution)/shard_map/ppermute | solution.py:25
  11.6 20.3 %collective-permute-start.6 = (bf16[16,32,256]{2,1,0:T(8,128)(2,1)S(1)}, bf16[16,32,256]{2,1,0:T(8,128)(2,1)S(1)}, u32[]{:S(2)}, u32[]{:S(2)}) collective-permute-start(bf16[16,32,256]{2,1,0:T(8,128)(2,1)S(1)} %reshape.90), channel_id=1, source_target_pairs={{8,0},{12,4},{0,8},{4,12},{9,1},{13,5},{1,9},{5,13},{10,2},{14,6},... | collective-permute-start | bytes 786440 | tf_op jit(solution)/shard_map/ppermute | solution.py:25
  14.2 14.9 %collective-permute-start.5 = (bf16[16,32,256]{2,1,0:T(8,128)(2,1)S(1)}, bf16[16,32,256]{2,1,0:T(8,128)(2,1)S(1)}, u32[]{:S(2)}, u32[]{:S(2)}) collective-permute-start(bf16[16,32,256]{2,1,0:T(8,128)(2,1)S(1)} %reshape.90), channel_id=1, source_target_pairs={{4,0},{8,4},{12,8},{0,12},{5,1},{9,5},{13,9},{1,13},{6,2},{10,6},{... | collective-permute-start | bytes 786440 | tf_op jit(solution)/shard_map/ppermute | solution.py:25
  36.2 2.2 %copy-start.4 = (f32[32]{0:T(128)S(1)}, f32[32]{0:T(128)}, u32[]{:S(2)}) copy-start(f32[32]{0:T(128)} %get-tuple-element.64) | copy-start | bytes 388
  36.3 2.2 %copy-start.5 = (f32[32]{0:T(128)S(1)}, f32[32]{0:T(128)}, u32[]{:S(2)}) copy-start(f32[32]{0:T(128)} %get-tuple-element.65) | copy-start | bytes 388
  36.3 2.2 %copy-start.6 = (f32[32]{0:T(128)S(1)}, f32[32]{0:T(128)}, u32[]{:S(2)}) copy-start(f32[32]{0:T(128)} %get-tuple-element.66) | copy-start | bytes 388
  36.3 2.2 %copy-start.7 = (f32[32]{0:T(128)S(1)}, f32[32]{0:T(128)}, u32[]{:S(2)}) copy-start(f32[32]{0:T(128)} %get-tuple-element.67) | copy-start | bytes 388
  36.3 2.2 %copy-start.8 = (f32[32]{0:T(128)S(1)}, f32[32]{0:T(128)}, u32[]{:S(2)}) copy-start(f32[32]{0:T(128)} %get-tuple-element.68) | copy-start | bytes 388
  36.3 2.2 %copy-start.9 = (f32[32]{0:T(128)S(1)}, f32[32]{0:T(128)}, u32[]{:S(2)}) copy-start(f32[32]{0:T(128)} %get-tuple-element.69) | copy-start | bytes 388
  36.3 2.2 %copy-start.10 = (f32[32]{0:T(128)S(1)}, f32[32]{0:T(128)}, u32[]{:S(2)}) copy-start(f32[32]{0:T(128)} %get-tuple-element.45) | copy-start | bytes 388
  36.3 2.2 %copy-start.11 = (f32[32]{0:T(128)S(1)}, f32[32]{0:T(128)}, u32[]{:S(2)}) copy-start(f32[32]{0:T(128)} %get-tuple-element.46) | copy-start | bytes 388
  36.3 2.2 %copy-start.12 = (f32[32]{0:T(128)S(1)}, f32[32]{0:T(128)}, u32[]{:S(2)}) copy-start(f32[32]{0:T(128)} %get-tuple-element.47) | copy-start | bytes 388
  36.3 2.2 %copy-start.13 = (f32[32]{0:T(128)S(1)}, f32[32]{0:T(128)}, u32[]{:S(2)}) copy-start(f32[32]{0:T(128)} %get-tuple-element.48) | copy-start | bytes 388
  36.3 2.2 %copy-start.14 = (f32[32]{0:T(128)S(1)}, f32[32]{0:T(128)}, u32[]{:S(2)}) copy-start(f32[32]{0:T(128)} %get-tuple-element.49) | copy-start | bytes 388
  36.4 2.2 %copy-start.15 = (f32[32]{0:T(128)S(1)}, f32[32]{0:T(128)}, u32[]{:S(2)}) copy-start(f32[32]{0:T(128)} %get-tuple-element.50) | copy-start | bytes 388
  36.4 2.2 %copy-start.16 = (f32[32]{0:T(128)S(1)}, f32[32]{0:T(128)}, u32[]{:S(2)}) copy-start(f32[32]{0:T(128)} %get-tuple-element.51) | copy-start | bytes 388
  36.4 2.2 %copy-start.17 = (f32[32]{0:T(128)S(1)}, f32[32]{0:T(128)}, u32[]{:S(2)}) copy-start(f32[32]{0:T(128)} %get-tuple-element.52) | copy-start | bytes 388
  36.4 2.2 %copy-start.18 = (f32[32]{0:T(128)S(1)}, f32[32]{0:T(128)}, u32[]{:S(2)}) copy-start(f32[32]{0:T(128)} %get-tuple-element.53) | copy-start | bytes 388
  36.4 2.2 %copy-start.19 = (f32[32]{0:T(128)S(1)}, f32[32]{0:T(128)}, u32[]{:S(2)}) copy-start(f32[32]{0:T(128)} %get-tuple-element.54) | copy-start | bytes 388
  36.4 2.2 %copy-start.20 = (f32[32]{0:T(128)S(1)}, f32[32]{0:T(128)}, u32[]{:S(2)}) copy-start(f32[32]{0:T(128)} %get-tuple-element.55) | copy-start | bytes 388
  36.4 2.2 %copy-start.21 = (f32[32]{0:T(128)S(1)}, f32[32]{0:T(128)}, u32[]{:S(2)}) copy-start(f32[32]{0:T(128)} %get-tuple-element.56) | copy-start | bytes 388
  36.4 2.2 %copy-start.23 = (f32[32]{0:T(128)S(1)}, f32[32]{0:T(128)}, u32[]{:S(2)}) copy-start(f32[32]{0:T(128)} %get-tuple-element.57) | copy-start | bytes 388
  36.4 2.2 %copy-start.25 = (f32[32]{0:T(128)S(1)}, f32[32]{0:T(128)}, u32[]{:S(2)}) copy-start(f32[32]{0:T(128)} %get-tuple-element.58) | copy-start | bytes 388
  36.4 2.2 %copy-start.27 = (f32[32]{0:T(128)S(1)}, f32[32]{0:T(128)}, u32[]{:S(2)}) copy-start(f32[32]{0:T(128)} %get-tuple-element.59) | copy-start | bytes 388
  36.5 2.2 %copy-start.29 = (f32[32]{0:T(128)S(1)}, f32[32]{0:T(128)}, u32[]{:S(2)}) copy-start(f32[32]{0:T(128)} %get-tuple-element.60) | copy-start | bytes 388
  36.5 2.2 %copy-start.31 = (f32[32]{0:T(128)S(1)}, f32[32]{0:T(128)}, u32[]{:S(2)}) copy-start(f32[32]{0:T(128)} %get-tuple-element.61) | copy-start | bytes 388
  36.5 2.2 %copy-start.33 = (f32[32]{0:T(128)S(1)}, f32[32]{0:T(128)}, u32[]{:S(2)}) copy-start(f32[32]{0:T(128)} %get-tuple-element.62) | copy-start | bytes 388
  36.5 2.2 %copy-start.35 = (f32[32]{0:T(128)S(1)}, f32[32]{0:T(128)}, u32[]{:S(2)}) copy-start(f32[32]{0:T(128)} %get-tuple-element.63) | copy-start | bytes 388
  47.9 1.7 %copy-start.37 = (f32[32]{0:T(128)S(1)}, f32[32]{0:T(128)}, u32[]{:S(2)}) copy-start(f32[32]{0:T(128)} %get-tuple-element.17) | copy-start | bytes 388
  47.9 1.7 %copy-start.38 = (f32[32]{0:T(128)S(1)}, f32[32]{0:T(128)}, u32[]{:S(2)}) copy-start(f32[32]{0:T(128)} %get-tuple-element.18) | copy-start | bytes 388
  48.0 1.7 %copy-start.39 = (f32[32]{0:T(128)S(1)}, f32[32]{0:T(128)}, u32[]{:S(2)}) copy-start(f32[32]{0:T(128)} %get-tuple-element.19) | copy-start | bytes 388
  48.0 1.7 %copy-start.40 = (f32[32]{0:T(128)S(1)}, f32[32]{0:T(128)}, u32[]{:S(2)}) copy-start(f32[32]{0:T(128)} %get-tuple-element.20) | copy-start | bytes 388
  48.0 1.7 %copy-start.41 = (f32[32]{0:T(128)S(1)}, f32[32]{0:T(128)}, u32[]{:S(2)}) copy-start(f32[32]{0:T(128)} %get-tuple-element.21) | copy-start | bytes 388
  48.0 1.7 %copy-start.42 = (f32[32]{0:T(128)S(1)}, f32[32]{0:T(128)}, u32[]{:S(2)}) copy-start(f32[32]{0:T(128)} %get-tuple-element.22) | copy-start | bytes 388
  48.0 1.7 %copy-start.43 = (f32[32]{0:T(128)S(1)}, f32[32]{0:T(128)}, u32[]{:S(2)}) copy-start(f32[32]{0:T(128)} %get-tuple-element.23) | copy-start | bytes 388
  50.3 9.3 %collective-permute-start.10 = (f32[8992]{0:T(1024)S(1)}, f32[8992]{0:T(1024)S(1)}, u32[]{:S(2)}, u32[]{:S(2)}) collective-permute-start(f32[8992]{0:T(1024)S(1)} %broadcast_multiply_fusion), channel_id=1, source_target_pairs={{0,1},{1,0},{2,3},{3,2},{4,5},{5,4},{6,7},{7,6},{8,9},{9,8},{10,11... | collective-permute-start | bytes 107912 | tf_op jit(solution)/shard_map/ppermute | solution.py:39
  50.4 28.3 %collective-permute-start.4 = (bf16[16,32,256]{2,1,0:T(8,128)(2,1)S(1)}, bf16[16,32,256]{2,1,0:T(8,128)(2,1)S(1)}, u32[]{:S(2)}, u32[]{:S(2)}) collective-permute-start(bf16[16,32,256]{2,1,0:T(8,128)(2,1)S(1)} %gather_fusion), channel_id=1, source_target_pairs={{12,0},{0,4},{4,8},{8,12},{13,1},{1,5},{5,9},{9,13},{14,2},{2,6},{... | collective-permute-start | bytes 786440 | tf_op jit(solution)/shard_map/ppermute | solution.py:25
  57.2 21.5 %collective-permute-start.3 = (bf16[16,32,256]{2,1,0:T(8,128)(2,1)S(1)}, bf16[16,32,256]{2,1,0:T(8,128)(2,1)S(1)}, u32[]{:S(2)}, u32[]{:S(2)}) collective-permute-start(bf16[16,32,256]{2,1,0:T(8,128)(2,1)S(1)} %gather_fusion), channel_id=1, source_target_pairs={{8,0},{12,4},{0,8},{4,12},{9,1},{13,5},{1,9},{5,13},{10,2},{14,6},... | collective-permute-start | bytes 786440 | tf_op jit(solution)/shard_map/ppermute | solution.py:25
  58.1 20.5 %collective-permute-start.2 = (bf16[16,32,256]{2,1,0:T(8,128)(2,1)S(1)}, bf16[16,32,256]{2,1,0:T(8,128)(2,1)S(1)}, u32[]{:S(2)}, u32[]{:S(2)}) collective-permute-start(bf16[16,32,256]{2,1,0:T(8,128)(2,1)S(1)} %gather_fusion), channel_id=1, source_target_pairs={{4,0},{8,4},{12,8},{0,12},{5,1},{9,5},{13,9},{1,13},{6,2},{10,6},{... | collective-permute-start | bytes 786440 | tf_op jit(solution)/shard_map/ppermute | solution.py:25
  59.6 4.0 %collective-permute-start.11 = (f32[8992]{0:T(1024)S(1)}, f32[8992]{0:T(1024)S(1)}, u32[]{:S(2)}, u32[]{:S(2)}) collective-permute-start(f32[8992]{0:T(1024)S(1)} %fusion.141), channel_id=1, source_target_pairs={{0,2},{2,0},{1,3},{3,1},{4,6},{6,4},{5,7},{7,5},{8,10},{10,8},{9,1... | collective-permute-start | bytes 107912 | tf_op jit(solution)/shard_map/ppermute | solution.py:39
  63.7 12.8 %collective-permute-start.12 = (f32[8992]{0:T(1024)S(1)}, f32[8992]{0:T(1024)S(1)}, u32[]{:S(2)}, u32[]{:S(2)}) collective-permute-start(f32[8992]{0:T(1024)S(1)} %add.386), channel_id=1, source_target_pairs={{0,4},{4,0},{8,12},{12,8},{1,5},{5,1},{9,13},{13,9},{2,6},{6,2},{1... | collective-permute-start | bytes 107912 | tf_op jit(solution)/shard_map/ppermute | solution.py:39
  64.2 18.7 %collective-permute-start.9 = (bf16[16,32,2,128]{3,1,2,0:T(8,128)(2,1)S(1)}, bf16[16,32,2,128]{3,1,2,0:T(8,128)(2,1)S(1)}, u32[]{:S(2)}, u32[]{:S(2)}) collective-permute-start(bf16[16,32,2,128]{3,1,2,0:T(8,128)(2,1)S(1)} %bitcast.343), channel_id=1, source_target_pairs={{1,0},{2,1},{3,2},{5,4},{6,5},{7,6},{9,8},{10,9},{11,10},{13,12},{... | collective-permute-start | bytes 786440 | tf_op jit(solution)/shard_map/ppermute | solution.py:17
  76.5 6.5 %collective-permute-start.8 = (bf16[16,32,2,128]{3,1,2,0:T(8,128)(2,1)S(1)}, bf16[16,32,2,128]{3,1,2,0:T(8,128)(2,1)S(1)}, u32[]{:S(2)}, u32[]{:S(2)}) collective-permute-start(bf16[16,32,2,128]{3,1,2,0:T(8,128)(2,1)S(1)} %bitcast.344), channel_id=1, source_target_pairs={{0,1},{1,2},{2,3},{4,5},{5,6},{6,7},{8,9},{9,10},{10,11},{12,13},{... | collective-permute-start | bytes 786440 | tf_op jit(solution)/shard_map/ppermute | solution.py:14
  78.7 10.2 %collective-permute-start.13 = (f32[8992]{0:T(1024)S(1)}, f32[8992]{0:T(1024)S(1)}, u32[]{:S(2)}, u32[]{:S(2)}) collective-permute-start(f32[8992]{0:T(1024)S(1)} %add.387), channel_id=1, source_target_pairs={{0,8},{4,12},{8,0},{12,4},{1,9},{5,13},{9,1},{13,5},{2,10},{6,14},... | collective-permute-start | bytes 107912 | tf_op jit(solution)/shard_map/ppermute | solution.py:39
  (27 other events, 39.2 us)

commit v15 on v7

--- a/solution.py
+++ b/solution.py
@@ -82,7 +82,8 @@
     device = lax.axis_index("chan")
     start = device * chans
     own = lax.dynamic_slice_in_dim(freq_table, start, chans) // n_chan
-    order = jnp.zeros((chans,), jnp.int32).at[own].set(jnp.arange(chans, dtype=jnp.int32))
+    slots = jnp.arange(chans, dtype=jnp.int32)
+    order = jnp.sum(jnp.where(own[None, :] == slots[:, None], slots[None, :], 0), axis=1)
     h_sorted = hidden_flat[order]
     g_sorted = grad_flat[order]
     h_taps = [h_sorted] * taps

time: 83.5 us -> 82.9 us (level)
  no operation moved by 1% of the time
where the time goes in v15:
time: 82.9 us; the launch traced here: 82.5 us
  starting transfers between devices  29.1 us (35%)
  waiting for transfers between devices  20.3 us (24%)
  other arithmetic  14.2 us (17%)
  local copies, waits for them, and re-layouts  11.7 us (14%)
  matrix products  5.29 us (6%)
  between operations  1.92 us (2%)
    ppermute x6, starting transfers between devices, passed_along(): return lax.ppermute(block, axis, route)  15.7 us
    ppermute x4, waiting for transfers between devices, all_summed(): lax.ppermute(value, axis, [(i, i ^ step) for i in range(count)])  13.5 us
    ppermute x6, waiting for transfers between devices, passed_along(): return lax.ppermute(block, axis, route)  6.81 us
    ppermute x2, starting transfers between devices, padded(): lax.ppermute(lax.slice_in_dim(block, block.shape[dim] - width, None, axis...  5.84 us
    ppermute x4, starting transfers between devices, all_summed(): lax.ppermute(value, axis, [(i, i ^ step) for i in range(count)])  5.02 us
    dot_general x2, other arithmetic, local(): jnp.einsum('cfhw,cfhw->f', dsmooth, xpad[:, :, i:i + rows, j:j + cols], p...  3.05 us
    convert_element_type x1, other arithmetic, local(): dirty_grad = (cotangent.astype(jnp.float32) + conv).astype(jnp.bfloat16)  3.04 us
    convert_element_type x1, other arithmetic, local(): smooth = total.astype(jnp.bfloat16)  3.03 us
  transfers between devices with their start and end apart: 14, of which 4 were waited for; matrix products, arithmetic and copies ran while one was open for 15% of the time, Pallas kernels for 0%

profile of v15, /device:TPU:0, one launch (start us, length us, event | category | flops | bytes accessed | tf_op | source)
XLA Modules:
  0.0 82.5 jit_solution(11602114427078465827)
XLA Ops:
  0.7 0.8 compare_select_fusion
  1.4 0.1 select_reduce_fusion
  1.6 1.1 %reshape.94 = bf16[16,32,256]{2,1,0:T(8,128)(2,1)S(1)} reshape(bf16[16,32,2,128]{3,2,1,0:T(2,128)(2,1)} %param.7) | data formatting | bytes 524288 | tf_op jit(solution)/shard_map/reshape | solution.py:81
  2.7 0.6 gather_fusion.2
  3.3 3.1 %collective-permute-start.7 = (bf16[16,32,256]{2,1,0:T(8,128)(2,1)S(1)}, bf16[16,32,256]{2,1,0:T(8,128)(2,1)S(1)}, u32[]{:S(2)}, u32[]{:S(2)}) collective-permute-start(bf16[16,32,256]{2,1,0:T(8,128)(2,1)S(1)} %gather_fusion.2), channel_id=1, source_target_pairs={{12,0},{0,4},{4,8},{8,12},{13,1},{1,5},{5,9},{9,13},{14,2},{2,6},{... | collective-permute-start | bytes 786440 | tf_op jit(solution)/shard_map/ppermute | solution.py:25
  6.3 2.6 %collective-permute-start.6 = (bf16[16,32,256]{2,1,0:T(8,128)(2,1)S(1)}, bf16[16,32,256]{2,1,0:T(8,128)(2,1)S(1)}, u32[]{:S(2)}, u32[]{:S(2)}) collective-permute-start(bf16[16,32,256]{2,1,0:T(8,128)(2,1)S(1)} %gather_fusion.2), channel_id=1, source_target_pairs={{8,0},{12,4},{0,8},{4,12},{9,1},{13,5},{1,9},{5,13},{10,2},{14,6},... | collective-permute-start | bytes 786440 | tf_op jit(solution)/shard_map/ppermute | solution.py:25
  8.9 1.3 %collective-permute-start.5 = (bf16[16,32,256]{2,1,0:T(8,128)(2,1)S(1)}, bf16[16,32,256]{2,1,0:T(8,128)(2,1)S(1)}, u32[]{:S(2)}, u32[]{:S(2)}) collective-permute-start(bf16[16,32,256]{2,1,0:T(8,128)(2,1)S(1)} %gather_fusion.2), channel_id=1, source_target_pairs={{4,0},{8,4},{12,8},{0,12},{5,1},{9,5},{13,9},{1,13},{6,2},{10,6},{... | collective-permute-start | bytes 786440 | tf_op jit(solution)/shard_map/ppermute | solution.py:25
  10.3 1.0 %copy.49 = bf16[16,32,2,128]{3,1,2,0:T(8,128)(2,1)S(1)} copy(bf16[16,32,2,128]{3,2,1,0:T(2,128)(2,1)} %param.6) | data formatting | bytes 524288 | tf_op args[0]
  11.3 1.3 %collective-permute-start.1 = (bf16[16,32,2,128]{3,1,2,0:T(8,128)(2,1)S(1)}, bf16[16,32,2,128]{3,1,2,0:T(8,128)(2,1)S(1)}, u32[]{:S(2)}, u32[]{:S(2)}) collective-permute-start(bf16[16,32,2,128]{3,1,2,0:T(8,128)(2,1)S(1)} %copy.49), channel_id=1, source_target_pairs={{1,0},{2,1},{3,2},{5,4},{6,5},{7,6},{9,8},{10,9},{11,10},{13,12},{... | collective-permute-start | bytes 786440 | tf_op jit(solution)/shard_map/ppermute | solution.py:17
  12.6 3.7 %collective-permute-start = (bf16[16,32,2,128]{3,1,2,0:T(8,128)(2,1)S(1)}, bf16[16,32,2,128]{3,1,2,0:T(8,128)(2,1)}, u32[]{:S(2)}, u32[]{:S(2)}) collective-permute-start(bf16[16,32,2,128]{3,1,2,0:T(8,128)(2,1)S(1)} %copy.49), channel_id=1, source_target_pairs={{0,1},{1,2},{2,3},{4,5},{5,6},{6,7},{8,9},{9,10},{10,11},{12,13},{... | collective-permute-start | bytes 786440 | tf_op jit(solution)/shard_map/ppermute | solution.py:14
  16.3 1.7 %slice_reduce_fusion.23 = (f32[32]{0:T(128)S(1)}, f32[32]{0:T(128)S(1)}, f32[32]{0:T(128)S(1)}, f32[32]{0:T(128)S(1)}, f32[32]{0:T(128)}, /*index=5*/f32[32]{0:T(128)}) fusion(f32[32,25]{1,0:T(8,128)} %param.8), kind=kLoop, calls=%fused_computation.285 | loop fusion | bytes 1536 | tf_op jit(solution)/shard_map/slice | solution.py:74
  18.0 1.1 %slice_reduce_fusion.24 = (f32[32]{0:T(128)}, f32[32]{0:T(128)}, f32[32]{0:T(128)}, f32[32]{0:T(128)}, f32[32]{0:T(128)}, /*index=5*/f32[32]{0:T(128)}, f32[32]{...) fusion(f32[32,25]{1,0:T(8,128)S(1)} %copy-done.1), kind=kLoop, calls=%fused_computation.286 | loop fusion | bytes 4864 | tf_op jit(solution)/shard_map/slice | solution.py:74
  19.2 4.0 %collective-permute-done.5 = bf16[16,32,256]{2,1,0:T(8,128)(2,1)S(1)} collective-permute-done((bf16[16,32,256]{2,1,0:T(8,128)(2,1)S(1)}, bf16[16,32,256]{2,1,0:T(8,128)(2,1)S(1)}, u32[]{:S(2)}, u32[]{:S(2)}) %collective-permute-start.5) | collective-permute-done | bytes 262176 | tf_op jit(solution)/shard_map/ppermute | solution.py:25
  23.2 2.8 %collective-permute-done.6 = bf16[16,32,256]{2,1,0:T(8,128)(2,1)S(1)} collective-permute-done((bf16[16,32,256]{2,1,0:T(8,128)(2,1)S(1)}, bf16[16,32,256]{2,1,0:T(8,128)(2,1)S(1)}, u32[]{:S(2)}, u32[]{:S(2)}) %collective-permute-start.6) | collective-permute-done | bytes 262176 | tf_op jit(solution)/shard_map/ppermute | solution.py:25
  26.4 0.5 fusion.8
  26.9 0.6 gather_fusion.3
  27.7 1.7 %select_maximum_fusion.2 = (bf16[16,32,6,132]{3,1,2,0:T(8,128)(2,1)S(1)}, f32[16,32,6,132]{3,1,2,0:T(8,128)S(1)}) fusion(bf16[16,32,2,128]{3,1,2,0:T(8,128)(2,1)S(1)} %collective-permute-done.1, bf16[16,32,2,128]{3,1,2,0:T(8,128)(2,1)S(1)} %copy.49, bf16[16,32,2,128]{3,1,2,0:T(8,128)(2,1)} %collective-permute-done), kind=kLoop, calls=%fused_computation.36 | loop fusion | flops 5271552 | bytes 3219456 | tf_op jit(solution)/shard_map/concatenate | solution.py:18
  29.6 3.0 %fusion.64 = bf16[16,32,2,128]{3,1,2,0:T(8,128)(2,1)S(1)} fusion(f32[16,32,6,132]{3,1,2,0:T(8,128)S(1)} %get-tuple-element.78, f32[32]{0:T(128)S(1)} %copy-done.6, f32[32]{0:T(128)S(1)} %copy-done.7, f32[32]{0:T(128)S(1)} %copy-done.9, f32[32]{0:T(128)S(1)} %copy-done.10, f32[32]{0:T(128)S(1)} %copy-done.11, f32[32]{0:T(128)S(1)} %copy-done.12, ...), kind=kLoop, calls=%fused_computation.128 | loop fusion | flops 6553600 | bytes 13372544 | tf_op jit(solution)/shard_map/convert_element_type | solution.py:77
  32.7 1.1 %fusion.36 = (bf16[16,32,2,128]{3,1,2,0:T(8,128)(2,1)S(1)}, bf16[16,2,4,8,128]{4,3,2,1,0:T(8,128)(2,1)}) fusion(bf16[16,32,2,128]{3,1,2,0:T(8,128)(2,1)S(1)} %fusion.64, bf16[32,32]{1,0:T(8,128)(2,1)S(1)} %copy-done, bf16[16,32,256]{2,1,0:T(8,128)(2,1)S(1)} %gather_fusion.3), kind=kOutput, calls=%fused_computation.74 | convolution fusion | flops 9961472 | bytes 1050624 | tf_op jit(solution)/shard_map/gf,cfhw->cghw/dot_general | solution.py:78
  33.8 0.2 convolution_bitcast_fusion.3
  34.0 2.3 %fusion.34 = (f32[32]{0:T(128)}, f32[32]{0:T(128)}, f32[32]{0:T(128)}, f32[32]{0:T(128)}, f32[32]{0:T(128)}, /*index=5*/f32[32]{0:T(128)}, bf16[16,2,128,32]{2,3,1,0:T(8,128)(2,1)S(1)}) fusion(bf16[16,32,6,132]{3,1,2,0:T(8,128)(2,1)S(1)} %get-tuple-element.77, bf16[16,32,2,128]{3,1,2,0:T(8,128)(2,1)} %collective-permute-done, ...), kind=kOutput, calls=%fused_computation.71 | convolution fusion | flops 11272000 | bytes 1837824 | tf_op jit(solution)/shard_map/gf,cghw->cfhw/dot_general | solution.py:123
  36.3 2.3 %fusion.35 = (f32[32]{0:T(128)}, f32[32]{0:T(128)}, f32[32]{0:T(128)}, f32[32]{0:T(128)}, f32[32]{0:T(128)}, /*index=5*/f32[32]{0:T(128)}, f32[32]{0:T(128)}, f3...) fusion(bf16[16,32,6,132]{3,1,2,0:T(8,128)(2,1)S(1)} %get-tuple-, ...), kind=kLoop, calls=%fused_computation.72 | loop fusion | flops 7208384 | bytes 4983040 | tf_op jit(solution)/shard_map/cfhw,cfhw->f/dot_general | solution.py:138
  38.8 0.6 gather_fusion
  39.6 0.6 fusion.9
  40.3 0.8 multiply_reduce_fusion
  41.3 0.1 stack.167
  41.5 0.1 reshape.95
  41.8 6.2 %collective-permute-start.4 = (bf16[16,32,256]{2,1,0:T(8,128)(2,1)S(1)}, bf16[16,32,256]{2,1,0:T(8,128)(2,1)S(1)}, u32[]{:S(2)}, u32[]{:S(2)}) collective-permute-start(bf16[16,32,256]{2,1,0:T(8,128)(2,1)S(1)} %gather_fusion), channel_id=1, source_target_pairs={{12,0},{0,4},{4,8},{8,12},{13,1},{1,5},{5,9},{9,13},{14,2},{2,6},{... | collective-permute-start | bytes 786440 | tf_op jit(solution)/shard_map/ppermute | solution.py:25
  48.0 1.5 %collective-permute-start.3 = (bf16[16,32,256]{2,1,0:T(8,128)(2,1)S(1)}, bf16[16,32,256]{2,1,0:T(8,128)(2,1)S(1)}, u32[]{:S(2)}, u32[]{:S(2)}) collective-permute-start(bf16[16,32,256]{2,1,0:T(8,128)(2,1)S(1)} %gather_fusion), channel_id=1, source_target_pairs={{8,0},{12,4},{0,8},{4,12},{9,1},{13,5},{1,9},{5,13},{10,2},{14,6},... | collective-permute-start | bytes 786440 | tf_op jit(solution)/shard_map/ppermute | solution.py:25
  49.5 0.9 %collective-permute-start.2 = (bf16[16,32,256]{2,1,0:T(8,128)(2,1)S(1)}, bf16[16,32,256]{2,1,0:T(8,128)(2,1)S(1)}, u32[]{:S(2)}, u32[]{:S(2)}) collective-permute-start(bf16[16,32,256]{2,1,0:T(8,128)(2,1)S(1)} %gather_fusion), channel_id=1, source_target_pairs={{4,0},{8,4},{12,8},{0,12},{5,1},{9,5},{13,9},{1,13},{6,2},{10,6},{... | collective-permute-start | bytes 786440 | tf_op jit(solution)/shard_map/ppermute | solution.py:25
  50.4 1.6 %collective-permute-start.11 = (f32[8992]{0:T(1024)S(1)}, f32[8992]{0:T(1024)S(1)}, u32[]{:S(2)}, u32[]{:S(2)}) collective-permute-start(f32[8992]{0:T(1024)S(1)} %fusion.133), channel_id=1, source_target_pairs={{0,2},{2,0},{1,3},{3,1},{4,6},{6,4},{5,7},{7,5},{8,10},{10,8},{9,1... | collective-permute-start | bytes 107912 | tf_op jit(solution)/shard_map/ppermute | solution.py:39
  52.0 2.5 %collective-permute-done.11 = f32[8992]{0:T(1024)S(1)} collective-permute-done((f32[8992]{0:T(1024)S(1)}, f32[8992]{0:T(1024)S(1)}, u32[]{:S(2)}, u32[]{:S(2)}) %collective-permute-start.11) | collective-permute-done | bytes 36000 | tf_op jit(solution)/shard_map/ppermute | solution.py:39
  54.5 1.1 %collective-permute-start.12 = (f32[8992]{0:T(1024)S(1)}, f32[8992]{0:T(1024)S(1)}, u32[]{:S(2)}, u32[]{:S(2)}) collective-permute-start(f32[8992]{0:T(1024)S(1)} %add.285), channel_id=1, source_target_pairs={{0,4},{4,0},{8,12},{12,8},{1,5},{5,1},{9,13},{13,9},{2,6},{6,2},{1... | collective-permute-start | bytes 107912 | tf_op jit(solution)/shard_map/ppermute | solution.py:39
  55.6 1.3 %collective-permute-start.9 = (bf16[16,32,2,128]{3,1,2,0:T(8,128)(2,1)S(1)}, bf16[16,32,2,128]{3,1,2,0:T(8,128)(2,1)S(1)}, u32[]{:S(2)}, u32[]{:S(2)}) collective-permute-start(bf16[16,32,2,128]{3,1,2,0:T(8,128)(2,1)S(1)} %bitcast.346), channel_id=1, source_target_pairs={{1,0},{2,1},{3,2},{5,4},{6,5},{7,6},{9,8},{10,9},{11,10},{13,12},{... | collective-permute-start | bytes 786440 | tf_op jit(solution)/shard_map/ppermute | solution.py:17
  56.8 11.0 %collective-permute-done.12 = f32[8992]{0:T(1024)S(1)} collective-permute-done((f32[8992]{0:T(1024)S(1)}, f32[8992]{0:T(1024)S(1)}, u32[]{:S(2)}, u32[]{:S(2)}) %collective-permute-start.12) | collective-permute-done | bytes 36000 | tf_op jit(solution)/shard_map/ppermute | solution.py:39
  67.9 2.1 %collective-permute-start.8 = (bf16[16,32,2,128]{3,1,2,0:T(8,128)(2,1)S(1)}, bf16[16,32,2,128]{3,1,2,0:T(8,128)(2,1)S(1)}, u32[]{:S(2)}, u32[]{:S(2)}) collective-permute-start(bf16[16,32,2,128]{3,1,2,0:T(8,128)(2,1)S(1)} %bitcast.347), channel_id=1, source_target_pairs={{0,1},{1,2},{2,3},{4,5},{5,6},{6,7},{8,9},{9,10},{10,11},{12,13},{... | collective-permute-start | bytes 786440 | tf_op jit(solution)/shard_map/ppermute | solution.py:14
  70.0 2.3 %collective-permute-start.13 = (f32[8992]{0:T(1024)S(1)}, f32[8992]{0:T(1024)S(1)}, u32[]{:S(2)}, u32[]{:S(2)}) collective-permute-start(f32[8992]{0:T(1024)S(1)} %add.286), channel_id=1, source_target_pairs={{0,8},{4,12},{8,0},{12,4},{1,9},{5,13},{9,1},{13,5},{2,10},{6,14},... | collective-permute-start | bytes 107912 | tf_op jit(solution)/shard_map/ppermute | solution.py:39
  72.7 0.6 fusion.7
  73.4 0.6 gather_fusion.1
  73.9 0.3 reshape.101
  74.4 0.7 fusion.3
  75.1 0.1 copy-done.3
  75.3 3.0 %fusion.39 = bf16[16,32,2,128]{3,1,2,0:T(8,128)(2,1)S(1)} fusion(f32[16,32,6,132]{3,1,2,0:T(8,128)S(1)} %fusion.3, bf16[16,32,2,128]{3,2,1,0:T(2,128)(2,1)S(1)} %copy-done.3, f32[32]{0:T(128)S(1)} %copy-done.6, f32[32]{0:T(128)S(1)} %copy-done.7, f32[32]{0:T(128)S(1)} %copy-done.9, f32[32]{0:T(128)S(1)} %copy-done.10, f32[32]{0:T(128)S(1)} %copy-done.11, ...), kind=kLoop, calls=%fused_computation.78 | loop fusion | flops 6815744 | bytes 13634688 | tf_op jit(solution)/shard_map/convert_element_type | solution.py:146
  78.3 1.0 %add_convert_fusion = bf16[16,32,2,128]{3,2,1,0:T(2,128)(2,1)} fusion(f32[16,32,2,128]{3,2,1,0:T(2,128)S(1)} %reshape.101, bf16[16,32,2,128]{3,2,1,0:T(2,128)(2,1)S(1)} %copy-done.2), kind=kLoop, calls=%fused_computation.178 | loop fusion | flops 393216 | bytes 1048576 | tf_op jit(solution)/shard_map/convert_element_type | solution.py:120
  79.3 0.9 %copy.69 = bf16[16,32,2,128]{3,2,1,0:T(2,128)(2,1)} copy(bf16[16,32,2,128]{3,1,2,0:T(8,128)(2,1)S(1)} %fusion.39) | data formatting | bytes 524288
  80.4 0.7 reshape.99
  81.1 0.7 split.13
  81.8 0.7 reshape.100
  (169 shorter events, 1.7 us)
Async XLA Ops:
  0.6 32.0 %copy-start = (bf16[32,32]{1,0:T(8,128)(2,1)S(1)}, bf16[32,32]{1,0:T(8,128)(2,1)}, u32[]{:S(2)}) copy-start(bf16[32,32]{1,0:T(8,128)(2,1)} %param.9) | copy-start | bytes 6148
  0.6 17.4 %copy-start.1 = (f32[32,25]{1,0:T(8,128)S(1)}, f32[32,25]{1,0:T(8,128)}, u32[]{:S(2)}) copy-start(f32[32,25]{1,0:T(8,128)} %param.8) | copy-start | bytes 9604
  0.7 18.5 %copy-start.5 = (bf16[7,32,32]{2,1,0:T(8,128)(2,1)S(1)}, bf16[7,32,32]{2,1,0:T(8,128)(2,1)}, u32[]{:S(2)}) copy-start(bf16[7,32,32]{2,1,0:T(8,128)(2,1)} %param.10) | copy-start | bytes 43012
  3.3 22.8 %collective-permute-start.7 = (bf16[16,32,256]{2,1,0:T(8,128)(2,1)S(1)}, bf16[16,32,256]{2,1,0:T(8,128)(2,1)S(1)}, u32[]{:S(2)}, u32[]{:S(2)}) collective-permute-start(bf16[16,32,256]{2,1,0:T(8,128)(2,1)S(1)} %gather_fusion.2), channel_id=1, source_target_pairs={{12,0},{0,4},{4,8},{8,12},{13,1},{1,5},{5,9},{9,13},{14,2},{2,6},{... | collective-permute-start | bytes 786440 | tf_op jit(solution)/shard_map/ppermute | solution.py:25
  6.3 19.7 %collective-permute-start.6 = (bf16[16,32,256]{2,1,0:T(8,128)(2,1)S(1)}, bf16[16,32,256]{2,1,0:T(8,128)(2,1)S(1)}, u32[]{:S(2)}, u32[]{:S(2)}) collective-permute-start(bf16[16,32,256]{2,1,0:T(8,128)(2,1)S(1)} %gather_fusion.2), channel_id=1, source_target_pairs={{8,0},{12,4},{0,8},{4,12},{9,1},{13,5},{1,9},{5,13},{10,2},{14,6},... | collective-permute-start | bytes 786440 | tf_op jit(solution)/shard_map/ppermute | solution.py:25
  8.9 14.3 %collective-permute-start.5 = (bf16[16,32,256]{2,1,0:T(8,128)(2,1)S(1)}, bf16[16,32,256]{2,1,0:T(8,128)(2,1)S(1)}, u32[]{:S(2)}, u32[]{:S(2)}) collective-permute-start(bf16[16,32,256]{2,1,0:T(8,128)(2,1)S(1)} %gather_fusion.2), channel_id=1, source_target_pairs={{4,0},{8,4},{12,8},{0,12},{5,1},{9,5},{13,9},{1,13},{6,2},{10,6},{... | collective-permute-start | bytes 786440 | tf_op jit(solution)/shard_map/ppermute | solution.py:25
  11.3 16.4 %collective-permute-start.1 = (bf16[16,32,2,128]{3,1,2,0:T(8,128)(2,1)S(1)}, bf16[16,32,2,128]{3,1,2,0:T(8,128)(2,1)S(1)}, u32[]{:S(2)}, u32[]{:S(2)}) collective-permute-start(bf16[16,32,2,128]{3,1,2,0:T(8,128)(2,1)S(1)} %copy.49), channel_id=1, source_target_pairs={{1,0},{2,1},{3,2},{5,4},{6,5},{7,6},{9,8},{10,9},{11,10},{13,12},{... | collective-permute-start | bytes 786440 | tf_op jit(solution)/shard_map/ppermute | solution.py:17
  12.6 15.1 %collective-permute-start = (bf16[16,32,2,128]{3,1,2,0:T(8,128)(2,1)S(1)}, bf16[16,32,2,128]{3,1,2,0:T(8,128)(2,1)}, u32[]{:S(2)}, u32[]{:S(2)}) collective-permute-start(bf16[16,32,2,128]{3,1,2,0:T(8,128)(2,1)S(1)} %copy.49), channel_id=1, source_target_pairs={{0,1},{1,2},{2,3},{4,5},{5,6},{6,7},{8,9},{9,10},{10,11},{12,13},{... | collective-permute-start | bytes 786440 | tf_op jit(solution)/shard_map/ppermute | solution.py:14
  27.4 2.0 %copy-start.6 = (f32[32]{0:T(128)S(1)}, f32[32]{0:T(128)}, u32[]{:S(2)}) copy-start(f32[32]{0:T(128)} %get-tuple-element.73) | copy-start | bytes 388
  27.4 2.0 %copy-start.7 = (f32[32]{0:T(128)S(1)}, f32[32]{0:T(128)}, u32[]{:S(2)}) copy-start(f32[32]{0:T(128)} %get-tuple-element.74) | copy-start | bytes 388
  27.5 2.0 %copy-start.8 = (f32[32]{0:T(128)S(1)}, f32[32]{0:T(128)}, u32[]{:S(2)}) copy-start(f32[32]{0:T(128)} %get-tuple-element.50) | copy-start | bytes 388
  27.5 2.0 %copy-start.9 = (f32[32]{0:T(128)S(1)}, f32[32]{0:T(128)}, u32[]{:S(2)}) copy-start(f32[32]{0:T(128)} %get-tuple-element.51) | copy-start | bytes 388
  27.5 2.0 %copy-start.10 = (f32[32]{0:T(128)S(1)}, f32[32]{0:T(128)}, u32[]{:S(2)}) copy-start(f32[32]{0:T(128)} %get-tuple-element.52) | copy-start | bytes 388
  27.5 2.0 %copy-start.11 = (f32[32]{0:T(128)S(1)}, f32[32]{0:T(128)}, u32[]{:S(2)}) copy-start(f32[32]{0:T(128)} %get-tuple-element.53) | copy-start | bytes 388
  27.5 2.0 %copy-start.12 = (f32[32]{0:T(128)S(1)}, f32[32]{0:T(128)}, u32[]{:S(2)}) copy-start(f32[32]{0:T(128)} %get-tuple-element.54) | copy-start | bytes 388
  27.5 2.0 %copy-start.13 = (f32[32]{0:T(128)S(1)}, f32[32]{0:T(128)}, u32[]{:S(2)}) copy-start(f32[32]{0:T(128)} %get-tuple-element.55) | copy-start | bytes 388
  27.5 2.0 %copy-start.14 = (f32[32]{0:T(128)S(1)}, f32[32]{0:T(128)}, u32[]{:S(2)}) copy-start(f32[32]{0:T(128)} %get-tuple-element.56) | copy-start | bytes 388
  27.5 2.0 %copy-start.15 = (f32[32]{0:T(128)S(1)}, f32[32]{0:T(128)}, u32[]{:S(2)}) copy-start(f32[32]{0:T(128)} %get-tuple-element.57) | copy-start | bytes 388
  27.5 2.0 %copy-start.17 = (f32[32]{0:T(128)S(1)}, f32[32]{0:T(128)}, u32[]{:S(2)}) copy-start(f32[32]{0:T(128)} %get-tuple-element.58) | copy-start | bytes 388
  27.6 2.0 %copy-start.19 = (f32[32]{0:T(128)S(1)}, f32[32]{0:T(128)}, u32[]{:S(2)}) copy-start(f32[32]{0:T(128)} %get-tuple-element.59) | copy-start | bytes 388
  27.6 2.0 %copy-start.21 = (f32[32]{0:T(128)S(1)}, f32[32]{0:T(128)}, u32[]{:S(2)}) copy-start(f32[32]{0:T(128)} %get-tuple-element.60) | copy-start | bytes 388
  27.6 2.0 %copy-start.23 = (f32[32]{0:T(128)S(1)}, f32[32]{0:T(128)}, u32[]{:S(2)}) copy-start(f32[32]{0:T(128)} %get-tuple-element.61) | copy-start | bytes 388
  27.6 2.0 %copy-start.25 = (f32[32]{0:T(128)S(1)}, f32[32]{0:T(128)}, u32[]{:S(2)}) copy-start(f32[32]{0:T(128)} %get-tuple-element.62) | copy-start | bytes 388
  27.6 2.0 %copy-start.27 = (f32[32]{0:T(128)S(1)}, f32[32]{0:T(128)}, u32[]{:S(2)}) copy-start(f32[32]{0:T(128)} %get-tuple-element.63) | copy-start | bytes 388
  27.6 2.0 %copy-start.29 = (f32[32]{0:T(128)S(1)}, f32[32]{0:T(128)}, u32[]{:S(2)}) copy-start(f32[32]{0:T(128)} %get-tuple-element.64) | copy-start | bytes 388
  27.6 2.0 %copy-start.31 = (f32[32]{0:T(128)S(1)}, f32[32]{0:T(128)}, u32[]{:S(2)}) copy-start(f32[32]{0:T(128)} %get-tuple-element.65) | copy-start | bytes 388
  27.6 2.0 %copy-start.33 = (f32[32]{0:T(128)S(1)}, f32[32]{0:T(128)}, u32[]{:S(2)}) copy-start(f32[32]{0:T(128)} %get-tuple-element.66) | copy-start | bytes 388
  27.6 2.0 %copy-start.35 = (f32[32]{0:T(128)S(1)}, f32[32]{0:T(128)}, u32[]{:S(2)}) copy-start(f32[32]{0:T(128)} %get-tuple-element.67) | copy-start | bytes 388
  27.6 2.0 %copy-start.37 = (f32[32]{0:T(128)S(1)}, f32[32]{0:T(128)}, u32[]{:S(2)}) copy-start(f32[32]{0:T(128)} %get-tuple-element.68) | copy-start | bytes 388
  36.3 2.4 %copy-start.4 = (bf16[16,2,4,8,128]{4,3,2,1,0:T(8,128)(2,1)S(1)}, bf16[16,2,4,8,128]{4,3,2,1,0:T(8,128)(2,1)}, u32[]{:S(2)}) copy-start(bf16[16,2,4,8,128]{4,3,2,1,0:T(8,128)(2,1)} %get-tuple-element.80) | copy-start | bytes 786436
  39.3 1.7 %copy-start.39 = (f32[32]{0:T(128)S(1)}, f32[32]{0:T(128)}, u32[]{:S(2)}) copy-start(f32[32]{0:T(128)} %get-tuple-element.22) | copy-start | bytes 388
  39.3 1.7 %copy-start.40 = (f32[32]{0:T(128)S(1)}, f32[32]{0:T(128)}, u32[]{:S(2)}) copy-start(f32[32]{0:T(128)} %get-tuple-element.23) | copy-start | bytes 388
  39.3 1.7 %copy-start.41 = (f32[32]{0:T(128)S(1)}, f32[32]{0:T(128)}, u32[]{:S(2)}) copy-start(f32[32]{0:T(128)} %get-tuple-element.24) | copy-start | bytes 388
  39.4 1.7 %copy-start.42 = (f32[32]{0:T(128)S(1)}, f32[32]{0:T(128)}, u32[]{:S(2)}) copy-start(f32[32]{0:T(128)} %get-tuple-element.25) | copy-start | bytes 388
  39.4 1.7 %copy-start.43 = (f32[32]{0:T(128)S(1)}, f32[32]{0:T(128)}, u32[]{:S(2)}) copy-start(f32[32]{0:T(128)} %get-tuple-element.26) | copy-start | bytes 388
  39.4 1.7 %copy-start.44 = (f32[32]{0:T(128)S(1)}, f32[32]{0:T(128)}, u32[]{:S(2)}) copy-start(f32[32]{0:T(128)} %get-tuple-element.27) | copy-start | bytes 388
  39.4 1.7 %copy-start.45 = (f32[32]{0:T(128)S(1)}, f32[32]{0:T(128)}, u32[]{:S(2)}) copy-start(f32[32]{0:T(128)} %get-tuple-element.28) | copy-start | bytes 388
  39.4 1.7 %copy-start.46 = (f32[32]{0:T(128)S(1)}, f32[32]{0:T(128)}, u32[]{:S(2)}) copy-start(f32[32]{0:T(128)} %get-tuple-element.29) | copy-start | bytes 388
  39.4 1.7 %copy-start.47 = (f32[32]{0:T(128)S(1)}, f32[32]{0:T(128)}, u32[]{:S(2)}) copy-start(f32[32]{0:T(128)} %get-tuple-element.30) | copy-start | bytes 388
  41.7 8.7 %collective-permute-start.10 = (f32[8992]{0:T(1024)S(1)}, f32[8992]{0:T(1024)S(1)}, u32[]{:S(2)}, u32[]{:S(2)}) collective-permute-start(f32[8992]{0:T(1024)S(1)} %broadcast_multiply_fusion), channel_id=1, source_target_pairs={{0,1},{1,0},{2,3},{3,2},{4,5},{5,4},{6,7},{7,6},{8,9},{9,8},{10,11... | collective-permute-start | bytes 107912 | tf_op jit(solution)/shard_map/ppermute | solution.py:39
  41.8 28.2 %collective-permute-start.4 = (bf16[16,32,256]{2,1,0:T(8,128)(2,1)S(1)}, bf16[16,32,256]{2,1,0:T(8,128)(2,1)S(1)}, u32[]{:S(2)}, u32[]{:S(2)}) collective-permute-start(bf16[16,32,256]{2,1,0:T(8,128)(2,1)S(1)} %gather_fusion), channel_id=1, source_target_pairs={{12,0},{0,4},{4,8},{8,12},{13,1},{1,5},{5,9},{9,13},{14,2},{2,6},{... | collective-permute-start | bytes 786440 | tf_op jit(solution)/shard_map/ppermute | solution.py:25
  48.0 22.0 %collective-permute-start.3 = (bf16[16,32,256]{2,1,0:T(8,128)(2,1)S(1)}, bf16[16,32,256]{2,1,0:T(8,128)(2,1)S(1)}, u32[]{:S(2)}, u32[]{:S(2)}) collective-permute-start(bf16[16,32,256]{2,1,0:T(8,128)(2,1)S(1)} %gather_fusion), channel_id=1, source_target_pairs={{8,0},{12,4},{0,8},{4,12},{9,1},{13,5},{1,9},{5,13},{10,2},{14,6},... | collective-permute-start | bytes 786440 | tf_op jit(solution)/shard_map/ppermute | solution.py:25
  49.5 20.5 %collective-permute-start.2 = (bf16[16,32,256]{2,1,0:T(8,128)(2,1)S(1)}, bf16[16,32,256]{2,1,0:T(8,128)(2,1)S(1)}, u32[]{:S(2)}, u32[]{:S(2)}) collective-permute-start(bf16[16,32,256]{2,1,0:T(8,128)(2,1)S(1)} %gather_fusion), channel_id=1, source_target_pairs={{4,0},{8,4},{12,8},{0,12},{5,1},{9,5},{13,9},{1,13},{6,2},{10,6},{... | collective-permute-start | bytes 786440 | tf_op jit(solution)/shard_map/ppermute | solution.py:25
  50.4 4.0 %collective-permute-start.11 = (f32[8992]{0:T(1024)S(1)}, f32[8992]{0:T(1024)S(1)}, u32[]{:S(2)}, u32[]{:S(2)}) collective-permute-start(f32[8992]{0:T(1024)S(1)} %fusion.133), channel_id=1, source_target_pairs={{0,2},{2,0},{1,3},{3,1},{4,6},{6,4},{5,7},{7,5},{8,10},{10,8},{9,1... | collective-permute-start | bytes 107912 | tf_op jit(solution)/shard_map/ppermute | solution.py:39
  54.5 13.4 %collective-permute-start.12 = (f32[8992]{0:T(1024)S(1)}, f32[8992]{0:T(1024)S(1)}, u32[]{:S(2)}, u32[]{:S(2)}) collective-permute-start(f32[8992]{0:T(1024)S(1)} %add.285), channel_id=1, source_target_pairs={{0,4},{4,0},{8,12},{12,8},{1,5},{5,1},{9,13},{13,9},{2,6},{6,2},{1... | collective-permute-start | bytes 107912 | tf_op jit(solution)/shard_map/ppermute | solution.py:39
  55.6 18.8 %collective-permute-start.9 = (bf16[16,32,2,128]{3,1,2,0:T(8,128)(2,1)S(1)}, bf16[16,32,2,128]{3,1,2,0:T(8,128)(2,1)S(1)}, u32[]{:S(2)}, u32[]{:S(2)}) collective-permute-start(bf16[16,32,2,128]{3,1,2,0:T(8,128)(2,1)S(1)} %bitcast.346), channel_id=1, source_target_pairs={{1,0},{2,1},{3,2},{5,4},{6,5},{7,6},{9,8},{10,9},{11,10},{13,12},{... | collective-permute-start | bytes 786440 | tf_op jit(solution)/shard_map/ppermute | solution.py:17
  67.9 6.5 %collective-permute-start.8 = (bf16[16,32,2,128]{3,1,2,0:T(8,128)(2,1)S(1)}, bf16[16,32,2,128]{3,1,2,0:T(8,128)(2,1)S(1)}, u32[]{:S(2)}, u32[]{:S(2)}) collective-permute-start(bf16[16,32,2,128]{3,1,2,0:T(8,128)(2,1)S(1)} %bitcast.347), channel_id=1, source_target_pairs={{0,1},{1,2},{2,3},{4,5},{5,6},{6,7},{8,9},{9,10},{10,11},{12,13},{... | collective-permute-start | bytes 786440 | tf_op jit(solution)/shard_map/ppermute | solution.py:14
  70.0 10.2 %collective-permute-start.13 = (f32[8992]{0:T(1024)S(1)}, f32[8992]{0:T(1024)S(1)}, u32[]{:S(2)}, u32[]{:S(2)}) collective-permute-start(f32[8992]{0:T(1024)S(1)} %add.286), channel_id=1, source_target_pairs={{0,8},{4,12},{8,0},{12,4},{1,9},{5,13},{9,1},{13,5},{2,10},{6,14},... | collective-permute-start | bytes 107912 | tf_op jit(solution)/shard_map/ppermute | solution.py:39
  (29 other events, 39.4 us)

commit v16 on v15

--- a/solution.py
+++ b/solution.py
@@ -3,6 +3,7 @@
 import jax
 import jax.numpy as jnp
 from jax import lax
+from jax.experimental.layout import Layout, with_layout_constraint
 from jax.sharding import PartitionSpec as P
 
 
@@ -144,6 +145,7 @@
             )
     kernel_term = jnp.stack(terms, 1)
     dirty_grad = (cotangent.astype(jnp.float32) + conv).astype(jnp.bfloat16)
+    dirty_grad = with_layout_constraint(dirty_grad, Layout((0, 1, 2, 3)))
     parts = (kernel_term, mix_term, spec_grad)
     flat = jnp.concatenate([part.reshape(-1) for part in parts]) * scale
     flat = all_summed(flat, ("sub", "tile", "chan"), tied=h_received, tie_at=3)

time: 82.9 us -> 119 us (1.44)
  other arithmetic: 14.2 us -> 47.2 us
  local copies, waits for them, and re-layouts: 11.7 us -> 16.1 us
    dot_general x2, other arithmetic: 3.05 us -> 14.5 us  [local(): jnp.einsum('cfhw,cfhw->f', dsmooth, xpad[:, :, i:i + rows, j:j + cols], p...]
    convert_element_type x1, other arithmetic: 3.04 us -> 12.7 us  [local(): dirty_grad = (cotangent.astype(jnp.float32) + conv).astype(jnp.bfloat16)]
    convert_element_type x1, other arithmetic: 3.03 us -> 12 us  [local(): smooth = total.astype(jnp.bfloat16)]
    dot_general x1, matrix products: 0.6 us -> 2.76 us  [local(): jnp.einsum('mKp,mfp->Kf', g_stack, h_sorted, preferred_element_type=jnp.f...]
    dot_general x1, matrix products: 2.31 us -> 0.29 us  [local(): jnp.einsum('gf,cghw->cfhw', feature_mix, dmixed, preferred_element_type=j...]
    convert_element_type x1, other arithmetic: 0.69 us -> 2.64 us  [local(): jnp.pad(grad_ext, ((0, 0), (0, 0), (0, 0), (2, 2))).astype(jnp.float32)]
  transfers between devices with their start and end apart: 14 -> 14, of which waited for: 4 -> 4; matrix products, arithmetic and copies ran while one was open for 15% -> 20% of each run, Pallas kernels for 0% -> 0%
where the time goes in v16:
time: 119 us
  other arithmetic  47.2 us (40%)
  starting transfers between devices  28.4 us (24%)
  waiting for transfers between devices  20.3 us (17%)
  local copies, waits for them, and re-layouts  16.1 us (14%)
  matrix products  4.72 us (4%)
  between operations  1.75 us (1%)
    ppermute x6, starting transfers between devices, passed_along(): return lax.ppermute(block, axis, route)  15.7 us
    dot_general x2, other arithmetic, local(): jnp.einsum('cfhw,cfhw->f', dsmooth, xpad[:, :, i:i + rows, j:j + cols], p...  14.5 us
    ppermute x4, waiting for transfers between devices, all_summed(): lax.ppermute(value, axis, [(i, i ^ step) for i in range(count)])  13.2 us
    convert_element_type x1, other arithmetic, local(): dirty_grad = (cotangent.astype(jnp.float32) + conv).astype(jnp.bfloat16)  12.7 us
    convert_element_type x1, other arithmetic, local(): smooth = total.astype(jnp.bfloat16)  12 us
    ppermute x6, waiting for transfers between devices, passed_along(): return lax.ppermute(block, axis, route)  7.09 us
    ppermute x4, starting transfers between devices, all_summed(): lax.ppermute(value, axis, [(i, i ^ step) for i in range(count)])  5.18 us
    ppermute x2, starting transfers between devices, padded(): lax.ppermute(lax.slice_in_dim(block, block.shape[dim] - width, None, axis...  4.98 us
  transfers between devices with their start and end apart: 14, of which 4 were waited for; matrix products, arithmetic and copies ran while one was open for 20% of the time, Pallas kernels for 0%

profile of v16, /device:TPU:0, one launch (start us, length us, event | category | flops | bytes accessed | tf_op | source)
XLA Modules:
  0.0 118.6 jit_solution(1591773298159479302)
XLA Ops:
  0.7 0.7 compare_select_fusion
  1.5 1.1 reshape.94
  2.7 0.6 gather_fusion.2
  3.2 3.1 %collective-permute-start.7 = (bf16[16,32,256]{2,1,0:T(8,128)(2,1)S(1)}, bf16[16,32,256]{2,1,0:T(8,128)(2,1)S(1)}, u32[]{:S(2)}, u32[]{:S(2)}) collective-permute-start(bf16[16,32,256]{2,1,0:T(8,128)(2,1)S(1)} %gather_fusion.2), channel_id=1, source_target_pairs={{12,0},{0,4},{4,8},{8,12},{13,1},{1,5},{5,9},{9,13},{14,2},{2,6},{... | collective-permute-start | bytes 786440 | tf_op jit(solution)/shard_map/ppermute | solution.py:26
  6.3 2.6 %collective-permute-start.6 = (bf16[16,32,256]{2,1,0:T(8,128)(2,1)S(1)}, bf16[16,32,256]{2,1,0:T(8,128)(2,1)S(1)}, u32[]{:S(2)}, u32[]{:S(2)}) collective-permute-start(bf16[16,32,256]{2,1,0:T(8,128)(2,1)S(1)} %gather_fusion.2), channel_id=1, source_target_pairs={{8,0},{12,4},{0,8},{4,12},{9,1},{13,5},{1,9},{5,13},{10,2},{14,6},... | collective-permute-start | bytes 786440 | tf_op jit(solution)/shard_map/ppermute | solution.py:26
  8.9 1.3 %collective-permute-start.5 = (bf16[16,32,256]{2,1,0:T(8,128)(2,1)S(1)}, bf16[16,32,256]{2,1,0:T(8,128)(2,1)S(1)}, u32[]{:S(2)}, u32[]{:S(2)}) collective-permute-start(bf16[16,32,256]{2,1,0:T(8,128)(2,1)S(1)} %gather_fusion.2), channel_id=1, source_target_pairs={{4,0},{8,4},{12,8},{0,12},{5,1},{9,5},{13,9},{1,13},{6,2},{10,6},{... | collective-permute-start | bytes 786440 | tf_op jit(solution)/shard_map/ppermute | solution.py:26
  10.2 1.3 %collective-permute-start.1 = (bf16[16,32,2,128]{3,2,1,0:T(2,128)(2,1)}, bf16[16,32,2,128]{3,2,1,0:T(2,128)(2,1)S(1)}, u32[]{:S(2)}, u32[]{:S(2)}) collective-permute-start(bf16[16,32,2,128]{3,2,1,0:T(2,128)(2,1)} %param.6), channel_id=1, source_target_pairs={{1,0},{2,1},{3,2},{5,4},{6,5},{7,6},{9,8},{10,9},{11,10},{13,12},{... | collective-permute-start | bytes 786440 | tf_op jit(solution)/shard_map/ppermute | solution.py:18
  11.5 3.1 %collective-permute-start = (bf16[16,32,2,128]{3,2,1,0:T(2,128)(2,1)}, bf16[16,32,2,128]{3,2,1,0:T(2,128)(2,1)S(1)}, u32[]{:S(2)}, u32[]{:S(2)}) collective-permute-start(bf16[16,32,2,128]{3,2,1,0:T(2,128)(2,1)} %param.6), channel_id=1, source_target_pairs={{0,1},{1,2},{2,3},{4,5},{5,6},{6,7},{8,9},{9,10},{10,11},{12,13},{... | collective-permute-start | bytes 786440 | tf_op jit(solution)/shard_map/ppermute | solution.py:15
  14.6 1.2 %slice_reduce_fusion.22 = (f32[32]{0:T(128)S(1)}, f32[32]{0:T(128)S(1)}, f32[32]{0:T(128)S(1)}, f32[32]{0:T(128)S(1)}, f32[32]{0:T(128)S(1)}, /*index=5*/f32[32]{0:T(128)S(1)}) fusion(f32[32,25]{1,0:T(8,128)} %param.8), kind=kLoop, calls=%fused_computation.286 | loop fusion | bytes 1536 | tf_op jit(solution)/shard_map/slice | solution.py:75
  15.8 2.0 %slice_reduce_fusion.23 = (f32[32]{0:T(128)S(1)}, f32[32]{0:T(128)S(1)}, f32[32]{0:T(128)S(1)}, f32[32]{0:T(128)S(1)}, f32[32]{0:T(128)S(1)}, /*index=5*/f32[32]...) fusion(f32[32,25]{1,0:T(8,128)} %param.8), kind=kLoop, calls=%fused_computation.287 | loop fusion | bytes 4864 | tf_op jit(solution)/shard_map/slice | solution.py:75
  18.0 0.8 rev.6
  18.9 4.3 %collective-permute-done.5 = bf16[16,32,256]{2,1,0:T(8,128)(2,1)S(1)} collective-permute-done((bf16[16,32,256]{2,1,0:T(8,128)(2,1)S(1)}, bf16[16,32,256]{2,1,0:T(8,128)(2,1)S(1)}, u32[]{:S(2)}, u32[]{:S(2)}) %collective-permute-start.5) | collective-permute-done | bytes 262176 | tf_op jit(solution)/shard_map/ppermute | solution.py:26
  23.2 2.8 %collective-permute-done.6 = bf16[16,32,256]{2,1,0:T(8,128)(2,1)S(1)} collective-permute-done((bf16[16,32,256]{2,1,0:T(8,128)(2,1)S(1)}, bf16[16,32,256]{2,1,0:T(8,128)(2,1)S(1)}, u32[]{:S(2)}, u32[]{:S(2)}) %collective-permute-start.6) | collective-permute-done | bytes 262176 | tf_op jit(solution)/shard_map/ppermute | solution.py:26
  26.4 1.2 %copy-done.1 = bf16[16,7,32,256]{3,2,0,1:T(8,128)(2,1)} copy-done((bf16[16,7,32,256]{3,2,0,1:T(8,128)(2,1)}, bf16[16,7,32,256]{3,2,0,1:T(8,128)(2,1)S(1)}, u32[]{:S(2)}) %copy-start.1) | copy-done | bytes 1835032
  27.6 0.4 fusion.8
  28.1 0.6 gather_fusion.3
  28.7 2.7 %select_maximum_fusion.2 = (bf16[16,32,6,132]{3,2,1,0:T(8,128)(2,1)S(1)}, f32[16,32,6,132]{3,2,1,0:T(8,128)S(1)}) fusion(bf16[16,32,2,128]{3,2,1,0:T(2,128)(2,1)S(1)} %collective-permute-done.1, bf16[16,32,2,128]{3,2,1,0:T(2,128)(2,1)S(1)} %copy-done.2, bf16[16,32,2,128]{3,2,1,0:T(2,128)(2,1)S(1)} %collective-permute-done), kind=kLoop, calls=%fused_computation.35 | loop fusion | flops 5271552 | bytes 3219456 | tf_op jit(solution)/shard_map/concatenate | solution.py:19
  31.6 12.0 %fusion.64 = bf16[16,32,2,128]{3,2,1,0:T(2,128)(2,1)S(1)} fusion(f32[16,32,6,132]{3,2,1,0:T(8,128)S(1)} %get-tuple-element.65, f32[32]{0:T(128)S(1)} %get-tuple-element.59, f32[32]{0:T(128)S(1)} %get-tuple-element.60, f32[32]{0:T(128)S(1)} %get-tuple-element.61, f32[32]{0:T(128)S(1)} %get-tuple-element.38, f32[32]{0:T(128)S(1)} %get-tuple-element.39, ...), kind=kLoop, calls=%fused_computation.129 | loop fusion | flops 6553600 | bytes 13372544 | tf_op jit(solution)/shard_map/convert_element_type | solution.py:78
  43.7 0.4 fusion.37
  44.3 0.3 convolution_convert_fusion
  44.7 0.7 copy.301
  45.4 1.5 %gather_fusion = bf16[16,32,256]{2,1,0:T(8,128)(2,1)S(1)} fusion(bf16[16,32,256]{2,1,0:T(8,128)(2,1)} %bitcast.347, s32[1024]{0:T(1024)S(1)} %pad_clamp_fusion.1), kind=kCustom, calls=%fused_computation | custom fusion | bytes 524352 | tf_op jit(solution)/shard_map/gather | solution.py:88
  46.9 2.8 %fusion.9 = f32[7,32,32]{2,1,0:T(8,128)} fusion(bf16[16,7,32,256]{3,2,0,1:T(8,128)(2,1)} %copy-done.1, bf16[16,32,256]{2,1,0:T(8,128)(2,1)S(1)} %gather_fusion), kind=kOutput, calls=%fused_computation.48 | convolution fusion | flops 58720256 | bytes 2125824 | tf_op jit(solution)/shard_map/mKp,mfp->Kf/dot_general | solution.py:114
  49.7 0.9 rev.7
  50.6 0.7 reshape.98
  51.3 10.7 %fusion.36 = (f32[32]{0:T(128)S(1)}, f32[32]{0:T(128)S(1)}, f32[32]{0:T(128)S(1)}, f32[32]{0:T(128)S(1)}, f32[32]{0:T(128)S(1)}, /*index=5*/f32[32]{0:T(128)S(1)...) fusion(bf16[16,32,6,132]{3,2,1,0:T(8,128)(2,1)S(1)} %get-tuple-, ...), kind=kLoop, calls=%fused_computation.74 | loop fusion | flops 7208384 | bytes 4983040 | tf_op jit(solution)/shard_map/cfhw,cfhw->f/dot_general | solution.py:139
  62.0 3.9 %fusion.35 = (f32[32]{0:T(128)S(1)}, f32[32]{0:T(128)S(1)}, f32[32]{0:T(128)S(1)}, f32[32]{0:T(128)S(1)}, f32[32]{0:T(128)S(1)}, /*index=5*/f32[32]{0:T(128)S(1)}, f32[32]{0:T(128)S(1)}) fusion(bf16[16,32,6,132]{3,2,1,0:T(8,128)(2,1)S(1)} %get-tuple-element.64, bf16[16,2,128,32]{2,3,1,0:T(8,128)(2,1)S(1)} %convolution_convert_fusion, ...), kind=kLoop, calls=%fused_computation.73 | loop fusion | flops 3931936 | bytes 1573760 | tf_op jit(solution)/shard_map/cfhw,cfhw->f/dot_general | solution.py:139
  65.9 0.8 stack.167
  67.0 6.2 %collective-permute-start.4 = (bf16[16,32,256]{2,1,0:T(8,128)(2,1)S(1)}, bf16[16,32,256]{2,1,0:T(8,128)(2,1)S(1)}, u32[]{:S(2)}, u32[]{:S(2)}) collective-permute-start(bf16[16,32,256]{2,1,0:T(8,128)(2,1)S(1)} %gather_fusion), channel_id=1, source_target_pairs={{12,0},{0,4},{4,8},{8,12},{13,1},{1,5},{5,9},{9,13},{14,2},{2,6},{... | collective-permute-start | bytes 786440 | tf_op jit(solution)/shard_map/ppermute | solution.py:26
  73.2 1.5 %collective-permute-start.3 = (bf16[16,32,256]{2,1,0:T(8,128)(2,1)S(1)}, bf16[16,32,256]{2,1,0:T(8,128)(2,1)S(1)}, u32[]{:S(2)}, u32[]{:S(2)}) collective-permute-start(bf16[16,32,256]{2,1,0:T(8,128)(2,1)S(1)} %gather_fusion), channel_id=1, source_target_pairs={{8,0},{12,4},{0,8},{4,12},{9,1},{13,5},{1,9},{5,13},{10,2},{14,6},... | collective-permute-start | bytes 786440 | tf_op jit(solution)/shard_map/ppermute | solution.py:26
  74.7 0.9 collective-permute-start.2
  75.7 1.5 %collective-permute-start.11 = (f32[8992]{0:T(1024)S(1)}, f32[8992]{0:T(1024)S(1)}, u32[]{:S(2)}, u32[]{:S(2)}) collective-permute-start(f32[8992]{0:T(1024)S(1)} %fusion.136), channel_id=1, source_target_pairs={{0,2},{2,0},{1,3},{3,1},{4,6},{6,4},{5,7},{7,5},{8,10},{10,8},{9,1... | collective-permute-start | bytes 107912 | tf_op jit(solution)/shard_map/ppermute | solution.py:40
  77.2 2.5 %collective-permute-done.11 = f32[8992]{0:T(1024)S(1)} collective-permute-done((f32[8992]{0:T(1024)S(1)}, f32[8992]{0:T(1024)S(1)}, u32[]{:S(2)}, u32[]{:S(2)}) %collective-permute-start.11) | collective-permute-done | bytes 36000 | tf_op jit(solution)/shard_map/ppermute | solution.py:40
  79.7 1.1 collective-permute-start.12
  80.8 0.2 copy.302
  81.1 1.3 %collective-permute-start.9 = (bf16[16,32,2,128]{3,2,1,0:T(2,128)(2,1)S(1)}, bf16[16,32,2,128]{3,2,1,0:T(2,128)(2,1)S(1)}, u32[]{:S(2)}, u32[]{:S(2)}) collective-permute-start(bf16[16,32,2,128]{3,2,1,0:T(2,128)(2,1)S(1)} %bitcast.344), channel_id=1, source_target_pairs={{1,0},{2,1},{3,2},{5,4},{6,5},{7,6},{9,8},{10,9},{11,10},{13,12},{... | collective-permute-start | bytes 786440 | tf_op jit(solution)/shard_map/ppermute | solution.py:18
  82.4 10.8 %collective-permute-done.12 = f32[8992]{0:T(1024)S(1)} collective-permute-done((f32[8992]{0:T(1024)S(1)}, f32[8992]{0:T(1024)S(1)}, u32[]{:S(2)}, u32[]{:S(2)}) %collective-permute-start.12) | collective-permute-done | bytes 36000 | tf_op jit(solution)/shard_map/ppermute | solution.py:40
  93.1 1.9 %collective-permute-start.8 = (bf16[16,32,2,128]{3,2,1,0:T(2,128)(2,1)S(1)}, bf16[16,32,2,128]{3,2,1,0:T(2,128)(2,1)S(1)}, u32[]{:S(2)}, u32[]{:S(2)}) collective-permute-start(bf16[16,32,2,128]{3,2,1,0:T(2,128)(2,1)S(1)} %bitcast.345), channel_id=1, source_target_pairs={{0,1},{1,2},{2,3},{4,5},{5,6},{6,7},{8,9},{9,10},{10,11},{12,13},{... | collective-permute-start | bytes 786440 | tf_op jit(solution)/shard_map/ppermute | solution.py:15
  95.1 2.5 %collective-permute-start.13 = (f32[8992]{0:T(1024)S(1)}, f32[8992]{0:T(1024)S(1)}, u32[]{:S(2)}, u32[]{:S(2)}) collective-permute-start(f32[8992]{0:T(1024)S(1)} %add.286), channel_id=1, source_target_pairs={{0,8},{4,12},{8,0},{12,4},{1,9},{5,13},{9,1},{13,5},{2,10},{6,14},... | collective-permute-start | bytes 107912 | tf_op jit(solution)/shard_map/ppermute | solution.py:40
  98.0 0.6 fusion.7
  98.6 0.6 gather_fusion.1
  99.2 0.3 reshape.101
  99.7 2.6 %fusion.1 = f32[16,32,6,132]{3,2,1,0:T(8,128)S(1)} fusion(bf16[16,32,2,128]{3,2,1,0:T(2,128)(2,1)S(1)} %collective-permute-done.9, bf16[16,32,2,128]{3,2,1,0:T(2,128)(2,1)S(1)} %bitcast.346, bf16[16,32,2,128]{3,2,1,0:T(2,128)(2,1)S(1)} %collective-permute-done.8), kind=kLoop, calls=%fused_computation.33 | loop fusion | flops 4866048 | bytes 2408448 | tf_op jit(solution)/shard_map/convert_element_type | solution.py:128
  102.6 12.7 %fusion.88 = bf16[16,32,2,128]{3,2,1,0:T(2,128)(2,1)} fusion(f32[16,32,6,132]{3,2,1,0:T(8,128)S(1)} %fusion.1, bf16[16,32,2,128]{3,2,1,0:T(2,128)(2,1)S(1)} %copy-done.3, f32[32]{0:T(128)S(1)} %get-tuple-element.59, f32[32]{0:T(128)S(1)} %copy-done.7, f32[32]{0:T(128)S(1)} %copy-done.9, f32[32]{0:T(128)S(1)} %copy-done.13, f32[32]{0:T(128)S(1)} %copy-done.15, ...), kind=kLoop, calls=%fused_computation.181 | loop fusion | flops 6815744 | bytes 13634688 | tf_op jit(solution)/shard_map/convert_element_type | solution.py:147
  115.3 1.0 add_convert_fusion
  116.4 0.7 reshape.99
  117.1 0.7 split.13
  117.8 0.7 reshape.100
  (137 shorter events, 1.9 us)
Async XLA Ops:
  0.6 43.1 %copy-start = (bf16[32,32]{1,0:T(8,128)(2,1)S(1)}, bf16[32,32]{1,0:T(8,128)(2,1)}, u32[]{:S(2)}) copy-start(bf16[32,32]{1,0:T(8,128)(2,1)} %param.9) | copy-start | bytes 6148
  3.2 22.8 %collective-permute-start.7 = (bf16[16,32,256]{2,1,0:T(8,128)(2,1)S(1)}, bf16[16,32,256]{2,1,0:T(8,128)(2,1)S(1)}, u32[]{:S(2)}, u32[]{:S(2)}) collective-permute-start(bf16[16,32,256]{2,1,0:T(8,128)(2,1)S(1)} %gather_fusion.2), channel_id=1, source_target_pairs={{12,0},{0,4},{4,8},{8,12},{13,1},{1,5},{5,9},{9,13},{14,2},{2,6},{... | collective-permute-start | bytes 786440 | tf_op jit(solution)/shard_map/ppermute | solution.py:26
  6.3 19.7 %collective-permute-start.6 = (bf16[16,32,256]{2,1,0:T(8,128)(2,1)S(1)}, bf16[16,32,256]{2,1,0:T(8,128)(2,1)S(1)}, u32[]{:S(2)}, u32[]{:S(2)}) collective-permute-start(bf16[16,32,256]{2,1,0:T(8,128)(2,1)S(1)} %gather_fusion.2), channel_id=1, source_target_pairs={{8,0},{12,4},{0,8},{4,12},{9,1},{13,5},{1,9},{5,13},{10,2},{14,6},... | collective-permute-start | bytes 786440 | tf_op jit(solution)/shard_map/ppermute | solution.py:26
  8.9 14.3 %collective-permute-start.5 = (bf16[16,32,256]{2,1,0:T(8,128)(2,1)S(1)}, bf16[16,32,256]{2,1,0:T(8,128)(2,1)S(1)}, u32[]{:S(2)}, u32[]{:S(2)}) collective-permute-start(bf16[16,32,256]{2,1,0:T(8,128)(2,1)S(1)} %gather_fusion.2), channel_id=1, source_target_pairs={{4,0},{8,4},{12,8},{0,12},{5,1},{9,5},{13,9},{1,13},{6,2},{10,6},{... | collective-permute-start | bytes 786440 | tf_op jit(solution)/shard_map/ppermute | solution.py:26
  10.2 18.4 %collective-permute-start.1 = (bf16[16,32,2,128]{3,2,1,0:T(2,128)(2,1)}, bf16[16,32,2,128]{3,2,1,0:T(2,128)(2,1)S(1)}, u32[]{:S(2)}, u32[]{:S(2)}) collective-permute-start(bf16[16,32,2,128]{3,2,1,0:T(2,128)(2,1)} %param.6), channel_id=1, source_target_pairs={{1,0},{2,1},{3,2},{5,4},{6,5},{7,6},{9,8},{10,9},{11,10},{13,12},{... | collective-permute-start | bytes 786440 | tf_op jit(solution)/shard_map/ppermute | solution.py:18
  11.5 17.1 %collective-permute-start = (bf16[16,32,2,128]{3,2,1,0:T(2,128)(2,1)}, bf16[16,32,2,128]{3,2,1,0:T(2,128)(2,1)S(1)}, u32[]{:S(2)}, u32[]{:S(2)}) collective-permute-start(bf16[16,32,2,128]{3,2,1,0:T(2,128)(2,1)} %param.6), channel_id=1, source_target_pairs={{0,1},{1,2},{2,3},{4,5},{5,6},{6,7},{8,9},{9,10},{10,11},{12,13},{... | collective-permute-start | bytes 786440 | tf_op jit(solution)/shard_map/ppermute | solution.py:15
  15.8 15.6 %copy-start.6 = (f32[32]{0:T(128)}, f32[32]{0:T(128)S(1)}, u32[]{:S(2)}) copy-start(f32[32]{0:T(128)S(1)} %get-tuple-element.60) | copy-start | bytes 388
  15.8 15.6 %copy-start.8 = (f32[32]{0:T(128)}, f32[32]{0:T(128)S(1)}, u32[]{:S(2)}) copy-start(f32[32]{0:T(128)S(1)} %get-tuple-element.61) | copy-start | bytes 388
  17.8 13.6 %copy-start.10 = (f32[32]{0:T(128)}, f32[32]{0:T(128)S(1)}, u32[]{:S(2)}) copy-start(f32[32]{0:T(128)S(1)} %get-tuple-element.37) | copy-start | bytes 388
  17.8 13.6 %copy-start.12 = (f32[32]{0:T(128)}, f32[32]{0:T(128)S(1)}, u32[]{:S(2)}) copy-start(f32[32]{0:T(128)S(1)} %get-tuple-element.38) | copy-start | bytes 388
  17.8 13.6 %copy-start.14 = (f32[32]{0:T(128)}, f32[32]{0:T(128)S(1)}, u32[]{:S(2)}) copy-start(f32[32]{0:T(128)S(1)} %get-tuple-element.39) | copy-start | bytes 388
  17.8 13.6 %copy-start.16 = (f32[32]{0:T(128)}, f32[32]{0:T(128)S(1)}, u32[]{:S(2)}) copy-start(f32[32]{0:T(128)S(1)} %get-tuple-element.40) | copy-start | bytes 388
  17.9 13.6 %copy-start.18 = (f32[32]{0:T(128)}, f32[32]{0:T(128)S(1)}, u32[]{:S(2)}) copy-start(f32[32]{0:T(128)S(1)} %get-tuple-element.41) | copy-start | bytes 388
  17.9 13.6 %copy-start.20 = (f32[32]{0:T(128)}, f32[32]{0:T(128)S(1)}, u32[]{:S(2)}) copy-start(f32[32]{0:T(128)S(1)} %get-tuple-element.42) | copy-start | bytes 388
  17.9 13.6 %copy-start.22 = (f32[32]{0:T(128)}, f32[32]{0:T(128)S(1)}, u32[]{:S(2)}) copy-start(f32[32]{0:T(128)S(1)} %get-tuple-element.43) | copy-start | bytes 388
  17.9 13.6 %copy-start.24 = (f32[32]{0:T(128)}, f32[32]{0:T(128)S(1)}, u32[]{:S(2)}) copy-start(f32[32]{0:T(128)S(1)} %get-tuple-element.44) | copy-start | bytes 388
  17.9 13.6 %copy-start.26 = (f32[32]{0:T(128)}, f32[32]{0:T(128)S(1)}, u32[]{:S(2)}) copy-start(f32[32]{0:T(128)S(1)} %get-tuple-element.45) | copy-start | bytes 388
  17.9 13.6 %copy-start.28 = (f32[32]{0:T(128)}, f32[32]{0:T(128)S(1)}, u32[]{:S(2)}) copy-start(f32[32]{0:T(128)S(1)} %get-tuple-element.46) | copy-start | bytes 388
  17.9 13.6 %copy-start.30 = (f32[32]{0:T(128)}, f32[32]{0:T(128)S(1)}, u32[]{:S(2)}) copy-start(f32[32]{0:T(128)S(1)} %get-tuple-element.47) | copy-start | bytes 388
  17.9 13.6 %copy-start.32 = (f32[32]{0:T(128)}, f32[32]{0:T(128)S(1)}, u32[]{:S(2)}) copy-start(f32[32]{0:T(128)S(1)} %get-tuple-element.48) | copy-start | bytes 388
  17.9 13.6 %copy-start.34 = (f32[32]{0:T(128)}, f32[32]{0:T(128)S(1)}, u32[]{:S(2)}) copy-start(f32[32]{0:T(128)S(1)} %get-tuple-element.49) | copy-start | bytes 388
  17.9 13.6 %copy-start.36 = (f32[32]{0:T(128)}, f32[32]{0:T(128)S(1)}, u32[]{:S(2)}) copy-start(f32[32]{0:T(128)S(1)} %get-tuple-element.50) | copy-start | bytes 388
  18.0 13.6 %copy-start.38 = (f32[32]{0:T(128)}, f32[32]{0:T(128)S(1)}, u32[]{:S(2)}) copy-start(f32[32]{0:T(128)S(1)} %get-tuple-element.51) | copy-start | bytes 388
  18.0 13.6 %copy-start.40 = (f32[32]{0:T(128)}, f32[32]{0:T(128)S(1)}, u32[]{:S(2)}) copy-start(f32[32]{0:T(128)S(1)} %get-tuple-element.52) | copy-start | bytes 388
  18.0 13.6 %copy-start.42 = (f32[32]{0:T(128)}, f32[32]{0:T(128)S(1)}, u32[]{:S(2)}) copy-start(f32[32]{0:T(128)S(1)} %get-tuple-element.53) | copy-start | bytes 388
  18.0 13.6 %copy-start.44 = (f32[32]{0:T(128)}, f32[32]{0:T(128)S(1)}, u32[]{:S(2)}) copy-start(f32[32]{0:T(128)S(1)} %get-tuple-element.54) | copy-start | bytes 388
  18.0 13.6 %copy-start.46 = (f32[32]{0:T(128)}, f32[32]{0:T(128)S(1)}, u32[]{:S(2)}) copy-start(f32[32]{0:T(128)S(1)} %get-tuple-element.55) | copy-start | bytes 388
  51.3 15.5 %copy-start.5 = (f32[7168]{0:T(1024)S(1)}, f32[7168]{0:T(1024)}, u32[]{:S(2)}) copy-start(f32[7168]{0:T(1024)} %reshape.98) | copy-start | bytes 86020
  66.9 8.8 %collective-permute-start.10 = (f32[8992]{0:T(1024)S(1)}, f32[8992]{0:T(1024)S(1)}, u32[]{:S(2)}, u32[]{:S(2)}) collective-permute-start(f32[8992]{0:T(1024)S(1)} %broadcast_multiply_fusion), channel_id=1, source_target_pairs={{0,1},{1,0},{2,3},{3,2},{4,5},{5,4},{6,7},{7,6},{8,9},{9,8},{10,11... | collective-permute-start | bytes 107912 | tf_op jit(solution)/shard_map/ppermute | solution.py:40
  67.0 28.1 %collective-permute-start.4 = (bf16[16,32,256]{2,1,0:T(8,128)(2,1)S(1)}, bf16[16,32,256]{2,1,0:T(8,128)(2,1)S(1)}, u32[]{:S(2)}, u32[]{:S(2)}) collective-permute-start(bf16[16,32,256]{2,1,0:T(8,128)(2,1)S(1)} %gather_fusion), channel_id=1, source_target_pairs={{12,0},{0,4},{4,8},{8,12},{13,1},{1,5},{5,9},{9,13},{14,2},{2,6},{... | collective-permute-start | bytes 786440 | tf_op jit(solution)/shard_map/ppermute | solution.py:26
  73.2 21.9 %collective-permute-start.3 = (bf16[16,32,256]{2,1,0:T(8,128)(2,1)S(1)}, bf16[16,32,256]{2,1,0:T(8,128)(2,1)S(1)}, u32[]{:S(2)}, u32[]{:S(2)}) collective-permute-start(bf16[16,32,256]{2,1,0:T(8,128)(2,1)S(1)} %gather_fusion), channel_id=1, source_target_pairs={{8,0},{12,4},{0,8},{4,12},{9,1},{13,5},{1,9},{5,13},{10,2},{14,6},... | collective-permute-start | bytes 786440 | tf_op jit(solution)/shard_map/ppermute | solution.py:26
  74.7 20.4 %collective-permute-start.2 = (bf16[16,32,256]{2,1,0:T(8,128)(2,1)S(1)}, bf16[16,32,256]{2,1,0:T(8,128)(2,1)S(1)}, u32[]{:S(2)}, u32[]{:S(2)}) collective-permute-start(bf16[16,32,256]{2,1,0:T(8,128)(2,1)S(1)} %gather_fusion), channel_id=1, source_target_pairs={{4,0},{8,4},{12,8},{0,12},{5,1},{9,5},{13,9},{1,13},{6,2},{10,6},{... | collective-permute-start | bytes 786440 | tf_op jit(solution)/shard_map/ppermute | solution.py:26
  75.7 4.0 %collective-permute-start.11 = (f32[8992]{0:T(1024)S(1)}, f32[8992]{0:T(1024)S(1)}, u32[]{:S(2)}, u32[]{:S(2)}) collective-permute-start(f32[8992]{0:T(1024)S(1)} %fusion.136), channel_id=1, source_target_pairs={{0,2},{2,0},{1,3},{3,1},{4,6},{6,4},{5,7},{7,5},{8,10},{10,8},{9,1... | collective-permute-start | bytes 107912 | tf_op jit(solution)/shard_map/ppermute | solution.py:40
  79.7 13.4 %collective-permute-start.12 = (f32[8992]{0:T(1024)S(1)}, f32[8992]{0:T(1024)S(1)}, u32[]{:S(2)}, u32[]{:S(2)}) collective-permute-start(f32[8992]{0:T(1024)S(1)} %add.285), channel_id=1, source_target_pairs={{0,4},{4,0},{8,12},{12,8},{1,5},{5,1},{9,13},{13,9},{2,6},{6,2},{1... | collective-permute-start | bytes 107912 | tf_op jit(solution)/shard_map/ppermute | solution.py:40
  81.1 18.6 %collective-permute-start.9 = (bf16[16,32,2,128]{3,2,1,0:T(2,128)(2,1)S(1)}, bf16[16,32,2,128]{3,2,1,0:T(2,128)(2,1)S(1)}, u32[]{:S(2)}, u32[]{:S(2)}) collective-permute-start(bf16[16,32,2,128]{3,2,1,0:T(2,128)(2,1)S(1)} %bitcast.344), channel_id=1, source_target_pairs={{1,0},{2,1},{3,2},{5,4},{6,5},{7,6},{9,8},{10,9},{11,10},{13,12},{... | collective-permute-start | bytes 786440 | tf_op jit(solution)/shard_map/ppermute | solution.py:18
  93.1 6.6 %collective-permute-start.8 = (bf16[16,32,2,128]{3,2,1,0:T(2,128)(2,1)S(1)}, bf16[16,32,2,128]{3,2,1,0:T(2,128)(2,1)S(1)}, u32[]{:S(2)}, u32[]{:S(2)}) collective-permute-start(bf16[16,32,2,128]{3,2,1,0:T(2,128)(2,1)S(1)} %bitcast.345), channel_id=1, source_target_pairs={{0,1},{1,2},{2,3},{4,5},{5,6},{6,7},{8,9},{9,10},{10,11},{12,13},{... | collective-permute-start | bytes 786440 | tf_op jit(solution)/shard_map/ppermute | solution.py:15
  95.1 2.9 %copy-start.4 = (bf16[7,32,32]{2,1,0:T(8,128)(2,1)S(1)}, bf16[7,32,32]{2,1,0:T(8,128)(2,1)}, u32[]{:S(2)}) copy-start(bf16[7,32,32]{2,1,0:T(8,128)(2,1)} %param.10) | copy-start | bytes 43012
  95.1 21.2 %collective-permute-start.13 = (f32[8992]{0:T(1024)S(1)}, f32[8992]{0:T(1024)S(1)}, u32[]{:S(2)}, u32[]{:S(2)}) collective-permute-start(f32[8992]{0:T(1024)S(1)} %add.286), channel_id=1, source_target_pairs={{0,8},{4,12},{8,0},{12,4},{1,9},{5,13},{9,1},{13,5},{2,10},{6,14},... | collective-permute-start | bytes 107912 | tf_op jit(solution)/shard_map/ppermute | solution.py:40
  99.5 2.9 %copy-start.3 = (bf16[16,32,2,128]{3,2,1,0:T(2,128)(2,1)S(1)}, bf16[16,32,2,128]{3,2,1,0:T(2,128)(2,1)}, u32[]{:S(2)}) copy-start(bf16[16,32,2,128]{3,2,1,0:T(2,128)(2,1)} %param.7) | copy-start | bytes 786436
  99.5 2.9 %copy-start.7 = (f32[32]{0:T(128)S(1)}, f32[32]{0:T(128)}, u32[]{:S(2)}) copy-start(f32[32]{0:T(128)} %copy-done.6) | copy-start | bytes 388
  99.5 2.9 %copy-start.9 = (f32[32]{0:T(128)S(1)}, f32[32]{0:T(128)}, u32[]{:S(2)}) copy-start(f32[32]{0:T(128)} %copy-done.8) | copy-start | bytes 388
  99.5 2.9 %copy-start.11 = (f32[32]{0:T(128)S(1)}, f32[32]{0:T(128)}, u32[]{:S(2)}) copy-start(f32[32]{0:T(128)} %copy-done.10) | copy-start | bytes 388
  99.5 2.9 %copy-start.13 = (f32[32]{0:T(128)S(1)}, f32[32]{0:T(128)}, u32[]{:S(2)}) copy-start(f32[32]{0:T(128)} %copy-done.12) | copy-start | bytes 388
  99.5 2.9 %copy-start.15 = (f32[32]{0:T(128)S(1)}, f32[32]{0:T(128)}, u32[]{:S(2)}) copy-start(f32[32]{0:T(128)} %copy-done.14) | copy-start | bytes 388
  99.5 2.9 %copy-start.17 = (f32[32]{0:T(128)S(1)}, f32[32]{0:T(128)}, u32[]{:S(2)}) copy-start(f32[32]{0:T(128)} %copy-done.16) | copy-start | bytes 388
  99.5 2.9 %copy-start.19 = (f32[32]{0:T(128)S(1)}, f32[32]{0:T(128)}, u32[]{:S(2)}) copy-start(f32[32]{0:T(128)} %copy-done.18) | copy-start | bytes 388
  99.6 2.9 %copy-start.21 = (f32[32]{0:T(128)S(1)}, f32[32]{0:T(128)}, u32[]{:S(2)}) copy-start(f32[32]{0:T(128)} %copy-done.20) | copy-start | bytes 388
  99.6 2.9 %copy-start.23 = (f32[32]{0:T(128)S(1)}, f32[32]{0:T(128)}, u32[]{:S(2)}) copy-start(f32[32]{0:T(128)} %copy-done.22) | copy-start | bytes 388
  (14 other events, 38.4 us)
